TPU v7x, 128 devices: a whole 4x4x4 slice. The times are simulated.
128 devices in a mesh: dom: 16 (over y_lo, z, core), mem: 8 (over y_hi, x).
Axes of the slice: x: 4, y: 4 (y_hi: 2, y_lo: 2; y = y_hi * 2 + y_lo), z: 4, core: 2. Of those that a mesh axis runs over, the one named last changes fastest.
Arguments:
- perturbations: float32 [64, 8, 128, 512], P('mem', None, 'dom'), may hold values from -50 to 50
- trajectory: bfloat16 [2, 5, 8, 128, 512], P(None, None, 'mem', 'dom'), may hold values from 0 to 1, as said below
Outputs:
- ritz: float32 [64, 8, 128, 512], P('mem', None, 'dom')
- projected: float32 [64, 64], replicated
Inputs may be any that keep to these rules, and one draw needn't show every extreme that they name: `trajectory`: every coefficient is nonnegative and the five coefficients of a cell sum to one up to rounding.
All inputs are finite; a program needn't handle non-finite values.
Results may differ from a plain program's by a relative error of at most 0.0003.
Values may be sent and summed in bfloat16 or wider, within the bound.
No kernel may reach another device: no remote copies, remote signals or barrier semaphores. Data moves between devices by JAX's collectives and lax.ppermute only.
A program may use at most 64 MiB of HBM per device.

v0:
```python
import jax
import jax.numpy as jnp
from jax import lax
from jax.sharding import PartitionSpec as P

STEPS = 2


def extended(block, sides, width):
    for axis, dim in sides:
        count = lax.axis_size(axis)
        forward = [(i, i + 1) for i in range(count - 1)]
        backward = [(target, source) for source, target in forward]
        low = lax.ppermute(
            lax.slice_in_dim(block, block.shape[dim] - width, None, axis=dim), axis, forward
        )
        high = lax.ppermute(lax.slice_in_dim(block, 0, width, axis=dim), axis, backward)
        block = jnp.concatenate([low, block, high], axis=dim)
    return block


def forward_step(field, coef):
    padded = extended(field, (("dom", 2),), 1)
    side = jnp.pad(field, ((0, 0), (0, 0), (0, 0), (1, 1)))
    result = coef[0] * field + coef[1] * padded[:, :, :-2, :] + coef[2] * padded[:, :, 2:, :]
    return result + coef[3] * side[:, :, :, :-2] + coef[4] * side[:, :, :, 2:]


def side_terms(field, coef):
    south_term = jnp.pad(coef[3] * field, ((0, 0), (0, 0), (0, 0), (0, 1)))[:, :, :, 1:]
    north_term = jnp.pad(coef[4] * field, ((0, 0), (0, 0), (0, 0), (1, 0)))[:, :, :, :-1]
    return coef[0] * field + south_term + north_term


def adjoint_weighted(field, coef):
    weighted = jnp.stack([coef[1] * field, coef[2] * field])
    padded = extended(weighted, (("dom", 3),), 1)
    return side_terms(field, coef) + padded[0, :, :, 2:, :] + padded[1, :, :, :-2, :]


def invert(gram):
    factor = jnp.linalg.cholesky(gram)
    return jax.scipy.linalg.cho_solve((factor, True), jnp.eye(gram.shape[0], dtype=jnp.float32))


def body(perturbations, trajectory):
    coeffs_low = lax.all_gather(trajectory, "mem", axis=2, tiled=True)
    coeffs = coeffs_low.astype(jnp.float32)
    field = perturbations
    for step in range(STEPS):
        field = forward_step(field, coeffs[step])
    for step in reversed(range(STEPS)):
        field = adjoint_weighted(field, coeffs[step])
    members = perturbations.shape[0]
    ncells_all = (
        perturbations.shape[1]
        * perturbations.shape[2]
        * perturbations.shape[3]
        * lax.axis_size("dom")
    )
    flat_v = perturbations.reshape(members, -1)
    flat_w = field.reshape(members, -1)
    hi = lax.Precision.HIGHEST
    all_v, all_w = (
        lax.all_gather(flat_v, "mem", axis=0, tiled=True),
        lax.all_gather(flat_w, "mem", axis=0, tiled=True),
    )
    gram = jnp.dot(all_v, all_v.T, precision=hi)
    cross = jnp.dot(all_v, all_w.T, precision=hi)
    gram, cross = lax.psum((gram, cross), "dom")
    gram = gram / ncells_all
    projected = cross / ncells_all
    inverse = invert(gram)
    rows = lax.dynamic_slice_in_dim(inverse, lax.axis_index("mem") * members, members, 0)
    ritz = jnp.dot(rows, all_w, precision=hi)
    return (ritz.reshape(perturbations.shape), projected)


def solution(mesh):
    return jax.shard_map(
        body,
        mesh=mesh,
        in_specs=(P("mem", None, "dom", None), P(None, None, "mem", "dom", None)),
        out_specs=(P("mem", None, "dom", None), P()),
        check_vma=False,
    )
```

profile of v0, /device:TPU:0, one launch (start us, length us, event | category | flops | bytes accessed | tf_op | source)
XLA Modules:
  0.0 334.4 jit_solution(14262640872063382332)
XLA Ops:
  7.2 0.0 copy-start
  7.2 0.0 all-gather.3.cloned.1.call-start
  7.2 2.9 copy.19
  10.1 0.0 all-gather.3.cloned.1.call-update
  10.2 0.0 all-gather.5.cloned.1.call-start
  10.2 1.8 fusion.41
  12.0 1.3 collective-permute-start
  13.4 1.3 collective-permute-start.1
  14.7 38.5 %all_gather.10 = bf16[2,5,8,8,512]{4,3,2,1,0:T(8,128)(2,1)S(1)} all-gather(bf16[2,5,1,8,512]{4,3,2,1,0:T(8,128)(2,1)} %param.3), channel_id=1, replica_groups=mesh['dom'=16,'mem'=8] {'mem'}, dimensions={2}, use_global_device_ids=true | all-gather | bytes 737280 | tf_op jit(solution)/shard_map/all_gather | solution.py:47
  53.1 0.2 convert_element_type.13
  53.3 0.1 slice_bitcast_fusion.8
  53.4 0.1 copy.11
  53.6 0.1 copy.13
  53.8 0.8 fusion.11
  54.5 0.2 fusion.40
  54.7 1.3 collective-permute-start.2
  56.0 1.3 collective-permute-start.3
  57.3 6.2 %collective-permute-done.3 = f32[8,8,1,512]{3,2,1,0:T(1,128)S(1)} collective-permute-done((f32[8,8,1,512]{3,2,1,0:T(1,128)S(1)}, f32[8,8,1,512]{3,2,1,0:T(1,128)S(1)}, u32[]{:S(2)}, u32[]{:S(2)}) %collective-permute-start.3) | collective-permute-done | bytes 131104 | tf_op jit(solution)/shard_map/ppermute | solution.py:17
  63.6 0.8 multiply_bitcast_fusion.3
  64.3 0.4 broadcast_multiply_fusion.1
  64.8 0.5 pad_maximum_fusion.15
  65.3 1.3 collective-permute-start.4
  66.6 6.5 %collective-permute-start.5 = (f32[2,8,8,1,512]{4,3,2,1,0:T(1,128)S(1)}, f32[2,8,8,1,512]{4,3,2,1,0:T(1,128)S(1)}, u32[]{:S(2)}, u32[]{:S(2)}) collective-permute-start(f32[2,8,8,1,512]{4,3,2,1,0:T(1,128)S(1)} %get-tuple-element.15), channel_id=1, source_target_pairs={{0,8},{8,16},{16,24},{24,32},{32,40},{40,48},{48,56},{56,64},{64,7... | collective-permute-start | bytes 786440 | tf_op jit(solution)/shard_map/ppermute | solution.py:14
  73.1 1.1 collective-permute-done.5
  74.2 0.9 multiply_bitcast_fusion.1
  75.1 0.3 multiply_bitcast_fusion
  75.4 0.5 pad_maximum_fusion.13
  75.9 1.3 collective-permute-start.6
  77.2 6.6 %collective-permute-start.7 = (f32[2,8,8,1,512]{4,3,2,1,0:T(1,128)S(1)}, f32[2,8,8,1,512]{4,3,2,1,0:T(1,128)S(1)}, u32[]{:S(2)}, u32[]{:S(2)}) collective-permute-start(f32[2,8,8,1,512]{4,3,2,1,0:T(1,128)S(1)} %get-tuple-element.13), channel_id=1, source_target_pairs={{0,8},{8,16},{16,24},{24,32},{32,40},{40,48},{48,56},{56,64},{64,7... | collective-permute-start | bytes 786440 | tf_op jit(solution)/shard_map/ppermute | solution.py:14
  83.8 0.9 collective-permute-done.7
  84.8 1.0 fusion.8
  85.8 1.6 copy.20
  87.3 0.0 all-gather.5.cloned.1.call-update
  87.4 38.5 %all-gather.3.cloned.1.call-done = f32[64,32768]{1,0:T(8,128)} async-done(((f32[8,32768]{1,0:T(8,128)}), f32[64,32768]{1,0:T(8,128)}) %all-gather.3.cloned.1.call-update) | async-done | bytes 8388624 | tf_op jit(solution)/shard_map/all_gather | solution.py:65
  125.9 10.4 %fusion.42 = f32[64,64]{0,1:T(8,128)S(1)} fusion(f32[64,32768]{1,0:T(8,128)} %all-gather.3.cloned.1.call-done), kind=kOutput, calls=%fused_computation.91 | convolution fusion | flops 1610612736 | bytes 8404992 | tf_op jit(solution)/shard_map/dot_general | solution.py:68
  136.3 105.0 %all-gather.5.cloned.1.call-done = f32[64,32768]{1,0:T(8,128)} async-done(((f32[8,32768]{1,0:T(8,128)}), f32[64,32768]{1,0:T(8,128)}) %all-gather.5.cloned.1.call-update) | async-done | bytes 8388624 | tf_op jit(solution)/shard_map/all_gather | solution.py:66
  241.3 10.4 %convolution_bitcast_fusion = f32[64,64]{0,1:T(8,128)S(1)} fusion(f32[64,32768]{1,0:T(8,128)} %all-gather.5.cloned.1.call-done, f32[64,32768]{1,0:T(8,128)} %all-gather.3.cloned.1.call-done), kind=kOutput, calls=%fused_computation.8 | convolution fusion | flops 1610612736 | bytes 16793600 | tf_op jit(solution)/shard_map/dot_general | solution.py:69
  251.7 54.5 %all-reduce.6 = (f32[64,64]{0,1:T(8,128)S(1)}, f32[64,64]{0,1:T(8,128)S(1)}) all-reduce(f32[64,64]{0,1:T(8,128)S(1)} %fusion.42, f32[64,64]{0,1:T(8,128)S(1)} %convolution_bitcast_fusion), channel_id=1, replica_groups=mesh['dom'=16,'mem'=8] {'dom'}, use_global_device_ids=true, to_apply=%region_0.1 | all-reduce | flops 8192 | bytes 65536 | tf_op jit(solution)/shard_map/psum | solution.py:70
  306.3 0.1 copy.9
  306.4 5.8 %cholesky.17 = f32[64,64]{1,0:T(8,128)S(1)} custom-call(f32[64,64]{1,0:T(8,128)S(1)} %fusion.34), custom_call_target="Cholesky" | custom-call | tf_op jit(solution)/shard_map/jit(cholesky)/cholesky | solution.py:42
  312.3 0.6 compare_reduce_fusion
  312.9 0.7 fusion.29
  313.6 4.9 %custom-call.10 = f32[1,64,64]{1,2,0:T(8,128)S(1)} custom-call(f32[1,64,64]{2,1,0:T(8,128)S(1)} %fusion.29), custom_call_target="InvertDiagBlocksLowerTriangular" | custom-call | tf_op jit(solution)/shard_map/jit(_cho_solve)/triangular_solve | solution.py:43
  318.5 0.2 fusion.32
  318.7 0.2 fusion.30
  318.9 6.4 %fusion.35 = f32[8,32768]{1,0:T(8,128)S(1)} fusion(f32[64,32768]{1,0:T(8,128)} %all-gather.5.cloned.1.call-done, f32[64,64]{1,0:T(8,128)S(1)} %fusion.30, s32[]{:T(128)S(6)} %select_n.8), kind=kOutput, calls=%fused_computation.85 | convolution fusion | flops 201326592 | bytes 9441284 | tf_op jit(solution)/shard_map/dot_general | solution.py:75
  325.3 1.6 copy.14
  326.8 0.7 copy.15
  (11 shorter events, 0.1 us)
Async XLA Ops:
  7.2 46.6 %copy-start = (f32[8,8,8,512]{3,2,1,0:T(8,128)S(1)}, f32[8,8,8,512]{3,2,1,0:T(8,128)}, u32[]{:S(2)}) copy-start(f32[8,8,8,512]{3,2,1,0:T(8,128)} %param.2) | copy-start | bytes 3145732
  7.2 118.7 %all-gather.3.cloned.1.call-start = ((), (), s32[]{:S(2)}) async-start(), calls=%async_computation | async-start | bytes 9437184 | tf_op jit(solution)/shard_map/all_gather | solution.py:65
  10.2 231.1 %all-gather.5.cloned.1.call-start = ((), (), s32[]{:S(2)}) async-start(), calls=%async_computation.1 | async-start | bytes 9437184 | tf_op jit(solution)/shard_map/all_gather | solution.py:66
  12.0 41.4 %collective-permute-start = (f32[8,8,1,512]{3,1,2,0:T(8,128)S(1)}, f32[8,8,1,512]{3,1,2,0:T(8,128)S(1)}, u32[]{:S(2)}, u32[]{:S(2)}) collective-permute-start(f32[8,8,1,512]{3,1,2,0:T(8,128)S(1)} %copy.17), channel_id=1, source_target_pairs={{0,8},{8,16},{16,24},{24,32},{32,40},{40,48},{48,56},{56,64},{64,7... | collective-permute-start | bytes 393224 | tf_op jit(solution)/shard_map/ppermute | solution.py:14
  13.4 40.2 %collective-permute-start.1 = (f32[8,8,1,512]{3,1,2,0:T(8,128)S(1)}, f32[8,8,1,512]{3,1,2,0:T(8,128)S(1)}, u32[]{:S(2)}, u32[]{:S(2)}) collective-permute-start(f32[8,8,1,512]{3,1,2,0:T(8,128)S(1)} %copy.18), channel_id=1, source_target_pairs={{8,0},{16,8},{24,16},{32,24},{40,32},{48,40},{56,48},{64,56},{72,6... | collective-permute-start | bytes 393224 | tf_op jit(solution)/shard_map/ppermute | solution.py:17
  54.7 2.6 collective-permute-start.2
  56.0 7.5 %collective-permute-start.3 = (f32[8,8,1,512]{3,2,1,0:T(1,128)S(1)}, f32[8,8,1,512]{3,2,1,0:T(1,128)S(1)}, u32[]{:S(2)}, u32[]{:S(2)}) collective-permute-start(f32[8,8,1,512]{3,2,1,0:T(1,128)S(1)} %get-tuple-element.33), channel_id=1, source_target_pairs={{8,0},{16,8},{24,16},{32,24},{40,32},{48,40},{56,48},{64,56},{72,6... | collective-permute-start | bytes 393224 | tf_op jit(solution)/shard_map/ppermute | solution.py:17
  65.3 7.8 %collective-permute-start.4 = (f32[2,8,8,1,512]{4,3,2,1,0:T(1,128)S(1)}, f32[2,8,8,1,512]{4,3,2,1,0:T(1,128)S(1)}, u32[]{:S(2)}, u32[]{:S(2)}) collective-permute-start(f32[2,8,8,1,512]{4,3,2,1,0:T(1,128)S(1)} %get-tuple-element.14), channel_id=1, source_target_pairs={{8,0},{16,8},{24,16},{32,24},{40,32},{48,40},{56,48},{64,56},{72,6... | collective-permute-start | bytes 786440 | tf_op jit(solution)/shard_map/ppermute | solution.py:17
  66.6 7.6 %collective-permute-start.5 = (f32[2,8,8,1,512]{4,3,2,1,0:T(1,128)S(1)}, f32[2,8,8,1,512]{4,3,2,1,0:T(1,128)S(1)}, u32[]{:S(2)}, u32[]{:S(2)}) collective-permute-start(f32[2,8,8,1,512]{4,3,2,1,0:T(1,128)S(1)} %get-tuple-element.15), channel_id=1, source_target_pairs={{0,8},{8,16},{16,24},{24,32},{32,40},{40,48},{48,56},{56,64},{64,7... | collective-permute-start | bytes 786440 | tf_op jit(solution)/shard_map/ppermute | solution.py:14
  75.9 7.9 %collective-permute-start.6 = (f32[2,8,8,1,512]{4,3,2,1,0:T(1,128)S(1)}, f32[2,8,8,1,512]{4,3,2,1,0:T(1,128)S(1)}, u32[]{:S(2)}, u32[]{:S(2)}) collective-permute-start(f32[2,8,8,1,512]{4,3,2,1,0:T(1,128)S(1)} %get-tuple-element.12), channel_id=1, source_target_pairs={{8,0},{16,8},{24,16},{32,24},{40,32},{48,40},{56,48},{64,56},{72,6... | collective-permute-start | bytes 786440 | tf_op jit(solution)/shard_map/ppermute | solution.py:17
  77.2 7.6 %collective-permute-start.7 = (f32[2,8,8,1,512]{4,3,2,1,0:T(1,128)S(1)}, f32[2,8,8,1,512]{4,3,2,1,0:T(1,128)S(1)}, u32[]{:S(2)}, u32[]{:S(2)}) collective-permute-start(f32[2,8,8,1,512]{4,3,2,1,0:T(1,128)S(1)} %get-tuple-element.13), channel_id=1, source_target_pairs={{0,8},{8,16},{16,24},{24,32},{32,40},{40,48},{48,56},{56,64},{64,7... | collective-permute-start | bytes 786440 | tf_op jit(solution)/shard_map/ppermute | solution.py:14
Sparse Core Ops, SparseCore 0:
  10.3 115.5 all-gather.2
  128.8 112.4 all-gather.4
where the time goes:
time: 335 us; the launch traced here: 334 us
  waiting for transfers between devices  152 us (45%)
  blocking collectives  93 us (28%)
  matrix products  27.6 us (8%)
  starting transfers between devices  21 us (6%)
  other arithmetic  17.4 us (5%)
  between operations  14.3 us (4%)
  local copies, waits for them, and re-layouts  9.26 us (3%)
    all_gather x1, waiting for transfers between devices, body(): lax.all_gather(flat_w, 'mem', axis=0, tiled=True)  105 us
    psum x1, blocking collectives, body(): gram, cross = lax.psum((gram, cross), 'dom')  54.5 us
    all_gather x1, waiting for transfers between devices, body(): lax.all_gather(flat_v, 'mem', axis=0, tiled=True)  38.5 us
    all_gather x1, blocking collectives, body(): coeffs_low = lax.all_gather(trajectory, 'mem', axis=2, tiled=True)  38.5 us
    ppermute x4, starting transfers between devices, extended(): lax.ppermute(lax.slice_in_dim(block, block.shape[dim] - width, None, axis...  15.7 us
    dot_general x1, matrix products, body(): gram = jnp.dot(all_v, all_v.T, precision=hi)  10.4 us
    dot_general x1, matrix products, body(): cross = jnp.dot(all_v, all_w.T, precision=hi)  10.4 us
    unnamed x8, local copies, waits for them, and re-layouts  6.79 us
  transfers between devices with their start and end apart: 10, of which 5 were waited for; matrix products, arithmetic and copies ran while one was open for 6% of the time, Pallas kernels for 0%

commit v1 on v0

v1 whole, which is shorter than its diff:
```python
import jax
import jax.numpy as jnp
from jax import lax
from jax.sharding import PartitionSpec as P

STEPS = 2


def halo_rows(low_src, high_src):
    count = lax.axis_size("dom")
    forward = [(i, i + 1) for i in range(count - 1)]
    backward = [(i + 1, i) for i in range(count - 1)]
    low = lax.ppermute(low_src, "dom", forward)
    high = lax.ppermute(high_src, "dom", backward)
    return low, high


def forward_step(field, coef):
    low, high = halo_rows(field[:, :, -1:, :], field[:, :, :1, :])
    padded = jnp.concatenate([low, field, high], axis=2)
    side = jnp.pad(field, ((0, 0), (0, 0), (0, 0), (1, 1)))
    result = coef[0] * field + coef[1] * padded[:, :, :-2, :] + coef[2] * padded[:, :, 2:, :]
    return result + coef[3] * side[:, :, :, :-2] + coef[4] * side[:, :, :, 2:]


def adjoint_step(field, coef):
    west = coef[1] * field
    east = coef[2] * field
    low, high = halo_rows(east[:, :, -1:, :], west[:, :, :1, :])
    west_p = jnp.concatenate([west, high], axis=2)[:, :, 1:, :]
    east_p = jnp.concatenate([low, east], axis=2)[:, :, :-1, :]
    south_term = jnp.pad(coef[3] * field, ((0, 0), (0, 0), (0, 0), (0, 1)))[:, :, :, 1:]
    north_term = jnp.pad(coef[4] * field, ((0, 0), (0, 0), (0, 0), (1, 0)))[:, :, :, :-1]
    return coef[0] * field + south_term + north_term + west_p + east_p


def invert(gram):
    factor = jnp.linalg.cholesky(gram)
    return jax.scipy.linalg.cho_solve((factor, True), jnp.eye(gram.shape[0], dtype=jnp.float32))


def body(perturbations, trajectory):
    groups = lax.axis_size("mem")
    v = lax.all_to_all(perturbations, "mem", 1, 0, tiled=True)
    coeffs = trajectory.astype(jnp.float32)
    field = v
    for step in range(STEPS):
        field = forward_step(field, coeffs[step])
    for step in reversed(range(STEPS)):
        field = adjoint_step(field, coeffs[step])
    members = v.shape[0]
    ncells_all = (
        perturbations.shape[1]
        * perturbations.shape[2]
        * perturbations.shape[3]
        * lax.axis_size("dom")
    )
    flat_v = v.reshape(members, -1)
    flat_w = field.reshape(members, -1)
    hi = lax.Precision.HIGHEST
    gram = jnp.dot(flat_v, flat_v.T, precision=hi)
    cross = jnp.dot(flat_v, flat_w.T, precision=hi)
    both = lax.psum(jnp.stack([gram, cross]), ("mem", "dom"))
    gram = both[0] / ncells_all
    projected = both[1] / ncells_all
    inverse = invert(gram)
    ritz = jnp.dot(inverse, flat_w, precision=hi).reshape(v.shape)
    ritz = lax.all_to_all(ritz, "mem", 0, 1, tiled=True)
    return (ritz, projected)


def solution(mesh):
    return jax.shard_map(
        body,
        mesh=mesh,
        in_specs=(P("mem", None, "dom", None), P(None, None, "mem", "dom", None)),
        out_specs=(P("mem", None, "dom", None), P()),
        check_vma=False,
    )
```

time: 335 us -> 180 us (0.54)
  waiting for transfers between devices: 152 us -> 41.6 us
  matrix products: 27.6 us -> 3.95 us
  blocking collectives: 93 us -> 75.1 us
  between operations: 14.3 us -> 0.92 us
  starting transfers between devices: 21 us -> 33.2 us
    all_gather x2 -> x0, waiting for transfers between devices: 143 us -> none  [the longest x1 105 us: body(): lax.all_gather(flat_w, 'mem', axis=0, tiled=True)]
    all_gather x1 -> x0, blocking collectives: 38.5 us -> none  [body(): coeffs_low = lax.all_gather(trajectory, 'mem', axis=2, tiled=True)]
    all_to_all x0 -> x2, waiting for transfers between devices: none -> 33.7 us  [the longest x1 17.2 us: body(): v = lax.all_to_all(perturbations, 'mem', 1, 0, tiled=True)]
    dot_general x3, matrix products: 27.3 us -> 3.56 us  [the longest x1 1.6 us: body(): ritz = jnp.dot(inverse, flat_w, precision=hi).reshape(v.shape)]
    psum x1, blocking collectives: 54.5 us -> 75.1 us  [body(): both = lax.psum(jnp.stack([gram, cross]), ('mem', 'dom'))]
    all_to_all x0 -> x2, starting transfers between devices: none -> 10.7 us  [the longest x1 7.17 us: body(): v = lax.all_to_all(perturbations, 'mem', 1, 0, tiled=True)]
    unnamed x8 -> x6, local copies, waits for them, and re-layouts: 6.79 us -> 4.2 us
  transfers between devices with their start and end apart: 10 -> 10, of which waited for: 5 -> 6; matrix products, arithmetic and copies ran while one was open for 6% -> 1% of each run, Pallas kernels for 0% -> 0%
where the time goes in v1:
time: 180 us; the launch traced here: 179 us
  blocking collectives  75.1 us (42%)
  waiting for transfers between devices  41.6 us (23%)
  starting transfers between devices  33.2 us (18%)
  other arithmetic  16.4 us (9%)
  local copies, waits for them, and re-layouts  7.65 us (4%)
  matrix products  3.95 us (2%)
    psum x1, blocking collectives, body(): both = lax.psum(jnp.stack([gram, cross]), ('mem', 'dom'))  75.1 us
    ppermute x4, starting transfers between devices, halo_rows(): low = lax.ppermute(low_src, 'dom', forward)  17.3 us
    all_to_all x1, waiting for transfers between devices, body(): v = lax.all_to_all(perturbations, 'mem', 1, 0, tiled=True)  17.2 us
    all_to_all x1, waiting for transfers between devices, body(): ritz = lax.all_to_all(ritz, 'mem', 0, 1, tiled=True)  16.5 us
    ppermute x4, waiting for transfers between devices, halo_rows(): high = lax.ppermute(high_src, 'dom', backward)  7.92 us
    all_to_all x1, starting transfers between devices, body(): v = lax.all_to_all(perturbations, 'mem', 1, 0, tiled=True)  7.17 us
    another operation x3, other arithmetic, invert(): factor = jnp.linalg.cholesky(gram)  6.52 us
    another operation x2, other arithmetic, invert(): jax.scipy.linalg.cho_solve((factor, True), jnp.eye(gram.shape[0], dtype=j...  5.55 us
  transfers between devices with their start and end apart: 10, of which 6 were waited for; matrix products, arithmetic and copies ran while one was open for 1% of the time, Pallas kernels for 0%

profile of v1, /device:TPU:0, one launch (start us, length us, event | category | flops | bytes accessed | tf_op | source)
XLA Modules:
  0.0 178.8 jit_solution(7549952302020914584)
XLA Ops:
  0.6 2.3 %copy.14 = f32[8,8,8,512]{3,2,0,1:T(8,128)} copy(f32[8,8,8,512]{3,2,1,0:T(8,128)} %param.2) | data formatting | bytes 2097152 | tf_op args[0]
  2.9 7.2 %all-to-all-start = ((f32[8,8,8,512]{3,2,0,1:T(8,128)}), f32[8,8,8,512]{3,2,0,1:T(8,128)S(1)}, u32[]{:S(2)}, u32[]{:S(2)}) async-start(f32[8,8,8,512]{3,2,0,1:T(8,128)} %copy.14), calls=%async_computation | async-start | bytes 2097152 | tf_op jit(solution)/shard_map/all_to_all | solution.py:44
  10.1 17.2 %all-to-all-done = f32[8,8,8,512]{3,2,0,1:T(8,128)S(1)} async-done(((f32[8,8,8,512]{3,2,0,1:T(8,128)}), f32[8,8,8,512]{3,2,0,1:T(8,128)S(1)}, u32[]{:S(2)}, u32[]{:S(2)}) %all-to-all-start) | async-done | bytes 1048608 | tf_op jit(solution)/shard_map/all_to_all | solution.py:44
  27.3 0.2 fusion.36
  27.5 1.6 collective-permute-start
  29.1 1.3 collective-permute-start.1
  30.4 0.0 collective-permute-done
  30.4 3.7 %collective-permute-done.1 = f32[64,1,1,512]{3,2,0,1:T(1,128)S(1)} collective-permute-done((f32[64,1,1,512]{3,2,0,1:T(1,128)S(1)}, f32[64,1,1,512]{3,2,0,1:T(1,128)S(1)}, u32[]{:S(2)}, u32[]{:S(2)}) %collective-permute-start.1) | collective-permute-done | bytes 131104 | tf_op jit(solution)/shard_map/ppermute | solution.py:14
  34.2 0.7 fusion.10
  34.9 0.2 fusion.35
  35.1 5.5 %collective-permute-start.2 = (f32[64,1,1,512]{3,2,0,1:T(1,128)S(1)}, f32[64,1,1,512]{3,2,0,1:T(1,128)S(1)}, u32[]{:S(2)}, u32[]{:S(2)}) collective-permute-start(f32[64,1,1,512]{3,2,0,1:T(1,128)S(1)} %get-tuple-element.18), channel_id=1, source_target_pairs={{0,8},{8,16},{16,24},{24,32},{32,40},{40,48},{48,56},{56,64},{64,7... | collective-permute-start | bytes 393224 | tf_op jit(solution)/shard_map/ppermute | solution.py:13
  40.5 1.3 collective-permute-start.3
  41.8 0.0 collective-permute-done.2
  41.8 1.9 %collective-permute-done.3 = f32[64,1,1,512]{3,2,0,1:T(1,128)S(1)} collective-permute-done((f32[64,1,1,512]{3,2,0,1:T(1,128)S(1)}, f32[64,1,1,512]{3,2,0,1:T(1,128)S(1)}, u32[]{:S(2)}, u32[]{:S(2)}) %collective-permute-start.3) | collective-permute-done | bytes 131104 | tf_op jit(solution)/shard_map/ppermute | solution.py:14
  43.8 0.8 broadcast_multiply_fusion.3
  44.6 0.5 broadcast_multiply_fusion.1
  45.0 0.1 slice.215
  45.2 5.3 %collective-permute-start.5 = (f32[64,1,1,512]{3,2,0,1:T(1,128)S(1)}, f32[64,1,1,512]{3,2,0,1:T(1,128)S(1)}, u32[]{:S(2)}, u32[]{:S(2)}) collective-permute-start(f32[64,1,1,512]{3,2,0,1:T(1,128)S(1)} %slice.215), channel_id=1, source_target_pairs={{0,8},{8,16},{16,24},{24,32},{32,40},{40,48},{48,56},{56,64},{64,7... | collective-permute-start | bytes 393224 | tf_op jit(solution)/shard_map/ppermute | solution.py:13
  50.4 0.1 slice.214
  50.5 1.3 collective-permute-start.4
  51.8 0.6 copy.23
  52.4 1.3 collective-permute-done.4
  53.8 0.9 broadcast_multiply_fusion.7
  54.7 0.4 broadcast_multiply_fusion.6
  55.1 0.1 slice.217
  55.3 5.0 %collective-permute-start.7 = (f32[64,1,1,512]{3,2,0,1:T(1,128)S(1)}, f32[64,1,1,512]{3,2,0,1:T(1,128)S(1)}, u32[]{:S(2)}, u32[]{:S(2)}) collective-permute-start(f32[64,1,1,512]{3,2,0,1:T(1,128)S(1)} %slice.217), channel_id=1, source_target_pairs={{0,8},{8,16},{16,24},{24,32},{32,40},{40,48},{48,56},{56,64},{64,7... | collective-permute-start | bytes 393224 | tf_op jit(solution)/shard_map/ppermute | solution.py:13
  60.2 0.1 slice.216
  60.3 1.3 collective-permute-start.6
  61.6 1.0 convolution_bitcast_fusion.3
  62.6 0.0 collective-permute-done.7
  62.6 1.0 collective-permute-done.6
  63.6 0.9 fusion.7
  64.5 0.6 copy.24
  65.1 1.0 convolution_bitcast_fusion.2
  66.1 75.1 %psum.7 = f32[2,64,64]{1,2,0:T(8,128)S(1)} all-reduce(f32[2,64,64]{1,2,0:T(8,128)S(1)} %pad_maximum_fusion.8), channel_id=1, replica_groups=mesh['dom'=16,'mem'=8] {'mem','dom'}, use_global_device_ids=true, to_apply=%region_0.1 | all-reduce | flops 8192 | bytes 65536 | tf_op jit(solution)/shard_map/psum | solution.py:63
  141.2 0.1 copy.16
  141.3 5.8 %cholesky.17 = f32[64,64]{1,0:T(8,128)S(1)} custom-call(f32[64,64]{1,0:T(8,128)S(1)} %fusion.28), custom_call_target="Cholesky" | custom-call | tf_op jit(solution)/shard_map/jit(cholesky)/cholesky | solution.py:38
  147.2 0.6 compare_reduce_fusion
  147.8 0.7 fusion.26
  148.5 4.9 %custom-call.10 = f32[1,64,64]{1,2,0:T(8,128)S(1)} custom-call(f32[1,64,64]{2,1,0:T(8,128)S(1)} %fusion.26), custom_call_target="InvertDiagBlocksLowerTriangular" | custom-call | tf_op jit(solution)/shard_map/jit(_cho_solve)/triangular_solve | solution.py:39
  153.4 0.2 fusion.30
  153.6 0.2 convolution_bitcast_fusion.1
  153.8 1.6 convolution_bitcast_fusion
  155.4 1.6 copy.18
  157.0 3.6 %all-to-all-start.1 = ((f32[64,1,8,512]{3,2,1,0:T(8,128)}), f32[64,1,8,512]{3,2,1,0:T(8,128)S(1)}, u32[]{:S(2)}, u32[]{:S(2)}) async-start(f32[64,1,8,512]{3,2,1,0:T(8,128)} %copy.18), calls=%async_computation.1 | async-start | bytes 2097152 | tf_op jit(solution)/shard_map/all_to_all | solution.py:68
  160.5 0.7 copy.20
  161.2 16.5 %all-to-all-done.1 = f32[64,1,8,512]{3,2,1,0:T(8,128)S(1)} async-done(((f32[64,1,8,512]{3,2,1,0:T(8,128)}), f32[64,1,8,512]{3,2,1,0:T(8,128)S(1)}, u32[]{:S(2)}, u32[]{:S(2)}) %all-to-all-start.1) | async-done | bytes 1048608 | tf_op jit(solution)/shard_map/all_to_all | solution.py:68
  177.7 1.1 copy.33
  (9 shorter events, 0.1 us)
Async XLA Ops:
  2.9 7.2 %copy-start = (bf16[2,5,1,8,512]{4,3,2,1,0:T(8,128)(2,1)S(1)}, bf16[2,5,1,8,512]{4,3,2,1,0:T(8,128)(2,1)}, u32[]{:S(2)}) copy-start(bf16[2,5,1,8,512]{4,3,2,1,0:T(8,128)(2,1)} %param.3) | copy-start | bytes 245764
  2.9 24.4 %all-to-all-start = ((f32[8,8,8,512]{3,2,0,1:T(8,128)}), f32[8,8,8,512]{3,2,0,1:T(8,128)S(1)}, u32[]{:S(2)}, u32[]{:S(2)}) async-start(f32[8,8,8,512]{3,2,0,1:T(8,128)} %copy.14), calls=%async_computation | async-start | bytes 2097152 | tf_op jit(solution)/shard_map/all_to_all | solution.py:44
  27.5 3.0 %collective-permute-start = (f32[64,1,1,512]{3,2,0,1:T(1,128)S(1)}, f32[64,1,1,512]{3,2,0,1:T(1,128)S(1)}, u32[]{:S(2)}, u32[]{:S(2)}) collective-permute-start(f32[64,1,1,512]{3,2,0,1:T(1,128)S(1)} %get-tuple-element.20), channel_id=1, source_target_pairs={{0,8},{8,16},{16,24},{24,32},{32,40},{40,48},{48,56},{56,64},{64,7... | collective-permute-start | bytes 393224 | tf_op jit(solution)/shard_map/ppermute | solution.py:13
  29.1 5.1 %collective-permute-start.1 = (f32[64,1,1,512]{3,2,0,1:T(1,128)S(1)}, f32[64,1,1,512]{3,2,0,1:T(1,128)S(1)}, u32[]{:S(2)}, u32[]{:S(2)}) collective-permute-start(f32[64,1,1,512]{3,2,0,1:T(1,128)S(1)} %get-tuple-element.21), channel_id=1, source_target_pairs={{8,0},{16,8},{24,16},{32,24},{40,32},{48,40},{56,48},{64,56},{72,6... | collective-permute-start | bytes 393224 | tf_op jit(solution)/shard_map/ppermute | solution.py:14
  35.1 6.8 %collective-permute-start.2 = (f32[64,1,1,512]{3,2,0,1:T(1,128)S(1)}, f32[64,1,1,512]{3,2,0,1:T(1,128)S(1)}, u32[]{:S(2)}, u32[]{:S(2)}) collective-permute-start(f32[64,1,1,512]{3,2,0,1:T(1,128)S(1)} %get-tuple-element.18), channel_id=1, source_target_pairs={{0,8},{8,16},{16,24},{24,32},{32,40},{40,48},{48,56},{56,64},{64,7... | collective-permute-start | bytes 393224 | tf_op jit(solution)/shard_map/ppermute | solution.py:13
  40.5 3.2 %collective-permute-start.3 = (f32[64,1,1,512]{3,2,0,1:T(1,128)S(1)}, f32[64,1,1,512]{3,2,0,1:T(1,128)S(1)}, u32[]{:S(2)}, u32[]{:S(2)}) collective-permute-start(f32[64,1,1,512]{3,2,0,1:T(1,128)S(1)} %get-tuple-element.19), channel_id=1, source_target_pairs={{8,0},{16,8},{24,16},{32,24},{40,32},{48,40},{56,48},{64,56},{72,6... | collective-permute-start | bytes 393224 | tf_op jit(solution)/shard_map/ppermute | solution.py:14
  45.2 7.3 %collective-permute-start.5 = (f32[64,1,1,512]{3,2,0,1:T(1,128)S(1)}, f32[64,1,1,512]{3,2,0,1:T(1,128)S(1)}, u32[]{:S(2)}, u32[]{:S(2)}) collective-permute-start(f32[64,1,1,512]{3,2,0,1:T(1,128)S(1)} %slice.215), channel_id=1, source_target_pairs={{0,8},{8,16},{16,24},{24,32},{32,40},{40,48},{48,56},{56,64},{64,7... | collective-permute-start | bytes 393224 | tf_op jit(solution)/shard_map/ppermute | solution.py:13
  50.5 3.2 %collective-permute-start.4 = (f32[64,1,1,512]{3,2,0,1:T(1,128)S(1)}, f32[64,1,1,512]{3,2,0,1:T(1,128)S(1)}, u32[]{:S(2)}, u32[]{:S(2)}) collective-permute-start(f32[64,1,1,512]{3,2,0,1:T(1,128)S(1)} %slice.214), channel_id=1, source_target_pairs={{8,0},{16,8},{24,16},{32,24},{40,32},{48,40},{56,48},{64,56},{72,6... | collective-permute-start | bytes 393224 | tf_op jit(solution)/shard_map/ppermute | solution.py:14
  55.3 7.3 %collective-permute-start.7 = (f32[64,1,1,512]{3,2,0,1:T(1,128)S(1)}, f32[64,1,1,512]{3,2,0,1:T(1,128)S(1)}, u32[]{:S(2)}, u32[]{:S(2)}) collective-permute-start(f32[64,1,1,512]{3,2,0,1:T(1,128)S(1)} %slice.217), channel_id=1, source_target_pairs={{0,8},{8,16},{16,24},{24,32},{32,40},{40,48},{48,56},{56,64},{64,7... | collective-permute-start | bytes 393224 | tf_op jit(solution)/shard_map/ppermute | solution.py:13
  60.3 3.2 %collective-permute-start.6 = (f32[64,1,1,512]{3,2,0,1:T(1,128)S(1)}, f32[64,1,1,512]{3,2,0,1:T(1,128)S(1)}, u32[]{:S(2)}, u32[]{:S(2)}) collective-permute-start(f32[64,1,1,512]{3,2,0,1:T(1,128)S(1)} %slice.216), channel_id=1, source_target_pairs={{8,0},{16,8},{24,16},{32,24},{40,32},{48,40},{56,48},{64,56},{72,6... | collective-permute-start | bytes 393224 | tf_op jit(solution)/shard_map/ppermute | solution.py:14
  157.0 20.8 %all-to-all-start.1 = ((f32[64,1,8,512]{3,2,1,0:T(8,128)}), f32[64,1,8,512]{3,2,1,0:T(8,128)S(1)}, u32[]{:S(2)}, u32[]{:S(2)}) async-start(f32[64,1,8,512]{3,2,1,0:T(8,128)} %copy.18), calls=%async_computation.1 | async-start | bytes 2097152 | tf_op jit(solution)/shard_map/all_to_all | solution.py:68

commit v2 on v1

v2 whole, which is shorter than its diff:
```python
import jax
import jax.numpy as jnp
from jax import lax
from jax.sharding import PartitionSpec as P

STEPS = 2


def halo(block, width, dim):
    count = lax.axis_size("dom")
    forward = [(i, i + 1) for i in range(count - 1)]
    backward = [(i + 1, i) for i in range(count - 1)]
    size = block.shape[dim]
    low = lax.ppermute(lax.slice_in_dim(block, size - width, size, axis=dim), "dom", forward)
    high = lax.ppermute(lax.slice_in_dim(block, 0, width, axis=dim), "dom", backward)
    return jnp.concatenate([low, block, high], axis=dim)


def shifted(x, offset, dim):
    pad = [(0, 0)] * x.ndim
    size = x.shape[dim]
    if offset > 0:
        pad[dim] = (0, offset)
        return lax.slice_in_dim(jnp.pad(x, pad), offset, offset + size, axis=dim)
    pad[dim] = (-offset, 0)
    return lax.slice_in_dim(jnp.pad(x, pad), 0, size, axis=dim)


def forward_step(field, coef):
    result = coef[0] * field + coef[1] * shifted(field, -1, 2) + coef[2] * shifted(field, 1, 2)
    return result + coef[3] * shifted(field, -1, 3) + coef[4] * shifted(field, 1, 3)


def adjoint_step(field, coef):
    result = coef[0] * field + shifted(coef[1] * field, 1, 2) + shifted(coef[2] * field, -1, 2)
    return result + shifted(coef[3] * field, 1, 3) + shifted(coef[4] * field, -1, 3)


def butterfly(x, axis):
    count = lax.axis_size(axis)
    bit = 1
    while bit < count:
        x = x + lax.ppermute(x, axis, [(i, i ^ bit) for i in range(count)])
        bit *= 2
    return x


def invert(gram):
    factor = jnp.linalg.cholesky(gram)
    return jax.scipy.linalg.cho_solve((factor, True), jnp.eye(gram.shape[0], dtype=jnp.float32))


def body(perturbations, trajectory):
    width = 2 * STEPS
    rows = perturbations.shape[2]
    assert width <= rows
    v = lax.all_to_all(perturbations, "mem", 1, 0, tiled=True)
    coeffs = halo(trajectory, width, 3).astype(jnp.float32)
    field = halo(v, width, 2)
    for step in range(STEPS):
        field = forward_step(field, coeffs[step])
    for step in reversed(range(STEPS)):
        field = adjoint_step(field, coeffs[step])
    field = field[:, :, width : width + rows, :]
    members = v.shape[0]
    ncells_all = (
        perturbations.shape[1]
        * perturbations.shape[2]
        * perturbations.shape[3]
        * lax.axis_size("dom")
    )
    flat_v = v.reshape(members, -1)
    flat_w = field.reshape(members, -1)
    hi = lax.Precision.HIGHEST
    gram = jnp.dot(flat_v, flat_v.T, precision=hi)
    cross = jnp.dot(flat_v, flat_w.T, precision=hi)
    both = butterfly(butterfly(jnp.stack([gram, cross]), "mem"), "dom")
    gram = both[0] / ncells_all
    projected = both[1] / ncells_all
    inverse = invert(gram)
    ritz = jnp.dot(inverse, flat_w, precision=hi).reshape(v.shape)
    ritz = lax.all_to_all(ritz, "mem", 0, 1, tiled=True)
    return (ritz, projected)


def solution(mesh):
    return jax.shard_map(
        body,
        mesh=mesh,
        in_specs=(P("mem", None, "dom", None), P(None, None, "mem", "dom", None)),
        out_specs=(P("mem", None, "dom", None), P()),
        check_vma=False,
    )
```

time: 180 us -> 119 us (0.66)
  blocking collectives: 75.1 us -> 0 us
  waiting for transfers between devices: 41.6 us -> 52.8 us
  other arithmetic: 16.4 us -> 20.2 us
    psum x1 -> x0, blocking collectives: 75.1 us -> none  [body(): both = lax.psum(jnp.stack([gram, cross]), ('mem', 'dom'))]
    ppermute x8 -> x11, waiting for transfers between devices: 7.93 us -> 24.6 us  [the longest x7 22 us: butterfly(): x = x + lax.ppermute(x, axis, [(i, i ^ bit) for i in range(count)])]
    all_to_all x1, waiting for transfers between devices: 17.2 us -> 14.4 us  [body(): v = lax.all_to_all(perturbations, 'mem', 1, 0, tiled=True)]
    all_to_all x1, waiting for transfers between devices: 16.5 us -> 13.9 us  [body(): ritz = lax.all_to_all(ritz, 'mem', 0, 1, tiled=True)]
    mul x4, other arithmetic: 2.61 us -> 5.04 us  [the longest x2 2.78 us: adjoint_step(): coef[1] * field]
    ppermute x8 -> x11, starting transfers between devices: 22.5 us -> 21.8 us  [the longest x7 16.1 us: butterfly(): x = x + lax.ppermute(x, axis, [(i, i ^ bit) for i in range(count)])]
  transfers between devices with their start and end apart: 10 -> 13, of which waited for: 6 -> 10; matrix products, arithmetic and copies ran while one was open for 1% -> 2% of each run, Pallas kernels for 0% -> 0%
where the time goes in v2:
time: 119 us
  waiting for transfers between devices  52.8 us (44%)
  starting transfers between devices  32.4 us (27%)
  other arithmetic  20.2 us (17%)
  local copies, waits for them, and re-layouts  8.67 us (7%)
  matrix products  3.94 us (3%)
    ppermute x7, waiting for transfers between devices, butterfly(): x = x + lax.ppermute(x, axis, [(i, i ^ bit) for i in range(count)])  22 us
    ppermute x7, starting transfers between devices, butterfly(): x = x + lax.ppermute(x, axis, [(i, i ^ bit) for i in range(count)])  16.1 us
    all_to_all x1, waiting for transfers between devices, body(): v = lax.all_to_all(perturbations, 'mem', 1, 0, tiled=True)  14.4 us
    all_to_all x1, waiting for transfers between devices, body(): ritz = lax.all_to_all(ritz, 'mem', 0, 1, tiled=True)  13.9 us
    all_to_all x1, starting transfers between devices, body(): v = lax.all_to_all(perturbations, 'mem', 1, 0, tiled=True)  7.04 us
    another operation x3, other arithmetic, invert(): factor = jnp.linalg.cholesky(gram)  6.52 us
    another operation x2, other arithmetic, invert(): jax.scipy.linalg.cho_solve((factor, True), jnp.eye(gram.shape[0], dtype=j...  5.55 us
    unnamed x6, local copies, waits for them, and re-layouts  4.24 us
  transfers between devices with their start and end apart: 13, of which 10 were waited for; matrix products, arithmetic and copies ran while one was open for 2% of the time, Pallas kernels for 0%

profile of v2, /device:TPU:0, one launch (start us, length us, event | category | flops | bytes accessed | tf_op | source)
XLA Modules:
  0.0 119.1 jit_solution(1339957531629805844)
XLA Ops:
  0.6 2.3 %copy.14 = f32[8,8,8,512]{3,2,0,1:T(8,128)} copy(f32[8,8,8,512]{3,2,1,0:T(8,128)} %param.2) | data formatting | bytes 2097152 | tf_op args[0]
  3.0 7.0 %all-to-all-start = ((f32[8,8,8,512]{3,2,0,1:T(8,128)}), f32[8,8,8,512]{3,2,0,1:T(8,128)S(1)}, u32[]{:S(2)}, u32[]{:S(2)}) async-start(f32[8,8,8,512]{3,2,0,1:T(8,128)} %copy.14), calls=%async_computation | async-start | bytes 2097152 | tf_op jit(solution)/shard_map/all_to_all | solution.py:57
  10.0 1.5 %collective-permute-start = (bf16[2,5,1,4,512]{4,3,2,1,0:T(4,128)(2,1)S(1)}, bf16[2,5,1,4,512]{4,3,2,1,0:T(4,128)(2,1)S(1)}, u32[]{:S(2)}, u32[]{:S(2)}) collective-permute-start(bf16[2,5,1,4,512]{4,3,2,1,0:T(4,128)(2,1)S(1)} %get-tuple-element.30), channel_id=1, source_target_pairs={{0,8},{8,16},{16,24},{24,32},{32,40},{40,48},{48,56},{56,64},{64,7... | collective-permute-start | bytes 122888 | tf_op jit(solution)/shard_map/ppermute | solution.py:14
  11.5 1.3 %collective-permute-start.1 = (bf16[2,5,1,4,512]{4,3,2,1,0:T(4,128)(2,1)S(1)}, bf16[2,5,1,4,512]{4,3,2,1,0:T(4,128)(2,1)S(1)}, u32[]{:S(2)}, u32[]{:S(2)}) collective-permute-start(bf16[2,5,1,4,512]{4,3,2,1,0:T(4,128)(2,1)S(1)} %get-tuple-element.31), channel_id=1, source_target_pairs={{8,0},{16,8},{24,16},{32,24},{40,32},{48,40},{56,48},{64,56},{72,6... | collective-permute-start | bytes 122888 | tf_op jit(solution)/shard_map/ppermute | solution.py:15
  12.8 14.4 %all-to-all-done = f32[8,8,8,512]{3,2,0,1:T(8,128)S(1)} async-done(((f32[8,8,8,512]{3,2,0,1:T(8,128)}), f32[8,8,8,512]{3,2,0,1:T(8,128)S(1)}, u32[]{:S(2)}, u32[]{:S(2)}) %all-to-all-start) | async-done | bytes 1048608 | tf_op jit(solution)/shard_map/all_to_all | solution.py:57
  27.4 1.7 %collective-permute-start.2 = (f32[64,1,4,512]{3,2,0,1:T(4,128)S(1)}, f32[64,1,4,512]{3,2,0,1:T(4,128)S(1)}, u32[]{:S(2)}, u32[]{:S(2)}) collective-permute-start(f32[64,1,4,512]{3,2,0,1:T(4,128)S(1)} %get-tuple-element.18), channel_id=1, source_target_pairs={{0,8},{8,16},{16,24},{24,32},{32,40},{40,48},{48,56},{56,64},{64,7... | collective-permute-start | bytes 1572872 | tf_op jit(solution)/shard_map/ppermute | solution.py:14
  29.0 1.3 %collective-permute-start.3 = (f32[64,1,4,512]{3,2,0,1:T(4,128)S(1)}, f32[64,1,4,512]{3,2,0,1:T(4,128)S(1)}, u32[]{:S(2)}, u32[]{:S(2)}) collective-permute-start(f32[64,1,4,512]{3,2,0,1:T(4,128)S(1)} %get-tuple-element.19), channel_id=1, source_target_pairs={{8,0},{16,8},{24,16},{32,24},{40,32},{48,40},{56,48},{64,56},{72,6... | collective-permute-start | bytes 1572872 | tf_op jit(solution)/shard_map/ppermute | solution.py:15
  30.5 0.6 copy.23
  31.1 1.0 convolution_bitcast_fusion.3
  32.1 2.5 %collective-permute-done.3 = f32[64,1,4,512]{3,2,0,1:T(4,128)S(1)} collective-permute-done((f32[64,1,4,512]{3,2,0,1:T(4,128)S(1)}, f32[64,1,4,512]{3,2,0,1:T(4,128)S(1)}, u32[]{:S(2)}, u32[]{:S(2)}) %collective-permute-start.3) | collective-permute-done | bytes 524320 | tf_op jit(solution)/shard_map/ppermute | solution.py:15
  34.6 0.4 pad_maximum_fusion
  35.0 1.2 %fusion.2 = f32[64,1,16,512]{3,2,0,1:T(8,128)S(1)} fusion(f32[64,1,16,512]{3,2,0,1:T(8,128)S(1)} %pad_maximum_fusion, f32[16,512]{1,0:T(8,128)S(1)} %get-tuple-element.25, f32[16,512]{1,0:T(8,128)S(1)} %get-tuple-element.26, f32[16,512]{1,0:T(8,128)S(1)} %get-tuple-element.27, f32[16,512]{1,0:T(8,128)S(1)} %get-tuple-element.28, ...), kind=kLoop, calls=%fused_computation.18 | loop fusion | flops 4718592 | bytes 4358144 | tf_op jit(solution)/shard_map/add | solution.py:31
  36.3 1.3 %broadcast_multiply_fusion.2 = (f32[64,1,16,512]{3,2,0,1:T(8,128)S(1)}, f32[64,1,16,512]{3,2,0,1:T(8,128)S(1)}) fusion(f32[16,512]{1,0:T(8,128)S(1)} %get-tuple-element.23, f32[64,1,16,512]{3,2,0,1:T(8,128)S(1)} %fusion.2, f32[16,512]{1,0:T(8,128)S(1)} %get-tuple-element.21, f32[16,512]{1,0:T(8,128)S(1)} %get-tuple-element.22, ...), kind=kLoop, calls=%fused_computation.51 | loop fusion | flops 5242880 | bytes 6455296 | tf_op jit(solution)/shard_map/mul | solution.py:35
  37.6 1.0 broadcast_multiply_fusion.3
  38.6 1.8 %broadcast_multiply_fusion.7 = (f32[64,1,16,512]{3,2,0,1:T(8,128)S(1)}, f32[64,1,16,512]{3,2,0,1:T(8,128)S(1)}) fusion(f32[16,512]{1,0:T(8,128)S(1)} %get-tuple-element.28, f32[64,1,16,512]{3,2,0,1:T(8,128)S(1)} %get-tuple-element.17, f32[64,1,16,512]{3,2,0,1:T(8,128)S(1)} %get-tuple-element.16, f32[64,1,16,512]{3,2,0,1:T(8,128)S(1)} %get-tuple-element.10, ...), kind=kLoop, calls=%fused_computation.56 | loop fusion | flops 3145728 | bytes 14745600 | tf_op jit(solution)/shard_map/mul | solution.py:35
  40.4 0.9 broadcast_multiply_fusion.6
  41.4 0.3 pad_slice_fusion
  41.6 0.6 pad_slice_fusion.8
  42.2 0.6 pad_slice_fusion.9
  42.9 1.3 %slice_add_fusion = f32[64,1,8,512]{3,2,0,1:T(8,128)S(1)} fusion(f32[64,1,16,512]{3,2,0,1:T(8,128)S(1)} %pad_slice_fusion.8, f32[64,1,16,512]{3,2,0,1:T(8,128)S(1)} %pad_slice_fusion.9, f32[64,1,16,512]{3,2,0,1:T(8,128)S(1)} %pad_slice_fusion, f32[64,1,16,512]{3,2,0,1:T(8,128)S(1)} %get-tuple-element.34, f32[64,1,16,512]{3,2,0,1:T(8,128)S(1)} %get-tuple-element.9, ...), kind=kLoop, calls=%fused_computation.43 | loop fusion | flops 1310720 | bytes 6307840 | tf_op jit(solution)/shard_map/add | solution.py:36
  44.2 0.6 copy.24
  44.8 1.0 convolution_bitcast_fusion.2
  45.8 1.1 collective-permute-start.4
  46.9 3.4 %collective-permute-done.4 = f32[2,64,64]{1,2,0:T(8,128)S(1)} collective-permute-done((f32[2,64,64]{1,2,0:T(8,128)S(1)}, f32[2,64,64]{1,2,0:T(8,128)S(1)}, u32[]{:S(2)}, u32[]{:S(2)}) %collective-permute-start.4) | collective-permute-done | bytes 32800 | tf_op jit(solution)/shard_map/ppermute | solution.py:43
  50.3 0.9 collective-permute-start.5
  51.3 5.3 %collective-permute-done.5 = f32[2,64,64]{1,2,0:T(8,128)S(1)} collective-permute-done((f32[2,64,64]{1,2,0:T(8,128)S(1)}, f32[2,64,64]{1,2,0:T(8,128)S(1)}, u32[]{:S(2)}, u32[]{:S(2)}) %collective-permute-start.5) | collective-permute-done | bytes 32800 | tf_op jit(solution)/shard_map/ppermute | solution.py:43
  56.6 0.3 collective-permute-start.6
  56.8 5.6 %collective-permute-done.6 = f32[2,64,64]{1,2,0:T(8,128)S(1)} collective-permute-done((f32[2,64,64]{1,2,0:T(8,128)S(1)}, f32[2,64,64]{1,2,0:T(8,128)S(1)}, u32[]{:S(2)}, u32[]{:S(2)}) %collective-permute-start.6) | collective-permute-done | bytes 32800 | tf_op jit(solution)/shard_map/ppermute | solution.py:43
  62.4 3.8 %collective-permute-start.7 = (f32[2,64,64]{1,2,0:T(8,128)S(1)}, f32[2,64,64]{1,2,0:T(8,128)S(1)}, u32[]{:S(2)}, u32[]{:S(2)}) collective-permute-start(f32[2,64,64]{1,2,0:T(8,128)S(1)} %add.134), channel_id=1, source_target_pairs={{0,8},{8,0},{16,24},{24,16},{32,40},{40,32},{48,56},{56,48},{64,72... | collective-permute-start | bytes 98312 | tf_op jit(solution)/shard_map/ppermute | solution.py:43
  66.2 0.9 collective-permute-done.7
  67.1 3.9 %collective-permute-start.8 = (f32[2,64,64]{1,2,0:T(8,128)S(1)}, f32[2,64,64]{1,2,0:T(8,128)S(1)}, u32[]{:S(2)}, u32[]{:S(2)}) collective-permute-start(f32[2,64,64]{1,2,0:T(8,128)S(1)} %add.135), channel_id=1, source_target_pairs={{0,16},{8,24},{16,0},{24,8},{32,48},{40,56},{48,32},{56,40},{64,80... | collective-permute-start | bytes 98312 | tf_op jit(solution)/shard_map/ppermute | solution.py:43
  71.0 2.4 %collective-permute-done.8 = f32[2,64,64]{1,2,0:T(8,128)S(1)} collective-permute-done((f32[2,64,64]{1,2,0:T(8,128)S(1)}, f32[2,64,64]{1,2,0:T(8,128)S(1)}, u32[]{:S(2)}, u32[]{:S(2)}) %collective-permute-start.8) | collective-permute-done | bytes 32800 | tf_op jit(solution)/shard_map/ppermute | solution.py:43
  73.5 3.8 %collective-permute-start.9 = (f32[2,64,64]{1,2,0:T(8,128)S(1)}, f32[2,64,64]{1,2,0:T(8,128)S(1)}, u32[]{:S(2)}, u32[]{:S(2)}) collective-permute-start(f32[2,64,64]{1,2,0:T(8,128)S(1)} %add.136), channel_id=1, source_target_pairs={{0,32},{8,40},{16,48},{24,56},{32,0},{40,8},{48,16},{56,24},{64,96... | collective-permute-start | bytes 98312 | tf_op jit(solution)/shard_map/ppermute | solution.py:43
  77.2 2.2 %collective-permute-done.9 = f32[2,64,64]{1,2,0:T(8,128)S(1)} collective-permute-done((f32[2,64,64]{1,2,0:T(8,128)S(1)}, f32[2,64,64]{1,2,0:T(8,128)S(1)}, u32[]{:S(2)}, u32[]{:S(2)}) %collective-permute-start.9) | collective-permute-done | bytes 32800 | tf_op jit(solution)/shard_map/ppermute | solution.py:43
  79.5 2.3 %collective-permute-start.10 = (f32[2,64,64]{1,2,0:T(8,128)S(1)}, f32[2,64,64]{1,2,0:T(8,128)S(1)}, u32[]{:S(2)}, u32[]{:S(2)}) collective-permute-start(f32[2,64,64]{1,2,0:T(8,128)S(1)} %add.137), channel_id=1, source_target_pairs={{0,64},{8,72},{16,80},{24,88},{32,96},{40,104},{48,112},{56,120},{... | collective-permute-start | bytes 98312 | tf_op jit(solution)/shard_map/ppermute | solution.py:43
  81.8 2.2 %collective-permute-done.10 = f32[2,64,64]{1,2,0:T(8,128)S(1)} collective-permute-done((f32[2,64,64]{1,2,0:T(8,128)S(1)}, f32[2,64,64]{1,2,0:T(8,128)S(1)}, u32[]{:S(2)}, u32[]{:S(2)}) %collective-permute-start.10) | collective-permute-done | bytes 32800 | tf_op jit(solution)/shard_map/ppermute | solution.py:43
  84.2 5.8 %cholesky.17 = f32[64,64]{1,0:T(8,128)S(1)} custom-call(f32[64,64]{1,0:T(8,128)S(1)} %fusion.24), custom_call_target="Cholesky" | custom-call | tf_op jit(solution)/shard_map/jit(cholesky)/cholesky | solution.py:49
  90.1 0.6 compare_reduce_fusion
  90.7 0.7 fusion.22
  91.4 4.9 %custom-call.10 = f32[1,64,64]{1,2,0:T(8,128)S(1)} custom-call(f32[1,64,64]{2,1,0:T(8,128)S(1)} %fusion.22), custom_call_target="InvertDiagBlocksLowerTriangular" | custom-call | tf_op jit(solution)/shard_map/jit(_cho_solve)/triangular_solve | solution.py:50
  96.3 0.2 fusion.26
  96.5 0.2 convolution_bitcast_fusion.1
  96.7 1.6 %convolution_bitcast_fusion = f32[64,1,8,512]{3,0,2,1:T(8,128)S(1)} fusion(f32[64,64,1]{1,0,2:T(8,128)S(1)} %convolution_bitcast_fusion.1, f32[8,8,8,512]{3,2,1,0:T(8,128)S(1)} %bitcast.86), kind=kOutput, calls=%fused_computation.37 | convolution fusion | flops 201326592 | bytes 2113536 | tf_op jit(solution)/shard_map/dot_general | solution.py:81
  98.3 1.6 %copy.18 = f32[64,1,8,512]{3,2,1,0:T(8,128)} copy(f32[64,1,8,512]{3,0,2,1:T(8,128)S(1)} %convolution_bitcast_fusion) | data formatting | bytes 2097152 | tf_op jit(solution)/shard_map/dot_general | solution.py:81
  99.9 3.6 %all-to-all-start.1 = ((f32[64,1,8,512]{3,2,1,0:T(8,128)}), f32[64,1,8,512]{3,2,1,0:T(8,128)S(1)}, u32[]{:S(2)}, u32[]{:S(2)}) async-start(f32[64,1,8,512]{3,2,1,0:T(8,128)} %copy.18), calls=%async_computation.1 | async-start | bytes 2097152 | tf_op jit(solution)/shard_map/all_to_all | solution.py:82
  103.4 0.7 copy.20
  104.1 13.9 %all-to-all-done.1 = f32[64,1,8,512]{3,2,1,0:T(8,128)S(1)} async-done(((f32[64,1,8,512]{3,2,1,0:T(8,128)}), f32[64,1,8,512]{3,2,1,0:T(8,128)S(1)}, u32[]{:S(2)}, u32[]{:S(2)}) %all-to-all-start.1) | async-done | bytes 1048608 | tf_op jit(solution)/shard_map/all_to_all | solution.py:82
  118.0 1.1 copy.33
  (22 shorter events, 0.5 us)
Async XLA Ops:
  0.6 9.4 %copy-start = (bf16[2,5,1,8,512]{4,3,2,1,0:T(8,128)(2,1)S(1)}, bf16[2,5,1,8,512]{4,3,2,1,0:T(8,128)(2,1)}, u32[]{:S(2)}) copy-start(bf16[2,5,1,8,512]{4,3,2,1,0:T(8,128)(2,1)} %param.3) | copy-start | bytes 245764
  3.0 24.2 %all-to-all-start = ((f32[8,8,8,512]{3,2,0,1:T(8,128)}), f32[8,8,8,512]{3,2,0,1:T(8,128)S(1)}, u32[]{:S(2)}, u32[]{:S(2)}) async-start(f32[8,8,8,512]{3,2,0,1:T(8,128)} %copy.14), calls=%async_computation | async-start | bytes 2097152 | tf_op jit(solution)/shard_map/all_to_all | solution.py:57
  10.0 20.3 %collective-permute-start = (bf16[2,5,1,4,512]{4,3,2,1,0:T(4,128)(2,1)S(1)}, bf16[2,5,1,4,512]{4,3,2,1,0:T(4,128)(2,1)S(1)}, u32[]{:S(2)}, u32[]{:S(2)}) collective-permute-start(bf16[2,5,1,4,512]{4,3,2,1,0:T(4,128)(2,1)S(1)} %get-tuple-element.30), channel_id=1, source_target_pairs={{0,8},{8,16},{16,24},{24,32},{32,40},{40,48},{48,56},{56,64},{64,7... | collective-permute-start | bytes 122888 | tf_op jit(solution)/shard_map/ppermute | solution.py:14
  11.5 18.8 %collective-permute-start.1 = (bf16[2,5,1,4,512]{4,3,2,1,0:T(4,128)(2,1)S(1)}, bf16[2,5,1,4,512]{4,3,2,1,0:T(4,128)(2,1)S(1)}, u32[]{:S(2)}, u32[]{:S(2)}) collective-permute-start(bf16[2,5,1,4,512]{4,3,2,1,0:T(4,128)(2,1)S(1)} %get-tuple-element.31), channel_id=1, source_target_pairs={{8,0},{16,8},{24,16},{32,24},{40,32},{48,40},{56,48},{64,56},{72,6... | collective-permute-start | bytes 122888 | tf_op jit(solution)/shard_map/ppermute | solution.py:15
  27.4 4.7 %collective-permute-start.2 = (f32[64,1,4,512]{3,2,0,1:T(4,128)S(1)}, f32[64,1,4,512]{3,2,0,1:T(4,128)S(1)}, u32[]{:S(2)}, u32[]{:S(2)}) collective-permute-start(f32[64,1,4,512]{3,2,0,1:T(4,128)S(1)} %get-tuple-element.18), channel_id=1, source_target_pairs={{0,8},{8,16},{16,24},{24,32},{32,40},{40,48},{48,56},{56,64},{64,7... | collective-permute-start | bytes 1572872 | tf_op jit(solution)/shard_map/ppermute | solution.py:14
  29.0 5.6 %collective-permute-start.3 = (f32[64,1,4,512]{3,2,0,1:T(4,128)S(1)}, f32[64,1,4,512]{3,2,0,1:T(4,128)S(1)}, u32[]{:S(2)}, u32[]{:S(2)}) collective-permute-start(f32[64,1,4,512]{3,2,0,1:T(4,128)S(1)} %get-tuple-element.19), channel_id=1, source_target_pairs={{8,0},{16,8},{24,16},{32,24},{40,32},{48,40},{56,48},{64,56},{72,6... | collective-permute-start | bytes 1572872 | tf_op jit(solution)/shard_map/ppermute | solution.py:15
  45.8 4.5 %collective-permute-start.4 = (f32[2,64,64]{1,2,0:T(8,128)S(1)}, f32[2,64,64]{1,2,0:T(8,128)S(1)}, u32[]{:S(2)}, u32[]{:S(2)}) collective-permute-start(f32[2,64,64]{1,2,0:T(8,128)S(1)} %pad_maximum_fusion.1), channel_id=1, source_target_pairs={{0,1},{1,0},{2,3},{3,2},{4,5},{5,4},{6,7},{7,6},{8,9},{9,8},{10,11... | collective-permute-start | bytes 98312 | tf_op jit(solution)/shard_map/ppermute | solution.py:43
  50.3 6.2 %collective-permute-start.5 = (f32[2,64,64]{1,2,0:T(8,128)S(1)}, f32[2,64,64]{1,2,0:T(8,128)S(1)}, u32[]{:S(2)}, u32[]{:S(2)}) collective-permute-start(f32[2,64,64]{1,2,0:T(8,128)S(1)} %fusion.29), channel_id=1, source_target_pairs={{0,2},{1,3},{2,0},{3,1},{4,6},{5,7},{6,4},{7,5},{8,10},{9,11},{10,... | collective-permute-start | bytes 98312 | tf_op jit(solution)/shard_map/ppermute | solution.py:43
  56.6 5.8 %collective-permute-start.6 = (f32[2,64,64]{1,2,0:T(8,128)S(1)}, f32[2,64,64]{1,2,0:T(8,128)S(1)}, u32[]{:S(2)}, u32[]{:S(2)}) collective-permute-start(f32[2,64,64]{1,2,0:T(8,128)S(1)} %fusion.40), channel_id=1, source_target_pairs={{0,4},{1,5},{2,6},{3,7},{4,0},{5,1},{6,2},{7,3},{8,12},{9,13},{10,... | collective-permute-start | bytes 98312 | tf_op jit(solution)/shard_map/ppermute | solution.py:43
  62.4 4.7 %collective-permute-start.7 = (f32[2,64,64]{1,2,0:T(8,128)S(1)}, f32[2,64,64]{1,2,0:T(8,128)S(1)}, u32[]{:S(2)}, u32[]{:S(2)}) collective-permute-start(f32[2,64,64]{1,2,0:T(8,128)S(1)} %add.134), channel_id=1, source_target_pairs={{0,8},{8,0},{16,24},{24,16},{32,40},{40,32},{48,56},{56,48},{64,72... | collective-permute-start | bytes 98312 | tf_op jit(solution)/shard_map/ppermute | solution.py:43
  67.1 6.4 %collective-permute-start.8 = (f32[2,64,64]{1,2,0:T(8,128)S(1)}, f32[2,64,64]{1,2,0:T(8,128)S(1)}, u32[]{:S(2)}, u32[]{:S(2)}) collective-permute-start(f32[2,64,64]{1,2,0:T(8,128)S(1)} %add.135), channel_id=1, source_target_pairs={{0,16},{8,24},{16,0},{24,8},{32,48},{40,56},{48,32},{56,40},{64,80... | collective-permute-start | bytes 98312 | tf_op jit(solution)/shard_map/ppermute | solution.py:43
  73.5 6.0 %collective-permute-start.9 = (f32[2,64,64]{1,2,0:T(8,128)S(1)}, f32[2,64,64]{1,2,0:T(8,128)S(1)}, u32[]{:S(2)}, u32[]{:S(2)}) collective-permute-start(f32[2,64,64]{1,2,0:T(8,128)S(1)} %add.136), channel_id=1, source_target_pairs={{0,32},{8,40},{16,48},{24,56},{32,0},{40,8},{48,16},{56,24},{64,96... | collective-permute-start | bytes 98312 | tf_op jit(solution)/shard_map/ppermute | solution.py:43
  79.5 4.6 %collective-permute-start.10 = (f32[2,64,64]{1,2,0:T(8,128)S(1)}, f32[2,64,64]{1,2,0:T(8,128)S(1)}, u32[]{:S(2)}, u32[]{:S(2)}) collective-permute-start(f32[2,64,64]{1,2,0:T(8,128)S(1)} %add.137), channel_id=1, source_target_pairs={{0,64},{8,72},{16,80},{24,88},{32,96},{40,104},{48,112},{56,120},{... | collective-permute-start | bytes 98312 | tf_op jit(solution)/shard_map/ppermute | solution.py:43
  99.9 18.1 %all-to-all-start.1 = ((f32[64,1,8,512]{3,2,1,0:T(8,128)}), f32[64,1,8,512]{3,2,1,0:T(8,128)S(1)}, u32[]{:S(2)}, u32[]{:S(2)}) async-start(f32[64,1,8,512]{3,2,1,0:T(8,128)} %copy.18), calls=%async_computation.1 | async-start | bytes 2097152 | tf_op jit(solution)/shard_map/all_to_all | solution.py:82

commit v3 on v2

--- a/solution.py
+++ b/solution.py
@@ -36,13 +36,19 @@
     return result + shifted(coef[3] * field, 1, 3) + shifted(coef[4] * field, -1, 3)
 
 
-def butterfly(x, axis):
+def butterfly_bits():
+    bits = []
+    for axis in ("mem", "dom"):
+        bit = 1
+        while bit < lax.axis_size(axis):
+            bits.append((axis, bit))
+            bit *= 2
+    return bits
+
+
+def exchange(x, axis, bit):
     count = lax.axis_size(axis)
-    bit = 1
-    while bit < count:
-        x = x + lax.ppermute(x, axis, [(i, i ^ bit) for i in range(count)])
-        bit *= 2
-    return x
+    return x + lax.ppermute(x, axis, [(i, i ^ bit) for i in range(count)])
 
 
 def invert(gram):
@@ -54,14 +60,8 @@
     width = 2 * STEPS
     rows = perturbations.shape[2]
     assert width <= rows
+    coeffs = halo(trajectory, width, 3).astype(jnp.float32)
     v = lax.all_to_all(perturbations, "mem", 1, 0, tiled=True)
-    coeffs = halo(trajectory, width, 3).astype(jnp.float32)
-    field = halo(v, width, 2)
-    for step in range(STEPS):
-        field = forward_step(field, coeffs[step])
-    for step in reversed(range(STEPS)):
-        field = adjoint_step(field, coeffs[step])
-    field = field[:, :, width : width + rows, :]
     members = v.shape[0]
     ncells_all = (
         perturbations.shape[1]
@@ -69,15 +69,31 @@
         * perturbations.shape[3]
         * lax.axis_size("dom")
     )
+    hi = lax.Precision.HIGHEST
     flat_v = v.reshape(members, -1)
+    gram = jnp.dot(flat_v, flat_v.T, precision=hi)
+    bits = butterfly_bits()
+    done = 0
+    field = halo(v, width, 2)
+    plan = [(forward_step, s) for s in range(STEPS)]
+    plan += [(adjoint_step, s) for s in reversed(range(STEPS))]
+    for apply, step in plan:
+        field = apply(field, coeffs[step])
+        if done < len(bits):
+            gram = exchange(gram, *bits[done])
+            done += 1
+        gram, field = lax.optimization_barrier((gram, field))
+    field = field[:, :, width : width + rows, :]
     flat_w = field.reshape(members, -1)
-    hi = lax.Precision.HIGHEST
-    gram = jnp.dot(flat_v, flat_v.T, precision=hi)
     cross = jnp.dot(flat_v, flat_w.T, precision=hi)
-    both = butterfly(butterfly(jnp.stack([gram, cross]), "mem"), "dom")
-    gram = both[0] / ncells_all
-    projected = both[1] / ncells_all
-    inverse = invert(gram)
+    both = jnp.stack([gram, cross])
+    for axis, bit in bits[done:]:
+        both = exchange(both, axis, bit)
+    gram, cross = both[0], both[1]
+    for axis, bit in bits[:done]:
+        cross = exchange(cross, axis, bit)
+    inverse = invert(gram / ncells_all)
+    projected = cross / ncells_all
     ritz = jnp.dot(inverse, flat_w, precision=hi).reshape(v.shape)
     ritz = lax.all_to_all(ritz, "mem", 0, 1, tiled=True)
     return (ritz, projected)

time: 119 us -> 120 us (level); the launches traced: 119 us -> 118 us
  starting transfers between devices: 32.4 us -> 39.3 us
  waiting for transfers between devices: 52.8 us -> 45.9 us
  local copies, waits for them, and re-layouts: 8.67 us -> 7.39 us
    all_to_all x1, waiting for transfers between devices: 13.9 us -> 0.01 us  [body(): ritz = lax.all_to_all(ritz, 'mem', 0, 1, tiled=True)]
    ppermute x7 -> x11, waiting for transfers between devices: 22 us -> 31.5 us  [exchange(): return x + lax.ppermute(x, axis, [(i, i ^ bit) for i in range(count)])]
    ppermute x7 -> x11, starting transfers between devices: 16.1 us -> 22.7 us  [exchange(): return x + lax.ppermute(x, axis, [(i, i ^ bit) for i in range(count)])]
    mul x2 -> x0, other arithmetic: 2.78 us -> none  [adjoint_step(): coef[1] * field]
    ppermute x2, waiting for transfers between devices: 2.54 us -> 0.01 us  [halo(): lax.ppermute(lax.slice_in_dim(block, 0, width, axis=dim), 'dom', backward)]
    add x1 -> x2, other arithmetic: 1.32 us -> 3.4 us  [adjoint_step(): result + shifted(coef[3] * field, 1, 3) + shifted(coef[4] * field, -1, 3)]
    slice x3 -> x0, local copies, waits for them, and re-layouts: 1.49 us -> none  [the longest x2 0.88 us: shifted(): return lax.slice_in_dim(jnp.pad(x, pad), 0, size, axis=dim)]
    add x1 -> x2, other arithmetic: 1.24 us -> 2.47 us  [forward_step(): result + coef[3] * shifted(field, -1, 3) + coef[4] * shifted(field, 1, 3)]
  transfers between devices with their start and end apart: 13 -> 17, of which waited for: 10 -> 11; matrix products, arithmetic and copies ran while one was open for 2% -> 8% of each run, Pallas kernels for 0% -> 0%
where the time goes in v3:
time: 120 us; the launch traced here: 118 us
  waiting for transfers between devices  45.9 us (38%)
  starting transfers between devices  39.3 us (33%)
  other arithmetic  20.8 us (17%)
  local copies, waits for them, and re-layouts  7.39 us (6%)
  matrix products  3.93 us (3%)
    ppermute x11, waiting for transfers between devices, exchange(): return x + lax.ppermute(x, axis, [(i, i ^ bit) for i in range(count)])  31.5 us
    ppermute x11, starting transfers between devices, exchange(): return x + lax.ppermute(x, axis, [(i, i ^ bit) for i in range(count)])  22.7 us
    all_to_all x1, waiting for transfers between devices, body(): v = lax.all_to_all(perturbations, 'mem', 1, 0, tiled=True)  14.4 us
    all_to_all x1, starting transfers between devices, body(): v = lax.all_to_all(perturbations, 'mem', 1, 0, tiled=True)  7.04 us
    another operation x3, other arithmetic, invert(): factor = jnp.linalg.cholesky(gram)  6.52 us
    another operation x2, other arithmetic, invert(): jax.scipy.linalg.cho_solve((factor, True), jnp.eye(gram.shape[0], dtype=j...  5.55 us
    unnamed x6, local copies, waits for them, and re-layouts  4.24 us
    all_to_all x1, starting transfers between devices, body(): ritz = lax.all_to_all(ritz, 'mem', 0, 1, tiled=True)  3.82 us
  transfers between devices with their start and end apart: 17, of which 11 were waited for; matrix products, arithmetic and copies ran while one was open for 8% of the time, Pallas kernels for 0%

profile of v3, /device:TPU:0, one launch (start us, length us, event | category | flops | bytes accessed | tf_op | source)
XLA Modules:
  0.0 118.2 jit_solution(18027409241222913486)
XLA Ops:
  0.6 2.3 %copy.16 = f32[8,8,8,512]{3,2,0,1:T(8,128)} copy(f32[8,8,8,512]{3,2,1,0:T(8,128)} %param.2) | data formatting | bytes 2097152 | tf_op args[0]
  3.0 7.0 %all-to-all-start = ((f32[8,8,8,512]{3,2,0,1:T(8,128)}), f32[8,8,8,512]{3,2,0,1:T(8,128)S(1)}, u32[]{:S(2)}, u32[]{:S(2)}) async-start(f32[8,8,8,512]{3,2,0,1:T(8,128)} %copy.16), calls=%async_computation | async-start | bytes 2097152 | tf_op jit(solution)/shard_map/all_to_all | solution.py:64
  10.0 1.5 %collective-permute-start.1 = (bf16[2,5,1,4,512]{4,3,2,1,0:T(4,128)(2,1)S(1)}, bf16[2,5,1,4,512]{4,3,2,1,0:T(4,128)(2,1)S(1)}, u32[]{:S(2)}, u32[]{:S(2)}) collective-permute-start(bf16[2,5,1,4,512]{4,3,2,1,0:T(4,128)(2,1)S(1)} %get-tuple-element.44), channel_id=1, source_target_pairs={{0,8},{8,16},{16,24},{24,32},{32,40},{40,48},{48,56},{56,64},{64,7... | collective-permute-start | bytes 122888 | tf_op jit(solution)/shard_map/ppermute | solution.py:14
  11.5 1.3 %collective-permute-start.2 = (bf16[2,5,1,4,512]{4,3,2,1,0:T(4,128)(2,1)S(1)}, bf16[2,5,1,4,512]{4,3,2,1,0:T(4,128)(2,1)S(1)}, u32[]{:S(2)}, u32[]{:S(2)}) collective-permute-start(bf16[2,5,1,4,512]{4,3,2,1,0:T(4,128)(2,1)S(1)} %get-tuple-element.45), channel_id=1, source_target_pairs={{8,0},{16,8},{24,16},{32,24},{40,32},{48,40},{56,48},{64,56},{72,6... | collective-permute-start | bytes 122888 | tf_op jit(solution)/shard_map/ppermute | solution.py:15
  12.8 14.4 %all-to-all-done = f32[8,8,8,512]{3,2,0,1:T(8,128)S(1)} async-done(((f32[8,8,8,512]{3,2,0,1:T(8,128)}), f32[8,8,8,512]{3,2,0,1:T(8,128)S(1)}, u32[]{:S(2)}, u32[]{:S(2)}) %all-to-all-start) | async-done | bytes 1048608 | tf_op jit(solution)/shard_map/all_to_all | solution.py:64
  27.4 1.7 %collective-permute-start.3 = (f32[64,1,4,512]{3,2,0,1:T(4,128)S(1)}, f32[64,1,4,512]{3,2,0,1:T(4,128)S(1)}, u32[]{:S(2)}, u32[]{:S(2)}) collective-permute-start(f32[64,1,4,512]{3,2,0,1:T(4,128)S(1)} %get-tuple-element.32), channel_id=1, source_target_pairs={{0,8},{8,16},{16,24},{24,32},{32,40},{40,48},{48,56},{56,64},{64,7... | collective-permute-start | bytes 1572872 | tf_op jit(solution)/shard_map/ppermute | solution.py:14
  29.0 1.3 %collective-permute-start.4 = (f32[64,1,4,512]{3,2,0,1:T(4,128)S(1)}, f32[64,1,4,512]{3,2,0,1:T(4,128)S(1)}, u32[]{:S(2)}, u32[]{:S(2)}) collective-permute-start(f32[64,1,4,512]{3,2,0,1:T(4,128)S(1)} %get-tuple-element.33), channel_id=1, source_target_pairs={{8,0},{16,8},{24,16},{32,24},{40,32},{48,40},{56,48},{64,56},{72,6... | collective-permute-start | bytes 1572872 | tf_op jit(solution)/shard_map/ppermute | solution.py:15
  30.4 0.6 copy.26
  31.1 1.0 fusion.36
  32.0 0.6 collective-permute-start
  32.7 3.4 %collective-permute-done = f32[64,64]{0,1:T(8,128)S(1)} collective-permute-done((f32[64,64]{0,1:T(8,128)S(1)}, f32[64,64]{0,1:T(8,128)S(1)}, u32[]{:S(2)}, u32[]{:S(2)}) %collective-permute-start) | collective-permute-done | bytes 16416 | tf_op jit(solution)/shard_map/ppermute | solution.py:51
  36.0 0.4 pad_maximum_fusion
  36.4 1.2 %fusion.2 = f32[64,1,16,512]{3,2,0,1:T(8,128)S(1)} fusion(f32[64,1,16,512]{3,2,0,1:T(8,128)S(1)} %pad_maximum_fusion, f32[16,512]{1,0:T(8,128)S(1)} %get-tuple-element.39, f32[16,512]{1,0:T(8,128)S(1)} %get-tuple-element.40, f32[16,512]{1,0:T(8,128)S(1)} %get-tuple-element.41, f32[16,512]{1,0:T(8,128)S(1)} %get-tuple-element.42, ...), kind=kLoop, calls=%fused_computation.18 | loop fusion | flops 4718592 | bytes 4358144 | tf_op jit(solution)/shard_map/add | solution.py:31
  37.7 1.2 %collective-permute-start.5 = (f32[64,64]{0,1:T(8,128)S(1)}, f32[64,64]{0,1:T(8,128)S(1)}, u32[]{:S(2)}, u32[]{:S(2)}) collective-permute-start(f32[64,64]{0,1:T(8,128)S(1)} %add.128), channel_id=1, source_target_pairs={{0,2},{1,3},{2,0},{3,1},{4,6},{5,7},{6,4},{7,5},{8,10},{9,11},{10,... | collective-permute-start | bytes 49160 | tf_op jit(solution)/shard_map/ppermute | solution.py:51
  38.9 1.2 %fusion.6 = f32[64,1,16,512]{3,2,0,1:T(8,128)S(1)} fusion(f32[64,1,16,512]{3,2,0,1:T(8,128)S(1)} %fusion.2, f32[16,512]{1,0:T(8,128)S(1)} %get-tuple-element.35, f32[16,512]{1,0:T(8,128)S(1)} %get-tuple-element.36, f32[16,512]{1,0:T(8,128)S(1)} %get-tuple-element.37, f32[16,512]{1,0:T(8,128)S(1)} %get-tuple-element.38, f32[16,512]{1,0:T(8,128)S(1)} %get-tuple-element.34), kind=kLoop, calls=%fused_computation.22 | loop fusion | flops 4718592 | bytes 4358144 | tf_op jit(solution)/shard_map/add | solution.py:31
  40.2 3.0 %collective-permute-done.5 = f32[64,64]{0,1:T(8,128)S(1)} collective-permute-done((f32[64,64]{0,1:T(8,128)S(1)}, f32[64,64]{0,1:T(8,128)S(1)}, u32[]{:S(2)}, u32[]{:S(2)}) %collective-permute-start.5) | collective-permute-done | bytes 16416 | tf_op jit(solution)/shard_map/ppermute | solution.py:51
  43.2 0.6 collective-permute-start.6
  43.8 1.2 %broadcast_multiply_fusion.2 = (f32[64,1,16,512]{3,2,0,1:T(8,128)S(1)}, f32[64,1,16,512]{3,2,0,1:T(8,128)S(1)}, f32[64,1,16,512]{3,2,0,1:T(8,128)S(1)}, f32[64,1,16,512]{3,2,0,1:T(8,128)S(1)}) fusion(f32[64,1,16,512]{3,2,0,1:T(8,128)S(1)} %fusion.6, f32[16,512]{1,0:T(8,128)S(1)} %get-tuple-element.37, f32[16,512]{1,0:T(8,128)S(1)} %get-tuple-element.35, ...), kind=kLoop, calls=%fused_computation.49 | loop fusion | flops 2097152 | bytes 10616832 | tf_op jit(solution)/shard_map/mul | solution.py:35
  45.0 1.7 %fusion.9 = f32[64,1,16,512]{3,2,0,1:T(8,128)S(1)} fusion(f32[64,1,16,512]{3,2,0,1:T(8,128)S(1)} %get-tuple-element.30, f32[64,1,16,512]{3,2,0,1:T(8,128)S(1)} %get-tuple-element.29, f32[64,1,16,512]{3,2,0,1:T(8,128)S(1)} %get-tuple-element.31, f32[64,1,16,512]{3,2,0,1:T(8,128)S(1)} %get-tuple-element.28, f32[64,1,16,512]{3,2,0,1:T(8,128)S(1)} %fusion.6, ...), kind=kLoop, calls=%fused_computation.25 | loop fusion | flops 2621440 | bytes 12615680 | tf_op jit(solution)/shard_map/add | solution.py:36
  46.7 1.9 %collective-permute-done.6 = f32[64,64]{0,1:T(8,128)S(1)} collective-permute-done((f32[64,64]{0,1:T(8,128)S(1)}, f32[64,64]{0,1:T(8,128)S(1)}, u32[]{:S(2)}, u32[]{:S(2)}) %collective-permute-start.6) | collective-permute-done | bytes 16416 | tf_op jit(solution)/shard_map/ppermute | solution.py:51
  48.6 3.5 %collective-permute-start.7 = (f32[64,64]{0,1:T(8,128)S(1)}, f32[64,64]{0,1:T(8,128)S(1)}, u32[]{:S(2)}, u32[]{:S(2)}) collective-permute-start(f32[64,64]{0,1:T(8,128)S(1)} %add.138), channel_id=1, source_target_pairs={{0,8},{8,0},{16,24},{24,16},{32,40},{40,32},{48,56},{56,48},{64,72... | collective-permute-start | bytes 49160 | tf_op jit(solution)/shard_map/ppermute | solution.py:51
  52.1 1.0 broadcast_multiply_fusion.6
  53.1 1.7 %fusion.11 = f32[64,1,16,512]{3,2,0,1:T(8,128)S(1)} fusion(f32[64,1,16,512]{3,2,0,1:T(8,128)S(1)} %get-tuple-element.26, f32[64,1,16,512]{3,2,0,1:T(8,128)S(1)} %get-tuple-element.25, f32[64,1,16,512]{3,2,0,1:T(8,128)S(1)} %get-tuple-element.27, f32[64,1,16,512]{3,2,0,1:T(8,128)S(1)} %get-tuple-element.24, f32[64,1,16,512]{3,2,0,1:T(8,128)S(1)} %fusion.9, ...), kind=kLoop, calls=%fused_computation.27 | loop fusion | flops 2621440 | bytes 12615680 | tf_op jit(solution)/shard_map/add | solution.py:36
  55.1 0.6 copy.27
  55.7 1.0 convolution_bitcast_fusion.2
  56.7 2.5 %collective-permute-start.8 = (f32[2,64,64]{1,2,0:T(8,128)S(1)}, f32[2,64,64]{1,2,0:T(8,128)S(1)}, u32[]{:S(2)}, u32[]{:S(2)}) collective-permute-start(f32[2,64,64]{1,2,0:T(8,128)S(1)} %pad_maximum_fusion.1), channel_id=1, source_target_pairs={{0,16},{8,24},{16,0},{24,8},{32,48},{40,56},{48,32},{56,40},{64,80... | collective-permute-start | bytes 98312 | tf_op jit(solution)/shard_map/ppermute | solution.py:51
  59.2 2.7 %collective-permute-done.8 = f32[2,64,64]{1,2,0:T(8,128)S(1)} collective-permute-done((f32[2,64,64]{1,2,0:T(8,128)S(1)}, f32[2,64,64]{1,2,0:T(8,128)S(1)}, u32[]{:S(2)}, u32[]{:S(2)}) %collective-permute-start.8) | collective-permute-done | bytes 32800 | tf_op jit(solution)/shard_map/ppermute | solution.py:51
  61.9 3.6 %collective-permute-start.9 = (f32[2,64,64]{1,2,0:T(8,128)S(1)}, f32[2,64,64]{1,2,0:T(8,128)S(1)}, u32[]{:S(2)}, u32[]{:S(2)}) collective-permute-start(f32[2,64,64]{1,2,0:T(8,128)S(1)} %fusion.33), channel_id=1, source_target_pairs={{0,32},{8,40},{16,48},{24,56},{32,0},{40,8},{48,16},{56,24},{64,96... | collective-permute-start | bytes 98312 | tf_op jit(solution)/shard_map/ppermute | solution.py:51
  65.5 2.2 %collective-permute-done.9 = f32[2,64,64]{1,2,0:T(8,128)S(1)} collective-permute-done((f32[2,64,64]{1,2,0:T(8,128)S(1)}, f32[2,64,64]{1,2,0:T(8,128)S(1)}, u32[]{:S(2)}, u32[]{:S(2)}) %collective-permute-start.9) | collective-permute-done | bytes 32800 | tf_op jit(solution)/shard_map/ppermute | solution.py:51
  67.8 2.7 %collective-permute-start.10 = (f32[2,64,64]{1,2,0:T(8,128)S(1)}, f32[2,64,64]{1,2,0:T(8,128)S(1)}, u32[]{:S(2)}, u32[]{:S(2)}) collective-permute-start(f32[2,64,64]{1,2,0:T(8,128)S(1)} %fusion.43), channel_id=1, source_target_pairs={{0,64},{8,72},{16,80},{24,88},{32,96},{40,104},{48,112},{56,120},{... | collective-permute-start | bytes 98312 | tf_op jit(solution)/shard_map/ppermute | solution.py:51
  70.4 2.2 %collective-permute-done.10 = f32[2,64,64]{1,2,0:T(8,128)S(1)} collective-permute-done((f32[2,64,64]{1,2,0:T(8,128)S(1)}, f32[2,64,64]{1,2,0:T(8,128)S(1)}, u32[]{:S(2)}, u32[]{:S(2)}) %collective-permute-start.10) | collective-permute-done | bytes 32800 | tf_op jit(solution)/shard_map/ppermute | solution.py:51
  72.8 5.8 %cholesky.17 = f32[64,64]{1,0:T(8,128)S(1)} custom-call(f32[64,64]{1,0:T(8,128)S(1)} %fusion.27), custom_call_target="Cholesky" | custom-call | tf_op jit(solution)/shard_map/jit(cholesky)/cholesky | solution.py:55
  78.7 0.6 compare_reduce_fusion
  79.3 0.7 fusion.26
  80.0 4.9 %custom-call.10 = f32[1,64,64]{1,2,0:T(8,128)S(1)} custom-call(f32[1,64,64]{2,1,0:T(8,128)S(1)} %fusion.26), custom_call_target="InvertDiagBlocksLowerTriangular" | custom-call | tf_op jit(solution)/shard_map/jit(_cho_solve)/triangular_solve | solution.py:56
  84.9 0.2 fusion.29
  85.3 1.6 %convolution_bitcast_fusion = f32[64,1,8,512]{3,0,2,1:T(8,128)S(1)} fusion(f32[64,64,1]{1,0,2:T(8,128)S(1)} %convolution_bitcast_fusion.1, f32[8,8,8,512]{3,2,1,0:T(8,128)S(1)} %bitcast.87), kind=kOutput, calls=%fused_computation.41 | convolution fusion | flops 201326592 | bytes 2113536 | tf_op jit(solution)/shard_map/dot_general | solution.py:97
  86.9 1.6 %copy.21 = f32[64,1,8,512]{3,2,1,0:T(8,128)} copy(f32[64,1,8,512]{3,0,2,1:T(8,128)S(1)} %convolution_bitcast_fusion) | data formatting | bytes 2097152 | tf_op jit(solution)/shard_map/dot_general | solution.py:97
  88.5 3.8 %all-to-all-start.1 = ((f32[64,1,8,512]{3,2,1,0:T(8,128)}), f32[64,1,8,512]{3,2,1,0:T(8,128)S(1)}, u32[]{:S(2)}, u32[]{:S(2)}) async-start(f32[64,1,8,512]{3,2,1,0:T(8,128)} %copy.21), calls=%async_computation.1 | async-start | bytes 2097152 | tf_op jit(solution)/shard_map/all_to_all | solution.py:98
  92.3 2.0 %collective-permute-start.11 = (f32[64,64]{0,1:T(8,128)S(1)}, f32[64,64]{0,1:T(8,128)S(1)}, u32[]{:S(2)}, u32[]{:S(2)}) collective-permute-start(f32[64,64]{0,1:T(8,128)S(1)} %get-tuple-element.46), channel_id=1, source_target_pairs={{0,1},{1,0},{2,3},{3,2},{4,5},{5,4},{6,7},{7,6},{8,9},{9,8},{10,11... | collective-permute-start | bytes 49160 | tf_op jit(solution)/shard_map/ppermute | solution.py:51
  94.3 10.0 %collective-permute-done.11 = f32[64,64]{0,1:T(8,128)S(1)} collective-permute-done((f32[64,64]{0,1:T(8,128)S(1)}, f32[64,64]{0,1:T(8,128)S(1)}, u32[]{:S(2)}, u32[]{:S(2)}) %collective-permute-start.11) | collective-permute-done | bytes 16416 | tf_op jit(solution)/shard_map/ppermute | solution.py:51
  104.4 3.1 %collective-permute-start.12 = (f32[64,64]{0,1:T(8,128)S(1)}, f32[64,64]{0,1:T(8,128)S(1)}, u32[]{:S(2)}, u32[]{:S(2)}) collective-permute-start(f32[64,64]{0,1:T(8,128)S(1)} %fusion.32), channel_id=1, source_target_pairs={{0,2},{1,3},{2,0},{3,1},{4,6},{5,7},{6,4},{7,5},{8,10},{9,11},{10,... | collective-permute-start | bytes 49160 | tf_op jit(solution)/shard_map/ppermute | solution.py:51
  107.4 2.3 %collective-permute-done.12 = f32[64,64]{0,1:T(8,128)S(1)} collective-permute-done((f32[64,64]{0,1:T(8,128)S(1)}, f32[64,64]{0,1:T(8,128)S(1)}, u32[]{:S(2)}, u32[]{:S(2)}) %collective-permute-start.12) | collective-permute-done | bytes 16416 | tf_op jit(solution)/shard_map/ppermute | solution.py:51
  109.8 3.0 %collective-permute-start.13 = (f32[64,64]{0,1:T(8,128)S(1)}, f32[64,64]{0,1:T(8,128)S(1)}, u32[]{:S(2)}, u32[]{:S(2)}) collective-permute-start(f32[64,64]{0,1:T(8,128)S(1)} %add.153), channel_id=1, source_target_pairs={{0,4},{1,5},{2,6},{3,7},{4,0},{5,1},{6,2},{7,3},{8,12},{9,13},{10,... | collective-permute-start | bytes 49160 | tf_op jit(solution)/shard_map/ppermute | solution.py:51
  112.8 2.4 %collective-permute-done.13 = f32[64,64]{0,1:T(8,128)S(1)} collective-permute-done((f32[64,64]{0,1:T(8,128)S(1)}, f32[64,64]{0,1:T(8,128)S(1)}, u32[]{:S(2)}, u32[]{:S(2)}) %collective-permute-start.13) | collective-permute-done | bytes 16416 | tf_op jit(solution)/shard_map/ppermute | solution.py:51
  115.2 1.2 %collective-permute-done.14 = f32[64,64]{0,1:T(8,128)S(1)} collective-permute-done((f32[64,64]{0,1:T(8,128)S(1)}, f32[64,64]{0,1:T(8,128)S(1)}, u32[]{:S(2)}, u32[]{:S(2)}) %collective-permute-start.14) | collective-permute-done | bytes 16416 | tf_op jit(solution)/shard_map/ppermute | solution.py:51
  116.4 0.7 copy.23
  117.1 1.1 copy.36
  (31 shorter events, 0.9 us)
Async XLA Ops:
  0.6 9.4 %copy-start = (bf16[2,5,1,8,512]{4,3,2,1,0:T(8,128)(2,1)S(1)}, bf16[2,5,1,8,512]{4,3,2,1,0:T(8,128)(2,1)}, u32[]{:S(2)}) copy-start(bf16[2,5,1,8,512]{4,3,2,1,0:T(8,128)(2,1)} %param.3) | copy-start | bytes 245764
  3.0 24.2 %all-to-all-start = ((f32[8,8,8,512]{3,2,0,1:T(8,128)}), f32[8,8,8,512]{3,2,0,1:T(8,128)S(1)}, u32[]{:S(2)}, u32[]{:S(2)}) async-start(f32[8,8,8,512]{3,2,0,1:T(8,128)} %copy.16), calls=%async_computation | async-start | bytes 2097152 | tf_op jit(solution)/shard_map/all_to_all | solution.py:64
  10.0 20.3 %collective-permute-start.1 = (bf16[2,5,1,4,512]{4,3,2,1,0:T(4,128)(2,1)S(1)}, bf16[2,5,1,4,512]{4,3,2,1,0:T(4,128)(2,1)S(1)}, u32[]{:S(2)}, u32[]{:S(2)}) collective-permute-start(bf16[2,5,1,4,512]{4,3,2,1,0:T(4,128)(2,1)S(1)} %get-tuple-element.44), channel_id=1, source_target_pairs={{0,8},{8,16},{16,24},{24,32},{32,40},{40,48},{48,56},{56,64},{64,7... | collective-permute-start | bytes 122888 | tf_op jit(solution)/shard_map/ppermute | solution.py:14
  11.5 18.8 %collective-permute-start.2 = (bf16[2,5,1,4,512]{4,3,2,1,0:T(4,128)(2,1)S(1)}, bf16[2,5,1,4,512]{4,3,2,1,0:T(4,128)(2,1)S(1)}, u32[]{:S(2)}, u32[]{:S(2)}) collective-permute-start(bf16[2,5,1,4,512]{4,3,2,1,0:T(4,128)(2,1)S(1)} %get-tuple-element.45), channel_id=1, source_target_pairs={{8,0},{16,8},{24,16},{32,24},{40,32},{48,40},{56,48},{64,56},{72,6... | collective-permute-start | bytes 122888 | tf_op jit(solution)/shard_map/ppermute | solution.py:15
  27.4 8.7 %collective-permute-start.3 = (f32[64,1,4,512]{3,2,0,1:T(4,128)S(1)}, f32[64,1,4,512]{3,2,0,1:T(4,128)S(1)}, u32[]{:S(2)}, u32[]{:S(2)}) collective-permute-start(f32[64,1,4,512]{3,2,0,1:T(4,128)S(1)} %get-tuple-element.32), channel_id=1, source_target_pairs={{0,8},{8,16},{16,24},{24,32},{32,40},{40,48},{48,56},{56,64},{64,7... | collective-permute-start | bytes 1572872 | tf_op jit(solution)/shard_map/ppermute | solution.py:14
  29.0 7.0 %collective-permute-start.4 = (f32[64,1,4,512]{3,2,0,1:T(4,128)S(1)}, f32[64,1,4,512]{3,2,0,1:T(4,128)S(1)}, u32[]{:S(2)}, u32[]{:S(2)}) collective-permute-start(f32[64,1,4,512]{3,2,0,1:T(4,128)S(1)} %get-tuple-element.33), channel_id=1, source_target_pairs={{8,0},{16,8},{24,16},{32,24},{40,32},{48,40},{56,48},{64,56},{72,6... | collective-permute-start | bytes 1572872 | tf_op jit(solution)/shard_map/ppermute | solution.py:15
  32.0 4.0 %collective-permute-start = (f32[64,64]{0,1:T(8,128)S(1)}, f32[64,64]{0,1:T(8,128)S(1)}, u32[]{:S(2)}, u32[]{:S(2)}) collective-permute-start(f32[64,64]{0,1:T(8,128)S(1)} %fusion.36), channel_id=1, source_target_pairs={{0,1},{1,0},{2,3},{3,2},{4,5},{5,4},{6,7},{7,6},{8,9},{9,8},{10,11... | collective-permute-start | bytes 49160 | tf_op jit(solution)/shard_map/ppermute | solution.py:51
  37.7 5.5 %collective-permute-start.5 = (f32[64,64]{0,1:T(8,128)S(1)}, f32[64,64]{0,1:T(8,128)S(1)}, u32[]{:S(2)}, u32[]{:S(2)}) collective-permute-start(f32[64,64]{0,1:T(8,128)S(1)} %add.128), channel_id=1, source_target_pairs={{0,2},{1,3},{2,0},{3,1},{4,6},{5,7},{6,4},{7,5},{8,10},{9,11},{10,... | collective-permute-start | bytes 49160 | tf_op jit(solution)/shard_map/ppermute | solution.py:51
  43.2 5.4 %collective-permute-start.6 = (f32[64,64]{0,1:T(8,128)S(1)}, f32[64,64]{0,1:T(8,128)S(1)}, u32[]{:S(2)}, u32[]{:S(2)}) collective-permute-start(f32[64,64]{0,1:T(8,128)S(1)} %add.133), channel_id=1, source_target_pairs={{0,4},{1,5},{2,6},{3,7},{4,0},{5,1},{6,2},{7,3},{8,12},{9,13},{10,... | collective-permute-start | bytes 49160 | tf_op jit(solution)/shard_map/ppermute | solution.py:51
  48.6 6.2 %collective-permute-start.7 = (f32[64,64]{0,1:T(8,128)S(1)}, f32[64,64]{0,1:T(8,128)S(1)}, u32[]{:S(2)}, u32[]{:S(2)}) collective-permute-start(f32[64,64]{0,1:T(8,128)S(1)} %add.138), channel_id=1, source_target_pairs={{0,8},{8,0},{16,24},{24,16},{32,40},{40,32},{48,56},{56,48},{64,72... | collective-permute-start | bytes 49160 | tf_op jit(solution)/shard_map/ppermute | solution.py:51
  56.7 5.1 %collective-permute-start.8 = (f32[2,64,64]{1,2,0:T(8,128)S(1)}, f32[2,64,64]{1,2,0:T(8,128)S(1)}, u32[]{:S(2)}, u32[]{:S(2)}) collective-permute-start(f32[2,64,64]{1,2,0:T(8,128)S(1)} %pad_maximum_fusion.1), channel_id=1, source_target_pairs={{0,16},{8,24},{16,0},{24,8},{32,48},{40,56},{48,32},{56,40},{64,80... | collective-permute-start | bytes 98312 | tf_op jit(solution)/shard_map/ppermute | solution.py:51
  61.9 5.9 %collective-permute-start.9 = (f32[2,64,64]{1,2,0:T(8,128)S(1)}, f32[2,64,64]{1,2,0:T(8,128)S(1)}, u32[]{:S(2)}, u32[]{:S(2)}) collective-permute-start(f32[2,64,64]{1,2,0:T(8,128)S(1)} %fusion.33), channel_id=1, source_target_pairs={{0,32},{8,40},{16,48},{24,56},{32,0},{40,8},{48,16},{56,24},{64,96... | collective-permute-start | bytes 98312 | tf_op jit(solution)/shard_map/ppermute | solution.py:51
  67.8 4.9 %collective-permute-start.10 = (f32[2,64,64]{1,2,0:T(8,128)S(1)}, f32[2,64,64]{1,2,0:T(8,128)S(1)}, u32[]{:S(2)}, u32[]{:S(2)}) collective-permute-start(f32[2,64,64]{1,2,0:T(8,128)S(1)} %fusion.43), channel_id=1, source_target_pairs={{0,64},{8,72},{16,80},{24,88},{32,96},{40,104},{48,112},{56,120},{... | collective-permute-start | bytes 98312 | tf_op jit(solution)/shard_map/ppermute | solution.py:51
  88.5 28.7 %all-to-all-start.1 = ((f32[64,1,8,512]{3,2,1,0:T(8,128)}), f32[64,1,8,512]{3,2,1,0:T(8,128)S(1)}, u32[]{:S(2)}, u32[]{:S(2)}) async-start(f32[64,1,8,512]{3,2,1,0:T(8,128)} %copy.21), calls=%async_computation.1 | async-start | bytes 2097152 | tf_op jit(solution)/shard_map/all_to_all | solution.py:98
  92.3 12.1 %collective-permute-start.11 = (f32[64,64]{0,1:T(8,128)S(1)}, f32[64,64]{0,1:T(8,128)S(1)}, u32[]{:S(2)}, u32[]{:S(2)}) collective-permute-start(f32[64,64]{0,1:T(8,128)S(1)} %get-tuple-element.46), channel_id=1, source_target_pairs={{0,1},{1,0},{2,3},{3,2},{4,5},{5,4},{6,7},{7,6},{8,9},{9,8},{10,11... | collective-permute-start | bytes 49160 | tf_op jit(solution)/shard_map/ppermute | solution.py:51
  104.4 5.4 %collective-permute-start.12 = (f32[64,64]{0,1:T(8,128)S(1)}, f32[64,64]{0,1:T(8,128)S(1)}, u32[]{:S(2)}, u32[]{:S(2)}) collective-permute-start(f32[64,64]{0,1:T(8,128)S(1)} %fusion.32), channel_id=1, source_target_pairs={{0,2},{1,3},{2,0},{3,1},{4,6},{5,7},{6,4},{7,5},{8,10},{9,11},{10,... | collective-permute-start | bytes 49160 | tf_op jit(solution)/shard_map/ppermute | solution.py:51
  109.8 5.4 %collective-permute-start.13 = (f32[64,64]{0,1:T(8,128)S(1)}, f32[64,64]{0,1:T(8,128)S(1)}, u32[]{:S(2)}, u32[]{:S(2)}) collective-permute-start(f32[64,64]{0,1:T(8,128)S(1)} %add.153), channel_id=1, source_target_pairs={{0,4},{1,5},{2,6},{3,7},{4,0},{5,1},{6,2},{7,3},{8,12},{9,13},{10,... | collective-permute-start | bytes 49160 | tf_op jit(solution)/shard_map/ppermute | solution.py:51
  115.2 1.2 %collective-permute-start.14 = (f32[64,64]{0,1:T(8,128)S(1)}, f32[64,64]{0,1:T(8,128)S(1)}, u32[]{:S(2)}, u32[]{:S(2)}) collective-permute-start(f32[64,64]{0,1:T(8,128)S(1)} %add.154), channel_id=1, source_target_pairs={{0,8},{8,0},{16,24},{24,16},{32,40},{40,32},{48,56},{56,48},{64,72... | collective-permute-start | bytes 49160 | tf_op jit(solution)/shard_map/ppermute | solution.py:51

commit v4 on v3

--- a/solution.py
+++ b/solution.py
@@ -51,9 +51,17 @@
     return x + lax.ppermute(x, axis, [(i, i ^ bit) for i in range(count)])
 
 
-def invert(gram):
+def invert_beside(gram, extra, bits):
     factor = jnp.linalg.cholesky(gram)
-    return jax.scipy.linalg.cho_solve((factor, True), jnp.eye(gram.shape[0], dtype=jnp.float32))
+    if bits:
+        extra = exchange(extra, *bits.pop(0))
+    factor, extra = lax.optimization_barrier((factor, extra))
+    eye = jnp.eye(gram.shape[0], dtype=jnp.float32)
+    inverse = jax.scipy.linalg.cho_solve((factor, True), eye)
+    if bits:
+        extra = exchange(extra, *bits.pop(0))
+    inverse, extra = lax.optimization_barrier((inverse, extra))
+    return inverse, extra
 
 
 def body(perturbations, trajectory):
@@ -72,30 +80,36 @@
     hi = lax.Precision.HIGHEST
     flat_v = v.reshape(members, -1)
     gram = jnp.dot(flat_v, flat_v.T, precision=hi)
-    bits = butterfly_bits()
-    done = 0
-    field = halo(v, width, 2)
-    plan = [(forward_step, s) for s in range(STEPS)]
-    plan += [(adjoint_step, s) for s in reversed(range(STEPS))]
-    for apply, step in plan:
-        field = apply(field, coeffs[step])
-        if done < len(bits):
-            gram = exchange(gram, *bits[done])
-            done += 1
-        gram, field = lax.optimization_barrier((gram, field))
+    pending = butterfly_bits()
+    done = []
+
+    def tick(acc, field):
+        if pending:
+            bit = pending.pop(0)
+            acc = exchange(acc, *bit)
+            done.append(bit)
+        return lax.optimization_barrier((acc, field))
+
+    gram, field = tick(gram, halo(v, width, 2))
+    for step in range(STEPS):
+        gram, field = tick(gram, forward_step(field, coeffs[step]))
+    flat_z = field[:, :, width : width + rows, :].reshape(members, -1)
+    cross = jnp.dot(flat_z, flat_z.T, precision=hi)
+    both = jnp.stack([gram, cross])
+    cross_bits = list(done)
+    for step in reversed(range(STEPS)):
+        both, field = tick(both, adjoint_step(field, coeffs[step]))
+    while pending:
+        both = exchange(both, *pending.pop(0))
+    gram, cross = both[0], both[1]
     field = field[:, :, width : width + rows, :]
     flat_w = field.reshape(members, -1)
-    cross = jnp.dot(flat_v, flat_w.T, precision=hi)
-    both = jnp.stack([gram, cross])
-    for axis, bit in bits[done:]:
-        both = exchange(both, axis, bit)
-    gram, cross = both[0], both[1]
-    for axis, bit in bits[:done]:
+    inverse, cross = invert_beside(gram / ncells_all, cross, cross_bits)
+    ritz = jnp.dot(inverse, flat_w, precision=hi)
+    for axis, bit in cross_bits:
         cross = exchange(cross, axis, bit)
-    inverse = invert(gram / ncells_all)
     projected = cross / ncells_all
-    ritz = jnp.dot(inverse, flat_w, precision=hi).reshape(v.shape)
-    ritz = lax.all_to_all(ritz, "mem", 0, 1, tiled=True)
+    ritz = lax.all_to_all(ritz.reshape(v.shape), "mem", 0, 1, tiled=True)
     return (ritz, projected)
 
 

time: 120 us -> 110 us (0.917); the launches traced: 118 us -> 110 us
  waiting for transfers between devices: 45.9 us -> 40.2 us
  starting transfers between devices: 39.3 us -> 37.7 us
    ppermute x11 -> x10, waiting for transfers between devices: 31.5 us -> 20.6 us  [exchange(): return x + lax.ppermute(x, axis, [(i, i ^ bit) for i in range(count)])]
    all_to_all x1, waiting for transfers between devices: 0.01 us -> 5.23 us  [body(): ritz = lax.all_to_all(ritz.reshape(v.shape), 'mem', 0, 1, tiled=True)]
    ppermute x11 -> x10, starting transfers between devices: 22.7 us -> 20.9 us  [exchange(): return x + lax.ppermute(x, axis, [(i, i ^ bit) for i in range(count)])]
    unnamed x6 -> x5, local copies, waits for them, and re-layouts: 4.24 us -> 3.63 us
  transfers between devices with their start and end apart: 17 -> 16, of which waited for: 11 -> 9; matrix products, arithmetic and copies ran while one was open for 8% -> 19% of each run, Pallas kernels for 0% -> 0%
where the time goes in v4:
time: 110 us
  waiting for transfers between devices  40.2 us (37%)
  starting transfers between devices  37.7 us (34%)
  other arithmetic  20.4 us (19%)
  local copies, waits for them, and re-layouts  7.08 us (6%)
  matrix products  3.34 us (3%)
    ppermute x10, starting transfers between devices, exchange(): return x + lax.ppermute(x, axis, [(i, i ^ bit) for i in range(count)])  20.9 us
    ppermute x10, waiting for transfers between devices, exchange(): return x + lax.ppermute(x, axis, [(i, i ^ bit) for i in range(count)])  20.6 us
    all_to_all x1, waiting for transfers between devices, body(): v = lax.all_to_all(perturbations, 'mem', 1, 0, tiled=True)  14.4 us
    all_to_all x1, starting transfers between devices, body(): v = lax.all_to_all(perturbations, 'mem', 1, 0, tiled=True)  7.04 us
    another operation x3, other arithmetic, invert_beside(): factor = jnp.linalg.cholesky(gram)  6.52 us
    all_to_all x1, waiting for transfers between devices, body(): ritz = lax.all_to_all(ritz.reshape(v.shape), 'mem', 0, 1, tiled=True)  5.23 us
    another operation x2, other arithmetic, invert_beside(): inverse = jax.scipy.linalg.cho_solve((factor, True), eye)  4.9 us
    all_to_all x1, starting transfers between devices, body(): ritz = lax.all_to_all(ritz.reshape(v.shape), 'mem', 0, 1, tiled=True)  3.97 us
  transfers between devices with their start and end apart: 16, of which 9 were waited for; matrix products, arithmetic and copies ran while one was open for 19% of the time, Pallas kernels for 0%

profile of v4, /device:TPU:0, one launch (start us, length us, event | category | flops | bytes accessed | tf_op | source)
XLA Modules:
  0.0 109.7 jit_solution(12997241896879267298)
XLA Ops:
  0.6 2.3 %copy.21 = f32[8,8,8,512]{3,2,0,1:T(8,128)} copy(f32[8,8,8,512]{3,2,1,0:T(8,128)} %param.2) | data formatting | bytes 2097152 | tf_op args[0]
  3.0 7.0 %all-to-all-start = ((f32[8,8,8,512]{3,2,0,1:T(8,128)}), f32[8,8,8,512]{3,2,0,1:T(8,128)S(1)}, u32[]{:S(2)}, u32[]{:S(2)}) async-start(f32[8,8,8,512]{3,2,0,1:T(8,128)} %copy.21), calls=%async_computation | async-start | bytes 2097152 | tf_op jit(solution)/shard_map/all_to_all | solution.py:72
  10.0 1.5 %collective-permute-start.4 = (bf16[2,5,1,4,512]{4,3,2,1,0:T(4,128)(2,1)S(1)}, bf16[2,5,1,4,512]{4,3,2,1,0:T(4,128)(2,1)S(1)}, u32[]{:S(2)}, u32[]{:S(2)}) collective-permute-start(bf16[2,5,1,4,512]{4,3,2,1,0:T(4,128)(2,1)S(1)} %get-tuple-element.56), channel_id=1, source_target_pairs={{0,8},{8,16},{16,24},{24,32},{32,40},{40,48},{48,56},{56,64},{64,7... | collective-permute-start | bytes 122888 | tf_op jit(solution)/shard_map/ppermute | solution.py:14
  11.5 1.3 %collective-permute-start.5 = (bf16[2,5,1,4,512]{4,3,2,1,0:T(4,128)(2,1)S(1)}, bf16[2,5,1,4,512]{4,3,2,1,0:T(4,128)(2,1)S(1)}, u32[]{:S(2)}, u32[]{:S(2)}) collective-permute-start(bf16[2,5,1,4,512]{4,3,2,1,0:T(4,128)(2,1)S(1)} %get-tuple-element.57), channel_id=1, source_target_pairs={{8,0},{16,8},{24,16},{32,24},{40,32},{48,40},{56,48},{64,56},{72,6... | collective-permute-start | bytes 122888 | tf_op jit(solution)/shard_map/ppermute | solution.py:15
  12.8 14.4 %all-to-all-done = f32[8,8,8,512]{3,2,0,1:T(8,128)S(1)} async-done(((f32[8,8,8,512]{3,2,0,1:T(8,128)}), f32[8,8,8,512]{3,2,0,1:T(8,128)S(1)}, u32[]{:S(2)}, u32[]{:S(2)}) %all-to-all-start) | async-done | bytes 1048608 | tf_op jit(solution)/shard_map/all_to_all | solution.py:72
  27.2 0.6 copy.49
  27.9 1.7 %collective-permute-start.1 = (f32[64,1,4,512]{3,0,2,1:T(8,128)S(1)}, f32[64,1,4,512]{3,0,2,1:T(8,128)S(1)}, u32[]{:S(2)}, u32[]{:S(2)}) collective-permute-start(f32[64,1,4,512]{3,0,2,1:T(8,128)S(1)} %get-tuple-element.44), channel_id=1, source_target_pairs={{0,8},{8,16},{16,24},{24,32},{32,40},{40,48},{48,56},{56,64},{64,7... | collective-permute-start | bytes 1572872 | tf_op jit(solution)/shard_map/ppermute | solution.py:14
  29.6 1.3 %collective-permute-start.2 = (f32[64,1,4,512]{3,0,2,1:T(8,128)S(1)}, f32[64,1,4,512]{3,0,2,1:T(8,128)S(1)}, u32[]{:S(2)}, u32[]{:S(2)}) collective-permute-start(f32[64,1,4,512]{3,0,2,1:T(8,128)S(1)} %get-tuple-element.45), channel_id=1, source_target_pairs={{8,0},{16,8},{24,16},{32,24},{40,32},{48,40},{56,48},{64,56},{72,6... | collective-permute-start | bytes 1572872 | tf_op jit(solution)/shard_map/ppermute | solution.py:15
  30.9 0.1 maximum_convert_fusion
  31.0 0.6 copy.36
  31.6 1.0 fusion.39
  32.6 0.6 collective-permute-start
  33.2 3.4 %collective-permute-done = f32[64,64]{0,1:T(8,128)S(1)} collective-permute-done((f32[64,64]{0,1:T(8,128)S(1)}, f32[64,64]{0,1:T(8,128)S(1)}, u32[]{:S(2)}, u32[]{:S(2)}) %collective-permute-start) | collective-permute-done | bytes 16416 | tf_op jit(solution)/shard_map/ppermute | solution.py:51
  36.6 0.2 pad_maximum_fusion
  36.8 1.2 %collective-permute-start.3 = (f32[64,64]{0,1:T(8,128)S(1)}, f32[64,64]{0,1:T(8,128)S(1)}, u32[]{:S(2)}, u32[]{:S(2)}) collective-permute-start(f32[64,64]{0,1:T(8,128)S(1)} %add.125), channel_id=1, source_target_pairs={{0,2},{1,3},{2,0},{3,1},{4,6},{5,7},{6,4},{7,5},{8,10},{9,11},{10,... | collective-permute-start | bytes 49160 | tf_op jit(solution)/shard_map/ppermute | solution.py:51
  38.0 1.3 %fusion.4 = f32[64,1,16,512]{3,0,2,1:T(8,128)S(1)} fusion(f32[64,1,16,512]{3,0,2,1:T(8,128)S(1)} %pad_maximum_fusion, f32[16,512]{1,0:T(8,128)S(1)} %get-tuple-element.51, f32[16,512]{1,0:T(8,128)S(1)} %get-tuple-element.52, f32[16,512]{1,0:T(8,128)S(1)} %get-tuple-element.53, f32[16,512]{1,0:T(8,128)S(1)} %get-tuple-element.54, ...), kind=kLoop, calls=%fused_computation.20 | loop fusion | flops 4718592 | bytes 4358144 | tf_op jit(solution)/shard_map/add | solution.py:31
  39.3 3.0 %collective-permute-done.3 = f32[64,64]{0,1:T(8,128)S(1)} collective-permute-done((f32[64,64]{0,1:T(8,128)S(1)}, f32[64,64]{0,1:T(8,128)S(1)}, u32[]{:S(2)}, u32[]{:S(2)}) %collective-permute-start.3) | collective-permute-done | bytes 16416 | tf_op jit(solution)/shard_map/ppermute | solution.py:51
  42.3 0.6 collective-permute-start.6
  42.9 1.3 %fusion.10 = f32[64,1,16,512]{3,0,2,1:T(8,128)S(1)} fusion(f32[64,1,16,512]{3,0,2,1:T(8,128)S(1)} %fusion.4, f32[16,512]{1,0:T(8,128)S(1)} %get-tuple-element.47, f32[16,512]{1,0:T(8,128)S(1)} %get-tuple-element.48, f32[16,512]{1,0:T(8,128)S(1)} %get-tuple-element.49, f32[16,512]{1,0:T(8,128)S(1)} %get-tuple-element.50, f32[16,512]{1,0:T(8,128)S(1)} %get-tuple-element.46), kind=kLoop, calls=%fused_computation.26 | loop fusion | flops 4718592 | bytes 4358144 | tf_op jit(solution)/shard_map/add | solution.py:31
  44.1 3.6 %collective-permute-done.6 = f32[64,64]{0,1:T(8,128)S(1)} collective-permute-done((f32[64,64]{0,1:T(8,128)S(1)}, f32[64,64]{0,1:T(8,128)S(1)}, u32[]{:S(2)}, u32[]{:S(2)}) %collective-permute-start.6) | collective-permute-done | bytes 16416 | tf_op jit(solution)/shard_map/ppermute | solution.py:51
  47.7 1.2 %broadcast_multiply_fusion = (f32[64,1,16,512]{3,0,2,1:T(8,128)S(1)}, f32[64,1,16,512]{3,0,2,1:T(8,128)S(1)}, f32[64,1,16,512]{3,0,2,1:T(8,128)S(1)}, f32[64,1,16,512]{3,0,2,1:T(8,128)S(1)}) fusion(f32[64,1,16,512]{3,0,2,1:T(8,128)S(1)} %fusion.10, f32[16,512]{1,0:T(8,128)S(1)} %get-tuple-element.47, f32[16,512]{1,0:T(8,128)S(1)} %get-tuple-element.48, ...), kind=kLoop, calls=%fused_computation.49 | loop fusion | flops 2097152 | bytes 10616832 | tf_op jit(solution)/shard_map/mul | solution.py:36
  49.0 1.0 convolution_bitcast_fusion.1
  50.0 3.6 %collective-permute-start.7 = (f32[2,64,64]{1,2,0:T(8,128)S(1)}, f32[2,64,64]{1,2,0:T(8,128)S(1)}, u32[]{:S(2)}, u32[]{:S(2)}) collective-permute-start(f32[2,64,64]{1,2,0:T(8,128)S(1)} %pad_maximum_fusion.1), channel_id=1, source_target_pairs={{0,8},{8,0},{16,24},{24,16},{32,40},{40,32},{48,56},{56,48},{64,72... | collective-permute-start | bytes 98312 | tf_op jit(solution)/shard_map/ppermute | solution.py:51
  53.6 1.5 %fusion.15 = f32[64,1,16,512]{3,0,2,1:T(8,128)S(1)} fusion(f32[64,1,16,512]{3,0,2,1:T(8,128)S(1)} %get-tuple-element.43, f32[64,1,16,512]{3,0,2,1:T(8,128)S(1)} %get-tuple-element.42, f32[64,1,16,512]{3,0,2,1:T(8,128)S(1)} %get-tuple-element.41, f32[64,1,16,512]{3,0,2,1:T(8,128)S(1)} %get-tuple-element.40, f32[64,1,16,512]{3,0,2,1:T(8,128)S(1)} %fusion.10, ...), kind=kLoop, calls=%fused_computation.31 | loop fusion | flops 2621440 | bytes 12615680 | tf_op jit(solution)/shard_map/add | solution.py:36
  55.1 1.2 %broadcast_multiply_fusion.4 = (f32[64,1,16,512]{3,0,2,1:T(8,128)S(1)}, f32[64,1,16,512]{3,0,2,1:T(8,128)S(1)}, f32[64,1,16,512]{3,0,2,1:T(8,128)S(1)}, f32[64,1,16,512]{3,0,2,1:T(8,128)S(1)}) fusion(f32[64,1,16,512]{3,0,2,1:T(8,128)S(1)} %fusion.15, f32[16,512]{1,0:T(8,128)S(1)} %get-tuple-element.51, f32[16,512]{1,0:T(8,128)S(1)} %get-tuple-element.52, ...), kind=kLoop, calls=%fused_computation.53 | loop fusion | flops 2097152 | bytes 10616832 | tf_op jit(solution)/shard_map/mul | solution.py:36
  56.4 2.6 %collective-permute-start.8 = (f32[2,64,64]{1,2,0:T(8,128)S(1)}, f32[2,64,64]{1,2,0:T(8,128)S(1)}, u32[]{:S(2)}, u32[]{:S(2)}) collective-permute-start(f32[2,64,64]{1,2,0:T(8,128)S(1)} %fusion.36), channel_id=1, source_target_pairs={{0,16},{8,24},{16,0},{24,8},{32,48},{40,56},{48,32},{56,40},{64,80... | collective-permute-start | bytes 98312 | tf_op jit(solution)/shard_map/ppermute | solution.py:51
  59.0 1.4 %fusion.19 = f32[64,1,16,512]{3,0,2,1:T(8,128)S(1)} fusion(f32[64,1,16,512]{3,0,2,1:T(8,128)S(1)} %get-tuple-element.39, f32[64,1,16,512]{3,0,2,1:T(8,128)S(1)} %get-tuple-element.38, f32[64,1,16,512]{3,0,2,1:T(8,128)S(1)} %get-tuple-element.37, f32[64,1,16,512]{3,0,2,1:T(8,128)S(1)} %get-tuple-element.36, f32[64,1,16,512]{3,0,2,1:T(8,128)S(1)} %fusion.15, ...), kind=kLoop, calls=%fused_computation.35 | loop fusion | flops 2621440 | bytes 12615680 | tf_op jit(solution)/shard_map/add | solution.py:36
  60.4 1.2 %collective-permute-done.8 = f32[2,64,64]{1,2,0:T(8,128)S(1)} collective-permute-done((f32[2,64,64]{1,2,0:T(8,128)S(1)}, f32[2,64,64]{1,2,0:T(8,128)S(1)}, u32[]{:S(2)}, u32[]{:S(2)}) %collective-permute-start.8) | collective-permute-done | bytes 32800 | tf_op jit(solution)/shard_map/ppermute | solution.py:51
  61.6 3.6 %collective-permute-start.9 = (f32[2,64,64]{1,2,0:T(8,128)S(1)}, f32[2,64,64]{1,2,0:T(8,128)S(1)}, u32[]{:S(2)}, u32[]{:S(2)}) collective-permute-start(f32[2,64,64]{1,2,0:T(8,128)S(1)} %add.141), channel_id=1, source_target_pairs={{0,32},{8,40},{16,48},{24,56},{32,0},{40,8},{48,16},{56,24},{64,96... | collective-permute-start | bytes 98312 | tf_op jit(solution)/shard_map/ppermute | solution.py:51
  65.3 2.2 %collective-permute-done.9 = f32[2,64,64]{1,2,0:T(8,128)S(1)} collective-permute-done((f32[2,64,64]{1,2,0:T(8,128)S(1)}, f32[2,64,64]{1,2,0:T(8,128)S(1)}, u32[]{:S(2)}, u32[]{:S(2)}) %collective-permute-start.9) | collective-permute-done | bytes 32800 | tf_op jit(solution)/shard_map/ppermute | solution.py:51
  67.5 2.7 %collective-permute-start.10 = (f32[2,64,64]{1,2,0:T(8,128)S(1)}, f32[2,64,64]{1,2,0:T(8,128)S(1)}, u32[]{:S(2)}, u32[]{:S(2)}) collective-permute-start(f32[2,64,64]{1,2,0:T(8,128)S(1)} %add.146), channel_id=1, source_target_pairs={{0,64},{8,72},{16,80},{24,88},{32,96},{40,104},{48,112},{56,120},{... | collective-permute-start | bytes 98312 | tf_op jit(solution)/shard_map/ppermute | solution.py:51
  70.2 2.2 %collective-permute-done.10 = f32[2,64,64]{1,2,0:T(8,128)S(1)} collective-permute-done((f32[2,64,64]{1,2,0:T(8,128)S(1)}, f32[2,64,64]{1,2,0:T(8,128)S(1)}, u32[]{:S(2)}, u32[]{:S(2)}) %collective-permute-start.10) | collective-permute-done | bytes 32800 | tf_op jit(solution)/shard_map/ppermute | solution.py:51
  72.5 0.6 collective-permute-start.11
  73.2 5.8 %cholesky.17 = f32[64,64]{1,0:T(8,128)S(1)} custom-call(f32[64,64]{1,0:T(8,128)S(1)} %fusion.28), custom_call_target="Cholesky" | custom-call | tf_op jit(solution)/shard_map/jit(cholesky)/cholesky | solution.py:55
  79.1 0.6 compare_reduce_fusion
  79.7 0.7 select_select_fusion
  80.4 1.8 %collective-permute-start.12 = (f32[64,64]{0,1:T(8,128)S(1)}, f32[64,64]{0,1:T(8,128)S(1)}, u32[]{:S(2)}, u32[]{:S(2)}) collective-permute-start(f32[64,64]{0,1:T(8,128)S(1)} %fusion.35), channel_id=1, source_target_pairs={{0,2},{1,3},{2,0},{3,1},{4,6},{5,7},{6,4},{7,5},{8,10},{9,11},{10,... | collective-permute-start | bytes 49160 | tf_op jit(solution)/shard_map/ppermute | solution.py:51
  82.3 4.9 %custom-call.10 = f32[1,64,64]{1,2,0:T(8,128)S(1)} custom-call(f32[1,64,64]{2,1,0:T(8,128)S(1)} %select_bitcast_fusion), custom_call_target="InvertDiagBlocksLowerTriangular" | custom-call | tf_op jit(solution)/shard_map/jit(_cho_solve)/triangular_solve | solution.py:60
  87.2 0.2 fusion.32
  87.4 0.2 fusion.30
  87.6 1.0 convolution_bitcast_fusion
  88.6 1.6 %copy.29 = f32[64,1,8,512]{3,2,1,0:T(8,128)} copy(f32[64,1,8,512]{3,0,2,1:T(8,128)S(1)} %convolution_bitcast_fusion) | data formatting | bytes 2097152 | tf_op jit(solution)/shard_map/dot_general | solution.py:108
  90.2 4.0 %all-to-all-start.1 = ((f32[64,1,8,512]{3,2,1,0:T(8,128)}), f32[64,1,8,512]{3,2,1,0:T(8,128)S(1)}, u32[]{:S(2)}, u32[]{:S(2)}) async-start(f32[64,1,8,512]{3,2,1,0:T(8,128)} %copy.29), calls=%async_computation.1 | async-start | bytes 2097152 | tf_op jit(solution)/shard_map/all_to_all | solution.py:112
  94.2 3.5 %collective-permute-start.13 = (f32[64,64]{0,1:T(8,128)S(1)}, f32[64,64]{0,1:T(8,128)S(1)}, u32[]{:S(2)}, u32[]{:S(2)}) collective-permute-start(f32[64,64]{0,1:T(8,128)S(1)} %add.150), channel_id=1, source_target_pairs={{0,4},{1,5},{2,6},{3,7},{4,0},{5,1},{6,2},{7,3},{8,12},{9,13},{10,... | collective-permute-start | bytes 49160 | tf_op jit(solution)/shard_map/ppermute | solution.py:51
  97.7 4.9 %collective-permute-done.13 = f32[64,64]{0,1:T(8,128)S(1)} collective-permute-done((f32[64,64]{0,1:T(8,128)S(1)}, f32[64,64]{0,1:T(8,128)S(1)}, u32[]{:S(2)}, u32[]{:S(2)}) %collective-permute-start.13) | collective-permute-done | bytes 16416 | tf_op jit(solution)/shard_map/ppermute | solution.py:51
  102.7 0.7 copy.31
  103.4 5.2 %all-to-all-done.1 = f32[64,1,8,512]{3,2,1,0:T(8,128)S(1)} async-done(((f32[64,1,8,512]{3,2,1,0:T(8,128)}), f32[64,1,8,512]{3,2,1,0:T(8,128)S(1)}, u32[]{:S(2)}, u32[]{:S(2)}) %all-to-all-start.1) | async-done | bytes 1048608 | tf_op jit(solution)/shard_map/all_to_all | solution.py:112
  108.6 1.1 copy.48
  (28 shorter events, 0.4 us)
Async XLA Ops:
  0.6 9.4 %copy-start = (bf16[2,5,1,8,512]{4,3,2,1,0:T(8,128)(2,1)S(1)}, bf16[2,5,1,8,512]{4,3,2,1,0:T(8,128)(2,1)}, u32[]{:S(2)}) copy-start(bf16[2,5,1,8,512]{4,3,2,1,0:T(8,128)(2,1)} %param.3) | copy-start | bytes 245764
  3.0 24.2 %all-to-all-start = ((f32[8,8,8,512]{3,2,0,1:T(8,128)}), f32[8,8,8,512]{3,2,0,1:T(8,128)S(1)}, u32[]{:S(2)}, u32[]{:S(2)}) async-start(f32[8,8,8,512]{3,2,0,1:T(8,128)} %copy.21), calls=%async_computation | async-start | bytes 2097152 | tf_op jit(solution)/shard_map/all_to_all | solution.py:72
  10.0 20.8 %collective-permute-start.4 = (bf16[2,5,1,4,512]{4,3,2,1,0:T(4,128)(2,1)S(1)}, bf16[2,5,1,4,512]{4,3,2,1,0:T(4,128)(2,1)S(1)}, u32[]{:S(2)}, u32[]{:S(2)}) collective-permute-start(bf16[2,5,1,4,512]{4,3,2,1,0:T(4,128)(2,1)S(1)} %get-tuple-element.56), channel_id=1, source_target_pairs={{0,8},{8,16},{16,24},{24,32},{32,40},{40,48},{48,56},{56,64},{64,7... | collective-permute-start | bytes 122888 | tf_op jit(solution)/shard_map/ppermute | solution.py:14
  11.5 19.4 %collective-permute-start.5 = (bf16[2,5,1,4,512]{4,3,2,1,0:T(4,128)(2,1)S(1)}, bf16[2,5,1,4,512]{4,3,2,1,0:T(4,128)(2,1)S(1)}, u32[]{:S(2)}, u32[]{:S(2)}) collective-permute-start(bf16[2,5,1,4,512]{4,3,2,1,0:T(4,128)(2,1)S(1)} %get-tuple-element.57), channel_id=1, source_target_pairs={{8,0},{16,8},{24,16},{32,24},{40,32},{48,40},{56,48},{64,56},{72,6... | collective-permute-start | bytes 122888 | tf_op jit(solution)/shard_map/ppermute | solution.py:15
  27.9 8.7 %collective-permute-start.1 = (f32[64,1,4,512]{3,0,2,1:T(8,128)S(1)}, f32[64,1,4,512]{3,0,2,1:T(8,128)S(1)}, u32[]{:S(2)}, u32[]{:S(2)}) collective-permute-start(f32[64,1,4,512]{3,0,2,1:T(8,128)S(1)} %get-tuple-element.44), channel_id=1, source_target_pairs={{0,8},{8,16},{16,24},{24,32},{32,40},{40,48},{48,56},{56,64},{64,7... | collective-permute-start | bytes 1572872 | tf_op jit(solution)/shard_map/ppermute | solution.py:14
  29.6 7.0 %collective-permute-start.2 = (f32[64,1,4,512]{3,0,2,1:T(8,128)S(1)}, f32[64,1,4,512]{3,0,2,1:T(8,128)S(1)}, u32[]{:S(2)}, u32[]{:S(2)}) collective-permute-start(f32[64,1,4,512]{3,0,2,1:T(8,128)S(1)} %get-tuple-element.45), channel_id=1, source_target_pairs={{8,0},{16,8},{24,16},{32,24},{40,32},{48,40},{56,48},{64,56},{72,6... | collective-permute-start | bytes 1572872 | tf_op jit(solution)/shard_map/ppermute | solution.py:15
  32.6 4.0 %collective-permute-start = (f32[64,64]{0,1:T(8,128)S(1)}, f32[64,64]{0,1:T(8,128)S(1)}, u32[]{:S(2)}, u32[]{:S(2)}) collective-permute-start(f32[64,64]{0,1:T(8,128)S(1)} %fusion.39), channel_id=1, source_target_pairs={{0,1},{1,0},{2,3},{3,2},{4,5},{5,4},{6,7},{7,6},{8,9},{9,8},{10,11... | collective-permute-start | bytes 49160 | tf_op jit(solution)/shard_map/ppermute | solution.py:51
  36.8 5.5 %collective-permute-start.3 = (f32[64,64]{0,1:T(8,128)S(1)}, f32[64,64]{0,1:T(8,128)S(1)}, u32[]{:S(2)}, u32[]{:S(2)}) collective-permute-start(f32[64,64]{0,1:T(8,128)S(1)} %add.125), channel_id=1, source_target_pairs={{0,2},{1,3},{2,0},{3,1},{4,6},{5,7},{6,4},{7,5},{8,10},{9,11},{10,... | collective-permute-start | bytes 49160 | tf_op jit(solution)/shard_map/ppermute | solution.py:51
  42.3 5.4 %collective-permute-start.6 = (f32[64,64]{0,1:T(8,128)S(1)}, f32[64,64]{0,1:T(8,128)S(1)}, u32[]{:S(2)}, u32[]{:S(2)}) collective-permute-start(f32[64,64]{0,1:T(8,128)S(1)} %add.126), channel_id=1, source_target_pairs={{0,4},{1,5},{2,6},{3,7},{4,0},{5,1},{6,2},{7,3},{8,12},{9,13},{10,... | collective-permute-start | bytes 49160 | tf_op jit(solution)/shard_map/ppermute | solution.py:51
  50.0 5.1 %collective-permute-start.7 = (f32[2,64,64]{1,2,0:T(8,128)S(1)}, f32[2,64,64]{1,2,0:T(8,128)S(1)}, u32[]{:S(2)}, u32[]{:S(2)}) collective-permute-start(f32[2,64,64]{1,2,0:T(8,128)S(1)} %pad_maximum_fusion.1), channel_id=1, source_target_pairs={{0,8},{8,0},{16,24},{24,16},{32,40},{40,32},{48,56},{56,48},{64,72... | collective-permute-start | bytes 98312 | tf_op jit(solution)/shard_map/ppermute | solution.py:51
  56.4 5.3 %collective-permute-start.8 = (f32[2,64,64]{1,2,0:T(8,128)S(1)}, f32[2,64,64]{1,2,0:T(8,128)S(1)}, u32[]{:S(2)}, u32[]{:S(2)}) collective-permute-start(f32[2,64,64]{1,2,0:T(8,128)S(1)} %fusion.36), channel_id=1, source_target_pairs={{0,16},{8,24},{16,0},{24,8},{32,48},{40,56},{48,32},{56,40},{64,80... | collective-permute-start | bytes 98312 | tf_op jit(solution)/shard_map/ppermute | solution.py:51
  61.6 5.9 %collective-permute-start.9 = (f32[2,64,64]{1,2,0:T(8,128)S(1)}, f32[2,64,64]{1,2,0:T(8,128)S(1)}, u32[]{:S(2)}, u32[]{:S(2)}) collective-permute-start(f32[2,64,64]{1,2,0:T(8,128)S(1)} %add.141), channel_id=1, source_target_pairs={{0,32},{8,40},{16,48},{24,56},{32,0},{40,8},{48,16},{56,24},{64,96... | collective-permute-start | bytes 98312 | tf_op jit(solution)/shard_map/ppermute | solution.py:51
  67.5 4.9 %collective-permute-start.10 = (f32[2,64,64]{1,2,0:T(8,128)S(1)}, f32[2,64,64]{1,2,0:T(8,128)S(1)}, u32[]{:S(2)}, u32[]{:S(2)}) collective-permute-start(f32[2,64,64]{1,2,0:T(8,128)S(1)} %add.146), channel_id=1, source_target_pairs={{0,64},{8,72},{16,80},{24,88},{32,96},{40,104},{48,112},{56,120},{... | collective-permute-start | bytes 98312 | tf_op jit(solution)/shard_map/ppermute | solution.py:51
  72.5 7.9 %collective-permute-start.11 = (f32[64,64]{0,1:T(8,128)S(1)}, f32[64,64]{0,1:T(8,128)S(1)}, u32[]{:S(2)}, u32[]{:S(2)}) collective-permute-start(f32[64,64]{0,1:T(8,128)S(1)} %get-tuple-element.58), channel_id=1, source_target_pairs={{0,1},{1,0},{2,3},{3,2},{4,5},{5,4},{6,7},{7,6},{8,9},{9,8},{10,11... | collective-permute-start | bytes 49160 | tf_op jit(solution)/shard_map/ppermute | solution.py:51
  80.4 7.2 %collective-permute-start.12 = (f32[64,64]{0,1:T(8,128)S(1)}, f32[64,64]{0,1:T(8,128)S(1)}, u32[]{:S(2)}, u32[]{:S(2)}) collective-permute-start(f32[64,64]{0,1:T(8,128)S(1)} %fusion.35), channel_id=1, source_target_pairs={{0,2},{1,3},{2,0},{3,1},{4,6},{5,7},{6,4},{7,5},{8,10},{9,11},{10,... | collective-permute-start | bytes 49160 | tf_op jit(solution)/shard_map/ppermute | solution.py:51
  90.2 18.4 %all-to-all-start.1 = ((f32[64,1,8,512]{3,2,1,0:T(8,128)}), f32[64,1,8,512]{3,2,1,0:T(8,128)S(1)}, u32[]{:S(2)}, u32[]{:S(2)}) async-start(f32[64,1,8,512]{3,2,1,0:T(8,128)} %copy.29), calls=%async_computation.1 | async-start | bytes 2097152 | tf_op jit(solution)/shard_map/all_to_all | solution.py:112
  94.2 8.5 %collective-permute-start.13 = (f32[64,64]{0,1:T(8,128)S(1)}, f32[64,64]{0,1:T(8,128)S(1)}, u32[]{:S(2)}, u32[]{:S(2)}) collective-permute-start(f32[64,64]{0,1:T(8,128)S(1)} %add.150), channel_id=1, source_target_pairs={{0,4},{1,5},{2,6},{3,7},{4,0},{5,1},{6,2},{7,3},{8,12},{9,13},{10,... | collective-permute-start | bytes 49160 | tf_op jit(solution)/shard_map/ppermute | solution.py:51

commit v5 on v4

--- a/solution.py
+++ b/solution.py
@@ -1,6 +1,8 @@
 import jax
 import jax.numpy as jnp
 from jax import lax
+from jax.experimental import pallas as pl
+from jax.experimental.pallas import tpu as pltpu
 from jax.sharding import PartitionSpec as P
 
 STEPS = 2
@@ -51,13 +53,47 @@
     return x + lax.ppermute(x, axis, [(i, i ^ bit) for i in range(count)])
 
 
+def chol_inv_kernel(g_ref, x_ref, a_ref):
+    n = g_ref.shape[0]
+    a_ref[...] = g_ref[...]
+    rows = lax.broadcasted_iota(jnp.int32, (n, n), 0)
+    cols = lax.broadcasted_iota(jnp.int32, (n, n), 1)
+    x_ref[...] = jnp.where(rows == cols, 1.0, 0.0).astype(jnp.float32)
+    lane = lax.broadcasted_iota(jnp.int32, (1, n), 1)
+    sub = lax.broadcasted_iota(jnp.int32, (n, 1), 0)
+
+    def step(k, carry):
+        a = a_ref[...]
+        row = a_ref[pl.ds(k, 1), :]
+        pivot = jnp.sum(jnp.where(lane == k, row, 0.0), axis=1, keepdims=True)
+        root = jnp.sqrt(pivot)
+        col = jnp.sum(jnp.where(cols == k, a, 0.0), axis=1, keepdims=True)
+        below = jnp.where(sub > k, col / root, 0.0)
+        right = jnp.where(lane > k, row / root, 0.0)
+        a_ref[...] = a - below * right
+        xrow = x_ref[pl.ds(k, 1), :] / root
+        x_ref[pl.ds(k, 1), :] = xrow
+        x_ref[...] = x_ref[...] - below * xrow
+        return carry
+
+    lax.fori_loop(0, n, step, 0)
+
+
+def lower_inverse(gram):
+    n = gram.shape[0]
+    return pl.pallas_call(
+        chol_inv_kernel,
+        out_shape=jax.ShapeDtypeStruct((n, n), jnp.float32),
+        scratch_shapes=[pltpu.VMEM((n, n), jnp.float32)],
+    )(gram)
+
+
 def invert_beside(gram, extra, bits):
-    factor = jnp.linalg.cholesky(gram)
+    solved = lower_inverse(gram)
     if bits:
         extra = exchange(extra, *bits.pop(0))
-    factor, extra = lax.optimization_barrier((factor, extra))
-    eye = jnp.eye(gram.shape[0], dtype=jnp.float32)
-    inverse = jax.scipy.linalg.cho_solve((factor, True), eye)
+    solved, extra = lax.optimization_barrier((solved, extra))
+    inverse = jnp.dot(solved.T, solved, precision=lax.Precision.HIGHEST)
     if bits:
         extra = exchange(extra, *bits.pop(0))
     inverse, extra = lax.optimization_barrier((inverse, extra))

time: 110 us -> 109 us (level)
  other arithmetic: 20.4 us -> 9.56 us
  Pallas kernels: 0 us -> 8.15 us
  waiting for transfers between devices: 40.2 us -> 42 us
    another operation x5 -> x0, other arithmetic: 11.4 us -> none  [the longest x3 6.52 us: invert_beside(): factor = jnp.linalg.cholesky(gram)]
    pallas_call x0 -> x1, Pallas kernels: none -> 8.15 us  [lower_inverse(): pl.pallas_call(chol_inv_kernel, out_shape=jax.ShapeDtypeStruct((n, n), jn...]
    ppermute x10, waiting for transfers between devices: 20.6 us -> 26.2 us  [exchange(): return x + lax.ppermute(x, axis, [(i, i ^ bit) for i in range(count)])]
    all_to_all x1, waiting for transfers between devices: 5.23 us -> 1.44 us  [body(): ritz = lax.all_to_all(ritz.reshape(v.shape), 'mem', 0, 1, tiled=True)]
    unnamed x5 -> x4, local copies, waits for them, and re-layouts: 3.63 us -> 2.93 us
  transfers between devices with their start and end apart: 16 -> 16, of which waited for: 9 -> 10; matrix products, arithmetic and copies ran while one was open for 19% -> 9% of each run, Pallas kernels for 0% -> 8%
where the time goes in v5:
time: 109 us; the launch traced here: 108 us
  waiting for transfers between devices  42 us (39%)
  starting transfers between devices  37.6 us (34%)
  other arithmetic  9.56 us (9%)
  Pallas kernels  8.15 us (7%)
  local copies, waits for them, and re-layouts  6.31 us (6%)
  matrix products  4.02 us (4%)
    ppermute x10, waiting for transfers between devices, exchange(): return x + lax.ppermute(x, axis, [(i, i ^ bit) for i in range(count)])  26.2 us
    ppermute x10, starting transfers between devices, exchange(): return x + lax.ppermute(x, axis, [(i, i ^ bit) for i in range(count)])  20.9 us
    all_to_all x1, waiting for transfers between devices, body(): v = lax.all_to_all(perturbations, 'mem', 1, 0, tiled=True)  14.4 us
    pallas_call x1, Pallas kernels, lower_inverse(): pl.pallas_call(chol_inv_kernel, out_shape=jax.ShapeDtypeStruct((n, n), jn...  8.15 us
    all_to_all x1, starting transfers between devices, body(): v = lax.all_to_all(perturbations, 'mem', 1, 0, tiled=True)  7.04 us
    all_to_all x1, starting transfers between devices, body(): ritz = lax.all_to_all(ritz.reshape(v.shape), 'mem', 0, 1, tiled=True)  3.95 us
    ppermute x2, starting transfers between devices, halo(): lax.ppermute(lax.slice_in_dim(block, size - width, size, axis=dim), 'dom'...  3.12 us
    add x2, other arithmetic, adjoint_step(): result + shifted(coef[3] * field, 1, 3) + shifted(coef[4] * field, -1, 3)  2.94 us
  transfers between devices with their start and end apart: 16, of which 10 were waited for; matrix products, arithmetic and copies ran while one was open for 9% of the time, Pallas kernels for 8%

profile of v5, /device:TPU:0, one launch (start us, length us, event | category | flops | bytes accessed | tf_op | source)
XLA Modules:
  0.0 108.5 jit_solution(14626546889327731089)
XLA Ops:
  0.6 2.3 %copy.11 = f32[8,8,8,512]{3,2,0,1:T(8,128)} copy(f32[8,8,8,512]{3,2,1,0:T(8,128)} %param.2) | data formatting | bytes 2097152 | tf_op args[0]
  3.0 7.0 %all-to-all-start = ((f32[8,8,8,512]{3,2,0,1:T(8,128)}), f32[8,8,8,512]{3,2,0,1:T(8,128)S(1)}, u32[]{:S(2)}, u32[]{:S(2)}) async-start(f32[8,8,8,512]{3,2,0,1:T(8,128)} %copy.11), calls=%async_computation | async-start | bytes 2097152 | tf_op jit(solution)/shard_map/all_to_all | solution.py:108
  10.0 1.5 %collective-permute-start.4 = (bf16[2,5,1,4,512]{4,3,2,1,0:T(4,128)(2,1)S(1)}, bf16[2,5,1,4,512]{4,3,2,1,0:T(4,128)(2,1)S(1)}, u32[]{:S(2)}, u32[]{:S(2)}) collective-permute-start(bf16[2,5,1,4,512]{4,3,2,1,0:T(4,128)(2,1)S(1)} %get-tuple-element.50), channel_id=1, source_target_pairs={{0,8},{8,16},{16,24},{24,32},{32,40},{40,48},{48,56},{56,64},{64,7... | collective-permute-start | bytes 122888 | tf_op jit(solution)/shard_map/ppermute | solution.py:16
  11.5 1.3 %collective-permute-start.5 = (bf16[2,5,1,4,512]{4,3,2,1,0:T(4,128)(2,1)S(1)}, bf16[2,5,1,4,512]{4,3,2,1,0:T(4,128)(2,1)S(1)}, u32[]{:S(2)}, u32[]{:S(2)}) collective-permute-start(bf16[2,5,1,4,512]{4,3,2,1,0:T(4,128)(2,1)S(1)} %get-tuple-element.51), channel_id=1, source_target_pairs={{8,0},{16,8},{24,16},{32,24},{40,32},{48,40},{56,48},{64,56},{72,6... | collective-permute-start | bytes 122888 | tf_op jit(solution)/shard_map/ppermute | solution.py:17
  12.8 14.4 %all-to-all-done = f32[8,8,8,512]{3,2,0,1:T(8,128)S(1)} async-done(((f32[8,8,8,512]{3,2,0,1:T(8,128)}), f32[8,8,8,512]{3,2,0,1:T(8,128)S(1)}, u32[]{:S(2)}, u32[]{:S(2)}) %all-to-all-start) | async-done | bytes 1048608 | tf_op jit(solution)/shard_map/all_to_all | solution.py:108
  27.2 0.6 copy.31
  27.8 0.1 fusion.32
  27.9 1.7 %collective-permute-start.1 = (f32[64,1,4,512]{3,0,2,1:T(8,128)S(1)}, f32[64,1,4,512]{3,0,2,1:T(8,128)S(1)}, u32[]{:S(2)}, u32[]{:S(2)}) collective-permute-start(f32[64,1,4,512]{3,0,2,1:T(8,128)S(1)} %get-tuple-element.38), channel_id=1, source_target_pairs={{0,8},{8,16},{16,24},{24,32},{32,40},{40,48},{48,56},{56,64},{64,7... | collective-permute-start | bytes 1572872 | tf_op jit(solution)/shard_map/ppermute | solution.py:16
  29.6 1.3 %collective-permute-start.2 = (f32[64,1,4,512]{3,0,2,1:T(8,128)S(1)}, f32[64,1,4,512]{3,0,2,1:T(8,128)S(1)}, u32[]{:S(2)}, u32[]{:S(2)}) collective-permute-start(f32[64,1,4,512]{3,0,2,1:T(8,128)S(1)} %get-tuple-element.39), channel_id=1, source_target_pairs={{8,0},{16,8},{24,16},{32,24},{40,32},{48,40},{56,48},{64,56},{72,6... | collective-permute-start | bytes 1572872 | tf_op jit(solution)/shard_map/ppermute | solution.py:17
  30.9 0.1 maximum_convert_fusion
  31.0 0.6 copy.18
  31.6 1.0 fusion.34
  32.6 0.6 collective-permute-start
  33.2 3.4 %collective-permute-done = f32[64,64]{1,0:T(8,128)S(1)} collective-permute-done((f32[64,64]{1,0:T(8,128)S(1)}, f32[64,64]{1,0:T(8,128)S(1)}, u32[]{:S(2)}, u32[]{:S(2)}) %collective-permute-start) | collective-permute-done | bytes 16416 | tf_op jit(solution)/shard_map/ppermute | solution.py:53
  36.6 0.0 collective-permute-done.1
  36.6 0.2 pad_maximum_fusion
  36.8 1.2 %collective-permute-start.3 = (f32[64,64]{1,0:T(8,128)S(1)}, f32[64,64]{1,0:T(8,128)S(1)}, u32[]{:S(2)}, u32[]{:S(2)}) collective-permute-start(f32[64,64]{1,0:T(8,128)S(1)} %add.110), channel_id=1, source_target_pairs={{0,2},{1,3},{2,0},{3,1},{4,6},{5,7},{6,4},{7,5},{8,10},{9,11},{10,... | collective-permute-start | bytes 49160 | tf_op jit(solution)/shard_map/ppermute | solution.py:53
  38.0 1.3 %fusion.4 = f32[64,1,16,512]{3,0,2,1:T(8,128)S(1)} fusion(f32[64,1,16,512]{3,0,2,1:T(8,128)S(1)} %pad_maximum_fusion, f32[16,512]{1,0:T(8,128)S(1)} %get-tuple-element.45, f32[16,512]{1,0:T(8,128)S(1)} %get-tuple-element.46, f32[16,512]{1,0:T(8,128)S(1)} %get-tuple-element.47, f32[16,512]{1,0:T(8,128)S(1)} %get-tuple-element.48, ...), kind=kLoop, calls=%fused_computation.20 | loop fusion | flops 4718592 | bytes 4358144 | tf_op jit(solution)/shard_map/add | solution.py:33
  39.3 3.0 %collective-permute-done.3 = f32[64,64]{1,0:T(8,128)S(1)} collective-permute-done((f32[64,64]{1,0:T(8,128)S(1)}, f32[64,64]{1,0:T(8,128)S(1)}, u32[]{:S(2)}, u32[]{:S(2)}) %collective-permute-start.3) | collective-permute-done | bytes 16416 | tf_op jit(solution)/shard_map/ppermute | solution.py:53
  42.3 0.6 collective-permute-start.6
  42.9 1.3 %fusion.10 = f32[64,1,16,512]{3,0,2,1:T(8,128)S(1)} fusion(f32[64,1,16,512]{3,0,2,1:T(8,128)S(1)} %fusion.4, f32[16,512]{1,0:T(8,128)S(1)} %get-tuple-element.41, f32[16,512]{1,0:T(8,128)S(1)} %get-tuple-element.42, f32[16,512]{1,0:T(8,128)S(1)} %get-tuple-element.43, f32[16,512]{1,0:T(8,128)S(1)} %get-tuple-element.44, f32[16,512]{1,0:T(8,128)S(1)} %get-tuple-element.40), kind=kLoop, calls=%fused_computation.26 | loop fusion | flops 4718592 | bytes 4358144 | tf_op jit(solution)/shard_map/add | solution.py:33
  44.1 3.6 %collective-permute-done.6 = f32[64,64]{1,0:T(8,128)S(1)} collective-permute-done((f32[64,64]{1,0:T(8,128)S(1)}, f32[64,64]{1,0:T(8,128)S(1)}, u32[]{:S(2)}, u32[]{:S(2)}) %collective-permute-start.6) | collective-permute-done | bytes 16416 | tf_op jit(solution)/shard_map/ppermute | solution.py:53
  47.7 1.2 %broadcast_multiply_fusion = (f32[64,1,16,512]{3,0,2,1:T(8,128)S(1)}, f32[64,1,16,512]{3,0,2,1:T(8,128)S(1)}, f32[64,1,16,512]{3,0,2,1:T(8,128)S(1)}, f32[64,1,16,512]{3,0,2,1:T(8,128)S(1)}) fusion(f32[64,1,16,512]{3,0,2,1:T(8,128)S(1)} %fusion.10, f32[16,512]{1,0:T(8,128)S(1)} %get-tuple-element.41, f32[16,512]{1,0:T(8,128)S(1)} %get-tuple-element.42, ...), kind=kLoop, calls=%fused_computation.49 | loop fusion | flops 2097152 | bytes 10616832 | tf_op jit(solution)/shard_map/mul | solution.py:38
  49.0 1.0 convolution_bitcast_fusion.1
  50.0 3.6 %collective-permute-start.7 = (f32[2,64,64]{2,1,0:T(8,128)S(1)}, f32[2,64,64]{2,1,0:T(8,128)S(1)}, u32[]{:S(2)}, u32[]{:S(2)}) collective-permute-start(f32[2,64,64]{2,1,0:T(8,128)S(1)} %pad_maximum_fusion.1), channel_id=1, source_target_pairs={{0,8},{8,0},{16,24},{24,16},{32,40},{40,32},{48,56},{56,48},{64,72... | collective-permute-start | bytes 98312 | tf_op jit(solution)/shard_map/ppermute | solution.py:53
  53.6 1.5 %fusion.15 = f32[64,1,16,512]{3,0,2,1:T(8,128)S(1)} fusion(f32[64,1,16,512]{3,0,2,1:T(8,128)S(1)} %get-tuple-element.37, f32[64,1,16,512]{3,0,2,1:T(8,128)S(1)} %get-tuple-element.36, f32[64,1,16,512]{3,0,2,1:T(8,128)S(1)} %get-tuple-element.35, f32[64,1,16,512]{3,0,2,1:T(8,128)S(1)} %get-tuple-element.34, f32[64,1,16,512]{3,0,2,1:T(8,128)S(1)} %fusion.10, ...), kind=kLoop, calls=%fused_computation.31 | loop fusion | flops 2621440 | bytes 12615680 | tf_op jit(solution)/shard_map/add | solution.py:38
  55.1 1.2 %broadcast_multiply_fusion.4 = (f32[64,1,16,512]{3,0,2,1:T(8,128)S(1)}, f32[64,1,16,512]{3,0,2,1:T(8,128)S(1)}, f32[64,1,16,512]{3,0,2,1:T(8,128)S(1)}, f32[64,1,16,512]{3,0,2,1:T(8,128)S(1)}) fusion(f32[64,1,16,512]{3,0,2,1:T(8,128)S(1)} %fusion.15, f32[16,512]{1,0:T(8,128)S(1)} %get-tuple-element.45, f32[16,512]{1,0:T(8,128)S(1)} %get-tuple-element.46, ...), kind=kLoop, calls=%fused_computation.53 | loop fusion | flops 2097152 | bytes 10616832 | tf_op jit(solution)/shard_map/mul | solution.py:38
  56.4 2.6 %collective-permute-start.8 = (f32[2,64,64]{2,1,0:T(8,128)S(1)}, f32[2,64,64]{2,1,0:T(8,128)S(1)}, u32[]{:S(2)}, u32[]{:S(2)}) collective-permute-start(f32[2,64,64]{2,1,0:T(8,128)S(1)} %fusion.31), channel_id=1, source_target_pairs={{0,16},{8,24},{16,0},{24,8},{32,48},{40,56},{48,32},{56,40},{64,80... | collective-permute-start | bytes 98312 | tf_op jit(solution)/shard_map/ppermute | solution.py:53
  59.0 1.4 %fusion.19 = f32[64,1,16,512]{3,0,2,1:T(8,128)S(1)} fusion(f32[64,1,16,512]{3,0,2,1:T(8,128)S(1)} %get-tuple-element.33, f32[64,1,16,512]{3,0,2,1:T(8,128)S(1)} %get-tuple-element.32, f32[64,1,16,512]{3,0,2,1:T(8,128)S(1)} %get-tuple-element.31, f32[64,1,16,512]{3,0,2,1:T(8,128)S(1)} %get-tuple-element.30, f32[64,1,16,512]{3,0,2,1:T(8,128)S(1)} %fusion.15, ...), kind=kLoop, calls=%fused_computation.35 | loop fusion | flops 2621440 | bytes 12615680 | tf_op jit(solution)/shard_map/add | solution.py:38
  60.4 1.2 %collective-permute-done.8 = f32[2,64,64]{2,1,0:T(8,128)S(1)} collective-permute-done((f32[2,64,64]{2,1,0:T(8,128)S(1)}, f32[2,64,64]{2,1,0:T(8,128)S(1)}, u32[]{:S(2)}, u32[]{:S(2)}) %collective-permute-start.8) | collective-permute-done | bytes 32800 | tf_op jit(solution)/shard_map/ppermute | solution.py:53
  61.6 3.6 %collective-permute-start.9 = (f32[2,64,64]{2,1,0:T(8,128)S(1)}, f32[2,64,64]{2,1,0:T(8,128)S(1)}, u32[]{:S(2)}, u32[]{:S(2)}) collective-permute-start(f32[2,64,64]{2,1,0:T(8,128)S(1)} %add.126), channel_id=1, source_target_pairs={{0,32},{8,40},{16,48},{24,56},{32,0},{40,8},{48,16},{56,24},{64,96... | collective-permute-start | bytes 98312 | tf_op jit(solution)/shard_map/ppermute | solution.py:53
  65.3 2.2 %collective-permute-done.9 = f32[2,64,64]{2,1,0:T(8,128)S(1)} collective-permute-done((f32[2,64,64]{2,1,0:T(8,128)S(1)}, f32[2,64,64]{2,1,0:T(8,128)S(1)}, u32[]{:S(2)}, u32[]{:S(2)}) %collective-permute-start.9) | collective-permute-done | bytes 32800 | tf_op jit(solution)/shard_map/ppermute | solution.py:53
  67.5 2.7 %collective-permute-start.10 = (f32[2,64,64]{2,1,0:T(8,128)S(1)}, f32[2,64,64]{2,1,0:T(8,128)S(1)}, u32[]{:S(2)}, u32[]{:S(2)}) collective-permute-start(f32[2,64,64]{2,1,0:T(8,128)S(1)} %add.131), channel_id=1, source_target_pairs={{0,64},{8,72},{16,80},{24,88},{32,96},{40,104},{48,112},{56,120},{... | collective-permute-start | bytes 98312 | tf_op jit(solution)/shard_map/ppermute | solution.py:53
  70.2 2.2 %collective-permute-done.10 = f32[2,64,64]{2,1,0:T(8,128)S(1)} collective-permute-done((f32[2,64,64]{2,1,0:T(8,128)S(1)}, f32[2,64,64]{2,1,0:T(8,128)S(1)}, u32[]{:S(2)}, u32[]{:S(2)}) %collective-permute-start.10) | collective-permute-done | bytes 32800 | tf_op jit(solution)/shard_map/ppermute | solution.py:53
  72.5 0.6 slice_bitcast_fusion
  73.1 0.5 collective-permute-start.11
  73.6 8.2 %shard_map.41 = f32[64,64]{1,0:T(8,128)} custom-call(f32[64,64]{1,0:T(8,128)} %get-tuple-element.53.g_ref), custom_call_target="tpu_custom_call" | custom-call | tf_op jit(solution)/shard_map/pallas_call | solution.py:84
  81.8 1.9 %collective-permute-start.12 = (f32[64,64]{1,0:T(8,128)S(1)}, f32[64,64]{1,0:T(8,128)S(1)}, u32[]{:S(2)}, u32[]{:S(2)}) collective-permute-start(f32[64,64]{1,0:T(8,128)S(1)} %fusion.30), channel_id=1, source_target_pairs={{0,2},{1,3},{2,0},{3,1},{4,6},{5,7},{6,4},{7,5},{8,10},{9,11},{10,... | collective-permute-start | bytes 49160 | tf_op jit(solution)/shard_map/ppermute | solution.py:53
  83.7 1.1 fusion.35
  84.7 2.6 %collective-permute-done.12 = f32[64,64]{1,0:T(8,128)S(1)} collective-permute-done((f32[64,64]{1,0:T(8,128)S(1)}, f32[64,64]{1,0:T(8,128)S(1)}, u32[]{:S(2)}, u32[]{:S(2)}) %collective-permute-start.12) | collective-permute-done | bytes 16416 | tf_op jit(solution)/shard_map/ppermute | solution.py:53
  87.3 1.0 convolution_bitcast_fusion
  88.3 1.6 %copy.15 = f32[64,1,8,512]{3,2,1,0:T(8,128)} copy(f32[64,1,8,512]{3,0,2,1:T(8,128)S(1)} %convolution_bitcast_fusion) | data formatting | bytes 2097152 | tf_op jit(solution)/shard_map/dot_general | solution.py:144
  89.9 3.9 %all-to-all-start.1 = ((f32[64,1,8,512]{3,2,1,0:T(8,128)}), f32[64,1,8,512]{3,2,1,0:T(8,128)S(1)}, u32[]{:S(2)}, u32[]{:S(2)}) async-start(f32[64,1,8,512]{3,2,1,0:T(8,128)} %copy.15), calls=%async_computation.1 | async-start | bytes 2097152 | tf_op jit(solution)/shard_map/all_to_all | solution.py:148
  93.9 3.5 %collective-permute-start.13 = (f32[64,64]{1,0:T(8,128)S(1)}, f32[64,64]{1,0:T(8,128)S(1)}, u32[]{:S(2)}, u32[]{:S(2)}) collective-permute-start(f32[64,64]{1,0:T(8,128)S(1)} %add.134), channel_id=1, source_target_pairs={{0,4},{1,5},{2,6},{3,7},{4,0},{5,1},{6,2},{7,3},{8,12},{9,13},{10,... | collective-permute-start | bytes 49160 | tf_op jit(solution)/shard_map/ppermute | solution.py:53
  97.4 8.0 %collective-permute-done.13 = f32[64,64]{1,0:T(8,128)S(1)} collective-permute-done((f32[64,64]{1,0:T(8,128)S(1)}, f32[64,64]{1,0:T(8,128)S(1)}, u32[]{:S(2)}, u32[]{:S(2)}) %collective-permute-start.13) | collective-permute-done | bytes 16416 | tf_op jit(solution)/shard_map/ppermute | solution.py:53
  105.4 0.6 add_multiply_fusion
  106.0 1.4 %all-to-all-done.1 = f32[64,1,8,512]{3,2,1,0:T(8,128)S(1)} async-done(((f32[64,1,8,512]{3,2,1,0:T(8,128)}), f32[64,1,8,512]{3,2,1,0:T(8,128)S(1)}, u32[]{:S(2)}, u32[]{:S(2)}) %all-to-all-start.1) | async-done | bytes 1048608 | tf_op jit(solution)/shard_map/all_to_all | solution.py:148
  107.4 1.1 copy.30
  (19 shorter events, 0.1 us)
Async XLA Ops:
  0.6 9.4 %copy-start = (bf16[2,5,1,8,512]{4,3,2,1,0:T(8,128)(2,1)S(1)}, bf16[2,5,1,8,512]{4,3,2,1,0:T(8,128)(2,1)}, u32[]{:S(2)}) copy-start(bf16[2,5,1,8,512]{4,3,2,1,0:T(8,128)(2,1)} %param.3) | copy-start | bytes 245764
  3.0 24.2 %all-to-all-start = ((f32[8,8,8,512]{3,2,0,1:T(8,128)}), f32[8,8,8,512]{3,2,0,1:T(8,128)S(1)}, u32[]{:S(2)}, u32[]{:S(2)}) async-start(f32[8,8,8,512]{3,2,0,1:T(8,128)} %copy.11), calls=%async_computation | async-start | bytes 2097152 | tf_op jit(solution)/shard_map/all_to_all | solution.py:108
  10.0 20.8 %collective-permute-start.4 = (bf16[2,5,1,4,512]{4,3,2,1,0:T(4,128)(2,1)S(1)}, bf16[2,5,1,4,512]{4,3,2,1,0:T(4,128)(2,1)S(1)}, u32[]{:S(2)}, u32[]{:S(2)}) collective-permute-start(bf16[2,5,1,4,512]{4,3,2,1,0:T(4,128)(2,1)S(1)} %get-tuple-element.50), channel_id=1, source_target_pairs={{0,8},{8,16},{16,24},{24,32},{32,40},{40,48},{48,56},{56,64},{64,7... | collective-permute-start | bytes 122888 | tf_op jit(solution)/shard_map/ppermute | solution.py:16
  11.5 19.4 %collective-permute-start.5 = (bf16[2,5,1,4,512]{4,3,2,1,0:T(4,128)(2,1)S(1)}, bf16[2,5,1,4,512]{4,3,2,1,0:T(4,128)(2,1)S(1)}, u32[]{:S(2)}, u32[]{:S(2)}) collective-permute-start(bf16[2,5,1,4,512]{4,3,2,1,0:T(4,128)(2,1)S(1)} %get-tuple-element.51), channel_id=1, source_target_pairs={{8,0},{16,8},{24,16},{32,24},{40,32},{48,40},{56,48},{64,56},{72,6... | collective-permute-start | bytes 122888 | tf_op jit(solution)/shard_map/ppermute | solution.py:17
  27.9 8.7 %collective-permute-start.1 = (f32[64,1,4,512]{3,0,2,1:T(8,128)S(1)}, f32[64,1,4,512]{3,0,2,1:T(8,128)S(1)}, u32[]{:S(2)}, u32[]{:S(2)}) collective-permute-start(f32[64,1,4,512]{3,0,2,1:T(8,128)S(1)} %get-tuple-element.38), channel_id=1, source_target_pairs={{0,8},{8,16},{16,24},{24,32},{32,40},{40,48},{48,56},{56,64},{64,7... | collective-permute-start | bytes 1572872 | tf_op jit(solution)/shard_map/ppermute | solution.py:16
  29.6 7.0 %collective-permute-start.2 = (f32[64,1,4,512]{3,0,2,1:T(8,128)S(1)}, f32[64,1,4,512]{3,0,2,1:T(8,128)S(1)}, u32[]{:S(2)}, u32[]{:S(2)}) collective-permute-start(f32[64,1,4,512]{3,0,2,1:T(8,128)S(1)} %get-tuple-element.39), channel_id=1, source_target_pairs={{8,0},{16,8},{24,16},{32,24},{40,32},{48,40},{56,48},{64,56},{72,6... | collective-permute-start | bytes 1572872 | tf_op jit(solution)/shard_map/ppermute | solution.py:17
  32.6 4.0 %collective-permute-start = (f32[64,64]{1,0:T(8,128)S(1)}, f32[64,64]{1,0:T(8,128)S(1)}, u32[]{:S(2)}, u32[]{:S(2)}) collective-permute-start(f32[64,64]{1,0:T(8,128)S(1)} %fusion.34), channel_id=1, source_target_pairs={{0,1},{1,0},{2,3},{3,2},{4,5},{5,4},{6,7},{7,6},{8,9},{9,8},{10,11... | collective-permute-start | bytes 49160 | tf_op jit(solution)/shard_map/ppermute | solution.py:53
  36.8 5.5 %collective-permute-start.3 = (f32[64,64]{1,0:T(8,128)S(1)}, f32[64,64]{1,0:T(8,128)S(1)}, u32[]{:S(2)}, u32[]{:S(2)}) collective-permute-start(f32[64,64]{1,0:T(8,128)S(1)} %add.110), channel_id=1, source_target_pairs={{0,2},{1,3},{2,0},{3,1},{4,6},{5,7},{6,4},{7,5},{8,10},{9,11},{10,... | collective-permute-start | bytes 49160 | tf_op jit(solution)/shard_map/ppermute | solution.py:53
  42.3 5.4 %collective-permute-start.6 = (f32[64,64]{1,0:T(8,128)S(1)}, f32[64,64]{1,0:T(8,128)S(1)}, u32[]{:S(2)}, u32[]{:S(2)}) collective-permute-start(f32[64,64]{1,0:T(8,128)S(1)} %add.111), channel_id=1, source_target_pairs={{0,4},{1,5},{2,6},{3,7},{4,0},{5,1},{6,2},{7,3},{8,12},{9,13},{10,... | collective-permute-start | bytes 49160 | tf_op jit(solution)/shard_map/ppermute | solution.py:53
  50.0 5.1 %collective-permute-start.7 = (f32[2,64,64]{2,1,0:T(8,128)S(1)}, f32[2,64,64]{2,1,0:T(8,128)S(1)}, u32[]{:S(2)}, u32[]{:S(2)}) collective-permute-start(f32[2,64,64]{2,1,0:T(8,128)S(1)} %pad_maximum_fusion.1), channel_id=1, source_target_pairs={{0,8},{8,0},{16,24},{24,16},{32,40},{40,32},{48,56},{56,48},{64,72... | collective-permute-start | bytes 98312 | tf_op jit(solution)/shard_map/ppermute | solution.py:53
  56.4 5.3 %collective-permute-start.8 = (f32[2,64,64]{2,1,0:T(8,128)S(1)}, f32[2,64,64]{2,1,0:T(8,128)S(1)}, u32[]{:S(2)}, u32[]{:S(2)}) collective-permute-start(f32[2,64,64]{2,1,0:T(8,128)S(1)} %fusion.31), channel_id=1, source_target_pairs={{0,16},{8,24},{16,0},{24,8},{32,48},{40,56},{48,32},{56,40},{64,80... | collective-permute-start | bytes 98312 | tf_op jit(solution)/shard_map/ppermute | solution.py:53
  61.6 5.9 %collective-permute-start.9 = (f32[2,64,64]{2,1,0:T(8,128)S(1)}, f32[2,64,64]{2,1,0:T(8,128)S(1)}, u32[]{:S(2)}, u32[]{:S(2)}) collective-permute-start(f32[2,64,64]{2,1,0:T(8,128)S(1)} %add.126), channel_id=1, source_target_pairs={{0,32},{8,40},{16,48},{24,56},{32,0},{40,8},{48,16},{56,24},{64,96... | collective-permute-start | bytes 98312 | tf_op jit(solution)/shard_map/ppermute | solution.py:53
  67.5 4.9 %collective-permute-start.10 = (f32[2,64,64]{2,1,0:T(8,128)S(1)}, f32[2,64,64]{2,1,0:T(8,128)S(1)}, u32[]{:S(2)}, u32[]{:S(2)}) collective-permute-start(f32[2,64,64]{2,1,0:T(8,128)S(1)} %add.131), channel_id=1, source_target_pairs={{0,64},{8,72},{16,80},{24,88},{32,96},{40,104},{48,112},{56,120},{... | collective-permute-start | bytes 98312 | tf_op jit(solution)/shard_map/ppermute | solution.py:53
  73.1 8.7 %collective-permute-start.11 = (f32[64,64]{1,0:T(8,128)S(1)}, f32[64,64]{1,0:T(8,128)S(1)}, u32[]{:S(2)}, u32[]{:S(2)}) collective-permute-start(f32[64,64]{1,0:T(8,128)S(1)} %get-tuple-element.52), channel_id=1, source_target_pairs={{0,1},{1,0},{2,3},{3,2},{4,5},{5,4},{6,7},{7,6},{8,9},{9,8},{10,11... | collective-permute-start | bytes 49160 | tf_op jit(solution)/shard_map/ppermute | solution.py:53
  81.8 5.5 %collective-permute-start.12 = (f32[64,64]{1,0:T(8,128)S(1)}, f32[64,64]{1,0:T(8,128)S(1)}, u32[]{:S(2)}, u32[]{:S(2)}) collective-permute-start(f32[64,64]{1,0:T(8,128)S(1)} %fusion.30), channel_id=1, source_target_pairs={{0,2},{1,3},{2,0},{3,1},{4,6},{5,7},{6,4},{7,5},{8,10},{9,11},{10,... | collective-permute-start | bytes 49160 | tf_op jit(solution)/shard_map/ppermute | solution.py:53
  89.9 17.5 %all-to-all-start.1 = ((f32[64,1,8,512]{3,2,1,0:T(8,128)}), f32[64,1,8,512]{3,2,1,0:T(8,128)S(1)}, u32[]{:S(2)}, u32[]{:S(2)}) async-start(f32[64,1,8,512]{3,2,1,0:T(8,128)} %copy.15), calls=%async_computation.1 | async-start | bytes 2097152 | tf_op jit(solution)/shard_map/all_to_all | solution.py:148
  93.9 11.5 %collective-permute-start.13 = (f32[64,64]{1,0:T(8,128)S(1)}, f32[64,64]{1,0:T(8,128)S(1)}, u32[]{:S(2)}, u32[]{:S(2)}) collective-permute-start(f32[64,64]{1,0:T(8,128)S(1)} %add.134), channel_id=1, source_target_pairs={{0,4},{1,5},{2,6},{3,7},{4,0},{5,1},{6,2},{7,3},{8,12},{9,13},{10,... | collective-permute-start | bytes 49160 | tf_op jit(solution)/shard_map/ppermute | solution.py:53

commit v6 on v5

--- a/solution.py
+++ b/solution.py
@@ -94,9 +94,6 @@
         extra = exchange(extra, *bits.pop(0))
     solved, extra = lax.optimization_barrier((solved, extra))
     inverse = jnp.dot(solved.T, solved, precision=lax.Precision.HIGHEST)
-    if bits:
-        extra = exchange(extra, *bits.pop(0))
-    inverse, extra = lax.optimization_barrier((inverse, extra))
     return inverse, extra
 
 

time: 109 us -> 111 us (1.018)
    ppermute x10, waiting for transfers between devices: 26.2 us -> 27.9 us  [exchange(): return x + lax.ppermute(x, axis, [(i, i ^ bit) for i in range(count)])]
    all_to_all x1, waiting for transfers between devices: 1.44 us -> 0.01 us  [body(): ritz = lax.all_to_all(ritz.reshape(v.shape), 'mem', 0, 1, tiled=True)]
    ppermute x10, starting transfers between devices: 20.9 us -> 22 us  [exchange(): return x + lax.ppermute(x, axis, [(i, i ^ bit) for i in range(count)])]
  transfers between devices with their start and end apart: 16 -> 16, of which waited for: 10 -> 9; matrix products, arithmetic and copies ran while one was open for 9% -> 8% of each run, Pallas kernels for 8% -> 7%
where the time goes in v6:
time: 111 us; the launch traced here: 110 us
  waiting for transfers between devices  42.3 us (38%)
  starting transfers between devices  38.7 us (35%)
  other arithmetic  9.56 us (9%)
  Pallas kernels  8.15 us (7%)
  local copies, waits for them, and re-layouts  6.31 us (6%)
  matrix products  4.02 us (4%)
    ppermute x10, waiting for transfers between devices, exchange(): return x + lax.ppermute(x, axis, [(i, i ^ bit) for i in range(count)])  27.9 us
    ppermute x10, starting transfers between devices, exchange(): return x + lax.ppermute(x, axis, [(i, i ^ bit) for i in range(count)])  22 us
    all_to_all x1, waiting for transfers between devices, body(): v = lax.all_to_all(perturbations, 'mem', 1, 0, tiled=True)  14.4 us
    pallas_call x1, Pallas kernels, lower_inverse(): pl.pallas_call(chol_inv_kernel, out_shape=jax.ShapeDtypeStruct((n, n), jn...  8.15 us
    all_to_all x1, starting transfers between devices, body(): v = lax.all_to_all(perturbations, 'mem', 1, 0, tiled=True)  7.04 us
    all_to_all x1, starting transfers between devices, body(): ritz = lax.all_to_all(ritz.reshape(v.shape), 'mem', 0, 1, tiled=True)  3.95 us
    ppermute x2, starting transfers between devices, halo(): lax.ppermute(lax.slice_in_dim(block, size - width, size, axis=dim), 'dom'...  3.12 us
    add x2, other arithmetic, adjoint_step(): result + shifted(coef[3] * field, 1, 3) + shifted(coef[4] * field, -1, 3)  2.94 us
  transfers between devices with their start and end apart: 16, of which 9 were waited for; matrix products, arithmetic and copies ran while one was open for 8% of the time, Pallas kernels for 7%

profile of v6, /device:TPU:0, one launch (start us, length us, event | category | flops | bytes accessed | tf_op | source)
XLA Modules:
  0.0 109.9 jit_solution(17999266039609213256)
XLA Ops:
  0.6 2.3 %copy.11 = f32[8,8,8,512]{3,2,0,1:T(8,128)} copy(f32[8,8,8,512]{3,2,1,0:T(8,128)} %param.2) | data formatting | bytes 2097152 | tf_op args[0]
  3.0 7.0 %all-to-all-start = ((f32[8,8,8,512]{3,2,0,1:T(8,128)}), f32[8,8,8,512]{3,2,0,1:T(8,128)S(1)}, u32[]{:S(2)}, u32[]{:S(2)}) async-start(f32[8,8,8,512]{3,2,0,1:T(8,128)} %copy.11), calls=%async_computation | async-start | bytes 2097152 | tf_op jit(solution)/shard_map/all_to_all | solution.py:105
  10.0 1.5 %collective-permute-start.4 = (bf16[2,5,1,4,512]{4,3,2,1,0:T(4,128)(2,1)S(1)}, bf16[2,5,1,4,512]{4,3,2,1,0:T(4,128)(2,1)S(1)}, u32[]{:S(2)}, u32[]{:S(2)}) collective-permute-start(bf16[2,5,1,4,512]{4,3,2,1,0:T(4,128)(2,1)S(1)} %get-tuple-element.46), channel_id=1, source_target_pairs={{0,8},{8,16},{16,24},{24,32},{32,40},{40,48},{48,56},{56,64},{64,7... | collective-permute-start | bytes 122888 | tf_op jit(solution)/shard_map/ppermute | solution.py:16
  11.5 1.3 %collective-permute-start.5 = (bf16[2,5,1,4,512]{4,3,2,1,0:T(4,128)(2,1)S(1)}, bf16[2,5,1,4,512]{4,3,2,1,0:T(4,128)(2,1)S(1)}, u32[]{:S(2)}, u32[]{:S(2)}) collective-permute-start(bf16[2,5,1,4,512]{4,3,2,1,0:T(4,128)(2,1)S(1)} %get-tuple-element.47), channel_id=1, source_target_pairs={{8,0},{16,8},{24,16},{32,24},{40,32},{48,40},{56,48},{64,56},{72,6... | collective-permute-start | bytes 122888 | tf_op jit(solution)/shard_map/ppermute | solution.py:17
  12.8 14.4 %all-to-all-done = f32[8,8,8,512]{3,2,0,1:T(8,128)S(1)} async-done(((f32[8,8,8,512]{3,2,0,1:T(8,128)}), f32[8,8,8,512]{3,2,0,1:T(8,128)S(1)}, u32[]{:S(2)}, u32[]{:S(2)}) %all-to-all-start) | async-done | bytes 1048608 | tf_op jit(solution)/shard_map/all_to_all | solution.py:105
  27.2 0.6 copy.31
  27.8 0.1 fusion.31
  27.9 1.7 %collective-permute-start.1 = (f32[64,1,4,512]{3,0,2,1:T(8,128)S(1)}, f32[64,1,4,512]{3,0,2,1:T(8,128)S(1)}, u32[]{:S(2)}, u32[]{:S(2)}) collective-permute-start(f32[64,1,4,512]{3,0,2,1:T(8,128)S(1)} %get-tuple-element.34), channel_id=1, source_target_pairs={{0,8},{8,16},{16,24},{24,32},{32,40},{40,48},{48,56},{56,64},{64,7... | collective-permute-start | bytes 1572872 | tf_op jit(solution)/shard_map/ppermute | solution.py:16
  29.6 1.3 %collective-permute-start.2 = (f32[64,1,4,512]{3,0,2,1:T(8,128)S(1)}, f32[64,1,4,512]{3,0,2,1:T(8,128)S(1)}, u32[]{:S(2)}, u32[]{:S(2)}) collective-permute-start(f32[64,1,4,512]{3,0,2,1:T(8,128)S(1)} %get-tuple-element.35), channel_id=1, source_target_pairs={{8,0},{16,8},{24,16},{32,24},{40,32},{48,40},{56,48},{64,56},{72,6... | collective-permute-start | bytes 1572872 | tf_op jit(solution)/shard_map/ppermute | solution.py:17
  30.9 0.1 maximum_convert_fusion
  31.0 0.6 copy.18
  31.6 1.0 fusion.33
  32.6 0.6 collective-permute-start
  33.2 3.4 %collective-permute-done = f32[64,64]{1,0:T(8,128)S(1)} collective-permute-done((f32[64,64]{1,0:T(8,128)S(1)}, f32[64,64]{1,0:T(8,128)S(1)}, u32[]{:S(2)}, u32[]{:S(2)}) %collective-permute-start) | collective-permute-done | bytes 16416 | tf_op jit(solution)/shard_map/ppermute | solution.py:53
  36.6 0.0 collective-permute-done.1
  36.6 0.0 collective-permute-done.2
  36.6 0.2 pad_maximum_fusion
  36.8 1.2 %collective-permute-start.3 = (f32[64,64]{1,0:T(8,128)S(1)}, f32[64,64]{1,0:T(8,128)S(1)}, u32[]{:S(2)}, u32[]{:S(2)}) collective-permute-start(f32[64,64]{1,0:T(8,128)S(1)} %add.110), channel_id=1, source_target_pairs={{0,2},{1,3},{2,0},{3,1},{4,6},{5,7},{6,4},{7,5},{8,10},{9,11},{10,... | collective-permute-start | bytes 49160 | tf_op jit(solution)/shard_map/ppermute | solution.py:53
  38.0 1.3 %fusion.4 = f32[64,1,16,512]{3,0,2,1:T(8,128)S(1)} fusion(f32[64,1,16,512]{3,0,2,1:T(8,128)S(1)} %pad_maximum_fusion, f32[16,512]{1,0:T(8,128)S(1)} %get-tuple-element.41, f32[16,512]{1,0:T(8,128)S(1)} %get-tuple-element.42, f32[16,512]{1,0:T(8,128)S(1)} %get-tuple-element.43, f32[16,512]{1,0:T(8,128)S(1)} %get-tuple-element.44, ...), kind=kLoop, calls=%fused_computation.20 | loop fusion | flops 4718592 | bytes 4358144 | tf_op jit(solution)/shard_map/add | solution.py:33
  39.3 3.0 %collective-permute-done.3 = f32[64,64]{1,0:T(8,128)S(1)} collective-permute-done((f32[64,64]{1,0:T(8,128)S(1)}, f32[64,64]{1,0:T(8,128)S(1)}, u32[]{:S(2)}, u32[]{:S(2)}) %collective-permute-start.3) | collective-permute-done | bytes 16416 | tf_op jit(solution)/shard_map/ppermute | solution.py:53
  42.3 0.6 collective-permute-start.6
  42.9 1.3 %fusion.10 = f32[64,1,16,512]{3,0,2,1:T(8,128)S(1)} fusion(f32[64,1,16,512]{3,0,2,1:T(8,128)S(1)} %fusion.4, f32[16,512]{1,0:T(8,128)S(1)} %get-tuple-element.37, f32[16,512]{1,0:T(8,128)S(1)} %get-tuple-element.38, f32[16,512]{1,0:T(8,128)S(1)} %get-tuple-element.39, f32[16,512]{1,0:T(8,128)S(1)} %get-tuple-element.40, f32[16,512]{1,0:T(8,128)S(1)} %get-tuple-element.36), kind=kLoop, calls=%fused_computation.26 | loop fusion | flops 4718592 | bytes 4358144 | tf_op jit(solution)/shard_map/add | solution.py:33
  44.1 3.6 %collective-permute-done.6 = f32[64,64]{1,0:T(8,128)S(1)} collective-permute-done((f32[64,64]{1,0:T(8,128)S(1)}, f32[64,64]{1,0:T(8,128)S(1)}, u32[]{:S(2)}, u32[]{:S(2)}) %collective-permute-start.6) | collective-permute-done | bytes 16416 | tf_op jit(solution)/shard_map/ppermute | solution.py:53
  47.7 1.2 %broadcast_multiply_fusion = (f32[64,1,16,512]{3,0,2,1:T(8,128)S(1)}, f32[64,1,16,512]{3,0,2,1:T(8,128)S(1)}, f32[64,1,16,512]{3,0,2,1:T(8,128)S(1)}, f32[64,1,16,512]{3,0,2,1:T(8,128)S(1)}) fusion(f32[64,1,16,512]{3,0,2,1:T(8,128)S(1)} %fusion.10, f32[16,512]{1,0:T(8,128)S(1)} %get-tuple-element.37, f32[16,512]{1,0:T(8,128)S(1)} %get-tuple-element.38, ...), kind=kLoop, calls=%fused_computation.50 | loop fusion | flops 2097152 | bytes 10616832 | tf_op jit(solution)/shard_map/mul | solution.py:38
  49.0 1.0 convolution_bitcast_fusion.2
  50.0 3.6 %collective-permute-start.7 = (f32[2,64,64]{2,1,0:T(8,128)S(1)}, f32[2,64,64]{2,1,0:T(8,128)S(1)}, u32[]{:S(2)}, u32[]{:S(2)}) collective-permute-start(f32[2,64,64]{2,1,0:T(8,128)S(1)} %pad_maximum_fusion.1), channel_id=1, source_target_pairs={{0,8},{8,0},{16,24},{24,16},{32,40},{40,32},{48,56},{56,48},{64,72... | collective-permute-start | bytes 98312 | tf_op jit(solution)/shard_map/ppermute | solution.py:53
  53.6 1.5 %fusion.15 = f32[64,1,16,512]{3,0,2,1:T(8,128)S(1)} fusion(f32[64,1,16,512]{3,0,2,1:T(8,128)S(1)} %get-tuple-element.33, f32[64,1,16,512]{3,0,2,1:T(8,128)S(1)} %get-tuple-element.32, f32[64,1,16,512]{3,0,2,1:T(8,128)S(1)} %get-tuple-element.31, f32[64,1,16,512]{3,0,2,1:T(8,128)S(1)} %get-tuple-element.30, f32[64,1,16,512]{3,0,2,1:T(8,128)S(1)} %fusion.10, ...), kind=kLoop, calls=%fused_computation.31 | loop fusion | flops 2621440 | bytes 12615680 | tf_op jit(solution)/shard_map/add | solution.py:38
  55.1 1.2 %broadcast_multiply_fusion.4 = (f32[64,1,16,512]{3,0,2,1:T(8,128)S(1)}, f32[64,1,16,512]{3,0,2,1:T(8,128)S(1)}, f32[64,1,16,512]{3,0,2,1:T(8,128)S(1)}, f32[64,1,16,512]{3,0,2,1:T(8,128)S(1)}) fusion(f32[64,1,16,512]{3,0,2,1:T(8,128)S(1)} %fusion.15, f32[16,512]{1,0:T(8,128)S(1)} %get-tuple-element.41, f32[16,512]{1,0:T(8,128)S(1)} %get-tuple-element.42, ...), kind=kLoop, calls=%fused_computation.54 | loop fusion | flops 2097152 | bytes 10616832 | tf_op jit(solution)/shard_map/mul | solution.py:38
  56.4 2.6 %collective-permute-start.8 = (f32[2,64,64]{2,1,0:T(8,128)S(1)}, f32[2,64,64]{2,1,0:T(8,128)S(1)}, u32[]{:S(2)}, u32[]{:S(2)}) collective-permute-start(f32[2,64,64]{2,1,0:T(8,128)S(1)} %fusion.30), channel_id=1, source_target_pairs={{0,16},{8,24},{16,0},{24,8},{32,48},{40,56},{48,32},{56,40},{64,80... | collective-permute-start | bytes 98312 | tf_op jit(solution)/shard_map/ppermute | solution.py:53
  59.0 1.4 %fusion.19 = f32[64,1,16,512]{3,0,2,1:T(8,128)S(1)} fusion(f32[64,1,16,512]{3,0,2,1:T(8,128)S(1)} %get-tuple-element.29, f32[64,1,16,512]{3,0,2,1:T(8,128)S(1)} %get-tuple-element.28, f32[64,1,16,512]{3,0,2,1:T(8,128)S(1)} %get-tuple-element.27, f32[64,1,16,512]{3,0,2,1:T(8,128)S(1)} %get-tuple-element.26, f32[64,1,16,512]{3,0,2,1:T(8,128)S(1)} %fusion.15, ...), kind=kLoop, calls=%fused_computation.35 | loop fusion | flops 2621440 | bytes 12615680 | tf_op jit(solution)/shard_map/add | solution.py:38
  60.4 1.2 %collective-permute-done.8 = f32[2,64,64]{2,1,0:T(8,128)S(1)} collective-permute-done((f32[2,64,64]{2,1,0:T(8,128)S(1)}, f32[2,64,64]{2,1,0:T(8,128)S(1)}, u32[]{:S(2)}, u32[]{:S(2)}) %collective-permute-start.8) | collective-permute-done | bytes 32800 | tf_op jit(solution)/shard_map/ppermute | solution.py:53
  61.6 3.6 %collective-permute-start.9 = (f32[2,64,64]{2,1,0:T(8,128)S(1)}, f32[2,64,64]{2,1,0:T(8,128)S(1)}, u32[]{:S(2)}, u32[]{:S(2)}) collective-permute-start(f32[2,64,64]{2,1,0:T(8,128)S(1)} %add.126), channel_id=1, source_target_pairs={{0,32},{8,40},{16,48},{24,56},{32,0},{40,8},{48,16},{56,24},{64,96... | collective-permute-start | bytes 98312 | tf_op jit(solution)/shard_map/ppermute | solution.py:53
  65.3 2.2 %collective-permute-done.9 = f32[2,64,64]{2,1,0:T(8,128)S(1)} collective-permute-done((f32[2,64,64]{2,1,0:T(8,128)S(1)}, f32[2,64,64]{2,1,0:T(8,128)S(1)}, u32[]{:S(2)}, u32[]{:S(2)}) %collective-permute-start.9) | collective-permute-done | bytes 32800 | tf_op jit(solution)/shard_map/ppermute | solution.py:53
  67.5 2.7 %collective-permute-start.10 = (f32[2,64,64]{2,1,0:T(8,128)S(1)}, f32[2,64,64]{2,1,0:T(8,128)S(1)}, u32[]{:S(2)}, u32[]{:S(2)}) collective-permute-start(f32[2,64,64]{2,1,0:T(8,128)S(1)} %add.131), channel_id=1, source_target_pairs={{0,64},{8,72},{16,80},{24,88},{32,96},{40,104},{48,112},{56,120},{... | collective-permute-start | bytes 98312 | tf_op jit(solution)/shard_map/ppermute | solution.py:53
  70.2 2.2 %collective-permute-done.10 = f32[2,64,64]{2,1,0:T(8,128)S(1)} collective-permute-done((f32[2,64,64]{2,1,0:T(8,128)S(1)}, f32[2,64,64]{2,1,0:T(8,128)S(1)}, u32[]{:S(2)}, u32[]{:S(2)}) %collective-permute-start.10) | collective-permute-done | bytes 32800 | tf_op jit(solution)/shard_map/ppermute | solution.py:53
  72.5 0.6 slice_bitcast_fusion
  73.1 0.5 collective-permute-start.11
  73.6 8.2 %shard_map.41 = f32[64,64]{1,0:T(8,128)} custom-call(f32[64,64]{1,0:T(8,128)} %get-tuple-element.49.g_ref), custom_call_target="tpu_custom_call" | custom-call | tf_op jit(solution)/shard_map/pallas_call | solution.py:84
  81.8 1.1 convolution_bitcast_fusion.1
  82.9 1.0 convolution_bitcast_fusion
  83.9 1.6 %copy.15 = f32[64,1,8,512]{3,2,1,0:T(8,128)} copy(f32[64,1,8,512]{3,0,2,1:T(8,128)S(1)} %convolution_bitcast_fusion) | data formatting | bytes 2097152 | tf_op jit(solution)/shard_map/dot_general | solution.py:141
  85.5 4.0 %all-to-all-start.1 = ((f32[64,1,8,512]{3,2,1,0:T(8,128)}), f32[64,1,8,512]{3,2,1,0:T(8,128)S(1)}, u32[]{:S(2)}, u32[]{:S(2)}) async-start(f32[64,1,8,512]{3,2,1,0:T(8,128)} %copy.15), calls=%async_computation.1 | async-start | bytes 2097152 | tf_op jit(solution)/shard_map/all_to_all | solution.py:145
  89.4 3.5 %collective-permute-start.12 = (f32[64,64]{1,0:T(8,128)S(1)}, f32[64,64]{1,0:T(8,128)S(1)}, u32[]{:S(2)}, u32[]{:S(2)}) collective-permute-start(f32[64,64]{1,0:T(8,128)S(1)} %fusion.29), channel_id=1, source_target_pairs={{0,2},{1,3},{2,0},{3,1},{4,6},{5,7},{6,4},{7,5},{8,10},{9,11},{10,... | collective-permute-start | bytes 49160 | tf_op jit(solution)/shard_map/ppermute | solution.py:53
  93.0 9.8 %collective-permute-done.12 = f32[64,64]{1,0:T(8,128)S(1)} collective-permute-done((f32[64,64]{1,0:T(8,128)S(1)}, f32[64,64]{1,0:T(8,128)S(1)}, u32[]{:S(2)}, u32[]{:S(2)}) %collective-permute-start.12) | collective-permute-done | bytes 16416 | tf_op jit(solution)/shard_map/ppermute | solution.py:53
  102.8 3.0 %collective-permute-start.13 = (f32[64,64]{1,0:T(8,128)S(1)}, f32[64,64]{1,0:T(8,128)S(1)}, u32[]{:S(2)}, u32[]{:S(2)}) collective-permute-start(f32[64,64]{1,0:T(8,128)S(1)} %add.134), channel_id=1, source_target_pairs={{0,4},{1,5},{2,6},{3,7},{4,0},{5,1},{6,2},{7,3},{8,12},{9,13},{10,... | collective-permute-start | bytes 49160 | tf_op jit(solution)/shard_map/ppermute | solution.py:53
  105.8 2.4 %collective-permute-done.13 = f32[64,64]{1,0:T(8,128)S(1)} collective-permute-done((f32[64,64]{1,0:T(8,128)S(1)}, f32[64,64]{1,0:T(8,128)S(1)}, u32[]{:S(2)}, u32[]{:S(2)}) %collective-permute-start.13) | collective-permute-done | bytes 16416 | tf_op jit(solution)/shard_map/ppermute | solution.py:53
  108.2 0.6 add_multiply_fusion
  108.8 1.1 copy.30
  (19 shorter events, 0.1 us)
Async XLA Ops:
  0.6 9.4 %copy-start = (bf16[2,5,1,8,512]{4,3,2,1,0:T(8,128)(2,1)S(1)}, bf16[2,5,1,8,512]{4,3,2,1,0:T(8,128)(2,1)}, u32[]{:S(2)}) copy-start(bf16[2,5,1,8,512]{4,3,2,1,0:T(8,128)(2,1)} %param.3) | copy-start | bytes 245764
  3.0 24.2 %all-to-all-start = ((f32[8,8,8,512]{3,2,0,1:T(8,128)}), f32[8,8,8,512]{3,2,0,1:T(8,128)S(1)}, u32[]{:S(2)}, u32[]{:S(2)}) async-start(f32[8,8,8,512]{3,2,0,1:T(8,128)} %copy.11), calls=%async_computation | async-start | bytes 2097152 | tf_op jit(solution)/shard_map/all_to_all | solution.py:105
  10.0 20.8 %collective-permute-start.4 = (bf16[2,5,1,4,512]{4,3,2,1,0:T(4,128)(2,1)S(1)}, bf16[2,5,1,4,512]{4,3,2,1,0:T(4,128)(2,1)S(1)}, u32[]{:S(2)}, u32[]{:S(2)}) collective-permute-start(bf16[2,5,1,4,512]{4,3,2,1,0:T(4,128)(2,1)S(1)} %get-tuple-element.46), channel_id=1, source_target_pairs={{0,8},{8,16},{16,24},{24,32},{32,40},{40,48},{48,56},{56,64},{64,7... | collective-permute-start | bytes 122888 | tf_op jit(solution)/shard_map/ppermute | solution.py:16
  11.5 19.4 %collective-permute-start.5 = (bf16[2,5,1,4,512]{4,3,2,1,0:T(4,128)(2,1)S(1)}, bf16[2,5,1,4,512]{4,3,2,1,0:T(4,128)(2,1)S(1)}, u32[]{:S(2)}, u32[]{:S(2)}) collective-permute-start(bf16[2,5,1,4,512]{4,3,2,1,0:T(4,128)(2,1)S(1)} %get-tuple-element.47), channel_id=1, source_target_pairs={{8,0},{16,8},{24,16},{32,24},{40,32},{48,40},{56,48},{64,56},{72,6... | collective-permute-start | bytes 122888 | tf_op jit(solution)/shard_map/ppermute | solution.py:17
  27.9 8.7 %collective-permute-start.1 = (f32[64,1,4,512]{3,0,2,1:T(8,128)S(1)}, f32[64,1,4,512]{3,0,2,1:T(8,128)S(1)}, u32[]{:S(2)}, u32[]{:S(2)}) collective-permute-start(f32[64,1,4,512]{3,0,2,1:T(8,128)S(1)} %get-tuple-element.34), channel_id=1, source_target_pairs={{0,8},{8,16},{16,24},{24,32},{32,40},{40,48},{48,56},{56,64},{64,7... | collective-permute-start | bytes 1572872 | tf_op jit(solution)/shard_map/ppermute | solution.py:16
  29.6 7.0 %collective-permute-start.2 = (f32[64,1,4,512]{3,0,2,1:T(8,128)S(1)}, f32[64,1,4,512]{3,0,2,1:T(8,128)S(1)}, u32[]{:S(2)}, u32[]{:S(2)}) collective-permute-start(f32[64,1,4,512]{3,0,2,1:T(8,128)S(1)} %get-tuple-element.35), channel_id=1, source_target_pairs={{8,0},{16,8},{24,16},{32,24},{40,32},{48,40},{56,48},{64,56},{72,6... | collective-permute-start | bytes 1572872 | tf_op jit(solution)/shard_map/ppermute | solution.py:17
  32.6 4.0 %collective-permute-start = (f32[64,64]{1,0:T(8,128)S(1)}, f32[64,64]{1,0:T(8,128)S(1)}, u32[]{:S(2)}, u32[]{:S(2)}) collective-permute-start(f32[64,64]{1,0:T(8,128)S(1)} %fusion.33), channel_id=1, source_target_pairs={{0,1},{1,0},{2,3},{3,2},{4,5},{5,4},{6,7},{7,6},{8,9},{9,8},{10,11... | collective-permute-start | bytes 49160 | tf_op jit(solution)/shard_map/ppermute | solution.py:53
  36.8 5.5 %collective-permute-start.3 = (f32[64,64]{1,0:T(8,128)S(1)}, f32[64,64]{1,0:T(8,128)S(1)}, u32[]{:S(2)}, u32[]{:S(2)}) collective-permute-start(f32[64,64]{1,0:T(8,128)S(1)} %add.110), channel_id=1, source_target_pairs={{0,2},{1,3},{2,0},{3,1},{4,6},{5,7},{6,4},{7,5},{8,10},{9,11},{10,... | collective-permute-start | bytes 49160 | tf_op jit(solution)/shard_map/ppermute | solution.py:53
  42.3 5.4 %collective-permute-start.6 = (f32[64,64]{1,0:T(8,128)S(1)}, f32[64,64]{1,0:T(8,128)S(1)}, u32[]{:S(2)}, u32[]{:S(2)}) collective-permute-start(f32[64,64]{1,0:T(8,128)S(1)} %add.111), channel_id=1, source_target_pairs={{0,4},{1,5},{2,6},{3,7},{4,0},{5,1},{6,2},{7,3},{8,12},{9,13},{10,... | collective-permute-start | bytes 49160 | tf_op jit(solution)/shard_map/ppermute | solution.py:53
  50.0 5.1 %collective-permute-start.7 = (f32[2,64,64]{2,1,0:T(8,128)S(1)}, f32[2,64,64]{2,1,0:T(8,128)S(1)}, u32[]{:S(2)}, u32[]{:S(2)}) collective-permute-start(f32[2,64,64]{2,1,0:T(8,128)S(1)} %pad_maximum_fusion.1), channel_id=1, source_target_pairs={{0,8},{8,0},{16,24},{24,16},{32,40},{40,32},{48,56},{56,48},{64,72... | collective-permute-start | bytes 98312 | tf_op jit(solution)/shard_map/ppermute | solution.py:53
  56.4 5.3 %collective-permute-start.8 = (f32[2,64,64]{2,1,0:T(8,128)S(1)}, f32[2,64,64]{2,1,0:T(8,128)S(1)}, u32[]{:S(2)}, u32[]{:S(2)}) collective-permute-start(f32[2,64,64]{2,1,0:T(8,128)S(1)} %fusion.30), channel_id=1, source_target_pairs={{0,16},{8,24},{16,0},{24,8},{32,48},{40,56},{48,32},{56,40},{64,80... | collective-permute-start | bytes 98312 | tf_op jit(solution)/shard_map/ppermute | solution.py:53
  61.6 5.9 %collective-permute-start.9 = (f32[2,64,64]{2,1,0:T(8,128)S(1)}, f32[2,64,64]{2,1,0:T(8,128)S(1)}, u32[]{:S(2)}, u32[]{:S(2)}) collective-permute-start(f32[2,64,64]{2,1,0:T(8,128)S(1)} %add.126), channel_id=1, source_target_pairs={{0,32},{8,40},{16,48},{24,56},{32,0},{40,8},{48,16},{56,24},{64,96... | collective-permute-start | bytes 98312 | tf_op jit(solution)/shard_map/ppermute | solution.py:53
  67.5 4.9 %collective-permute-start.10 = (f32[2,64,64]{2,1,0:T(8,128)S(1)}, f32[2,64,64]{2,1,0:T(8,128)S(1)}, u32[]{:S(2)}, u32[]{:S(2)}) collective-permute-start(f32[2,64,64]{2,1,0:T(8,128)S(1)} %add.131), channel_id=1, source_target_pairs={{0,64},{8,72},{16,80},{24,88},{32,96},{40,104},{48,112},{56,120},{... | collective-permute-start | bytes 98312 | tf_op jit(solution)/shard_map/ppermute | solution.py:53
  73.1 8.7 %collective-permute-start.11 = (f32[64,64]{1,0:T(8,128)S(1)}, f32[64,64]{1,0:T(8,128)S(1)}, u32[]{:S(2)}, u32[]{:S(2)}) collective-permute-start(f32[64,64]{1,0:T(8,128)S(1)} %get-tuple-element.48), channel_id=1, source_target_pairs={{0,1},{1,0},{2,3},{3,2},{4,5},{5,4},{6,7},{7,6},{8,9},{9,8},{10,11... | collective-permute-start | bytes 49160 | tf_op jit(solution)/shard_map/ppermute | solution.py:53
  85.5 23.3 %all-to-all-start.1 = ((f32[64,1,8,512]{3,2,1,0:T(8,128)}), f32[64,1,8,512]{3,2,1,0:T(8,128)S(1)}, u32[]{:S(2)}, u32[]{:S(2)}) async-start(f32[64,1,8,512]{3,2,1,0:T(8,128)} %copy.15), calls=%async_computation.1 | async-start | bytes 2097152 | tf_op jit(solution)/shard_map/all_to_all | solution.py:145
  89.4 13.3 %collective-permute-start.12 = (f32[64,64]{1,0:T(8,128)S(1)}, f32[64,64]{1,0:T(8,128)S(1)}, u32[]{:S(2)}, u32[]{:S(2)}) collective-permute-start(f32[64,64]{1,0:T(8,128)S(1)} %fusion.29), channel_id=1, source_target_pairs={{0,2},{1,3},{2,0},{3,1},{4,6},{5,7},{6,4},{7,5},{8,10},{9,11},{10,... | collective-permute-start | bytes 49160 | tf_op jit(solution)/shard_map/ppermute | solution.py:53
  102.8 5.4 %collective-permute-start.13 = (f32[64,64]{1,0:T(8,128)S(1)}, f32[64,64]{1,0:T(8,128)S(1)}, u32[]{:S(2)}, u32[]{:S(2)}) collective-permute-start(f32[64,64]{1,0:T(8,128)S(1)} %add.134), channel_id=1, source_target_pairs={{0,4},{1,5},{2,6},{3,7},{4,0},{5,1},{6,2},{7,3},{8,12},{9,13},{10,... | collective-permute-start | bytes 49160 | tf_op jit(solution)/shard_map/ppermute | solution.py:53

commit v7 on v6

--- a/solution.py
+++ b/solution.py
@@ -1,8 +1,9 @@
+import functools
+
 import jax
 import jax.numpy as jnp
 from jax import lax
 from jax.experimental import pallas as pl
-from jax.experimental.pallas import tpu as pltpu
 from jax.sharding import PartitionSpec as P
 
 STEPS = 2
@@ -53,12 +54,11 @@
     return x + lax.ppermute(x, axis, [(i, i ^ bit) for i in range(count)])
 
 
-def chol_inv_kernel(g_ref, x_ref, a_ref):
-    n = g_ref.shape[0]
-    a_ref[...] = g_ref[...]
-    rows = lax.broadcasted_iota(jnp.int32, (n, n), 0)
+def chol_inv_kernel(first, last, a_in, x_in, a_ref, x_ref):
+    n = a_in.shape[0]
+    a_ref[...] = a_in[...]
+    x_ref[...] = x_in[...]
     cols = lax.broadcasted_iota(jnp.int32, (n, n), 1)
-    x_ref[...] = jnp.where(rows == cols, 1.0, 0.0).astype(jnp.float32)
     lane = lax.broadcasted_iota(jnp.int32, (1, n), 1)
     sub = lax.broadcasted_iota(jnp.int32, (n, 1), 0)
 
@@ -76,24 +76,28 @@
         x_ref[...] = x_ref[...] - below * xrow
         return carry
 
-    lax.fori_loop(0, n, step, 0)
+    lax.fori_loop(first, last, step, 0)
 
 
-def lower_inverse(gram):
-    n = gram.shape[0]
+def cholesky_steps(a, x, first, last):
+    n = a.shape[0]
+    shape = jax.ShapeDtypeStruct((n, n), jnp.float32)
     return pl.pallas_call(
-        chol_inv_kernel,
-        out_shape=jax.ShapeDtypeStruct((n, n), jnp.float32),
-        scratch_shapes=[pltpu.VMEM((n, n), jnp.float32)],
-    )(gram)
+        functools.partial(chol_inv_kernel, first, last),
+        out_shape=(shape, shape),
+    )(a, x)
 
 
 def invert_beside(gram, extra, bits):
-    solved = lower_inverse(gram)
-    if bits:
-        extra = exchange(extra, *bits.pop(0))
-    solved, extra = lax.optimization_barrier((solved, extra))
-    inverse = jnp.dot(solved.T, solved, precision=lax.Precision.HIGHEST)
+    n = gram.shape[0]
+    bounds = [0, n // 2, n]
+    a, x = gram, jnp.eye(n, dtype=jnp.float32)
+    for first, last in zip(bounds[:-1], bounds[1:]):
+        a, x = cholesky_steps(a, x, first, last)
+        if bits:
+            extra = exchange(extra, *bits.pop(0))
+        a, x, extra = lax.optimization_barrier((a, x, extra))
+    inverse = jnp.dot(x.T, x, precision=lax.Precision.HIGHEST)
     return inverse, extra
 
 

time: 111 us -> 109 us (0.982)
  waiting for transfers between devices: 42.3 us -> 40.3 us
  Pallas kernels: 8.15 us -> 9.61 us
    ppermute x10, waiting for transfers between devices: 27.9 us -> 20.6 us  [exchange(): return x + lax.ppermute(x, axis, [(i, i ^ bit) for i in range(count)])]
    all_to_all x1, waiting for transfers between devices: 0.01 us -> 5.33 us  [body(): ritz = lax.all_to_all(ritz.reshape(v.shape), 'mem', 0, 1, tiled=True)]
    pallas_call x1 -> x2, Pallas kernels: 8.15 us -> 9.61 us  [cholesky_steps(): pl.pallas_call(functools.partial(chol_inv_kernel, first, last), out_shape...]
    ppermute x10, starting transfers between devices: 22 us -> 20.9 us  [exchange(): return x + lax.ppermute(x, axis, [(i, i ^ bit) for i in range(count)])]
  transfers between devices with their start and end apart: 16 -> 16, of which waited for: 9 -> 9; matrix products, arithmetic and copies ran while one was open for 8% -> 8% of each run, Pallas kernels for 7% -> 9%
where the time goes in v7:
time: 109 us
  waiting for transfers between devices  40.3 us (37%)
  starting transfers between devices  37.6 us (34%)
  other arithmetic  10.2 us (9%)
  Pallas kernels  9.61 us (9%)
  local copies, waits for them, and re-layouts  6.31 us (6%)
  matrix products  4.02 us (4%)
    ppermute x10, starting transfers between devices, exchange(): return x + lax.ppermute(x, axis, [(i, i ^ bit) for i in range(count)])  20.9 us
    ppermute x10, waiting for transfers between devices, exchange(): return x + lax.ppermute(x, axis, [(i, i ^ bit) for i in range(count)])  20.6 us
    all_to_all x1, waiting for transfers between devices, body(): v = lax.all_to_all(perturbations, 'mem', 1, 0, tiled=True)  14.4 us
    pallas_call x2, Pallas kernels, cholesky_steps(): pl.pallas_call(functools.partial(chol_inv_kernel, first, last), out_shape...  9.61 us
    all_to_all x1, starting transfers between devices, body(): v = lax.all_to_all(perturbations, 'mem', 1, 0, tiled=True)  7.04 us
    all_to_all x1, waiting for transfers between devices, body(): ritz = lax.all_to_all(ritz.reshape(v.shape), 'mem', 0, 1, tiled=True)  5.33 us
    all_to_all x1, starting transfers between devices, body(): ritz = lax.all_to_all(ritz.reshape(v.shape), 'mem', 0, 1, tiled=True)  3.96 us
    ppermute x2, starting transfers between devices, halo(): lax.ppermute(lax.slice_in_dim(block, size - width, size, axis=dim), 'dom'...  3.12 us
  transfers between devices with their start and end apart: 16, of which 9 were waited for; matrix products, arithmetic and copies ran while one was open for 8% of the time, Pallas kernels for 9%

profile of v7, /device:TPU:0, one launch (start us, length us, event | category | flops | bytes accessed | tf_op | source)
XLA Modules:
  0.0 108.9 jit_solution(3059915531988612236)
XLA Ops:
  0.6 2.3 %copy.11 = f32[8,8,8,512]{3,2,0,1:T(8,128)} copy(f32[8,8,8,512]{3,2,1,0:T(8,128)} %param.2) | data formatting | bytes 2097152 | tf_op args[0]
  3.0 7.0 %all-to-all-start = ((f32[8,8,8,512]{3,2,0,1:T(8,128)}), f32[8,8,8,512]{3,2,0,1:T(8,128)S(1)}, u32[]{:S(2)}, u32[]{:S(2)}) async-start(f32[8,8,8,512]{3,2,0,1:T(8,128)} %copy.11), calls=%async_computation | async-start | bytes 2097152 | tf_op jit(solution)/shard_map/all_to_all | solution.py:109
  10.0 1.5 %collective-permute-start.4 = (bf16[2,5,1,4,512]{4,3,2,1,0:T(4,128)(2,1)S(1)}, bf16[2,5,1,4,512]{4,3,2,1,0:T(4,128)(2,1)S(1)}, u32[]{:S(2)}, u32[]{:S(2)}) collective-permute-start(bf16[2,5,1,4,512]{4,3,2,1,0:T(4,128)(2,1)S(1)} %get-tuple-element.58), channel_id=1, source_target_pairs={{0,8},{8,16},{16,24},{24,32},{32,40},{40,48},{48,56},{56,64},{64,7... | collective-permute-start | bytes 122888 | tf_op jit(solution)/shard_map/ppermute | solution.py:17
  11.5 1.3 %collective-permute-start.5 = (bf16[2,5,1,4,512]{4,3,2,1,0:T(4,128)(2,1)S(1)}, bf16[2,5,1,4,512]{4,3,2,1,0:T(4,128)(2,1)S(1)}, u32[]{:S(2)}, u32[]{:S(2)}) collective-permute-start(bf16[2,5,1,4,512]{4,3,2,1,0:T(4,128)(2,1)S(1)} %get-tuple-element.59), channel_id=1, source_target_pairs={{8,0},{16,8},{24,16},{32,24},{40,32},{48,40},{56,48},{64,56},{72,6... | collective-permute-start | bytes 122888 | tf_op jit(solution)/shard_map/ppermute | solution.py:18
  12.8 14.4 %all-to-all-done = f32[8,8,8,512]{3,2,0,1:T(8,128)S(1)} async-done(((f32[8,8,8,512]{3,2,0,1:T(8,128)}), f32[8,8,8,512]{3,2,0,1:T(8,128)S(1)}, u32[]{:S(2)}, u32[]{:S(2)}) %all-to-all-start) | async-done | bytes 1048608 | tf_op jit(solution)/shard_map/all_to_all | solution.py:109
  27.2 0.6 copy.31
  27.8 0.1 fusion.32
  27.9 1.7 %collective-permute-start.1 = (f32[64,1,4,512]{3,0,2,1:T(8,128)S(1)}, f32[64,1,4,512]{3,0,2,1:T(8,128)S(1)}, u32[]{:S(2)}, u32[]{:S(2)}) collective-permute-start(f32[64,1,4,512]{3,0,2,1:T(8,128)S(1)} %get-tuple-element.46), channel_id=1, source_target_pairs={{0,8},{8,16},{16,24},{24,32},{32,40},{40,48},{48,56},{56,64},{64,7... | collective-permute-start | bytes 1572872 | tf_op jit(solution)/shard_map/ppermute | solution.py:17
  29.6 1.3 %collective-permute-start.2 = (f32[64,1,4,512]{3,0,2,1:T(8,128)S(1)}, f32[64,1,4,512]{3,0,2,1:T(8,128)S(1)}, u32[]{:S(2)}, u32[]{:S(2)}) collective-permute-start(f32[64,1,4,512]{3,0,2,1:T(8,128)S(1)} %get-tuple-element.47), channel_id=1, source_target_pairs={{8,0},{16,8},{24,16},{32,24},{40,32},{48,40},{56,48},{64,56},{72,6... | collective-permute-start | bytes 1572872 | tf_op jit(solution)/shard_map/ppermute | solution.py:18
  30.9 0.1 maximum_convert_fusion
  31.0 0.6 copy.18
  31.6 1.0 fusion.34
  32.6 0.6 collective-permute-start
  33.2 3.4 %collective-permute-done = f32[64,64]{1,0:T(8,128)S(1)} collective-permute-done((f32[64,64]{1,0:T(8,128)S(1)}, f32[64,64]{1,0:T(8,128)S(1)}, u32[]{:S(2)}, u32[]{:S(2)}) %collective-permute-start) | collective-permute-done | bytes 16416 | tf_op jit(solution)/shard_map/ppermute | solution.py:54
  36.6 0.2 pad_maximum_fusion
  36.8 1.2 %collective-permute-start.3 = (f32[64,64]{1,0:T(8,128)S(1)}, f32[64,64]{1,0:T(8,128)S(1)}, u32[]{:S(2)}, u32[]{:S(2)}) collective-permute-start(f32[64,64]{1,0:T(8,128)S(1)} %add.110), channel_id=1, source_target_pairs={{0,2},{1,3},{2,0},{3,1},{4,6},{5,7},{6,4},{7,5},{8,10},{9,11},{10,... | collective-permute-start | bytes 49160 | tf_op jit(solution)/shard_map/ppermute | solution.py:54
  38.0 1.3 %fusion.4 = f32[64,1,16,512]{3,0,2,1:T(8,128)S(1)} fusion(f32[64,1,16,512]{3,0,2,1:T(8,128)S(1)} %pad_maximum_fusion, f32[16,512]{1,0:T(8,128)S(1)} %get-tuple-element.53, f32[16,512]{1,0:T(8,128)S(1)} %get-tuple-element.54, f32[16,512]{1,0:T(8,128)S(1)} %get-tuple-element.55, f32[16,512]{1,0:T(8,128)S(1)} %get-tuple-element.56, ...), kind=kLoop, calls=%fused_computation.20 | loop fusion | flops 4718592 | bytes 4358144 | tf_op jit(solution)/shard_map/add | solution.py:34
  39.3 3.0 %collective-permute-done.3 = f32[64,64]{1,0:T(8,128)S(1)} collective-permute-done((f32[64,64]{1,0:T(8,128)S(1)}, f32[64,64]{1,0:T(8,128)S(1)}, u32[]{:S(2)}, u32[]{:S(2)}) %collective-permute-start.3) | collective-permute-done | bytes 16416 | tf_op jit(solution)/shard_map/ppermute | solution.py:54
  42.3 0.6 collective-permute-start.6
  42.9 1.3 %fusion.10 = f32[64,1,16,512]{3,0,2,1:T(8,128)S(1)} fusion(f32[64,1,16,512]{3,0,2,1:T(8,128)S(1)} %fusion.4, f32[16,512]{1,0:T(8,128)S(1)} %get-tuple-element.49, f32[16,512]{1,0:T(8,128)S(1)} %get-tuple-element.50, f32[16,512]{1,0:T(8,128)S(1)} %get-tuple-element.51, f32[16,512]{1,0:T(8,128)S(1)} %get-tuple-element.52, f32[16,512]{1,0:T(8,128)S(1)} %get-tuple-element.48), kind=kLoop, calls=%fused_computation.26 | loop fusion | flops 4718592 | bytes 4358144 | tf_op jit(solution)/shard_map/add | solution.py:34
  44.1 3.6 %collective-permute-done.6 = f32[64,64]{1,0:T(8,128)S(1)} collective-permute-done((f32[64,64]{1,0:T(8,128)S(1)}, f32[64,64]{1,0:T(8,128)S(1)}, u32[]{:S(2)}, u32[]{:S(2)}) %collective-permute-start.6) | collective-permute-done | bytes 16416 | tf_op jit(solution)/shard_map/ppermute | solution.py:54
  47.7 1.2 %broadcast_multiply_fusion = (f32[64,1,16,512]{3,0,2,1:T(8,128)S(1)}, f32[64,1,16,512]{3,0,2,1:T(8,128)S(1)}, f32[64,1,16,512]{3,0,2,1:T(8,128)S(1)}, f32[64,1,16,512]{3,0,2,1:T(8,128)S(1)}) fusion(f32[64,1,16,512]{3,0,2,1:T(8,128)S(1)} %fusion.10, f32[16,512]{1,0:T(8,128)S(1)} %get-tuple-element.49, f32[16,512]{1,0:T(8,128)S(1)} %get-tuple-element.50, ...), kind=kLoop, calls=%fused_computation.50 | loop fusion | flops 2097152 | bytes 10616832 | tf_op jit(solution)/shard_map/mul | solution.py:39
  49.0 1.0 convolution_bitcast_fusion.2
  50.0 3.6 %collective-permute-start.7 = (f32[2,64,64]{2,1,0:T(8,128)S(1)}, f32[2,64,64]{2,1,0:T(8,128)S(1)}, u32[]{:S(2)}, u32[]{:S(2)}) collective-permute-start(f32[2,64,64]{2,1,0:T(8,128)S(1)} %pad_maximum_fusion.1), channel_id=1, source_target_pairs={{0,8},{8,0},{16,24},{24,16},{32,40},{40,32},{48,56},{56,48},{64,72... | collective-permute-start | bytes 98312 | tf_op jit(solution)/shard_map/ppermute | solution.py:54
  53.6 1.5 %fusion.15 = f32[64,1,16,512]{3,0,2,1:T(8,128)S(1)} fusion(f32[64,1,16,512]{3,0,2,1:T(8,128)S(1)} %get-tuple-element.45, f32[64,1,16,512]{3,0,2,1:T(8,128)S(1)} %get-tuple-element.44, f32[64,1,16,512]{3,0,2,1:T(8,128)S(1)} %get-tuple-element.43, f32[64,1,16,512]{3,0,2,1:T(8,128)S(1)} %get-tuple-element.42, f32[64,1,16,512]{3,0,2,1:T(8,128)S(1)} %fusion.10, ...), kind=kLoop, calls=%fused_computation.31 | loop fusion | flops 2621440 | bytes 12615680 | tf_op jit(solution)/shard_map/add | solution.py:39
  55.1 1.2 %broadcast_multiply_fusion.4 = (f32[64,1,16,512]{3,0,2,1:T(8,128)S(1)}, f32[64,1,16,512]{3,0,2,1:T(8,128)S(1)}, f32[64,1,16,512]{3,0,2,1:T(8,128)S(1)}, f32[64,1,16,512]{3,0,2,1:T(8,128)S(1)}) fusion(f32[64,1,16,512]{3,0,2,1:T(8,128)S(1)} %fusion.15, f32[16,512]{1,0:T(8,128)S(1)} %get-tuple-element.53, f32[16,512]{1,0:T(8,128)S(1)} %get-tuple-element.54, ...), kind=kLoop, calls=%fused_computation.54 | loop fusion | flops 2097152 | bytes 10616832 | tf_op jit(solution)/shard_map/mul | solution.py:39
  56.4 2.6 %collective-permute-start.8 = (f32[2,64,64]{2,1,0:T(8,128)S(1)}, f32[2,64,64]{2,1,0:T(8,128)S(1)}, u32[]{:S(2)}, u32[]{:S(2)}) collective-permute-start(f32[2,64,64]{2,1,0:T(8,128)S(1)} %fusion.31), channel_id=1, source_target_pairs={{0,16},{8,24},{16,0},{24,8},{32,48},{40,56},{48,32},{56,40},{64,80... | collective-permute-start | bytes 98312 | tf_op jit(solution)/shard_map/ppermute | solution.py:54
  59.0 1.4 %fusion.19 = f32[64,1,16,512]{3,0,2,1:T(8,128)S(1)} fusion(f32[64,1,16,512]{3,0,2,1:T(8,128)S(1)} %get-tuple-element.41, f32[64,1,16,512]{3,0,2,1:T(8,128)S(1)} %get-tuple-element.40, f32[64,1,16,512]{3,0,2,1:T(8,128)S(1)} %get-tuple-element.39, f32[64,1,16,512]{3,0,2,1:T(8,128)S(1)} %get-tuple-element.38, f32[64,1,16,512]{3,0,2,1:T(8,128)S(1)} %fusion.15, ...), kind=kLoop, calls=%fused_computation.35 | loop fusion | flops 2621440 | bytes 12615680 | tf_op jit(solution)/shard_map/add | solution.py:39
  60.4 1.2 %collective-permute-done.8 = f32[2,64,64]{2,1,0:T(8,128)S(1)} collective-permute-done((f32[2,64,64]{2,1,0:T(8,128)S(1)}, f32[2,64,64]{2,1,0:T(8,128)S(1)}, u32[]{:S(2)}, u32[]{:S(2)}) %collective-permute-start.8) | collective-permute-done | bytes 32800 | tf_op jit(solution)/shard_map/ppermute | solution.py:54
  61.6 3.6 %collective-permute-start.9 = (f32[2,64,64]{2,1,0:T(8,128)S(1)}, f32[2,64,64]{2,1,0:T(8,128)S(1)}, u32[]{:S(2)}, u32[]{:S(2)}) collective-permute-start(f32[2,64,64]{2,1,0:T(8,128)S(1)} %add.126), channel_id=1, source_target_pairs={{0,32},{8,40},{16,48},{24,56},{32,0},{40,8},{48,16},{56,24},{64,96... | collective-permute-start | bytes 98312 | tf_op jit(solution)/shard_map/ppermute | solution.py:54
  65.3 2.2 %collective-permute-done.9 = f32[2,64,64]{2,1,0:T(8,128)S(1)} collective-permute-done((f32[2,64,64]{2,1,0:T(8,128)S(1)}, f32[2,64,64]{2,1,0:T(8,128)S(1)}, u32[]{:S(2)}, u32[]{:S(2)}) %collective-permute-start.9) | collective-permute-done | bytes 32800 | tf_op jit(solution)/shard_map/ppermute | solution.py:54
  67.5 2.7 %collective-permute-start.10 = (f32[2,64,64]{2,1,0:T(8,128)S(1)}, f32[2,64,64]{2,1,0:T(8,128)S(1)}, u32[]{:S(2)}, u32[]{:S(2)}) collective-permute-start(f32[2,64,64]{2,1,0:T(8,128)S(1)} %add.131), channel_id=1, source_target_pairs={{0,64},{8,72},{16,80},{24,88},{32,96},{40,104},{48,112},{56,120},{... | collective-permute-start | bytes 98312 | tf_op jit(solution)/shard_map/ppermute | solution.py:54
  70.2 2.2 %collective-permute-done.10 = f32[2,64,64]{2,1,0:T(8,128)S(1)} collective-permute-done((f32[2,64,64]{2,1,0:T(8,128)S(1)}, f32[2,64,64]{2,1,0:T(8,128)S(1)}, u32[]{:S(2)}, u32[]{:S(2)}) %collective-permute-start.10) | collective-permute-done | bytes 32800 | tf_op jit(solution)/shard_map/ppermute | solution.py:54
  72.5 0.6 slice_bitcast_fusion
  73.1 0.5 collective-permute-start.11
  73.6 0.6 fusion.29.x_in
  74.3 4.8 %shard_map.41 = (f32[64,64]{1,0:T(8,128)}, f32[64,64]{1,0:T(8,128)}) custom-call(f32[64,64]{1,0:T(8,128)} %get-tuple-element.61.a_in, f32[64,64]{1,0:T(8,128)} %fusion.29.x_in), custom_call_target="tpu_custom_call" | custom-call | tf_op jit(solution)/shard_map/pallas_call | solution.py:85
  79.1 1.9 %collective-permute-start.12 = (f32[64,64]{1,0:T(8,128)S(1)}, f32[64,64]{1,0:T(8,128)S(1)}, u32[]{:S(2)}, u32[]{:S(2)}) collective-permute-start(f32[64,64]{1,0:T(8,128)S(1)} %fusion.30), channel_id=1, source_target_pairs={{0,2},{1,3},{2,0},{3,1},{4,6},{5,7},{6,4},{7,5},{8,10},{9,11},{10,... | collective-permute-start | bytes 49160 | tf_op jit(solution)/shard_map/ppermute | solution.py:54
  80.9 4.8 %shard_map.42 = (f32[64,64]{1,0:T(8,128)}, f32[64,64]{1,0:T(8,128)}) custom-call(f32[64,64]{1,0:T(8,128)} %get-tuple-element.31.a_in, f32[64,64]{1,0:T(8,128)} %get-tuple-element.32.x_in), custom_call_target="tpu_custom_call" | custom-call | tf_op jit(solution)/shard_map/pallas_call | solution.py:85
  85.8 1.1 convolution_bitcast_fusion.1
  86.8 1.0 convolution_bitcast_fusion
  87.8 1.6 %copy.15 = f32[64,1,8,512]{3,2,1,0:T(8,128)} copy(f32[64,1,8,512]{3,0,2,1:T(8,128)S(1)} %convolution_bitcast_fusion) | data formatting | bytes 2097152 | tf_op jit(solution)/shard_map/dot_general | solution.py:145
  89.4 4.0 %all-to-all-start.1 = ((f32[64,1,8,512]{3,2,1,0:T(8,128)}), f32[64,1,8,512]{3,2,1,0:T(8,128)S(1)}, u32[]{:S(2)}, u32[]{:S(2)}) async-start(f32[64,1,8,512]{3,2,1,0:T(8,128)} %copy.15), calls=%async_computation.1 | async-start | bytes 2097152 | tf_op jit(solution)/shard_map/all_to_all | solution.py:149
  93.4 3.5 %collective-permute-start.13 = (f32[64,64]{1,0:T(8,128)S(1)}, f32[64,64]{1,0:T(8,128)S(1)}, u32[]{:S(2)}, u32[]{:S(2)}) collective-permute-start(f32[64,64]{1,0:T(8,128)S(1)} %add.134), channel_id=1, source_target_pairs={{0,4},{1,5},{2,6},{3,7},{4,0},{5,1},{6,2},{7,3},{8,12},{9,13},{10,... | collective-permute-start | bytes 49160 | tf_op jit(solution)/shard_map/ppermute | solution.py:54
  96.9 4.9 %collective-permute-done.13 = f32[64,64]{1,0:T(8,128)S(1)} collective-permute-done((f32[64,64]{1,0:T(8,128)S(1)}, f32[64,64]{1,0:T(8,128)S(1)}, u32[]{:S(2)}, u32[]{:S(2)}) %collective-permute-start.13) | collective-permute-done | bytes 16416 | tf_op jit(solution)/shard_map/ppermute | solution.py:54
  101.9 0.6 add_multiply_fusion
  102.5 5.3 %all-to-all-done.1 = f32[64,1,8,512]{3,2,1,0:T(8,128)S(1)} async-done(((f32[64,1,8,512]{3,2,1,0:T(8,128)}), f32[64,1,8,512]{3,2,1,0:T(8,128)S(1)}, u32[]{:S(2)}, u32[]{:S(2)}) %all-to-all-start.1) | async-done | bytes 1048608 | tf_op jit(solution)/shard_map/all_to_all | solution.py:149
  107.8 1.1 copy.30
  (21 shorter events, 0.1 us)
Async XLA Ops:
  0.6 9.4 %copy-start = (bf16[2,5,1,8,512]{4,3,2,1,0:T(8,128)(2,1)S(1)}, bf16[2,5,1,8,512]{4,3,2,1,0:T(8,128)(2,1)}, u32[]{:S(2)}) copy-start(bf16[2,5,1,8,512]{4,3,2,1,0:T(8,128)(2,1)} %param.3) | copy-start | bytes 245764
  3.0 24.2 %all-to-all-start = ((f32[8,8,8,512]{3,2,0,1:T(8,128)}), f32[8,8,8,512]{3,2,0,1:T(8,128)S(1)}, u32[]{:S(2)}, u32[]{:S(2)}) async-start(f32[8,8,8,512]{3,2,0,1:T(8,128)} %copy.11), calls=%async_computation | async-start | bytes 2097152 | tf_op jit(solution)/shard_map/all_to_all | solution.py:109
  10.0 20.8 %collective-permute-start.4 = (bf16[2,5,1,4,512]{4,3,2,1,0:T(4,128)(2,1)S(1)}, bf16[2,5,1,4,512]{4,3,2,1,0:T(4,128)(2,1)S(1)}, u32[]{:S(2)}, u32[]{:S(2)}) collective-permute-start(bf16[2,5,1,4,512]{4,3,2,1,0:T(4,128)(2,1)S(1)} %get-tuple-element.58), channel_id=1, source_target_pairs={{0,8},{8,16},{16,24},{24,32},{32,40},{40,48},{48,56},{56,64},{64,7... | collective-permute-start | bytes 122888 | tf_op jit(solution)/shard_map/ppermute | solution.py:17
  11.5 19.4 %collective-permute-start.5 = (bf16[2,5,1,4,512]{4,3,2,1,0:T(4,128)(2,1)S(1)}, bf16[2,5,1,4,512]{4,3,2,1,0:T(4,128)(2,1)S(1)}, u32[]{:S(2)}, u32[]{:S(2)}) collective-permute-start(bf16[2,5,1,4,512]{4,3,2,1,0:T(4,128)(2,1)S(1)} %get-tuple-element.59), channel_id=1, source_target_pairs={{8,0},{16,8},{24,16},{32,24},{40,32},{48,40},{56,48},{64,56},{72,6... | collective-permute-start | bytes 122888 | tf_op jit(solution)/shard_map/ppermute | solution.py:18
  27.9 8.7 %collective-permute-start.1 = (f32[64,1,4,512]{3,0,2,1:T(8,128)S(1)}, f32[64,1,4,512]{3,0,2,1:T(8,128)S(1)}, u32[]{:S(2)}, u32[]{:S(2)}) collective-permute-start(f32[64,1,4,512]{3,0,2,1:T(8,128)S(1)} %get-tuple-element.46), channel_id=1, source_target_pairs={{0,8},{8,16},{16,24},{24,32},{32,40},{40,48},{48,56},{56,64},{64,7... | collective-permute-start | bytes 1572872 | tf_op jit(solution)/shard_map/ppermute | solution.py:17
  29.6 7.0 %collective-permute-start.2 = (f32[64,1,4,512]{3,0,2,1:T(8,128)S(1)}, f32[64,1,4,512]{3,0,2,1:T(8,128)S(1)}, u32[]{:S(2)}, u32[]{:S(2)}) collective-permute-start(f32[64,1,4,512]{3,0,2,1:T(8,128)S(1)} %get-tuple-element.47), channel_id=1, source_target_pairs={{8,0},{16,8},{24,16},{32,24},{40,32},{48,40},{56,48},{64,56},{72,6... | collective-permute-start | bytes 1572872 | tf_op jit(solution)/shard_map/ppermute | solution.py:18
  32.6 4.0 %collective-permute-start = (f32[64,64]{1,0:T(8,128)S(1)}, f32[64,64]{1,0:T(8,128)S(1)}, u32[]{:S(2)}, u32[]{:S(2)}) collective-permute-start(f32[64,64]{1,0:T(8,128)S(1)} %fusion.34), channel_id=1, source_target_pairs={{0,1},{1,0},{2,3},{3,2},{4,5},{5,4},{6,7},{7,6},{8,9},{9,8},{10,11... | collective-permute-start | bytes 49160 | tf_op jit(solution)/shard_map/ppermute | solution.py:54
  36.8 5.5 %collective-permute-start.3 = (f32[64,64]{1,0:T(8,128)S(1)}, f32[64,64]{1,0:T(8,128)S(1)}, u32[]{:S(2)}, u32[]{:S(2)}) collective-permute-start(f32[64,64]{1,0:T(8,128)S(1)} %add.110), channel_id=1, source_target_pairs={{0,2},{1,3},{2,0},{3,1},{4,6},{5,7},{6,4},{7,5},{8,10},{9,11},{10,... | collective-permute-start | bytes 49160 | tf_op jit(solution)/shard_map/ppermute | solution.py:54
  42.3 5.4 %collective-permute-start.6 = (f32[64,64]{1,0:T(8,128)S(1)}, f32[64,64]{1,0:T(8,128)S(1)}, u32[]{:S(2)}, u32[]{:S(2)}) collective-permute-start(f32[64,64]{1,0:T(8,128)S(1)} %add.111), channel_id=1, source_target_pairs={{0,4},{1,5},{2,6},{3,7},{4,0},{5,1},{6,2},{7,3},{8,12},{9,13},{10,... | collective-permute-start | bytes 49160 | tf_op jit(solution)/shard_map/ppermute | solution.py:54
  50.0 5.1 %collective-permute-start.7 = (f32[2,64,64]{2,1,0:T(8,128)S(1)}, f32[2,64,64]{2,1,0:T(8,128)S(1)}, u32[]{:S(2)}, u32[]{:S(2)}) collective-permute-start(f32[2,64,64]{2,1,0:T(8,128)S(1)} %pad_maximum_fusion.1), channel_id=1, source_target_pairs={{0,8},{8,0},{16,24},{24,16},{32,40},{40,32},{48,56},{56,48},{64,72... | collective-permute-start | bytes 98312 | tf_op jit(solution)/shard_map/ppermute | solution.py:54
  56.4 5.3 %collective-permute-start.8 = (f32[2,64,64]{2,1,0:T(8,128)S(1)}, f32[2,64,64]{2,1,0:T(8,128)S(1)}, u32[]{:S(2)}, u32[]{:S(2)}) collective-permute-start(f32[2,64,64]{2,1,0:T(8,128)S(1)} %fusion.31), channel_id=1, source_target_pairs={{0,16},{8,24},{16,0},{24,8},{32,48},{40,56},{48,32},{56,40},{64,80... | collective-permute-start | bytes 98312 | tf_op jit(solution)/shard_map/ppermute | solution.py:54
  61.6 5.9 %collective-permute-start.9 = (f32[2,64,64]{2,1,0:T(8,128)S(1)}, f32[2,64,64]{2,1,0:T(8,128)S(1)}, u32[]{:S(2)}, u32[]{:S(2)}) collective-permute-start(f32[2,64,64]{2,1,0:T(8,128)S(1)} %add.126), channel_id=1, source_target_pairs={{0,32},{8,40},{16,48},{24,56},{32,0},{40,8},{48,16},{56,24},{64,96... | collective-permute-start | bytes 98312 | tf_op jit(solution)/shard_map/ppermute | solution.py:54
  67.5 4.9 %collective-permute-start.10 = (f32[2,64,64]{2,1,0:T(8,128)S(1)}, f32[2,64,64]{2,1,0:T(8,128)S(1)}, u32[]{:S(2)}, u32[]{:S(2)}) collective-permute-start(f32[2,64,64]{2,1,0:T(8,128)S(1)} %add.131), channel_id=1, source_target_pairs={{0,64},{8,72},{16,80},{24,88},{32,96},{40,104},{48,112},{56,120},{... | collective-permute-start | bytes 98312 | tf_op jit(solution)/shard_map/ppermute | solution.py:54
  73.1 6.0 %collective-permute-start.11 = (f32[64,64]{1,0:T(8,128)S(1)}, f32[64,64]{1,0:T(8,128)S(1)}, u32[]{:S(2)}, u32[]{:S(2)}) collective-permute-start(f32[64,64]{1,0:T(8,128)S(1)} %get-tuple-element.60), channel_id=1, source_target_pairs={{0,1},{1,0},{2,3},{3,2},{4,5},{5,4},{6,7},{7,6},{8,9},{9,8},{10,11... | collective-permute-start | bytes 49160 | tf_op jit(solution)/shard_map/ppermute | solution.py:54
  79.1 6.7 %collective-permute-start.12 = (f32[64,64]{1,0:T(8,128)S(1)}, f32[64,64]{1,0:T(8,128)S(1)}, u32[]{:S(2)}, u32[]{:S(2)}) collective-permute-start(f32[64,64]{1,0:T(8,128)S(1)} %fusion.30), channel_id=1, source_target_pairs={{0,2},{1,3},{2,0},{3,1},{4,6},{5,7},{6,4},{7,5},{8,10},{9,11},{10,... | collective-permute-start | bytes 49160 | tf_op jit(solution)/shard_map/ppermute | solution.py:54
  89.4 18.4 %all-to-all-start.1 = ((f32[64,1,8,512]{3,2,1,0:T(8,128)}), f32[64,1,8,512]{3,2,1,0:T(8,128)S(1)}, u32[]{:S(2)}, u32[]{:S(2)}) async-start(f32[64,1,8,512]{3,2,1,0:T(8,128)} %copy.15), calls=%async_computation.1 | async-start | bytes 2097152 | tf_op jit(solution)/shard_map/all_to_all | solution.py:149
  93.4 8.5 %collective-permute-start.13 = (f32[64,64]{1,0:T(8,128)S(1)}, f32[64,64]{1,0:T(8,128)S(1)}, u32[]{:S(2)}, u32[]{:S(2)}) collective-permute-start(f32[64,64]{1,0:T(8,128)S(1)} %add.134), channel_id=1, source_target_pairs={{0,4},{1,5},{2,6},{3,7},{4,0},{5,1},{6,2},{7,3},{8,12},{9,13},{10,... | collective-permute-start | bytes 49160 | tf_op jit(solution)/shard_map/ppermute | solution.py:54

commit v8 on v5

--- a/solution.py
+++ b/solution.py
@@ -66,12 +66,12 @@
         a = a_ref[...]
         row = a_ref[pl.ds(k, 1), :]
         pivot = jnp.sum(jnp.where(lane == k, row, 0.0), axis=1, keepdims=True)
-        root = jnp.sqrt(pivot)
+        scale = 1.0 / jnp.sqrt(pivot)
         col = jnp.sum(jnp.where(cols == k, a, 0.0), axis=1, keepdims=True)
-        below = jnp.where(sub > k, col / root, 0.0)
-        right = jnp.where(lane > k, row / root, 0.0)
+        below = jnp.where(sub > k, col * scale, 0.0)
+        right = jnp.where(lane > k, row * scale, 0.0)
         a_ref[...] = a - below * right
-        xrow = x_ref[pl.ds(k, 1), :] / root
+        xrow = x_ref[pl.ds(k, 1), :] * scale
         x_ref[pl.ds(k, 1), :] = xrow
         x_ref[...] = x_ref[...] - below * xrow
         return carry

time: 109 us -> 109 us (level)
  no operation moved by 1% of the time
where the time goes in v8:
time: 109 us; the launch traced here: 108 us
  waiting for transfers between devices  42 us (39%)
  starting transfers between devices  37.6 us (34%)
  other arithmetic  9.56 us (9%)
  Pallas kernels  8.15 us (7%)
  local copies, waits for them, and re-layouts  6.31 us (6%)
  matrix products  4.02 us (4%)
    ppermute x10, waiting for transfers between devices, exchange(): return x + lax.ppermute(x, axis, [(i, i ^ bit) for i in range(count)])  26.2 us
    ppermute x10, starting transfers between devices, exchange(): return x + lax.ppermute(x, axis, [(i, i ^ bit) for i in range(count)])  20.9 us
    all_to_all x1, waiting for transfers between devices, body(): v = lax.all_to_all(perturbations, 'mem', 1, 0, tiled=True)  14.4 us
    pallas_call x1, Pallas kernels, lower_inverse(): pl.pallas_call(chol_inv_kernel, out_shape=jax.ShapeDtypeStruct((n, n), jn...  8.15 us
    all_to_all x1, starting transfers between devices, body(): v = lax.all_to_all(perturbations, 'mem', 1, 0, tiled=True)  7.04 us
    all_to_all x1, starting transfers between devices, body(): ritz = lax.all_to_all(ritz.reshape(v.shape), 'mem', 0, 1, tiled=True)  3.95 us
    ppermute x2, starting transfers between devices, halo(): lax.ppermute(lax.slice_in_dim(block, size - width, size, axis=dim), 'dom'...  3.12 us
    add x2, other arithmetic, adjoint_step(): result + shifted(coef[3] * field, 1, 3) + shifted(coef[4] * field, -1, 3)  2.94 us
  transfers between devices with their start and end apart: 16, of which 10 were waited for; matrix products, arithmetic and copies ran while one was open for 9% of the time, Pallas kernels for 8%

profile of v8, /device:TPU:0, one launch (start us, length us, event | category | flops | bytes accessed | tf_op | source)
XLA Modules:
  0.0 108.5 jit_solution(17953284721248435598)
XLA Ops:
  0.6 2.3 %copy.11 = f32[8,8,8,512]{3,2,0,1:T(8,128)} copy(f32[8,8,8,512]{3,2,1,0:T(8,128)} %param.2) | data formatting | bytes 2097152 | tf_op args[0]
  3.0 7.0 %all-to-all-start = ((f32[8,8,8,512]{3,2,0,1:T(8,128)}), f32[8,8,8,512]{3,2,0,1:T(8,128)S(1)}, u32[]{:S(2)}, u32[]{:S(2)}) async-start(f32[8,8,8,512]{3,2,0,1:T(8,128)} %copy.11), calls=%async_computation | async-start | bytes 2097152 | tf_op jit(solution)/shard_map/all_to_all | solution.py:108
  10.0 1.5 %collective-permute-start.4 = (bf16[2,5,1,4,512]{4,3,2,1,0:T(4,128)(2,1)S(1)}, bf16[2,5,1,4,512]{4,3,2,1,0:T(4,128)(2,1)S(1)}, u32[]{:S(2)}, u32[]{:S(2)}) collective-permute-start(bf16[2,5,1,4,512]{4,3,2,1,0:T(4,128)(2,1)S(1)} %get-tuple-element.50), channel_id=1, source_target_pairs={{0,8},{8,16},{16,24},{24,32},{32,40},{40,48},{48,56},{56,64},{64,7... | collective-permute-start | bytes 122888 | tf_op jit(solution)/shard_map/ppermute | solution.py:16
  11.5 1.3 %collective-permute-start.5 = (bf16[2,5,1,4,512]{4,3,2,1,0:T(4,128)(2,1)S(1)}, bf16[2,5,1,4,512]{4,3,2,1,0:T(4,128)(2,1)S(1)}, u32[]{:S(2)}, u32[]{:S(2)}) collective-permute-start(bf16[2,5,1,4,512]{4,3,2,1,0:T(4,128)(2,1)S(1)} %get-tuple-element.51), channel_id=1, source_target_pairs={{8,0},{16,8},{24,16},{32,24},{40,32},{48,40},{56,48},{64,56},{72,6... | collective-permute-start | bytes 122888 | tf_op jit(solution)/shard_map/ppermute | solution.py:17
  12.8 14.4 %all-to-all-done = f32[8,8,8,512]{3,2,0,1:T(8,128)S(1)} async-done(((f32[8,8,8,512]{3,2,0,1:T(8,128)}), f32[8,8,8,512]{3,2,0,1:T(8,128)S(1)}, u32[]{:S(2)}, u32[]{:S(2)}) %all-to-all-start) | async-done | bytes 1048608 | tf_op jit(solution)/shard_map/all_to_all | solution.py:108
  27.2 0.6 copy.31
  27.8 0.1 fusion.32
  27.9 1.7 %collective-permute-start.1 = (f32[64,1,4,512]{3,0,2,1:T(8,128)S(1)}, f32[64,1,4,512]{3,0,2,1:T(8,128)S(1)}, u32[]{:S(2)}, u32[]{:S(2)}) collective-permute-start(f32[64,1,4,512]{3,0,2,1:T(8,128)S(1)} %get-tuple-element.38), channel_id=1, source_target_pairs={{0,8},{8,16},{16,24},{24,32},{32,40},{40,48},{48,56},{56,64},{64,7... | collective-permute-start | bytes 1572872 | tf_op jit(solution)/shard_map/ppermute | solution.py:16
  29.6 1.3 %collective-permute-start.2 = (f32[64,1,4,512]{3,0,2,1:T(8,128)S(1)}, f32[64,1,4,512]{3,0,2,1:T(8,128)S(1)}, u32[]{:S(2)}, u32[]{:S(2)}) collective-permute-start(f32[64,1,4,512]{3,0,2,1:T(8,128)S(1)} %get-tuple-element.39), channel_id=1, source_target_pairs={{8,0},{16,8},{24,16},{32,24},{40,32},{48,40},{56,48},{64,56},{72,6... | collective-permute-start | bytes 1572872 | tf_op jit(solution)/shard_map/ppermute | solution.py:17
  30.9 0.1 maximum_convert_fusion
  31.0 0.6 copy.18
  31.6 1.0 fusion.34
  32.6 0.6 collective-permute-start
  33.2 3.4 %collective-permute-done = f32[64,64]{1,0:T(8,128)S(1)} collective-permute-done((f32[64,64]{1,0:T(8,128)S(1)}, f32[64,64]{1,0:T(8,128)S(1)}, u32[]{:S(2)}, u32[]{:S(2)}) %collective-permute-start) | collective-permute-done | bytes 16416 | tf_op jit(solution)/shard_map/ppermute | solution.py:53
  36.6 0.0 collective-permute-done.1
  36.6 0.2 pad_maximum_fusion
  36.8 1.2 %collective-permute-start.3 = (f32[64,64]{1,0:T(8,128)S(1)}, f32[64,64]{1,0:T(8,128)S(1)}, u32[]{:S(2)}, u32[]{:S(2)}) collective-permute-start(f32[64,64]{1,0:T(8,128)S(1)} %add.110), channel_id=1, source_target_pairs={{0,2},{1,3},{2,0},{3,1},{4,6},{5,7},{6,4},{7,5},{8,10},{9,11},{10,... | collective-permute-start | bytes 49160 | tf_op jit(solution)/shard_map/ppermute | solution.py:53
  38.0 1.3 %fusion.4 = f32[64,1,16,512]{3,0,2,1:T(8,128)S(1)} fusion(f32[64,1,16,512]{3,0,2,1:T(8,128)S(1)} %pad_maximum_fusion, f32[16,512]{1,0:T(8,128)S(1)} %get-tuple-element.45, f32[16,512]{1,0:T(8,128)S(1)} %get-tuple-element.46, f32[16,512]{1,0:T(8,128)S(1)} %get-tuple-element.47, f32[16,512]{1,0:T(8,128)S(1)} %get-tuple-element.48, ...), kind=kLoop, calls=%fused_computation.20 | loop fusion | flops 4718592 | bytes 4358144 | tf_op jit(solution)/shard_map/add | solution.py:33
  39.3 3.0 %collective-permute-done.3 = f32[64,64]{1,0:T(8,128)S(1)} collective-permute-done((f32[64,64]{1,0:T(8,128)S(1)}, f32[64,64]{1,0:T(8,128)S(1)}, u32[]{:S(2)}, u32[]{:S(2)}) %collective-permute-start.3) | collective-permute-done | bytes 16416 | tf_op jit(solution)/shard_map/ppermute | solution.py:53
  42.3 0.6 collective-permute-start.6
  42.9 1.3 %fusion.10 = f32[64,1,16,512]{3,0,2,1:T(8,128)S(1)} fusion(f32[64,1,16,512]{3,0,2,1:T(8,128)S(1)} %fusion.4, f32[16,512]{1,0:T(8,128)S(1)} %get-tuple-element.41, f32[16,512]{1,0:T(8,128)S(1)} %get-tuple-element.42, f32[16,512]{1,0:T(8,128)S(1)} %get-tuple-element.43, f32[16,512]{1,0:T(8,128)S(1)} %get-tuple-element.44, f32[16,512]{1,0:T(8,128)S(1)} %get-tuple-element.40), kind=kLoop, calls=%fused_computation.26 | loop fusion | flops 4718592 | bytes 4358144 | tf_op jit(solution)/shard_map/add | solution.py:33
  44.1 3.6 %collective-permute-done.6 = f32[64,64]{1,0:T(8,128)S(1)} collective-permute-done((f32[64,64]{1,0:T(8,128)S(1)}, f32[64,64]{1,0:T(8,128)S(1)}, u32[]{:S(2)}, u32[]{:S(2)}) %collective-permute-start.6) | collective-permute-done | bytes 16416 | tf_op jit(solution)/shard_map/ppermute | solution.py:53
  47.7 1.2 %broadcast_multiply_fusion = (f32[64,1,16,512]{3,0,2,1:T(8,128)S(1)}, f32[64,1,16,512]{3,0,2,1:T(8,128)S(1)}, f32[64,1,16,512]{3,0,2,1:T(8,128)S(1)}, f32[64,1,16,512]{3,0,2,1:T(8,128)S(1)}) fusion(f32[64,1,16,512]{3,0,2,1:T(8,128)S(1)} %fusion.10, f32[16,512]{1,0:T(8,128)S(1)} %get-tuple-element.41, f32[16,512]{1,0:T(8,128)S(1)} %get-tuple-element.42, ...), kind=kLoop, calls=%fused_computation.49 | loop fusion | flops 2097152 | bytes 10616832 | tf_op jit(solution)/shard_map/mul | solution.py:38
  49.0 1.0 convolution_bitcast_fusion.1
  50.0 3.6 %collective-permute-start.7 = (f32[2,64,64]{2,1,0:T(8,128)S(1)}, f32[2,64,64]{2,1,0:T(8,128)S(1)}, u32[]{:S(2)}, u32[]{:S(2)}) collective-permute-start(f32[2,64,64]{2,1,0:T(8,128)S(1)} %pad_maximum_fusion.1), channel_id=1, source_target_pairs={{0,8},{8,0},{16,24},{24,16},{32,40},{40,32},{48,56},{56,48},{64,72... | collective-permute-start | bytes 98312 | tf_op jit(solution)/shard_map/ppermute | solution.py:53
  53.6 1.5 %fusion.15 = f32[64,1,16,512]{3,0,2,1:T(8,128)S(1)} fusion(f32[64,1,16,512]{3,0,2,1:T(8,128)S(1)} %get-tuple-element.37, f32[64,1,16,512]{3,0,2,1:T(8,128)S(1)} %get-tuple-element.36, f32[64,1,16,512]{3,0,2,1:T(8,128)S(1)} %get-tuple-element.35, f32[64,1,16,512]{3,0,2,1:T(8,128)S(1)} %get-tuple-element.34, f32[64,1,16,512]{3,0,2,1:T(8,128)S(1)} %fusion.10, ...), kind=kLoop, calls=%fused_computation.31 | loop fusion | flops 2621440 | bytes 12615680 | tf_op jit(solution)/shard_map/add | solution.py:38
  55.1 1.2 %broadcast_multiply_fusion.4 = (f32[64,1,16,512]{3,0,2,1:T(8,128)S(1)}, f32[64,1,16,512]{3,0,2,1:T(8,128)S(1)}, f32[64,1,16,512]{3,0,2,1:T(8,128)S(1)}, f32[64,1,16,512]{3,0,2,1:T(8,128)S(1)}) fusion(f32[64,1,16,512]{3,0,2,1:T(8,128)S(1)} %fusion.15, f32[16,512]{1,0:T(8,128)S(1)} %get-tuple-element.45, f32[16,512]{1,0:T(8,128)S(1)} %get-tuple-element.46, ...), kind=kLoop, calls=%fused_computation.53 | loop fusion | flops 2097152 | bytes 10616832 | tf_op jit(solution)/shard_map/mul | solution.py:38
  56.4 2.6 %collective-permute-start.8 = (f32[2,64,64]{2,1,0:T(8,128)S(1)}, f32[2,64,64]{2,1,0:T(8,128)S(1)}, u32[]{:S(2)}, u32[]{:S(2)}) collective-permute-start(f32[2,64,64]{2,1,0:T(8,128)S(1)} %fusion.31), channel_id=1, source_target_pairs={{0,16},{8,24},{16,0},{24,8},{32,48},{40,56},{48,32},{56,40},{64,80... | collective-permute-start | bytes 98312 | tf_op jit(solution)/shard_map/ppermute | solution.py:53
  59.0 1.4 %fusion.19 = f32[64,1,16,512]{3,0,2,1:T(8,128)S(1)} fusion(f32[64,1,16,512]{3,0,2,1:T(8,128)S(1)} %get-tuple-element.33, f32[64,1,16,512]{3,0,2,1:T(8,128)S(1)} %get-tuple-element.32, f32[64,1,16,512]{3,0,2,1:T(8,128)S(1)} %get-tuple-element.31, f32[64,1,16,512]{3,0,2,1:T(8,128)S(1)} %get-tuple-element.30, f32[64,1,16,512]{3,0,2,1:T(8,128)S(1)} %fusion.15, ...), kind=kLoop, calls=%fused_computation.35 | loop fusion | flops 2621440 | bytes 12615680 | tf_op jit(solution)/shard_map/add | solution.py:38
  60.4 1.2 %collective-permute-done.8 = f32[2,64,64]{2,1,0:T(8,128)S(1)} collective-permute-done((f32[2,64,64]{2,1,0:T(8,128)S(1)}, f32[2,64,64]{2,1,0:T(8,128)S(1)}, u32[]{:S(2)}, u32[]{:S(2)}) %collective-permute-start.8) | collective-permute-done | bytes 32800 | tf_op jit(solution)/shard_map/ppermute | solution.py:53
  61.6 3.6 %collective-permute-start.9 = (f32[2,64,64]{2,1,0:T(8,128)S(1)}, f32[2,64,64]{2,1,0:T(8,128)S(1)}, u32[]{:S(2)}, u32[]{:S(2)}) collective-permute-start(f32[2,64,64]{2,1,0:T(8,128)S(1)} %add.126), channel_id=1, source_target_pairs={{0,32},{8,40},{16,48},{24,56},{32,0},{40,8},{48,16},{56,24},{64,96... | collective-permute-start | bytes 98312 | tf_op jit(solution)/shard_map/ppermute | solution.py:53
  65.3 2.2 %collective-permute-done.9 = f32[2,64,64]{2,1,0:T(8,128)S(1)} collective-permute-done((f32[2,64,64]{2,1,0:T(8,128)S(1)}, f32[2,64,64]{2,1,0:T(8,128)S(1)}, u32[]{:S(2)}, u32[]{:S(2)}) %collective-permute-start.9) | collective-permute-done | bytes 32800 | tf_op jit(solution)/shard_map/ppermute | solution.py:53
  67.5 2.7 %collective-permute-start.10 = (f32[2,64,64]{2,1,0:T(8,128)S(1)}, f32[2,64,64]{2,1,0:T(8,128)S(1)}, u32[]{:S(2)}, u32[]{:S(2)}) collective-permute-start(f32[2,64,64]{2,1,0:T(8,128)S(1)} %add.131), channel_id=1, source_target_pairs={{0,64},{8,72},{16,80},{24,88},{32,96},{40,104},{48,112},{56,120},{... | collective-permute-start | bytes 98312 | tf_op jit(solution)/shard_map/ppermute | solution.py:53
  70.2 2.2 %collective-permute-done.10 = f32[2,64,64]{2,1,0:T(8,128)S(1)} collective-permute-done((f32[2,64,64]{2,1,0:T(8,128)S(1)}, f32[2,64,64]{2,1,0:T(8,128)S(1)}, u32[]{:S(2)}, u32[]{:S(2)}) %collective-permute-start.10) | collective-permute-done | bytes 32800 | tf_op jit(solution)/shard_map/ppermute | solution.py:53
  72.5 0.6 slice_bitcast_fusion
  73.1 0.5 collective-permute-start.11
  73.6 8.2 %shard_map.41 = f32[64,64]{1,0:T(8,128)} custom-call(f32[64,64]{1,0:T(8,128)} %get-tuple-element.53.g_ref), custom_call_target="tpu_custom_call" | custom-call | tf_op jit(solution)/shard_map/pallas_call | solution.py:84
  81.8 1.9 %collective-permute-start.12 = (f32[64,64]{1,0:T(8,128)S(1)}, f32[64,64]{1,0:T(8,128)S(1)}, u32[]{:S(2)}, u32[]{:S(2)}) collective-permute-start(f32[64,64]{1,0:T(8,128)S(1)} %fusion.30), channel_id=1, source_target_pairs={{0,2},{1,3},{2,0},{3,1},{4,6},{5,7},{6,4},{7,5},{8,10},{9,11},{10,... | collective-permute-start | bytes 49160 | tf_op jit(solution)/shard_map/ppermute | solution.py:53
  83.7 1.1 fusion.35
  84.7 2.6 %collective-permute-done.12 = f32[64,64]{1,0:T(8,128)S(1)} collective-permute-done((f32[64,64]{1,0:T(8,128)S(1)}, f32[64,64]{1,0:T(8,128)S(1)}, u32[]{:S(2)}, u32[]{:S(2)}) %collective-permute-start.12) | collective-permute-done | bytes 16416 | tf_op jit(solution)/shard_map/ppermute | solution.py:53
  87.3 1.0 convolution_bitcast_fusion
  88.3 1.6 %copy.15 = f32[64,1,8,512]{3,2,1,0:T(8,128)} copy(f32[64,1,8,512]{3,0,2,1:T(8,128)S(1)} %convolution_bitcast_fusion) | data formatting | bytes 2097152 | tf_op jit(solution)/shard_map/dot_general | solution.py:144
  89.9 3.9 %all-to-all-start.1 = ((f32[64,1,8,512]{3,2,1,0:T(8,128)}), f32[64,1,8,512]{3,2,1,0:T(8,128)S(1)}, u32[]{:S(2)}, u32[]{:S(2)}) async-start(f32[64,1,8,512]{3,2,1,0:T(8,128)} %copy.15), calls=%async_computation.1 | async-start | bytes 2097152 | tf_op jit(solution)/shard_map/all_to_all | solution.py:148
  93.9 3.5 %collective-permute-start.13 = (f32[64,64]{1,0:T(8,128)S(1)}, f32[64,64]{1,0:T(8,128)S(1)}, u32[]{:S(2)}, u32[]{:S(2)}) collective-permute-start(f32[64,64]{1,0:T(8,128)S(1)} %add.134), channel_id=1, source_target_pairs={{0,4},{1,5},{2,6},{3,7},{4,0},{5,1},{6,2},{7,3},{8,12},{9,13},{10,... | collective-permute-start | bytes 49160 | tf_op jit(solution)/shard_map/ppermute | solution.py:53
  97.4 8.0 %collective-permute-done.13 = f32[64,64]{1,0:T(8,128)S(1)} collective-permute-done((f32[64,64]{1,0:T(8,128)S(1)}, f32[64,64]{1,0:T(8,128)S(1)}, u32[]{:S(2)}, u32[]{:S(2)}) %collective-permute-start.13) | collective-permute-done | bytes 16416 | tf_op jit(solution)/shard_map/ppermute | solution.py:53
  105.4 0.6 add_multiply_fusion
  106.0 1.4 %all-to-all-done.1 = f32[64,1,8,512]{3,2,1,0:T(8,128)S(1)} async-done(((f32[64,1,8,512]{3,2,1,0:T(8,128)}), f32[64,1,8,512]{3,2,1,0:T(8,128)S(1)}, u32[]{:S(2)}, u32[]{:S(2)}) %all-to-all-start.1) | async-done | bytes 1048608 | tf_op jit(solution)/shard_map/all_to_all | solution.py:148
  107.4 1.1 copy.30
  (19 shorter events, 0.1 us)
Async XLA Ops:
  0.6 9.4 %copy-start = (bf16[2,5,1,8,512]{4,3,2,1,0:T(8,128)(2,1)S(1)}, bf16[2,5,1,8,512]{4,3,2,1,0:T(8,128)(2,1)}, u32[]{:S(2)}) copy-start(bf16[2,5,1,8,512]{4,3,2,1,0:T(8,128)(2,1)} %param.3) | copy-start | bytes 245764
  3.0 24.2 %all-to-all-start = ((f32[8,8,8,512]{3,2,0,1:T(8,128)}), f32[8,8,8,512]{3,2,0,1:T(8,128)S(1)}, u32[]{:S(2)}, u32[]{:S(2)}) async-start(f32[8,8,8,512]{3,2,0,1:T(8,128)} %copy.11), calls=%async_computation | async-start | bytes 2097152 | tf_op jit(solution)/shard_map/all_to_all | solution.py:108
  10.0 20.8 %collective-permute-start.4 = (bf16[2,5,1,4,512]{4,3,2,1,0:T(4,128)(2,1)S(1)}, bf16[2,5,1,4,512]{4,3,2,1,0:T(4,128)(2,1)S(1)}, u32[]{:S(2)}, u32[]{:S(2)}) collective-permute-start(bf16[2,5,1,4,512]{4,3,2,1,0:T(4,128)(2,1)S(1)} %get-tuple-element.50), channel_id=1, source_target_pairs={{0,8},{8,16},{16,24},{24,32},{32,40},{40,48},{48,56},{56,64},{64,7... | collective-permute-start | bytes 122888 | tf_op jit(solution)/shard_map/ppermute | solution.py:16
  11.5 19.4 %collective-permute-start.5 = (bf16[2,5,1,4,512]{4,3,2,1,0:T(4,128)(2,1)S(1)}, bf16[2,5,1,4,512]{4,3,2,1,0:T(4,128)(2,1)S(1)}, u32[]{:S(2)}, u32[]{:S(2)}) collective-permute-start(bf16[2,5,1,4,512]{4,3,2,1,0:T(4,128)(2,1)S(1)} %get-tuple-element.51), channel_id=1, source_target_pairs={{8,0},{16,8},{24,16},{32,24},{40,32},{48,40},{56,48},{64,56},{72,6... | collective-permute-start | bytes 122888 | tf_op jit(solution)/shard_map/ppermute | solution.py:17
  27.9 8.7 %collective-permute-start.1 = (f32[64,1,4,512]{3,0,2,1:T(8,128)S(1)}, f32[64,1,4,512]{3,0,2,1:T(8,128)S(1)}, u32[]{:S(2)}, u32[]{:S(2)}) collective-permute-start(f32[64,1,4,512]{3,0,2,1:T(8,128)S(1)} %get-tuple-element.38), channel_id=1, source_target_pairs={{0,8},{8,16},{16,24},{24,32},{32,40},{40,48},{48,56},{56,64},{64,7... | collective-permute-start | bytes 1572872 | tf_op jit(solution)/shard_map/ppermute | solution.py:16
  29.6 7.0 %collective-permute-start.2 = (f32[64,1,4,512]{3,0,2,1:T(8,128)S(1)}, f32[64,1,4,512]{3,0,2,1:T(8,128)S(1)}, u32[]{:S(2)}, u32[]{:S(2)}) collective-permute-start(f32[64,1,4,512]{3,0,2,1:T(8,128)S(1)} %get-tuple-element.39), channel_id=1, source_target_pairs={{8,0},{16,8},{24,16},{32,24},{40,32},{48,40},{56,48},{64,56},{72,6... | collective-permute-start | bytes 1572872 | tf_op jit(solution)/shard_map/ppermute | solution.py:17
  32.6 4.0 %collective-permute-start = (f32[64,64]{1,0:T(8,128)S(1)}, f32[64,64]{1,0:T(8,128)S(1)}, u32[]{:S(2)}, u32[]{:S(2)}) collective-permute-start(f32[64,64]{1,0:T(8,128)S(1)} %fusion.34), channel_id=1, source_target_pairs={{0,1},{1,0},{2,3},{3,2},{4,5},{5,4},{6,7},{7,6},{8,9},{9,8},{10,11... | collective-permute-start | bytes 49160 | tf_op jit(solution)/shard_map/ppermute | solution.py:53
  36.8 5.5 %collective-permute-start.3 = (f32[64,64]{1,0:T(8,128)S(1)}, f32[64,64]{1,0:T(8,128)S(1)}, u32[]{:S(2)}, u32[]{:S(2)}) collective-permute-start(f32[64,64]{1,0:T(8,128)S(1)} %add.110), channel_id=1, source_target_pairs={{0,2},{1,3},{2,0},{3,1},{4,6},{5,7},{6,4},{7,5},{8,10},{9,11},{10,... | collective-permute-start | bytes 49160 | tf_op jit(solution)/shard_map/ppermute | solution.py:53
  42.3 5.4 %collective-permute-start.6 = (f32[64,64]{1,0:T(8,128)S(1)}, f32[64,64]{1,0:T(8,128)S(1)}, u32[]{:S(2)}, u32[]{:S(2)}) collective-permute-start(f32[64,64]{1,0:T(8,128)S(1)} %add.111), channel_id=1, source_target_pairs={{0,4},{1,5},{2,6},{3,7},{4,0},{5,1},{6,2},{7,3},{8,12},{9,13},{10,... | collective-permute-start | bytes 49160 | tf_op jit(solution)/shard_map/ppermute | solution.py:53
  50.0 5.1 %collective-permute-start.7 = (f32[2,64,64]{2,1,0:T(8,128)S(1)}, f32[2,64,64]{2,1,0:T(8,128)S(1)}, u32[]{:S(2)}, u32[]{:S(2)}) collective-permute-start(f32[2,64,64]{2,1,0:T(8,128)S(1)} %pad_maximum_fusion.1), channel_id=1, source_target_pairs={{0,8},{8,0},{16,24},{24,16},{32,40},{40,32},{48,56},{56,48},{64,72... | collective-permute-start | bytes 98312 | tf_op jit(solution)/shard_map/ppermute | solution.py:53
  56.4 5.3 %collective-permute-start.8 = (f32[2,64,64]{2,1,0:T(8,128)S(1)}, f32[2,64,64]{2,1,0:T(8,128)S(1)}, u32[]{:S(2)}, u32[]{:S(2)}) collective-permute-start(f32[2,64,64]{2,1,0:T(8,128)S(1)} %fusion.31), channel_id=1, source_target_pairs={{0,16},{8,24},{16,0},{24,8},{32,48},{40,56},{48,32},{56,40},{64,80... | collective-permute-start | bytes 98312 | tf_op jit(solution)/shard_map/ppermute | solution.py:53
  61.6 5.9 %collective-permute-start.9 = (f32[2,64,64]{2,1,0:T(8,128)S(1)}, f32[2,64,64]{2,1,0:T(8,128)S(1)}, u32[]{:S(2)}, u32[]{:S(2)}) collective-permute-start(f32[2,64,64]{2,1,0:T(8,128)S(1)} %add.126), channel_id=1, source_target_pairs={{0,32},{8,40},{16,48},{24,56},{32,0},{40,8},{48,16},{56,24},{64,96... | collective-permute-start | bytes 98312 | tf_op jit(solution)/shard_map/ppermute | solution.py:53
  67.5 4.9 %collective-permute-start.10 = (f32[2,64,64]{2,1,0:T(8,128)S(1)}, f32[2,64,64]{2,1,0:T(8,128)S(1)}, u32[]{:S(2)}, u32[]{:S(2)}) collective-permute-start(f32[2,64,64]{2,1,0:T(8,128)S(1)} %add.131), channel_id=1, source_target_pairs={{0,64},{8,72},{16,80},{24,88},{32,96},{40,104},{48,112},{56,120},{... | collective-permute-start | bytes 98312 | tf_op jit(solution)/shard_map/ppermute | solution.py:53
  73.1 8.7 %collective-permute-start.11 = (f32[64,64]{1,0:T(8,128)S(1)}, f32[64,64]{1,0:T(8,128)S(1)}, u32[]{:S(2)}, u32[]{:S(2)}) collective-permute-start(f32[64,64]{1,0:T(8,128)S(1)} %get-tuple-element.52), channel_id=1, source_target_pairs={{0,1},{1,0},{2,3},{3,2},{4,5},{5,4},{6,7},{7,6},{8,9},{9,8},{10,11... | collective-permute-start | bytes 49160 | tf_op jit(solution)/shard_map/ppermute | solution.py:53
  81.8 5.5 %collective-permute-start.12 = (f32[64,64]{1,0:T(8,128)S(1)}, f32[64,64]{1,0:T(8,128)S(1)}, u32[]{:S(2)}, u32[]{:S(2)}) collective-permute-start(f32[64,64]{1,0:T(8,128)S(1)} %fusion.30), channel_id=1, source_target_pairs={{0,2},{1,3},{2,0},{3,1},{4,6},{5,7},{6,4},{7,5},{8,10},{9,11},{10,... | collective-permute-start | bytes 49160 | tf_op jit(solution)/shard_map/ppermute | solution.py:53
  89.9 17.5 %all-to-all-start.1 = ((f32[64,1,8,512]{3,2,1,0:T(8,128)}), f32[64,1,8,512]{3,2,1,0:T(8,128)S(1)}, u32[]{:S(2)}, u32[]{:S(2)}) async-start(f32[64,1,8,512]{3,2,1,0:T(8,128)} %copy.15), calls=%async_computation.1 | async-start | bytes 2097152 | tf_op jit(solution)/shard_map/all_to_all | solution.py:148
  93.9 11.5 %collective-permute-start.13 = (f32[64,64]{1,0:T(8,128)S(1)}, f32[64,64]{1,0:T(8,128)S(1)}, u32[]{:S(2)}, u32[]{:S(2)}) collective-permute-start(f32[64,64]{1,0:T(8,128)S(1)} %add.134), channel_id=1, source_target_pairs={{0,4},{1,5},{2,6},{3,7},{4,0},{5,1},{6,2},{7,3},{8,12},{9,13},{10,... | collective-permute-start | bytes 49160 | tf_op jit(solution)/shard_map/ppermute | solution.py:53

commit v9 on v8

--- a/solution.py
+++ b/solution.py
@@ -94,9 +94,6 @@
         extra = exchange(extra, *bits.pop(0))
     solved, extra = lax.optimization_barrier((solved, extra))
     inverse = jnp.dot(solved.T, solved, precision=lax.Precision.HIGHEST)
-    if bits:
-        extra = exchange(extra, *bits.pop(0))
-    inverse, extra = lax.optimization_barrier((inverse, extra))
     return inverse, extra
 
 
@@ -126,7 +123,7 @@
             done.append(bit)
         return lax.optimization_barrier((acc, field))
 
-    gram, field = tick(gram, halo(v, width, 2))
+    field = halo(v, width, 2)
     for step in range(STEPS):
         gram, field = tick(gram, forward_step(field, coeffs[step]))
     flat_z = field[:, :, width : width + rows, :].reshape(members, -1)

time: 109 us -> 108 us (level)
  starting transfers between devices: 37.6 us -> 35.8 us
    ppermute x10 -> x9, starting transfers between devices: 20.9 us -> 19.2 us  [exchange(): return x + lax.ppermute(x, axis, [(i, i ^ bit) for i in range(count)])]
    ppermute x10 -> x9, waiting for transfers between devices: 26.2 us -> 27 us  [exchange(): return x + lax.ppermute(x, axis, [(i, i ^ bit) for i in range(count)])]
  transfers between devices with their start and end apart: 16 -> 15, of which waited for: 10 -> 9; matrix products, arithmetic and copies ran while one was open for 9% -> 7% of each run, Pallas kernels for 8% -> 8%
where the time goes in v9:
time: 108 us; the launch traced here: 107 us
  waiting for transfers between devices  42.5 us (39%)
  starting transfers between devices  35.8 us (33%)
  other arithmetic  9.57 us (9%)
  Pallas kernels  8.15 us (8%)
  local copies, waits for them, and re-layouts  6.31 us (6%)
  matrix products  4.02 us (4%)
    ppermute x9, waiting for transfers between devices, exchange(): return x + lax.ppermute(x, axis, [(i, i ^ bit) for i in range(count)])  27 us
    ppermute x9, starting transfers between devices, exchange(): return x + lax.ppermute(x, axis, [(i, i ^ bit) for i in range(count)])  19.2 us
    all_to_all x1, waiting for transfers between devices, body(): v = lax.all_to_all(perturbations, 'mem', 1, 0, tiled=True)  14.4 us
    pallas_call x1, Pallas kernels, lower_inverse(): pl.pallas_call(chol_inv_kernel, out_shape=jax.ShapeDtypeStruct((n, n), jn...  8.15 us
    all_to_all x1, starting transfers between devices, body(): v = lax.all_to_all(perturbations, 'mem', 1, 0, tiled=True)  7.04 us
    all_to_all x1, starting transfers between devices, body(): ritz = lax.all_to_all(ritz.reshape(v.shape), 'mem', 0, 1, tiled=True)  3.87 us
    ppermute x2, starting transfers between devices, halo(): lax.ppermute(lax.slice_in_dim(block, size - width, size, axis=dim), 'dom'...  3.12 us
    add x2, other arithmetic, adjoint_step(): result + shifted(coef[3] * field, 1, 3) + shifted(coef[4] * field, -1, 3)  2.94 us
  transfers between devices with their start and end apart: 15, of which 9 were waited for; matrix products, arithmetic and copies ran while one was open for 7% of the time, Pallas kernels for 8%

profile of v9, /device:TPU:0, one launch (start us, length us, event | category | flops | bytes accessed | tf_op | source)
XLA Modules:
  0.0 107.2 jit_solution(9817629924072110782)
XLA Ops:
  0.6 2.3 %copy.11 = f32[8,8,8,512]{3,2,0,1:T(8,128)} copy(f32[8,8,8,512]{3,2,1,0:T(8,128)} %param.2) | data formatting | bytes 2097152 | tf_op args[0]
  3.0 7.0 %all-to-all-start = ((f32[8,8,8,512]{3,2,0,1:T(8,128)}), f32[8,8,8,512]{3,2,0,1:T(8,128)S(1)}, u32[]{:S(2)}, u32[]{:S(2)}) async-start(f32[8,8,8,512]{3,2,0,1:T(8,128)} %copy.11), calls=%async_computation | async-start | bytes 2097152 | tf_op jit(solution)/shard_map/all_to_all | solution.py:105
  10.0 1.5 %collective-permute-start.1 = (bf16[2,5,1,4,512]{4,3,2,1,0:T(4,128)(2,1)S(1)}, bf16[2,5,1,4,512]{4,3,2,1,0:T(4,128)(2,1)S(1)}, u32[]{:S(2)}, u32[]{:S(2)}) collective-permute-start(bf16[2,5,1,4,512]{4,3,2,1,0:T(4,128)(2,1)S(1)} %get-tuple-element.42), channel_id=1, source_target_pairs={{0,8},{8,16},{16,24},{24,32},{32,40},{40,48},{48,56},{56,64},{64,7... | collective-permute-start | bytes 122888 | tf_op jit(solution)/shard_map/ppermute | solution.py:16
  11.5 1.3 %collective-permute-start.2 = (bf16[2,5,1,4,512]{4,3,2,1,0:T(4,128)(2,1)S(1)}, bf16[2,5,1,4,512]{4,3,2,1,0:T(4,128)(2,1)S(1)}, u32[]{:S(2)}, u32[]{:S(2)}) collective-permute-start(bf16[2,5,1,4,512]{4,3,2,1,0:T(4,128)(2,1)S(1)} %get-tuple-element.43), channel_id=1, source_target_pairs={{8,0},{16,8},{24,16},{32,24},{40,32},{48,40},{56,48},{64,56},{72,6... | collective-permute-start | bytes 122888 | tf_op jit(solution)/shard_map/ppermute | solution.py:17
  12.8 14.4 %all-to-all-done = f32[8,8,8,512]{3,2,0,1:T(8,128)S(1)} async-done(((f32[8,8,8,512]{3,2,0,1:T(8,128)}), f32[8,8,8,512]{3,2,0,1:T(8,128)S(1)}, u32[]{:S(2)}, u32[]{:S(2)}) %all-to-all-start) | async-done | bytes 1048608 | tf_op jit(solution)/shard_map/all_to_all | solution.py:105
  27.2 0.6 copy.31
  27.8 0.1 fusion.31
  27.9 1.7 %collective-permute-start.3 = (f32[64,1,4,512]{3,0,2,1:T(8,128)S(1)}, f32[64,1,4,512]{3,0,2,1:T(8,128)S(1)}, u32[]{:S(2)}, u32[]{:S(2)}) collective-permute-start(f32[64,1,4,512]{3,0,2,1:T(8,128)S(1)} %get-tuple-element.30), channel_id=1, source_target_pairs={{0,8},{8,16},{16,24},{24,32},{32,40},{40,48},{48,56},{56,64},{64,7... | collective-permute-start | bytes 1572872 | tf_op jit(solution)/shard_map/ppermute | solution.py:16
  29.6 1.3 %collective-permute-start.4 = (f32[64,1,4,512]{3,0,2,1:T(8,128)S(1)}, f32[64,1,4,512]{3,0,2,1:T(8,128)S(1)}, u32[]{:S(2)}, u32[]{:S(2)}) collective-permute-start(f32[64,1,4,512]{3,0,2,1:T(8,128)S(1)} %get-tuple-element.31), channel_id=1, source_target_pairs={{8,0},{16,8},{24,16},{32,24},{40,32},{48,40},{56,48},{64,56},{72,6... | collective-permute-start | bytes 1572872 | tf_op jit(solution)/shard_map/ppermute | solution.py:17
  30.9 0.0 collective-permute-done.2
  30.9 0.1 maximum_convert_fusion
  31.0 0.6 copy.18
  31.6 1.0 fusion.33
  32.6 0.6 collective-permute-start
  33.2 3.4 %collective-permute-done = f32[64,64]{1,0:T(8,128)S(1)} collective-permute-done((f32[64,64]{1,0:T(8,128)S(1)}, f32[64,64]{1,0:T(8,128)S(1)}, u32[]{:S(2)}, u32[]{:S(2)}) %collective-permute-start) | collective-permute-done | bytes 16416 | tf_op jit(solution)/shard_map/ppermute | solution.py:53
  36.6 0.0 collective-permute-done.3
  36.6 0.0 collective-permute-done.4
  36.6 0.2 pad_maximum_fusion
  36.8 1.3 %fusion.4 = f32[64,1,16,512]{3,0,2,1:T(8,128)S(1)} fusion(f32[64,1,16,512]{3,0,2,1:T(8,128)S(1)} %pad_maximum_fusion, f32[16,512]{1,0:T(8,128)S(1)} %get-tuple-element.37, f32[16,512]{1,0:T(8,128)S(1)} %get-tuple-element.38, f32[16,512]{1,0:T(8,128)S(1)} %get-tuple-element.39, f32[16,512]{1,0:T(8,128)S(1)} %get-tuple-element.40, ...), kind=kLoop, calls=%fused_computation.20 | loop fusion | flops 4718592 | bytes 4358144 | tf_op jit(solution)/shard_map/add | solution.py:33
  38.1 1.2 %collective-permute-start.5 = (f32[64,64]{1,0:T(8,128)S(1)}, f32[64,64]{1,0:T(8,128)S(1)}, u32[]{:S(2)}, u32[]{:S(2)}) collective-permute-start(f32[64,64]{1,0:T(8,128)S(1)} %add.107), channel_id=1, source_target_pairs={{0,2},{1,3},{2,0},{3,1},{4,6},{5,7},{6,4},{7,5},{8,10},{9,11},{10,... | collective-permute-start | bytes 49160 | tf_op jit(solution)/shard_map/ppermute | solution.py:53
  39.3 1.3 %fusion.10 = f32[64,1,16,512]{3,0,2,1:T(8,128)S(1)} fusion(f32[64,1,16,512]{3,0,2,1:T(8,128)S(1)} %fusion.4, f32[16,512]{1,0:T(8,128)S(1)} %get-tuple-element.33, f32[16,512]{1,0:T(8,128)S(1)} %get-tuple-element.34, f32[16,512]{1,0:T(8,128)S(1)} %get-tuple-element.35, f32[16,512]{1,0:T(8,128)S(1)} %get-tuple-element.36, f32[16,512]{1,0:T(8,128)S(1)} %get-tuple-element.32), kind=kLoop, calls=%fused_computation.26 | loop fusion | flops 4718592 | bytes 4358144 | tf_op jit(solution)/shard_map/add | solution.py:33
  40.6 3.0 %collective-permute-done.5 = f32[64,64]{1,0:T(8,128)S(1)} collective-permute-done((f32[64,64]{1,0:T(8,128)S(1)}, f32[64,64]{1,0:T(8,128)S(1)}, u32[]{:S(2)}, u32[]{:S(2)}) %collective-permute-start.5) | collective-permute-done | bytes 16416 | tf_op jit(solution)/shard_map/ppermute | solution.py:53
  43.6 1.2 %broadcast_multiply_fusion = (f32[64,1,16,512]{3,0,2,1:T(8,128)S(1)}, f32[64,1,16,512]{3,0,2,1:T(8,128)S(1)}, f32[64,1,16,512]{3,0,2,1:T(8,128)S(1)}, f32[64,1,16,512]{3,0,2,1:T(8,128)S(1)}) fusion(f32[64,1,16,512]{3,0,2,1:T(8,128)S(1)} %fusion.10, f32[16,512]{1,0:T(8,128)S(1)} %get-tuple-element.33, f32[16,512]{1,0:T(8,128)S(1)} %get-tuple-element.34, ...), kind=kLoop, calls=%fused_computation.50 | loop fusion | flops 2097152 | bytes 10616832 | tf_op jit(solution)/shard_map/mul | solution.py:38
  44.8 1.0 convolution_bitcast_fusion.2
  45.8 0.6 collective-permute-start.6
  46.5 1.5 %fusion.15 = f32[64,1,16,512]{3,0,2,1:T(8,128)S(1)} fusion(f32[64,1,16,512]{3,0,2,1:T(8,128)S(1)} %get-tuple-element.29, f32[64,1,16,512]{3,0,2,1:T(8,128)S(1)} %get-tuple-element.28, f32[64,1,16,512]{3,0,2,1:T(8,128)S(1)} %get-tuple-element.27, f32[64,1,16,512]{3,0,2,1:T(8,128)S(1)} %get-tuple-element.26, f32[64,1,16,512]{3,0,2,1:T(8,128)S(1)} %fusion.10, ...), kind=kLoop, calls=%fused_computation.31 | loop fusion | flops 2621440 | bytes 12615680 | tf_op jit(solution)/shard_map/add | solution.py:38
  48.0 3.7 %collective-permute-done.6 = f32[2,64,64]{2,1,0:T(8,128)S(1)} collective-permute-done((f32[2,64,64]{2,1,0:T(8,128)S(1)}, f32[2,64,64]{2,1,0:T(8,128)S(1)}, u32[]{:S(2)}, u32[]{:S(2)}) %collective-permute-start.6) | collective-permute-done | bytes 32800 | tf_op jit(solution)/shard_map/ppermute | solution.py:53
  51.7 1.2 %broadcast_multiply_fusion.4 = (f32[64,1,16,512]{3,0,2,1:T(8,128)S(1)}, f32[64,1,16,512]{3,0,2,1:T(8,128)S(1)}, f32[64,1,16,512]{3,0,2,1:T(8,128)S(1)}, f32[64,1,16,512]{3,0,2,1:T(8,128)S(1)}) fusion(f32[64,1,16,512]{3,0,2,1:T(8,128)S(1)} %fusion.15, f32[16,512]{1,0:T(8,128)S(1)} %get-tuple-element.37, f32[16,512]{1,0:T(8,128)S(1)} %get-tuple-element.38, ...), kind=kLoop, calls=%fused_computation.54 | loop fusion | flops 2097152 | bytes 10616832 | tf_op jit(solution)/shard_map/mul | solution.py:38
  52.9 3.7 %collective-permute-start.7 = (f32[2,64,64]{2,1,0:T(8,128)S(1)}, f32[2,64,64]{2,1,0:T(8,128)S(1)}, u32[]{:S(2)}, u32[]{:S(2)}) collective-permute-start(f32[2,64,64]{2,1,0:T(8,128)S(1)} %fusion.30), channel_id=1, source_target_pairs={{0,8},{8,0},{16,24},{24,16},{32,40},{40,32},{48,56},{56,48},{64,72... | collective-permute-start | bytes 98312 | tf_op jit(solution)/shard_map/ppermute | solution.py:53
  56.7 1.4 %fusion.19 = f32[64,1,16,512]{3,0,2,1:T(8,128)S(1)} fusion(f32[64,1,16,512]{3,0,2,1:T(8,128)S(1)} %get-tuple-element.25, f32[64,1,16,512]{3,0,2,1:T(8,128)S(1)} %get-tuple-element.24, f32[64,1,16,512]{3,0,2,1:T(8,128)S(1)} %get-tuple-element.23, f32[64,1,16,512]{3,0,2,1:T(8,128)S(1)} %get-tuple-element.22, f32[64,1,16,512]{3,0,2,1:T(8,128)S(1)} %fusion.15, ...), kind=kLoop, calls=%fused_computation.35 | loop fusion | flops 2621440 | bytes 12615680 | tf_op jit(solution)/shard_map/add | solution.py:38
  58.1 2.8 %collective-permute-start.8 = (f32[2,64,64]{2,1,0:T(8,128)S(1)}, f32[2,64,64]{2,1,0:T(8,128)S(1)}, u32[]{:S(2)}, u32[]{:S(2)}) collective-permute-start(f32[2,64,64]{2,1,0:T(8,128)S(1)} %add.122), channel_id=1, source_target_pairs={{0,16},{8,24},{16,0},{24,8},{32,48},{40,56},{48,32},{56,40},{64,80... | collective-permute-start | bytes 98312 | tf_op jit(solution)/shard_map/ppermute | solution.py:53
  61.0 2.7 %collective-permute-done.8 = f32[2,64,64]{2,1,0:T(8,128)S(1)} collective-permute-done((f32[2,64,64]{2,1,0:T(8,128)S(1)}, f32[2,64,64]{2,1,0:T(8,128)S(1)}, u32[]{:S(2)}, u32[]{:S(2)}) %collective-permute-start.8) | collective-permute-done | bytes 32800 | tf_op jit(solution)/shard_map/ppermute | solution.py:53
  63.6 3.6 %collective-permute-start.9 = (f32[2,64,64]{2,1,0:T(8,128)S(1)}, f32[2,64,64]{2,1,0:T(8,128)S(1)}, u32[]{:S(2)}, u32[]{:S(2)}) collective-permute-start(f32[2,64,64]{2,1,0:T(8,128)S(1)} %add.127), channel_id=1, source_target_pairs={{0,32},{8,40},{16,48},{24,56},{32,0},{40,8},{48,16},{56,24},{64,96... | collective-permute-start | bytes 98312 | tf_op jit(solution)/shard_map/ppermute | solution.py:53
  67.3 2.2 %collective-permute-done.9 = f32[2,64,64]{2,1,0:T(8,128)S(1)} collective-permute-done((f32[2,64,64]{2,1,0:T(8,128)S(1)}, f32[2,64,64]{2,1,0:T(8,128)S(1)}, u32[]{:S(2)}, u32[]{:S(2)}) %collective-permute-start.9) | collective-permute-done | bytes 32800 | tf_op jit(solution)/shard_map/ppermute | solution.py:53
  69.5 2.3 %collective-permute-start.10 = (f32[2,64,64]{2,1,0:T(8,128)S(1)}, f32[2,64,64]{2,1,0:T(8,128)S(1)}, u32[]{:S(2)}, u32[]{:S(2)}) collective-permute-start(f32[2,64,64]{2,1,0:T(8,128)S(1)} %add.128), channel_id=1, source_target_pairs={{0,64},{8,72},{16,80},{24,88},{32,96},{40,104},{48,112},{56,120},{... | collective-permute-start | bytes 98312 | tf_op jit(solution)/shard_map/ppermute | solution.py:53
  71.9 2.2 %collective-permute-done.10 = f32[2,64,64]{2,1,0:T(8,128)S(1)} collective-permute-done((f32[2,64,64]{2,1,0:T(8,128)S(1)}, f32[2,64,64]{2,1,0:T(8,128)S(1)}, u32[]{:S(2)}, u32[]{:S(2)}) %collective-permute-start.10) | collective-permute-done | bytes 32800 | tf_op jit(solution)/shard_map/ppermute | solution.py:53
  74.1 0.6 slice_bitcast_fusion
  74.8 0.6 collective-permute-start.11
  75.4 8.2 %shard_map.41 = f32[64,64]{1,0:T(8,128)} custom-call(f32[64,64]{1,0:T(8,128)} %get-tuple-element.45.g_ref), custom_call_target="tpu_custom_call" | custom-call | tf_op jit(solution)/shard_map/pallas_call | solution.py:84
  83.5 1.1 convolution_bitcast_fusion.1
  84.6 1.0 convolution_bitcast_fusion
  85.6 1.6 %copy.15 = f32[64,1,8,512]{3,2,1,0:T(8,128)} copy(f32[64,1,8,512]{3,0,2,1:T(8,128)S(1)} %convolution_bitcast_fusion) | data formatting | bytes 2097152 | tf_op jit(solution)/shard_map/dot_general | solution.py:141
  87.2 3.9 %all-to-all-start.1 = ((f32[64,1,8,512]{3,2,1,0:T(8,128)}), f32[64,1,8,512]{3,2,1,0:T(8,128)S(1)}, u32[]{:S(2)}, u32[]{:S(2)}) async-start(f32[64,1,8,512]{3,2,1,0:T(8,128)} %copy.15), calls=%async_computation.1 | async-start | bytes 2097152 | tf_op jit(solution)/shard_map/all_to_all | solution.py:145
  91.1 3.5 %collective-permute-start.12 = (f32[64,64]{1,0:T(8,128)S(1)}, f32[64,64]{1,0:T(8,128)S(1)}, u32[]{:S(2)}, u32[]{:S(2)}) collective-permute-start(f32[64,64]{1,0:T(8,128)S(1)} %fusion.29), channel_id=1, source_target_pairs={{0,2},{1,3},{2,0},{3,1},{4,6},{5,7},{6,4},{7,5},{8,10},{9,11},{10,... | collective-permute-start | bytes 49160 | tf_op jit(solution)/shard_map/ppermute | solution.py:53
  94.6 9.8 %collective-permute-done.12 = f32[64,64]{1,0:T(8,128)S(1)} collective-permute-done((f32[64,64]{1,0:T(8,128)S(1)}, f32[64,64]{1,0:T(8,128)S(1)}, u32[]{:S(2)}, u32[]{:S(2)}) %collective-permute-start.12) | collective-permute-done | bytes 16416 | tf_op jit(solution)/shard_map/ppermute | solution.py:53
  104.4 0.6 add_multiply_fusion
  105.1 1.1 %all-to-all-done.1 = f32[64,1,8,512]{3,2,1,0:T(8,128)S(1)} async-done(((f32[64,1,8,512]{3,2,1,0:T(8,128)}), f32[64,1,8,512]{3,2,1,0:T(8,128)S(1)}, u32[]{:S(2)}, u32[]{:S(2)}) %all-to-all-start.1) | async-done | bytes 1048608 | tf_op jit(solution)/shard_map/all_to_all | solution.py:145
  106.2 1.1 copy.30
  (16 shorter events, 0.1 us)
Async XLA Ops:
  0.6 9.4 %copy-start = (bf16[2,5,1,8,512]{4,3,2,1,0:T(8,128)(2,1)S(1)}, bf16[2,5,1,8,512]{4,3,2,1,0:T(8,128)(2,1)}, u32[]{:S(2)}) copy-start(bf16[2,5,1,8,512]{4,3,2,1,0:T(8,128)(2,1)} %param.3) | copy-start | bytes 245764
  3.0 24.2 %all-to-all-start = ((f32[8,8,8,512]{3,2,0,1:T(8,128)}), f32[8,8,8,512]{3,2,0,1:T(8,128)S(1)}, u32[]{:S(2)}, u32[]{:S(2)}) async-start(f32[8,8,8,512]{3,2,0,1:T(8,128)} %copy.11), calls=%async_computation | async-start | bytes 2097152 | tf_op jit(solution)/shard_map/all_to_all | solution.py:105
  10.0 20.8 %collective-permute-start.1 = (bf16[2,5,1,4,512]{4,3,2,1,0:T(4,128)(2,1)S(1)}, bf16[2,5,1,4,512]{4,3,2,1,0:T(4,128)(2,1)S(1)}, u32[]{:S(2)}, u32[]{:S(2)}) collective-permute-start(bf16[2,5,1,4,512]{4,3,2,1,0:T(4,128)(2,1)S(1)} %get-tuple-element.42), channel_id=1, source_target_pairs={{0,8},{8,16},{16,24},{24,32},{32,40},{40,48},{48,56},{56,64},{64,7... | collective-permute-start | bytes 122888 | tf_op jit(solution)/shard_map/ppermute | solution.py:16
  11.5 19.4 %collective-permute-start.2 = (bf16[2,5,1,4,512]{4,3,2,1,0:T(4,128)(2,1)S(1)}, bf16[2,5,1,4,512]{4,3,2,1,0:T(4,128)(2,1)S(1)}, u32[]{:S(2)}, u32[]{:S(2)}) collective-permute-start(bf16[2,5,1,4,512]{4,3,2,1,0:T(4,128)(2,1)S(1)} %get-tuple-element.43), channel_id=1, source_target_pairs={{8,0},{16,8},{24,16},{32,24},{40,32},{48,40},{56,48},{64,56},{72,6... | collective-permute-start | bytes 122888 | tf_op jit(solution)/shard_map/ppermute | solution.py:17
  27.9 8.7 %collective-permute-start.3 = (f32[64,1,4,512]{3,0,2,1:T(8,128)S(1)}, f32[64,1,4,512]{3,0,2,1:T(8,128)S(1)}, u32[]{:S(2)}, u32[]{:S(2)}) collective-permute-start(f32[64,1,4,512]{3,0,2,1:T(8,128)S(1)} %get-tuple-element.30), channel_id=1, source_target_pairs={{0,8},{8,16},{16,24},{24,32},{32,40},{40,48},{48,56},{56,64},{64,7... | collective-permute-start | bytes 1572872 | tf_op jit(solution)/shard_map/ppermute | solution.py:16
  29.6 7.0 %collective-permute-start.4 = (f32[64,1,4,512]{3,0,2,1:T(8,128)S(1)}, f32[64,1,4,512]{3,0,2,1:T(8,128)S(1)}, u32[]{:S(2)}, u32[]{:S(2)}) collective-permute-start(f32[64,1,4,512]{3,0,2,1:T(8,128)S(1)} %get-tuple-element.31), channel_id=1, source_target_pairs={{8,0},{16,8},{24,16},{32,24},{40,32},{48,40},{56,48},{64,56},{72,6... | collective-permute-start | bytes 1572872 | tf_op jit(solution)/shard_map/ppermute | solution.py:17
  32.6 4.0 %collective-permute-start = (f32[64,64]{1,0:T(8,128)S(1)}, f32[64,64]{1,0:T(8,128)S(1)}, u32[]{:S(2)}, u32[]{:S(2)}) collective-permute-start(f32[64,64]{1,0:T(8,128)S(1)} %fusion.33), channel_id=1, source_target_pairs={{0,1},{1,0},{2,3},{3,2},{4,5},{5,4},{6,7},{7,6},{8,9},{9,8},{10,11... | collective-permute-start | bytes 49160 | tf_op jit(solution)/shard_map/ppermute | solution.py:53
  38.1 5.5 %collective-permute-start.5 = (f32[64,64]{1,0:T(8,128)S(1)}, f32[64,64]{1,0:T(8,128)S(1)}, u32[]{:S(2)}, u32[]{:S(2)}) collective-permute-start(f32[64,64]{1,0:T(8,128)S(1)} %add.107), channel_id=1, source_target_pairs={{0,2},{1,3},{2,0},{3,1},{4,6},{5,7},{6,4},{7,5},{8,10},{9,11},{10,... | collective-permute-start | bytes 49160 | tf_op jit(solution)/shard_map/ppermute | solution.py:53
  45.8 5.8 %collective-permute-start.6 = (f32[2,64,64]{2,1,0:T(8,128)S(1)}, f32[2,64,64]{2,1,0:T(8,128)S(1)}, u32[]{:S(2)}, u32[]{:S(2)}) collective-permute-start(f32[2,64,64]{2,1,0:T(8,128)S(1)} %pad_maximum_fusion.1), channel_id=1, source_target_pairs={{0,4},{1,5},{2,6},{3,7},{4,0},{5,1},{6,2},{7,3},{8,12},{9,13},{10,... | collective-permute-start | bytes 98312 | tf_op jit(solution)/shard_map/ppermute | solution.py:53
  52.9 5.2 %collective-permute-start.7 = (f32[2,64,64]{2,1,0:T(8,128)S(1)}, f32[2,64,64]{2,1,0:T(8,128)S(1)}, u32[]{:S(2)}, u32[]{:S(2)}) collective-permute-start(f32[2,64,64]{2,1,0:T(8,128)S(1)} %fusion.30), channel_id=1, source_target_pairs={{0,8},{8,0},{16,24},{24,16},{32,40},{40,32},{48,56},{56,48},{64,72... | collective-permute-start | bytes 98312 | tf_op jit(solution)/shard_map/ppermute | solution.py:53
  58.1 5.5 %collective-permute-start.8 = (f32[2,64,64]{2,1,0:T(8,128)S(1)}, f32[2,64,64]{2,1,0:T(8,128)S(1)}, u32[]{:S(2)}, u32[]{:S(2)}) collective-permute-start(f32[2,64,64]{2,1,0:T(8,128)S(1)} %add.122), channel_id=1, source_target_pairs={{0,16},{8,24},{16,0},{24,8},{32,48},{40,56},{48,32},{56,40},{64,80... | collective-permute-start | bytes 98312 | tf_op jit(solution)/shard_map/ppermute | solution.py:53
  63.6 5.9 %collective-permute-start.9 = (f32[2,64,64]{2,1,0:T(8,128)S(1)}, f32[2,64,64]{2,1,0:T(8,128)S(1)}, u32[]{:S(2)}, u32[]{:S(2)}) collective-permute-start(f32[2,64,64]{2,1,0:T(8,128)S(1)} %add.127), channel_id=1, source_target_pairs={{0,32},{8,40},{16,48},{24,56},{32,0},{40,8},{48,16},{56,24},{64,96... | collective-permute-start | bytes 98312 | tf_op jit(solution)/shard_map/ppermute | solution.py:53
  69.5 4.6 %collective-permute-start.10 = (f32[2,64,64]{2,1,0:T(8,128)S(1)}, f32[2,64,64]{2,1,0:T(8,128)S(1)}, u32[]{:S(2)}, u32[]{:S(2)}) collective-permute-start(f32[2,64,64]{2,1,0:T(8,128)S(1)} %add.128), channel_id=1, source_target_pairs={{0,64},{8,72},{16,80},{24,88},{32,96},{40,104},{48,112},{56,120},{... | collective-permute-start | bytes 98312 | tf_op jit(solution)/shard_map/ppermute | solution.py:53
  74.8 8.8 %collective-permute-start.11 = (f32[64,64]{1,0:T(8,128)S(1)}, f32[64,64]{1,0:T(8,128)S(1)}, u32[]{:S(2)}, u32[]{:S(2)}) collective-permute-start(f32[64,64]{1,0:T(8,128)S(1)} %get-tuple-element.44), channel_id=1, source_target_pairs={{0,1},{1,0},{2,3},{3,2},{4,5},{5,4},{6,7},{7,6},{8,9},{9,8},{10,11... | collective-permute-start | bytes 49160 | tf_op jit(solution)/shard_map/ppermute | solution.py:53
  87.2 18.9 %all-to-all-start.1 = ((f32[64,1,8,512]{3,2,1,0:T(8,128)}), f32[64,1,8,512]{3,2,1,0:T(8,128)S(1)}, u32[]{:S(2)}, u32[]{:S(2)}) async-start(f32[64,1,8,512]{3,2,1,0:T(8,128)} %copy.15), calls=%async_computation.1 | async-start | bytes 2097152 | tf_op jit(solution)/shard_map/all_to_all | solution.py:145
  91.1 13.3 %collective-permute-start.12 = (f32[64,64]{1,0:T(8,128)S(1)}, f32[64,64]{1,0:T(8,128)S(1)}, u32[]{:S(2)}, u32[]{:S(2)}) collective-permute-start(f32[64,64]{1,0:T(8,128)S(1)} %fusion.29), channel_id=1, source_target_pairs={{0,2},{1,3},{2,0},{3,1},{4,6},{5,7},{6,4},{7,5},{8,10},{9,11},{10,... | collective-permute-start | bytes 49160 | tf_op jit(solution)/shard_map/ppermute | solution.py:53

commit v10 on v9

--- a/solution.py
+++ b/solution.py
@@ -2,7 +2,6 @@
 import jax.numpy as jnp
 from jax import lax
 from jax.experimental import pallas as pl
-from jax.experimental.pallas import tpu as pltpu
 from jax.sharding import PartitionSpec as P
 
 STEPS = 2
@@ -53,30 +52,29 @@
     return x + lax.ppermute(x, axis, [(i, i ^ bit) for i in range(count)])
 
 
-def chol_inv_kernel(g_ref, x_ref, a_ref):
+def chol_inv_kernel(g_ref, x_ref):
     n = g_ref.shape[0]
-    a_ref[...] = g_ref[...]
     rows = lax.broadcasted_iota(jnp.int32, (n, n), 0)
     cols = lax.broadcasted_iota(jnp.int32, (n, n), 1)
-    x_ref[...] = jnp.where(rows == cols, 1.0, 0.0).astype(jnp.float32)
     lane = lax.broadcasted_iota(jnp.int32, (1, n), 1)
     sub = lax.broadcasted_iota(jnp.int32, (n, 1), 0)
 
     def step(k, carry):
-        a = a_ref[...]
-        row = a_ref[pl.ds(k, 1), :]
+        a, x = carry
+        row = jnp.sum(jnp.where(rows == k, a, 0.0), axis=0, keepdims=True)
+        col = jnp.sum(jnp.where(cols == k, a, 0.0), axis=1, keepdims=True)
         pivot = jnp.sum(jnp.where(lane == k, row, 0.0), axis=1, keepdims=True)
         scale = 1.0 / jnp.sqrt(pivot)
-        col = jnp.sum(jnp.where(cols == k, a, 0.0), axis=1, keepdims=True)
         below = jnp.where(sub > k, col * scale, 0.0)
         right = jnp.where(lane > k, row * scale, 0.0)
-        a_ref[...] = a - below * right
-        xrow = x_ref[pl.ds(k, 1), :] * scale
-        x_ref[pl.ds(k, 1), :] = xrow
-        x_ref[...] = x_ref[...] - below * xrow
-        return carry
+        a = a - below * right
+        xrow = jnp.sum(jnp.where(rows == k, x, 0.0), axis=0, keepdims=True) * scale
+        x = jnp.where(rows == k, xrow, x - below * xrow)
+        return a, x
 
-    lax.fori_loop(0, n, step, 0)
+    eye = jnp.where(rows == cols, 1.0, 0.0).astype(jnp.float32)
+    _, x = lax.fori_loop(0, n, step, (g_ref[...], eye), unroll=4)
+    x_ref[...] = x
 
 
 def lower_inverse(gram):
@@ -84,7 +82,6 @@
     return pl.pallas_call(
         chol_inv_kernel,
         out_shape=jax.ShapeDtypeStruct((n, n), jnp.float32),
-        scratch_shapes=[pltpu.VMEM((n, n), jnp.float32)],
     )(gram)
 
 

time: 108 us -> 108 us (level)
  no operation moved by 1% of the time
where the time goes in v10:
time: 108 us
  waiting for transfers between devices  42.5 us (39%)
  starting transfers between devices  35.8 us (33%)
  other arithmetic  9.57 us (9%)
  Pallas kernels  8.56 us (8%)
  local copies, waits for them, and re-layouts  6.31 us (6%)
  matrix products  4.02 us (4%)
    ppermute x9, waiting for transfers between devices, exchange(): return x + lax.ppermute(x, axis, [(i, i ^ bit) for i in range(count)])  27 us
    ppermute x9, starting transfers between devices, exchange(): return x + lax.ppermute(x, axis, [(i, i ^ bit) for i in range(count)])  19.2 us
    all_to_all x1, waiting for transfers between devices, body(): v = lax.all_to_all(perturbations, 'mem', 1, 0, tiled=True)  14.4 us
    pallas_call x1, Pallas kernels, lower_inverse(): pl.pallas_call(chol_inv_kernel, out_shape=jax.ShapeDtypeStruct((n, n), jn...  8.56 us
    all_to_all x1, starting transfers between devices, body(): v = lax.all_to_all(perturbations, 'mem', 1, 0, tiled=True)  7.04 us
    all_to_all x1, starting transfers between devices, body(): ritz = lax.all_to_all(ritz.reshape(v.shape), 'mem', 0, 1, tiled=True)  3.88 us
    ppermute x2, starting transfers between devices, halo(): lax.ppermute(lax.slice_in_dim(block, size - width, size, axis=dim), 'dom'...  3.12 us
    add x2, other arithmetic, adjoint_step(): result + shifted(coef[3] * field, 1, 3) + shifted(coef[4] * field, -1, 3)  2.94 us
  transfers between devices with their start and end apart: 15, of which 9 were waited for; matrix products, arithmetic and copies ran while one was open for 7% of the time, Pallas kernels for 8%

profile of v10, /device:TPU:0, one launch (start us, length us, event | category | flops | bytes accessed | tf_op | source)
XLA Modules:
  0.0 107.6 jit_solution(15095234704040846483)
XLA Ops:
  0.6 2.3 %copy.11 = f32[8,8,8,512]{3,2,0,1:T(8,128)} copy(f32[8,8,8,512]{3,2,1,0:T(8,128)} %param.2) | data formatting | bytes 2097152 | tf_op args[0]
  3.0 7.0 %all-to-all-start = ((f32[8,8,8,512]{3,2,0,1:T(8,128)}), f32[8,8,8,512]{3,2,0,1:T(8,128)S(1)}, u32[]{:S(2)}, u32[]{:S(2)}) async-start(f32[8,8,8,512]{3,2,0,1:T(8,128)} %copy.11), calls=%async_computation | async-start | bytes 2097152 | tf_op jit(solution)/shard_map/all_to_all | solution.py:102
  10.0 1.5 %collective-permute-start.1 = (bf16[2,5,1,4,512]{4,3,2,1,0:T(4,128)(2,1)S(1)}, bf16[2,5,1,4,512]{4,3,2,1,0:T(4,128)(2,1)S(1)}, u32[]{:S(2)}, u32[]{:S(2)}) collective-permute-start(bf16[2,5,1,4,512]{4,3,2,1,0:T(4,128)(2,1)S(1)} %get-tuple-element.42), channel_id=1, source_target_pairs={{0,8},{8,16},{16,24},{24,32},{32,40},{40,48},{48,56},{56,64},{64,7... | collective-permute-start | bytes 122888 | tf_op jit(solution)/shard_map/ppermute | solution.py:15
  11.5 1.3 %collective-permute-start.2 = (bf16[2,5,1,4,512]{4,3,2,1,0:T(4,128)(2,1)S(1)}, bf16[2,5,1,4,512]{4,3,2,1,0:T(4,128)(2,1)S(1)}, u32[]{:S(2)}, u32[]{:S(2)}) collective-permute-start(bf16[2,5,1,4,512]{4,3,2,1,0:T(4,128)(2,1)S(1)} %get-tuple-element.43), channel_id=1, source_target_pairs={{8,0},{16,8},{24,16},{32,24},{40,32},{48,40},{56,48},{64,56},{72,6... | collective-permute-start | bytes 122888 | tf_op jit(solution)/shard_map/ppermute | solution.py:16
  12.8 14.4 %all-to-all-done = f32[8,8,8,512]{3,2,0,1:T(8,128)S(1)} async-done(((f32[8,8,8,512]{3,2,0,1:T(8,128)}), f32[8,8,8,512]{3,2,0,1:T(8,128)S(1)}, u32[]{:S(2)}, u32[]{:S(2)}) %all-to-all-start) | async-done | bytes 1048608 | tf_op jit(solution)/shard_map/all_to_all | solution.py:102
  27.2 0.6 copy.31
  27.8 0.1 fusion.31
  27.9 1.7 %collective-permute-start.3 = (f32[64,1,4,512]{3,0,2,1:T(8,128)S(1)}, f32[64,1,4,512]{3,0,2,1:T(8,128)S(1)}, u32[]{:S(2)}, u32[]{:S(2)}) collective-permute-start(f32[64,1,4,512]{3,0,2,1:T(8,128)S(1)} %get-tuple-element.30), channel_id=1, source_target_pairs={{0,8},{8,16},{16,24},{24,32},{32,40},{40,48},{48,56},{56,64},{64,7... | collective-permute-start | bytes 1572872 | tf_op jit(solution)/shard_map/ppermute | solution.py:15
  29.6 1.3 %collective-permute-start.4 = (f32[64,1,4,512]{3,0,2,1:T(8,128)S(1)}, f32[64,1,4,512]{3,0,2,1:T(8,128)S(1)}, u32[]{:S(2)}, u32[]{:S(2)}) collective-permute-start(f32[64,1,4,512]{3,0,2,1:T(8,128)S(1)} %get-tuple-element.31), channel_id=1, source_target_pairs={{8,0},{16,8},{24,16},{32,24},{40,32},{48,40},{56,48},{64,56},{72,6... | collective-permute-start | bytes 1572872 | tf_op jit(solution)/shard_map/ppermute | solution.py:16
  30.9 0.0 collective-permute-done.1
  30.9 0.0 collective-permute-done.2
  30.9 0.1 maximum_convert_fusion
  31.0 0.6 copy.18
  31.6 1.0 fusion.33
  32.6 0.6 collective-permute-start
  33.2 3.4 %collective-permute-done = f32[64,64]{1,0:T(8,128)S(1)} collective-permute-done((f32[64,64]{1,0:T(8,128)S(1)}, f32[64,64]{1,0:T(8,128)S(1)}, u32[]{:S(2)}, u32[]{:S(2)}) %collective-permute-start) | collective-permute-done | bytes 16416 | tf_op jit(solution)/shard_map/ppermute | solution.py:52
  36.6 0.0 collective-permute-done.4
  36.6 0.2 pad_maximum_fusion
  36.8 1.3 %fusion.4 = f32[64,1,16,512]{3,0,2,1:T(8,128)S(1)} fusion(f32[64,1,16,512]{3,0,2,1:T(8,128)S(1)} %pad_maximum_fusion, f32[16,512]{1,0:T(8,128)S(1)} %get-tuple-element.37, f32[16,512]{1,0:T(8,128)S(1)} %get-tuple-element.38, f32[16,512]{1,0:T(8,128)S(1)} %get-tuple-element.39, f32[16,512]{1,0:T(8,128)S(1)} %get-tuple-element.40, ...), kind=kLoop, calls=%fused_computation.20 | loop fusion | flops 4718592 | bytes 4358144 | tf_op jit(solution)/shard_map/add | solution.py:32
  38.1 1.2 %collective-permute-start.5 = (f32[64,64]{1,0:T(8,128)S(1)}, f32[64,64]{1,0:T(8,128)S(1)}, u32[]{:S(2)}, u32[]{:S(2)}) collective-permute-start(f32[64,64]{1,0:T(8,128)S(1)} %add.107), channel_id=1, source_target_pairs={{0,2},{1,3},{2,0},{3,1},{4,6},{5,7},{6,4},{7,5},{8,10},{9,11},{10,... | collective-permute-start | bytes 49160 | tf_op jit(solution)/shard_map/ppermute | solution.py:52
  39.3 1.3 %fusion.10 = f32[64,1,16,512]{3,0,2,1:T(8,128)S(1)} fusion(f32[64,1,16,512]{3,0,2,1:T(8,128)S(1)} %fusion.4, f32[16,512]{1,0:T(8,128)S(1)} %get-tuple-element.33, f32[16,512]{1,0:T(8,128)S(1)} %get-tuple-element.34, f32[16,512]{1,0:T(8,128)S(1)} %get-tuple-element.35, f32[16,512]{1,0:T(8,128)S(1)} %get-tuple-element.36, f32[16,512]{1,0:T(8,128)S(1)} %get-tuple-element.32), kind=kLoop, calls=%fused_computation.26 | loop fusion | flops 4718592 | bytes 4358144 | tf_op jit(solution)/shard_map/add | solution.py:32
  40.6 3.0 %collective-permute-done.5 = f32[64,64]{1,0:T(8,128)S(1)} collective-permute-done((f32[64,64]{1,0:T(8,128)S(1)}, f32[64,64]{1,0:T(8,128)S(1)}, u32[]{:S(2)}, u32[]{:S(2)}) %collective-permute-start.5) | collective-permute-done | bytes 16416 | tf_op jit(solution)/shard_map/ppermute | solution.py:52
  43.6 1.2 %broadcast_multiply_fusion = (f32[64,1,16,512]{3,0,2,1:T(8,128)S(1)}, f32[64,1,16,512]{3,0,2,1:T(8,128)S(1)}, f32[64,1,16,512]{3,0,2,1:T(8,128)S(1)}, f32[64,1,16,512]{3,0,2,1:T(8,128)S(1)}) fusion(f32[64,1,16,512]{3,0,2,1:T(8,128)S(1)} %fusion.10, f32[16,512]{1,0:T(8,128)S(1)} %get-tuple-element.33, f32[16,512]{1,0:T(8,128)S(1)} %get-tuple-element.34, ...), kind=kLoop, calls=%fused_computation.50 | loop fusion | flops 2097152 | bytes 10616832 | tf_op jit(solution)/shard_map/mul | solution.py:37
  44.8 1.0 convolution_bitcast_fusion.2
  45.8 0.6 collective-permute-start.6
  46.5 1.5 %fusion.15 = f32[64,1,16,512]{3,0,2,1:T(8,128)S(1)} fusion(f32[64,1,16,512]{3,0,2,1:T(8,128)S(1)} %get-tuple-element.29, f32[64,1,16,512]{3,0,2,1:T(8,128)S(1)} %get-tuple-element.28, f32[64,1,16,512]{3,0,2,1:T(8,128)S(1)} %get-tuple-element.27, f32[64,1,16,512]{3,0,2,1:T(8,128)S(1)} %get-tuple-element.26, f32[64,1,16,512]{3,0,2,1:T(8,128)S(1)} %fusion.10, ...), kind=kLoop, calls=%fused_computation.31 | loop fusion | flops 2621440 | bytes 12615680 | tf_op jit(solution)/shard_map/add | solution.py:37
  48.0 3.7 %collective-permute-done.6 = f32[2,64,64]{2,1,0:T(8,128)S(1)} collective-permute-done((f32[2,64,64]{2,1,0:T(8,128)S(1)}, f32[2,64,64]{2,1,0:T(8,128)S(1)}, u32[]{:S(2)}, u32[]{:S(2)}) %collective-permute-start.6) | collective-permute-done | bytes 32800 | tf_op jit(solution)/shard_map/ppermute | solution.py:52
  51.7 1.2 %broadcast_multiply_fusion.4 = (f32[64,1,16,512]{3,0,2,1:T(8,128)S(1)}, f32[64,1,16,512]{3,0,2,1:T(8,128)S(1)}, f32[64,1,16,512]{3,0,2,1:T(8,128)S(1)}, f32[64,1,16,512]{3,0,2,1:T(8,128)S(1)}) fusion(f32[64,1,16,512]{3,0,2,1:T(8,128)S(1)} %fusion.15, f32[16,512]{1,0:T(8,128)S(1)} %get-tuple-element.37, f32[16,512]{1,0:T(8,128)S(1)} %get-tuple-element.38, ...), kind=kLoop, calls=%fused_computation.54 | loop fusion | flops 2097152 | bytes 10616832 | tf_op jit(solution)/shard_map/mul | solution.py:37
  52.9 3.7 %collective-permute-start.7 = (f32[2,64,64]{2,1,0:T(8,128)S(1)}, f32[2,64,64]{2,1,0:T(8,128)S(1)}, u32[]{:S(2)}, u32[]{:S(2)}) collective-permute-start(f32[2,64,64]{2,1,0:T(8,128)S(1)} %fusion.30), channel_id=1, source_target_pairs={{0,8},{8,0},{16,24},{24,16},{32,40},{40,32},{48,56},{56,48},{64,72... | collective-permute-start | bytes 98312 | tf_op jit(solution)/shard_map/ppermute | solution.py:52
  56.7 1.4 %fusion.19 = f32[64,1,16,512]{3,0,2,1:T(8,128)S(1)} fusion(f32[64,1,16,512]{3,0,2,1:T(8,128)S(1)} %get-tuple-element.25, f32[64,1,16,512]{3,0,2,1:T(8,128)S(1)} %get-tuple-element.24, f32[64,1,16,512]{3,0,2,1:T(8,128)S(1)} %get-tuple-element.23, f32[64,1,16,512]{3,0,2,1:T(8,128)S(1)} %get-tuple-element.22, f32[64,1,16,512]{3,0,2,1:T(8,128)S(1)} %fusion.15, ...), kind=kLoop, calls=%fused_computation.35 | loop fusion | flops 2621440 | bytes 12615680 | tf_op jit(solution)/shard_map/add | solution.py:37
  58.1 2.8 %collective-permute-start.8 = (f32[2,64,64]{2,1,0:T(8,128)S(1)}, f32[2,64,64]{2,1,0:T(8,128)S(1)}, u32[]{:S(2)}, u32[]{:S(2)}) collective-permute-start(f32[2,64,64]{2,1,0:T(8,128)S(1)} %add.122), channel_id=1, source_target_pairs={{0,16},{8,24},{16,0},{24,8},{32,48},{40,56},{48,32},{56,40},{64,80... | collective-permute-start | bytes 98312 | tf_op jit(solution)/shard_map/ppermute | solution.py:52
  61.0 2.7 %collective-permute-done.8 = f32[2,64,64]{2,1,0:T(8,128)S(1)} collective-permute-done((f32[2,64,64]{2,1,0:T(8,128)S(1)}, f32[2,64,64]{2,1,0:T(8,128)S(1)}, u32[]{:S(2)}, u32[]{:S(2)}) %collective-permute-start.8) | collective-permute-done | bytes 32800 | tf_op jit(solution)/shard_map/ppermute | solution.py:52
  63.6 3.6 %collective-permute-start.9 = (f32[2,64,64]{2,1,0:T(8,128)S(1)}, f32[2,64,64]{2,1,0:T(8,128)S(1)}, u32[]{:S(2)}, u32[]{:S(2)}) collective-permute-start(f32[2,64,64]{2,1,0:T(8,128)S(1)} %add.127), channel_id=1, source_target_pairs={{0,32},{8,40},{16,48},{24,56},{32,0},{40,8},{48,16},{56,24},{64,96... | collective-permute-start | bytes 98312 | tf_op jit(solution)/shard_map/ppermute | solution.py:52
  67.3 2.2 %collective-permute-done.9 = f32[2,64,64]{2,1,0:T(8,128)S(1)} collective-permute-done((f32[2,64,64]{2,1,0:T(8,128)S(1)}, f32[2,64,64]{2,1,0:T(8,128)S(1)}, u32[]{:S(2)}, u32[]{:S(2)}) %collective-permute-start.9) | collective-permute-done | bytes 32800 | tf_op jit(solution)/shard_map/ppermute | solution.py:52
  69.5 2.3 %collective-permute-start.10 = (f32[2,64,64]{2,1,0:T(8,128)S(1)}, f32[2,64,64]{2,1,0:T(8,128)S(1)}, u32[]{:S(2)}, u32[]{:S(2)}) collective-permute-start(f32[2,64,64]{2,1,0:T(8,128)S(1)} %add.128), channel_id=1, source_target_pairs={{0,64},{8,72},{16,80},{24,88},{32,96},{40,104},{48,112},{56,120},{... | collective-permute-start | bytes 98312 | tf_op jit(solution)/shard_map/ppermute | solution.py:52
  71.9 2.2 %collective-permute-done.10 = f32[2,64,64]{2,1,0:T(8,128)S(1)} collective-permute-done((f32[2,64,64]{2,1,0:T(8,128)S(1)}, f32[2,64,64]{2,1,0:T(8,128)S(1)}, u32[]{:S(2)}, u32[]{:S(2)}) %collective-permute-start.10) | collective-permute-done | bytes 32800 | tf_op jit(solution)/shard_map/ppermute | solution.py:52
  74.1 0.6 slice_bitcast_fusion
  74.8 0.6 collective-permute-start.11
  75.4 8.6 %shard_map.41 = f32[64,64]{1,0:T(8,128)} custom-call(f32[64,64]{1,0:T(8,128)} %get-tuple-element.45.g_ref), custom_call_target="tpu_custom_call" | custom-call | tf_op jit(solution)/shard_map/pallas_call | solution.py:82
  84.0 1.1 convolution_bitcast_fusion.1
  85.0 1.0 convolution_bitcast_fusion
  86.1 1.6 %copy.15 = f32[64,1,8,512]{3,2,1,0:T(8,128)} copy(f32[64,1,8,512]{3,0,2,1:T(8,128)S(1)} %convolution_bitcast_fusion) | data formatting | bytes 2097152 | tf_op jit(solution)/shard_map/dot_general | solution.py:138
  87.6 3.9 %all-to-all-start.1 = ((f32[64,1,8,512]{3,2,1,0:T(8,128)}), f32[64,1,8,512]{3,2,1,0:T(8,128)S(1)}, u32[]{:S(2)}, u32[]{:S(2)}) async-start(f32[64,1,8,512]{3,2,1,0:T(8,128)} %copy.15), calls=%async_computation.1 | async-start | bytes 2097152 | tf_op jit(solution)/shard_map/all_to_all | solution.py:142
  91.5 3.5 %collective-permute-start.12 = (f32[64,64]{1,0:T(8,128)S(1)}, f32[64,64]{1,0:T(8,128)S(1)}, u32[]{:S(2)}, u32[]{:S(2)}) collective-permute-start(f32[64,64]{1,0:T(8,128)S(1)} %fusion.29), channel_id=1, source_target_pairs={{0,2},{1,3},{2,0},{3,1},{4,6},{5,7},{6,4},{7,5},{8,10},{9,11},{10,... | collective-permute-start | bytes 49160 | tf_op jit(solution)/shard_map/ppermute | solution.py:52
  95.0 9.8 %collective-permute-done.12 = f32[64,64]{1,0:T(8,128)S(1)} collective-permute-done((f32[64,64]{1,0:T(8,128)S(1)}, f32[64,64]{1,0:T(8,128)S(1)}, u32[]{:S(2)}, u32[]{:S(2)}) %collective-permute-start.12) | collective-permute-done | bytes 16416 | tf_op jit(solution)/shard_map/ppermute | solution.py:52
  104.8 0.6 add_multiply_fusion
  105.5 1.1 %all-to-all-done.1 = f32[64,1,8,512]{3,2,1,0:T(8,128)S(1)} async-done(((f32[64,1,8,512]{3,2,1,0:T(8,128)}), f32[64,1,8,512]{3,2,1,0:T(8,128)S(1)}, u32[]{:S(2)}, u32[]{:S(2)}) %all-to-all-start.1) | async-done | bytes 1048608 | tf_op jit(solution)/shard_map/all_to_all | solution.py:142
  106.6 1.1 copy.30
  (16 shorter events, 0.1 us)
Async XLA Ops:
  0.6 9.4 %copy-start = (bf16[2,5,1,8,512]{4,3,2,1,0:T(8,128)(2,1)S(1)}, bf16[2,5,1,8,512]{4,3,2,1,0:T(8,128)(2,1)}, u32[]{:S(2)}) copy-start(bf16[2,5,1,8,512]{4,3,2,1,0:T(8,128)(2,1)} %param.3) | copy-start | bytes 245764
  3.0 24.2 %all-to-all-start = ((f32[8,8,8,512]{3,2,0,1:T(8,128)}), f32[8,8,8,512]{3,2,0,1:T(8,128)S(1)}, u32[]{:S(2)}, u32[]{:S(2)}) async-start(f32[8,8,8,512]{3,2,0,1:T(8,128)} %copy.11), calls=%async_computation | async-start | bytes 2097152 | tf_op jit(solution)/shard_map/all_to_all | solution.py:102
  10.0 20.8 %collective-permute-start.1 = (bf16[2,5,1,4,512]{4,3,2,1,0:T(4,128)(2,1)S(1)}, bf16[2,5,1,4,512]{4,3,2,1,0:T(4,128)(2,1)S(1)}, u32[]{:S(2)}, u32[]{:S(2)}) collective-permute-start(bf16[2,5,1,4,512]{4,3,2,1,0:T(4,128)(2,1)S(1)} %get-tuple-element.42), channel_id=1, source_target_pairs={{0,8},{8,16},{16,24},{24,32},{32,40},{40,48},{48,56},{56,64},{64,7... | collective-permute-start | bytes 122888 | tf_op jit(solution)/shard_map/ppermute | solution.py:15
  11.5 19.4 %collective-permute-start.2 = (bf16[2,5,1,4,512]{4,3,2,1,0:T(4,128)(2,1)S(1)}, bf16[2,5,1,4,512]{4,3,2,1,0:T(4,128)(2,1)S(1)}, u32[]{:S(2)}, u32[]{:S(2)}) collective-permute-start(bf16[2,5,1,4,512]{4,3,2,1,0:T(4,128)(2,1)S(1)} %get-tuple-element.43), channel_id=1, source_target_pairs={{8,0},{16,8},{24,16},{32,24},{40,32},{48,40},{56,48},{64,56},{72,6... | collective-permute-start | bytes 122888 | tf_op jit(solution)/shard_map/ppermute | solution.py:16
  27.9 8.7 %collective-permute-start.3 = (f32[64,1,4,512]{3,0,2,1:T(8,128)S(1)}, f32[64,1,4,512]{3,0,2,1:T(8,128)S(1)}, u32[]{:S(2)}, u32[]{:S(2)}) collective-permute-start(f32[64,1,4,512]{3,0,2,1:T(8,128)S(1)} %get-tuple-element.30), channel_id=1, source_target_pairs={{0,8},{8,16},{16,24},{24,32},{32,40},{40,48},{48,56},{56,64},{64,7... | collective-permute-start | bytes 1572872 | tf_op jit(solution)/shard_map/ppermute | solution.py:15
  29.6 7.0 %collective-permute-start.4 = (f32[64,1,4,512]{3,0,2,1:T(8,128)S(1)}, f32[64,1,4,512]{3,0,2,1:T(8,128)S(1)}, u32[]{:S(2)}, u32[]{:S(2)}) collective-permute-start(f32[64,1,4,512]{3,0,2,1:T(8,128)S(1)} %get-tuple-element.31), channel_id=1, source_target_pairs={{8,0},{16,8},{24,16},{32,24},{40,32},{48,40},{56,48},{64,56},{72,6... | collective-permute-start | bytes 1572872 | tf_op jit(solution)/shard_map/ppermute | solution.py:16
  32.6 4.0 %collective-permute-start = (f32[64,64]{1,0:T(8,128)S(1)}, f32[64,64]{1,0:T(8,128)S(1)}, u32[]{:S(2)}, u32[]{:S(2)}) collective-permute-start(f32[64,64]{1,0:T(8,128)S(1)} %fusion.33), channel_id=1, source_target_pairs={{0,1},{1,0},{2,3},{3,2},{4,5},{5,4},{6,7},{7,6},{8,9},{9,8},{10,11... | collective-permute-start | bytes 49160 | tf_op jit(solution)/shard_map/ppermute | solution.py:52
  38.1 5.5 %collective-permute-start.5 = (f32[64,64]{1,0:T(8,128)S(1)}, f32[64,64]{1,0:T(8,128)S(1)}, u32[]{:S(2)}, u32[]{:S(2)}) collective-permute-start(f32[64,64]{1,0:T(8,128)S(1)} %add.107), channel_id=1, source_target_pairs={{0,2},{1,3},{2,0},{3,1},{4,6},{5,7},{6,4},{7,5},{8,10},{9,11},{10,... | collective-permute-start | bytes 49160 | tf_op jit(solution)/shard_map/ppermute | solution.py:52
  45.8 5.8 %collective-permute-start.6 = (f32[2,64,64]{2,1,0:T(8,128)S(1)}, f32[2,64,64]{2,1,0:T(8,128)S(1)}, u32[]{:S(2)}, u32[]{:S(2)}) collective-permute-start(f32[2,64,64]{2,1,0:T(8,128)S(1)} %pad_maximum_fusion.1), channel_id=1, source_target_pairs={{0,4},{1,5},{2,6},{3,7},{4,0},{5,1},{6,2},{7,3},{8,12},{9,13},{10,... | collective-permute-start | bytes 98312 | tf_op jit(solution)/shard_map/ppermute | solution.py:52
  52.9 5.2 %collective-permute-start.7 = (f32[2,64,64]{2,1,0:T(8,128)S(1)}, f32[2,64,64]{2,1,0:T(8,128)S(1)}, u32[]{:S(2)}, u32[]{:S(2)}) collective-permute-start(f32[2,64,64]{2,1,0:T(8,128)S(1)} %fusion.30), channel_id=1, source_target_pairs={{0,8},{8,0},{16,24},{24,16},{32,40},{40,32},{48,56},{56,48},{64,72... | collective-permute-start | bytes 98312 | tf_op jit(solution)/shard_map/ppermute | solution.py:52
  58.1 5.5 %collective-permute-start.8 = (f32[2,64,64]{2,1,0:T(8,128)S(1)}, f32[2,64,64]{2,1,0:T(8,128)S(1)}, u32[]{:S(2)}, u32[]{:S(2)}) collective-permute-start(f32[2,64,64]{2,1,0:T(8,128)S(1)} %add.122), channel_id=1, source_target_pairs={{0,16},{8,24},{16,0},{24,8},{32,48},{40,56},{48,32},{56,40},{64,80... | collective-permute-start | bytes 98312 | tf_op jit(solution)/shard_map/ppermute | solution.py:52
  63.6 5.9 %collective-permute-start.9 = (f32[2,64,64]{2,1,0:T(8,128)S(1)}, f32[2,64,64]{2,1,0:T(8,128)S(1)}, u32[]{:S(2)}, u32[]{:S(2)}) collective-permute-start(f32[2,64,64]{2,1,0:T(8,128)S(1)} %add.127), channel_id=1, source_target_pairs={{0,32},{8,40},{16,48},{24,56},{32,0},{40,8},{48,16},{56,24},{64,96... | collective-permute-start | bytes 98312 | tf_op jit(solution)/shard_map/ppermute | solution.py:52
  69.5 4.6 %collective-permute-start.10 = (f32[2,64,64]{2,1,0:T(8,128)S(1)}, f32[2,64,64]{2,1,0:T(8,128)S(1)}, u32[]{:S(2)}, u32[]{:S(2)}) collective-permute-start(f32[2,64,64]{2,1,0:T(8,128)S(1)} %add.128), channel_id=1, source_target_pairs={{0,64},{8,72},{16,80},{24,88},{32,96},{40,104},{48,112},{56,120},{... | collective-permute-start | bytes 98312 | tf_op jit(solution)/shard_map/ppermute | solution.py:52
  74.8 9.2 %collective-permute-start.11 = (f32[64,64]{1,0:T(8,128)S(1)}, f32[64,64]{1,0:T(8,128)S(1)}, u32[]{:S(2)}, u32[]{:S(2)}) collective-permute-start(f32[64,64]{1,0:T(8,128)S(1)} %get-tuple-element.44), channel_id=1, source_target_pairs={{0,1},{1,0},{2,3},{3,2},{4,5},{5,4},{6,7},{7,6},{8,9},{9,8},{10,11... | collective-permute-start | bytes 49160 | tf_op jit(solution)/shard_map/ppermute | solution.py:52
  87.6 18.9 %all-to-all-start.1 = ((f32[64,1,8,512]{3,2,1,0:T(8,128)}), f32[64,1,8,512]{3,2,1,0:T(8,128)S(1)}, u32[]{:S(2)}, u32[]{:S(2)}) async-start(f32[64,1,8,512]{3,2,1,0:T(8,128)} %copy.15), calls=%async_computation.1 | async-start | bytes 2097152 | tf_op jit(solution)/shard_map/all_to_all | solution.py:142
  91.5 13.3 %collective-permute-start.12 = (f32[64,64]{1,0:T(8,128)S(1)}, f32[64,64]{1,0:T(8,128)S(1)}, u32[]{:S(2)}, u32[]{:S(2)}) collective-permute-start(f32[64,64]{1,0:T(8,128)S(1)} %fusion.29), channel_id=1, source_target_pairs={{0,2},{1,3},{2,0},{3,1},{4,6},{5,7},{6,4},{7,5},{8,10},{9,11},{10,... | collective-permute-start | bytes 49160 | tf_op jit(solution)/shard_map/ppermute | solution.py:52

commit v11 on v9

--- a/solution.py
+++ b/solution.py
@@ -131,7 +131,8 @@
     both = jnp.stack([gram, cross])
     cross_bits = list(done)
     for step in reversed(range(STEPS)):
-        both, field = tick(both, adjoint_step(field, coeffs[step]))
+        field = adjoint_step(field, coeffs[step])
+    both, field = tick(both, field)
     while pending:
         both = exchange(both, *pending.pop(0))
     gram, cross = both[0], both[1]

time: 108 us -> 108 us (level)
    mul x0 -> x2, other arithmetic: none -> 2.04 us  [the longest x1 1.23 us: adjoint_step(): coef[1] * field]
    add x2 -> x1, other arithmetic: 2.94 us -> 1.45 us  [adjoint_step(): result + shifted(coef[3] * field, 1, 3) + shifted(coef[4] * field, -1, 3)]
    mul x2 -> x1, other arithmetic: 2.47 us -> 1.7 us  [adjoint_step(): coef[4] * field]
  transfers between devices with their start and end apart: 15 -> 15, of which waited for: 9 -> 10; matrix products, arithmetic and copies ran while one was open for 7% -> 5% of each run, Pallas kernels for 8% -> 8%
where the time goes in v11:
time: 108 us; the launch traced here: 107 us
  waiting for transfers between devices  42.6 us (39%)
  starting transfers between devices  36.1 us (33%)
  other arithmetic  9.39 us (9%)
  Pallas kernels  8.15 us (8%)
  local copies, waits for them, and re-layouts  6.31 us (6%)
  matrix products  4.03 us (4%)
    ppermute x9, waiting for transfers between devices, exchange(): return x + lax.ppermute(x, axis, [(i, i ^ bit) for i in range(count)])  27.1 us
    ppermute x9, starting transfers between devices, exchange(): return x + lax.ppermute(x, axis, [(i, i ^ bit) for i in range(count)])  19.5 us
    all_to_all x1, waiting for transfers between devices, body(): v = lax.all_to_all(perturbations, 'mem', 1, 0, tiled=True)  14.4 us
    pallas_call x1, Pallas kernels, lower_inverse(): pl.pallas_call(chol_inv_kernel, out_shape=jax.ShapeDtypeStruct((n, n), jn...  8.15 us
    all_to_all x1, starting transfers between devices, body(): v = lax.all_to_all(perturbations, 'mem', 1, 0, tiled=True)  7.04 us
    all_to_all x1, starting transfers between devices, body(): ritz = lax.all_to_all(ritz.reshape(v.shape), 'mem', 0, 1, tiled=True)  3.88 us
    ppermute x2, starting transfers between devices, halo(): lax.ppermute(lax.slice_in_dim(block, size - width, size, axis=dim), 'dom'...  3.12 us
    unnamed x4, local copies, waits for them, and re-layouts  2.93 us
  transfers between devices with their start and end apart: 15, of which 10 were waited for; matrix products, arithmetic and copies ran while one was open for 5% of the time, Pallas kernels for 8%

profile of v11, /device:TPU:0, one launch (start us, length us, event | category | flops | bytes accessed | tf_op | source)
XLA Modules:
  0.0 107.5 jit_solution(18162642429257201381)
XLA Ops:
  0.6 2.3 %copy.11 = f32[8,8,8,512]{3,2,0,1:T(8,128)} copy(f32[8,8,8,512]{3,2,1,0:T(8,128)} %param.2) | data formatting | bytes 2097152 | tf_op args[0]
  3.0 7.0 %all-to-all-start = ((f32[8,8,8,512]{3,2,0,1:T(8,128)}), f32[8,8,8,512]{3,2,0,1:T(8,128)S(1)}, u32[]{:S(2)}, u32[]{:S(2)}) async-start(f32[8,8,8,512]{3,2,0,1:T(8,128)} %copy.11), calls=%async_computation | async-start | bytes 2097152 | tf_op jit(solution)/shard_map/all_to_all | solution.py:105
  10.0 1.5 %collective-permute-start.1 = (bf16[2,5,1,4,512]{4,3,2,1,0:T(4,128)(2,1)S(1)}, bf16[2,5,1,4,512]{4,3,2,1,0:T(4,128)(2,1)S(1)}, u32[]{:S(2)}, u32[]{:S(2)}) collective-permute-start(bf16[2,5,1,4,512]{4,3,2,1,0:T(4,128)(2,1)S(1)} %get-tuple-element.39), channel_id=1, source_target_pairs={{0,8},{8,16},{16,24},{24,32},{32,40},{40,48},{48,56},{56,64},{64,7... | collective-permute-start | bytes 122888 | tf_op jit(solution)/shard_map/ppermute | solution.py:16
  11.5 1.3 %collective-permute-start.2 = (bf16[2,5,1,4,512]{4,3,2,1,0:T(4,128)(2,1)S(1)}, bf16[2,5,1,4,512]{4,3,2,1,0:T(4,128)(2,1)S(1)}, u32[]{:S(2)}, u32[]{:S(2)}) collective-permute-start(bf16[2,5,1,4,512]{4,3,2,1,0:T(4,128)(2,1)S(1)} %get-tuple-element.40), channel_id=1, source_target_pairs={{8,0},{16,8},{24,16},{32,24},{40,32},{48,40},{56,48},{64,56},{72,6... | collective-permute-start | bytes 122888 | tf_op jit(solution)/shard_map/ppermute | solution.py:17
  12.8 14.4 %all-to-all-done = f32[8,8,8,512]{3,2,0,1:T(8,128)S(1)} async-done(((f32[8,8,8,512]{3,2,0,1:T(8,128)}), f32[8,8,8,512]{3,2,0,1:T(8,128)S(1)}, u32[]{:S(2)}, u32[]{:S(2)}) %all-to-all-start) | async-done | bytes 1048608 | tf_op jit(solution)/shard_map/all_to_all | solution.py:105
  27.2 0.6 copy.31
  27.8 0.1 fusion.32
  27.9 1.7 %collective-permute-start.3 = (f32[64,1,4,512]{3,0,2,1:T(8,128)S(1)}, f32[64,1,4,512]{3,0,2,1:T(8,128)S(1)}, u32[]{:S(2)}, u32[]{:S(2)}) collective-permute-start(f32[64,1,4,512]{3,0,2,1:T(8,128)S(1)} %get-tuple-element.27), channel_id=1, source_target_pairs={{0,8},{8,16},{16,24},{24,32},{32,40},{40,48},{48,56},{56,64},{64,7... | collective-permute-start | bytes 1572872 | tf_op jit(solution)/shard_map/ppermute | solution.py:16
  29.6 1.3 %collective-permute-start.4 = (f32[64,1,4,512]{3,0,2,1:T(8,128)S(1)}, f32[64,1,4,512]{3,0,2,1:T(8,128)S(1)}, u32[]{:S(2)}, u32[]{:S(2)}) collective-permute-start(f32[64,1,4,512]{3,0,2,1:T(8,128)S(1)} %get-tuple-element.28), channel_id=1, source_target_pairs={{8,0},{16,8},{24,16},{32,24},{40,32},{48,40},{56,48},{64,56},{72,6... | collective-permute-start | bytes 1572872 | tf_op jit(solution)/shard_map/ppermute | solution.py:17
  30.9 0.0 collective-permute-done.1
  30.9 0.0 collective-permute-done.2
  30.9 0.1 maximum_convert_fusion
  31.0 0.6 copy.18
  31.6 1.0 fusion.34
  32.6 0.6 collective-permute-start
  33.2 3.4 %collective-permute-done = f32[64,64]{1,0:T(8,128)S(1)} collective-permute-done((f32[64,64]{1,0:T(8,128)S(1)}, f32[64,64]{1,0:T(8,128)S(1)}, u32[]{:S(2)}, u32[]{:S(2)}) %collective-permute-start) | collective-permute-done | bytes 16416 | tf_op jit(solution)/shard_map/ppermute | solution.py:53
  36.6 0.2 pad_maximum_fusion
  36.8 1.3 %fusion.4 = f32[64,1,16,512]{3,0,2,1:T(8,128)S(1)} fusion(f32[64,1,16,512]{3,0,2,1:T(8,128)S(1)} %pad_maximum_fusion, f32[16,512]{1,0:T(8,128)S(1)} %get-tuple-element.34, f32[16,512]{1,0:T(8,128)S(1)} %get-tuple-element.35, f32[16,512]{1,0:T(8,128)S(1)} %get-tuple-element.36, f32[16,512]{1,0:T(8,128)S(1)} %get-tuple-element.37, ...), kind=kLoop, calls=%fused_computation.20 | loop fusion | flops 4718592 | bytes 4358144 | tf_op jit(solution)/shard_map/add | solution.py:33
  38.1 1.2 %collective-permute-start.5 = (f32[64,64]{1,0:T(8,128)S(1)}, f32[64,64]{1,0:T(8,128)S(1)}, u32[]{:S(2)}, u32[]{:S(2)}) collective-permute-start(f32[64,64]{1,0:T(8,128)S(1)} %add.107), channel_id=1, source_target_pairs={{0,2},{1,3},{2,0},{3,1},{4,6},{5,7},{6,4},{7,5},{8,10},{9,11},{10,... | collective-permute-start | bytes 49160 | tf_op jit(solution)/shard_map/ppermute | solution.py:53
  39.3 1.3 %fusion.10 = f32[64,1,16,512]{3,0,2,1:T(8,128)S(1)} fusion(f32[64,1,16,512]{3,0,2,1:T(8,128)S(1)} %fusion.4, f32[16,512]{1,0:T(8,128)S(1)} %get-tuple-element.30, f32[16,512]{1,0:T(8,128)S(1)} %get-tuple-element.31, f32[16,512]{1,0:T(8,128)S(1)} %get-tuple-element.32, f32[16,512]{1,0:T(8,128)S(1)} %get-tuple-element.33, f32[16,512]{1,0:T(8,128)S(1)} %get-tuple-element.29), kind=kLoop, calls=%fused_computation.26 | loop fusion | flops 4718592 | bytes 4358144 | tf_op jit(solution)/shard_map/add | solution.py:33
  40.6 3.0 %collective-permute-done.5 = f32[64,64]{1,0:T(8,128)S(1)} collective-permute-done((f32[64,64]{1,0:T(8,128)S(1)}, f32[64,64]{1,0:T(8,128)S(1)}, u32[]{:S(2)}, u32[]{:S(2)}) %collective-permute-start.5) | collective-permute-done | bytes 16416 | tf_op jit(solution)/shard_map/ppermute | solution.py:53
  43.6 1.2 %broadcast_multiply_fusion.3 = (f32[64,1,16,512]{3,0,2,1:T(8,128)S(1)}, f32[64,1,16,512]{3,0,2,1:T(8,128)S(1)}, f32[64,1,16,512]{3,0,2,1:T(8,128)S(1)}, f32[64,1,16,512]{3,0,2,1:T(8,128)S(1)}) fusion(f32[64,1,16,512]{3,0,2,1:T(8,128)S(1)} %fusion.10, f32[16,512]{1,0:T(8,128)S(1)} %get-tuple-element.33, f32[16,512]{1,0:T(8,128)S(1)} %get-tuple-element.30, ...), kind=kLoop, calls=%fused_computation.53 | loop fusion | flops 2097152 | bytes 10616832 | tf_op jit(solution)/shard_map/mul | solution.py:37
  44.8 1.0 convolution_bitcast_fusion.2
  45.8 1.7 %broadcast_multiply_fusion.4 = (f32[64,1,16,512]{3,0,2,1:T(8,128)S(1)}, f32[64,1,16,512]{3,0,2,1:T(8,128)S(1)}) fusion(f32[16,512]{1,0:T(8,128)S(1)} %get-tuple-element.34, f32[64,1,16,512]{3,0,2,1:T(8,128)S(1)} %get-tuple-element.24, f32[64,1,16,512]{3,0,2,1:T(8,128)S(1)} %get-tuple-element.25, f32[64,1,16,512]{3,0,2,1:T(8,128)S(1)} %get-tuple-element.26, ...), kind=kLoop, calls=%fused_computation.54 | loop fusion | flops 3145728 | bytes 14745600 | tf_op jit(solution)/shard_map/mul | solution.py:38
  47.5 0.8 broadcast_multiply_fusion.5
  48.4 0.6 collective-permute-start.6
  49.0 1.4 %fusion.19 = f32[64,1,16,512]{3,0,2,1:T(8,128)S(1)} fusion(f32[64,1,16,512]{3,0,2,1:T(8,128)S(1)} %get-tuple-element.22, f32[64,1,16,512]{3,0,2,1:T(8,128)S(1)} %get-tuple-element.21, f32[64,1,16,512]{3,0,2,1:T(8,128)S(1)} %get-tuple-element.20, f32[64,1,16,512]{3,0,2,1:T(8,128)S(1)} %get-tuple-element.18, f32[64,1,16,512]{3,0,2,1:T(8,128)S(1)} %get-tuple-element.19, ...), kind=kLoop, calls=%fused_computation.35 | loop fusion | flops 2621440 | bytes 12615680 | tf_op jit(solution)/shard_map/add | solution.py:38
  50.5 3.8 %collective-permute-done.6 = f32[2,64,64]{2,1,0:T(8,128)S(1)} collective-permute-done((f32[2,64,64]{2,1,0:T(8,128)S(1)}, f32[2,64,64]{2,1,0:T(8,128)S(1)}, u32[]{:S(2)}, u32[]{:S(2)}) %collective-permute-start.6) | collective-permute-done | bytes 32800 | tf_op jit(solution)/shard_map/ppermute | solution.py:53
  54.2 3.7 %collective-permute-start.7 = (f32[2,64,64]{2,1,0:T(8,128)S(1)}, f32[2,64,64]{2,1,0:T(8,128)S(1)}, u32[]{:S(2)}, u32[]{:S(2)}) collective-permute-start(f32[2,64,64]{2,1,0:T(8,128)S(1)} %fusion.30), channel_id=1, source_target_pairs={{0,8},{8,0},{16,24},{24,16},{32,40},{40,32},{48,56},{56,48},{64,72... | collective-permute-start | bytes 98312 | tf_op jit(solution)/shard_map/ppermute | solution.py:53
  58.0 0.9 collective-permute-done.7
  58.9 3.1 %collective-permute-start.8 = (f32[2,64,64]{2,1,0:T(8,128)S(1)}, f32[2,64,64]{2,1,0:T(8,128)S(1)}, u32[]{:S(2)}, u32[]{:S(2)}) collective-permute-start(f32[2,64,64]{2,1,0:T(8,128)S(1)} %add.126), channel_id=1, source_target_pairs={{0,16},{8,24},{16,0},{24,8},{32,48},{40,56},{48,32},{56,40},{64,80... | collective-permute-start | bytes 98312 | tf_op jit(solution)/shard_map/ppermute | solution.py:53
  62.0 2.4 %collective-permute-done.8 = f32[2,64,64]{2,1,0:T(8,128)S(1)} collective-permute-done((f32[2,64,64]{2,1,0:T(8,128)S(1)}, f32[2,64,64]{2,1,0:T(8,128)S(1)}, u32[]{:S(2)}, u32[]{:S(2)}) %collective-permute-start.8) | collective-permute-done | bytes 32800 | tf_op jit(solution)/shard_map/ppermute | solution.py:53
  64.4 3.8 %collective-permute-start.9 = (f32[2,64,64]{2,1,0:T(8,128)S(1)}, f32[2,64,64]{2,1,0:T(8,128)S(1)}, u32[]{:S(2)}, u32[]{:S(2)}) collective-permute-start(f32[2,64,64]{2,1,0:T(8,128)S(1)} %add.127), channel_id=1, source_target_pairs={{0,32},{8,40},{16,48},{24,56},{32,0},{40,8},{48,16},{56,24},{64,96... | collective-permute-start | bytes 98312 | tf_op jit(solution)/shard_map/ppermute | solution.py:53
  68.1 2.2 %collective-permute-done.9 = f32[2,64,64]{2,1,0:T(8,128)S(1)} collective-permute-done((f32[2,64,64]{2,1,0:T(8,128)S(1)}, f32[2,64,64]{2,1,0:T(8,128)S(1)}, u32[]{:S(2)}, u32[]{:S(2)}) %collective-permute-start.9) | collective-permute-done | bytes 32800 | tf_op jit(solution)/shard_map/ppermute | solution.py:53
  70.4 2.3 %collective-permute-start.10 = (f32[2,64,64]{2,1,0:T(8,128)S(1)}, f32[2,64,64]{2,1,0:T(8,128)S(1)}, u32[]{:S(2)}, u32[]{:S(2)}) collective-permute-start(f32[2,64,64]{2,1,0:T(8,128)S(1)} %add.128), channel_id=1, source_target_pairs={{0,64},{8,72},{16,80},{24,88},{32,96},{40,104},{48,112},{56,120},{... | collective-permute-start | bytes 98312 | tf_op jit(solution)/shard_map/ppermute | solution.py:53
  72.7 2.2 %collective-permute-done.10 = f32[2,64,64]{2,1,0:T(8,128)S(1)} collective-permute-done((f32[2,64,64]{2,1,0:T(8,128)S(1)}, f32[2,64,64]{2,1,0:T(8,128)S(1)}, u32[]{:S(2)}, u32[]{:S(2)}) %collective-permute-start.10) | collective-permute-done | bytes 32800 | tf_op jit(solution)/shard_map/ppermute | solution.py:53
  75.0 0.6 slice_bitcast_fusion
  75.6 0.6 collective-permute-start.11
  76.2 8.2 %shard_map.41 = f32[64,64]{1,0:T(8,128)} custom-call(f32[64,64]{1,0:T(8,128)} %get-tuple-element.42.g_ref), custom_call_target="tpu_custom_call" | custom-call | tf_op jit(solution)/shard_map/pallas_call | solution.py:84
  84.4 1.1 convolution_bitcast_fusion.1
  85.5 1.0 convolution_bitcast_fusion
  86.5 1.6 %copy.15 = f32[64,1,8,512]{3,2,1,0:T(8,128)} copy(f32[64,1,8,512]{3,0,2,1:T(8,128)S(1)} %convolution_bitcast_fusion) | data formatting | bytes 2097152 | tf_op jit(solution)/shard_map/dot_general | solution.py:142
  88.1 3.9 %all-to-all-start.1 = ((f32[64,1,8,512]{3,2,1,0:T(8,128)}), f32[64,1,8,512]{3,2,1,0:T(8,128)S(1)}, u32[]{:S(2)}, u32[]{:S(2)}) async-start(f32[64,1,8,512]{3,2,1,0:T(8,128)} %copy.15), calls=%async_computation.1 | async-start | bytes 2097152 | tf_op jit(solution)/shard_map/all_to_all | solution.py:146
  92.0 3.5 %collective-permute-start.12 = (f32[64,64]{1,0:T(8,128)S(1)}, f32[64,64]{1,0:T(8,128)S(1)}, u32[]{:S(2)}, u32[]{:S(2)}) collective-permute-start(f32[64,64]{1,0:T(8,128)S(1)} %fusion.29), channel_id=1, source_target_pairs={{0,2},{1,3},{2,0},{3,1},{4,6},{5,7},{6,4},{7,5},{8,10},{9,11},{10,... | collective-permute-start | bytes 49160 | tf_op jit(solution)/shard_map/ppermute | solution.py:53
  95.5 9.2 %collective-permute-done.12 = f32[64,64]{1,0:T(8,128)S(1)} collective-permute-done((f32[64,64]{1,0:T(8,128)S(1)}, f32[64,64]{1,0:T(8,128)S(1)}, u32[]{:S(2)}, u32[]{:S(2)}) %collective-permute-start.12) | collective-permute-done | bytes 16416 | tf_op jit(solution)/shard_map/ppermute | solution.py:53
  104.7 0.6 add_multiply_fusion
  105.3 1.1 %all-to-all-done.1 = f32[64,1,8,512]{3,2,1,0:T(8,128)S(1)} async-done(((f32[64,1,8,512]{3,2,1,0:T(8,128)}), f32[64,1,8,512]{3,2,1,0:T(8,128)S(1)}, u32[]{:S(2)}, u32[]{:S(2)}) %all-to-all-start.1) | async-done | bytes 1048608 | tf_op jit(solution)/shard_map/all_to_all | solution.py:146
  106.4 1.1 copy.30
  (16 shorter events, 0.1 us)
Async XLA Ops:
  0.6 9.4 %copy-start = (bf16[2,5,1,8,512]{4,3,2,1,0:T(8,128)(2,1)S(1)}, bf16[2,5,1,8,512]{4,3,2,1,0:T(8,128)(2,1)}, u32[]{:S(2)}) copy-start(bf16[2,5,1,8,512]{4,3,2,1,0:T(8,128)(2,1)} %param.3) | copy-start | bytes 245764
  3.0 24.2 %all-to-all-start = ((f32[8,8,8,512]{3,2,0,1:T(8,128)}), f32[8,8,8,512]{3,2,0,1:T(8,128)S(1)}, u32[]{:S(2)}, u32[]{:S(2)}) async-start(f32[8,8,8,512]{3,2,0,1:T(8,128)} %copy.11), calls=%async_computation | async-start | bytes 2097152 | tf_op jit(solution)/shard_map/all_to_all | solution.py:105
  10.0 20.8 %collective-permute-start.1 = (bf16[2,5,1,4,512]{4,3,2,1,0:T(4,128)(2,1)S(1)}, bf16[2,5,1,4,512]{4,3,2,1,0:T(4,128)(2,1)S(1)}, u32[]{:S(2)}, u32[]{:S(2)}) collective-permute-start(bf16[2,5,1,4,512]{4,3,2,1,0:T(4,128)(2,1)S(1)} %get-tuple-element.39), channel_id=1, source_target_pairs={{0,8},{8,16},{16,24},{24,32},{32,40},{40,48},{48,56},{56,64},{64,7... | collective-permute-start | bytes 122888 | tf_op jit(solution)/shard_map/ppermute | solution.py:16
  11.5 19.4 %collective-permute-start.2 = (bf16[2,5,1,4,512]{4,3,2,1,0:T(4,128)(2,1)S(1)}, bf16[2,5,1,4,512]{4,3,2,1,0:T(4,128)(2,1)S(1)}, u32[]{:S(2)}, u32[]{:S(2)}) collective-permute-start(bf16[2,5,1,4,512]{4,3,2,1,0:T(4,128)(2,1)S(1)} %get-tuple-element.40), channel_id=1, source_target_pairs={{8,0},{16,8},{24,16},{32,24},{40,32},{48,40},{56,48},{64,56},{72,6... | collective-permute-start | bytes 122888 | tf_op jit(solution)/shard_map/ppermute | solution.py:17
  27.9 8.7 %collective-permute-start.3 = (f32[64,1,4,512]{3,0,2,1:T(8,128)S(1)}, f32[64,1,4,512]{3,0,2,1:T(8,128)S(1)}, u32[]{:S(2)}, u32[]{:S(2)}) collective-permute-start(f32[64,1,4,512]{3,0,2,1:T(8,128)S(1)} %get-tuple-element.27), channel_id=1, source_target_pairs={{0,8},{8,16},{16,24},{24,32},{32,40},{40,48},{48,56},{56,64},{64,7... | collective-permute-start | bytes 1572872 | tf_op jit(solution)/shard_map/ppermute | solution.py:16
  29.6 7.0 %collective-permute-start.4 = (f32[64,1,4,512]{3,0,2,1:T(8,128)S(1)}, f32[64,1,4,512]{3,0,2,1:T(8,128)S(1)}, u32[]{:S(2)}, u32[]{:S(2)}) collective-permute-start(f32[64,1,4,512]{3,0,2,1:T(8,128)S(1)} %get-tuple-element.28), channel_id=1, source_target_pairs={{8,0},{16,8},{24,16},{32,24},{40,32},{48,40},{56,48},{64,56},{72,6... | collective-permute-start | bytes 1572872 | tf_op jit(solution)/shard_map/ppermute | solution.py:17
  32.6 4.0 %collective-permute-start = (f32[64,64]{1,0:T(8,128)S(1)}, f32[64,64]{1,0:T(8,128)S(1)}, u32[]{:S(2)}, u32[]{:S(2)}) collective-permute-start(f32[64,64]{1,0:T(8,128)S(1)} %fusion.34), channel_id=1, source_target_pairs={{0,1},{1,0},{2,3},{3,2},{4,5},{5,4},{6,7},{7,6},{8,9},{9,8},{10,11... | collective-permute-start | bytes 49160 | tf_op jit(solution)/shard_map/ppermute | solution.py:53
  38.1 5.5 %collective-permute-start.5 = (f32[64,64]{1,0:T(8,128)S(1)}, f32[64,64]{1,0:T(8,128)S(1)}, u32[]{:S(2)}, u32[]{:S(2)}) collective-permute-start(f32[64,64]{1,0:T(8,128)S(1)} %add.107), channel_id=1, source_target_pairs={{0,2},{1,3},{2,0},{3,1},{4,6},{5,7},{6,4},{7,5},{8,10},{9,11},{10,... | collective-permute-start | bytes 49160 | tf_op jit(solution)/shard_map/ppermute | solution.py:53
  48.4 5.8 %collective-permute-start.6 = (f32[2,64,64]{2,1,0:T(8,128)S(1)}, f32[2,64,64]{2,1,0:T(8,128)S(1)}, u32[]{:S(2)}, u32[]{:S(2)}) collective-permute-start(f32[2,64,64]{2,1,0:T(8,128)S(1)} %pad_maximum_fusion.1), channel_id=1, source_target_pairs={{0,4},{1,5},{2,6},{3,7},{4,0},{5,1},{6,2},{7,3},{8,12},{9,13},{10,... | collective-permute-start | bytes 98312 | tf_op jit(solution)/shard_map/ppermute | solution.py:53
  54.2 4.6 %collective-permute-start.7 = (f32[2,64,64]{2,1,0:T(8,128)S(1)}, f32[2,64,64]{2,1,0:T(8,128)S(1)}, u32[]{:S(2)}, u32[]{:S(2)}) collective-permute-start(f32[2,64,64]{2,1,0:T(8,128)S(1)} %fusion.30), channel_id=1, source_target_pairs={{0,8},{8,0},{16,24},{24,16},{32,40},{40,32},{48,56},{56,48},{64,72... | collective-permute-start | bytes 98312 | tf_op jit(solution)/shard_map/ppermute | solution.py:53
  58.9 5.5 %collective-permute-start.8 = (f32[2,64,64]{2,1,0:T(8,128)S(1)}, f32[2,64,64]{2,1,0:T(8,128)S(1)}, u32[]{:S(2)}, u32[]{:S(2)}) collective-permute-start(f32[2,64,64]{2,1,0:T(8,128)S(1)} %add.126), channel_id=1, source_target_pairs={{0,16},{8,24},{16,0},{24,8},{32,48},{40,56},{48,32},{56,40},{64,80... | collective-permute-start | bytes 98312 | tf_op jit(solution)/shard_map/ppermute | solution.py:53
  64.4 6.0 %collective-permute-start.9 = (f32[2,64,64]{2,1,0:T(8,128)S(1)}, f32[2,64,64]{2,1,0:T(8,128)S(1)}, u32[]{:S(2)}, u32[]{:S(2)}) collective-permute-start(f32[2,64,64]{2,1,0:T(8,128)S(1)} %add.127), channel_id=1, source_target_pairs={{0,32},{8,40},{16,48},{24,56},{32,0},{40,8},{48,16},{56,24},{64,96... | collective-permute-start | bytes 98312 | tf_op jit(solution)/shard_map/ppermute | solution.py:53
  70.4 4.6 %collective-permute-start.10 = (f32[2,64,64]{2,1,0:T(8,128)S(1)}, f32[2,64,64]{2,1,0:T(8,128)S(1)}, u32[]{:S(2)}, u32[]{:S(2)}) collective-permute-start(f32[2,64,64]{2,1,0:T(8,128)S(1)} %add.128), channel_id=1, source_target_pairs={{0,64},{8,72},{16,80},{24,88},{32,96},{40,104},{48,112},{56,120},{... | collective-permute-start | bytes 98312 | tf_op jit(solution)/shard_map/ppermute | solution.py:53
  75.6 8.8 %collective-permute-start.11 = (f32[64,64]{1,0:T(8,128)S(1)}, f32[64,64]{1,0:T(8,128)S(1)}, u32[]{:S(2)}, u32[]{:S(2)}) collective-permute-start(f32[64,64]{1,0:T(8,128)S(1)} %get-tuple-element.41), channel_id=1, source_target_pairs={{0,1},{1,0},{2,3},{3,2},{4,5},{5,4},{6,7},{7,6},{8,9},{9,8},{10,11... | collective-permute-start | bytes 49160 | tf_op jit(solution)/shard_map/ppermute | solution.py:53
  88.1 18.3 %all-to-all-start.1 = ((f32[64,1,8,512]{3,2,1,0:T(8,128)}), f32[64,1,8,512]{3,2,1,0:T(8,128)S(1)}, u32[]{:S(2)}, u32[]{:S(2)}) async-start(f32[64,1,8,512]{3,2,1,0:T(8,128)} %copy.15), calls=%async_computation.1 | async-start | bytes 2097152 | tf_op jit(solution)/shard_map/all_to_all | solution.py:146
  92.0 12.8 %collective-permute-start.12 = (f32[64,64]{1,0:T(8,128)S(1)}, f32[64,64]{1,0:T(8,128)S(1)}, u32[]{:S(2)}, u32[]{:S(2)}) collective-permute-start(f32[64,64]{1,0:T(8,128)S(1)} %fusion.29), channel_id=1, source_target_pairs={{0,2},{1,3},{2,0},{3,1},{4,6},{5,7},{6,4},{7,5},{8,10},{9,11},{10,... | collective-permute-start | bytes 49160 | tf_op jit(solution)/shard_map/ppermute | solution.py:53

commit v12 on v9

--- a/solution.py
+++ b/solution.py
@@ -111,8 +111,7 @@
         * lax.axis_size("dom")
     )
     hi = lax.Precision.HIGHEST
-    flat_v = v.reshape(members, -1)
-    gram = jnp.dot(flat_v, flat_v.T, precision=hi)
+    gram = jnp.einsum("alij,blij->ab", v, v, precision=hi)
     pending = butterfly_bits()
     done = []
 
@@ -126,8 +125,8 @@
     field = halo(v, width, 2)
     for step in range(STEPS):
         gram, field = tick(gram, forward_step(field, coeffs[step]))
-    flat_z = field[:, :, width : width + rows, :].reshape(members, -1)
-    cross = jnp.dot(flat_z, flat_z.T, precision=hi)
+    own = field[:, :, width : width + rows, :]
+    cross = jnp.einsum("alij,blij->ab", own, own, precision=hi)
     both = jnp.stack([gram, cross])
     cross_bits = list(done)
     for step in reversed(range(STEPS)):
@@ -136,13 +135,12 @@
         both = exchange(both, *pending.pop(0))
     gram, cross = both[0], both[1]
     field = field[:, :, width : width + rows, :]
-    flat_w = field.reshape(members, -1)
     inverse, cross = invert_beside(gram / ncells_all, cross, cross_bits)
-    ritz = jnp.dot(inverse, flat_w, precision=hi)
+    ritz = jnp.einsum("ab,blij->alij", inverse, field, precision=hi)
     for axis, bit in cross_bits:
         cross = exchange(cross, axis, bit)
     projected = cross / ncells_all
-    ritz = lax.all_to_all(ritz.reshape(v.shape), "mem", 0, 1, tiled=True)
+    ritz = lax.all_to_all(ritz, "mem", 0, 1, tiled=True)
     return (ritz, projected)
 
 

time: 108 us -> 108 us (level)
  matrix products: 4.02 us -> 5.15 us
    dot_general x3, matrix products: 2.96 us -> 4.09 us  [the longest x1 2.1 us: body(): gram = jnp.einsum('alij,blij->ab', v, v, precision=hi)]
    unnamed x4 -> x3, local copies, waits for them, and re-layouts: 2.93 us -> 2.32 us
where the time goes in v12:
time: 108 us; the launch traced here: 107 us
  waiting for transfers between devices  42.5 us (39%)
  starting transfers between devices  35.3 us (33%)
  other arithmetic  9.57 us (9%)
  Pallas kernels  8.15 us (8%)
  local copies, waits for them, and re-layouts  5.7 us (5%)
  matrix products  5.15 us (5%)
    ppermute x9, waiting for transfers between devices, exchange(): return x + lax.ppermute(x, axis, [(i, i ^ bit) for i in range(count)])  27 us
    ppermute x9, starting transfers between devices, exchange(): return x + lax.ppermute(x, axis, [(i, i ^ bit) for i in range(count)])  18.7 us
    all_to_all x1, waiting for transfers between devices, body(): v = lax.all_to_all(perturbations, 'mem', 1, 0, tiled=True)  14.4 us
    pallas_call x1, Pallas kernels, lower_inverse(): pl.pallas_call(chol_inv_kernel, out_shape=jax.ShapeDtypeStruct((n, n), jn...  8.15 us
    all_to_all x1, starting transfers between devices, body(): v = lax.all_to_all(perturbations, 'mem', 1, 0, tiled=True)  7.04 us
    all_to_all x1, starting transfers between devices, body(): ritz = lax.all_to_all(ritz, 'mem', 0, 1, tiled=True)  3.87 us
    ppermute x2, starting transfers between devices, halo(): lax.ppermute(lax.slice_in_dim(block, size - width, size, axis=dim), 'dom'...  3.12 us
    add x2, other arithmetic, adjoint_step(): result + shifted(coef[3] * field, 1, 3) + shifted(coef[4] * field, -1, 3)  2.94 us
  transfers between devices with their start and end apart: 15, of which 9 were waited for; matrix products, arithmetic and copies ran while one was open for 7% of the time, Pallas kernels for 8%

profile of v12, /device:TPU:0, one launch (start us, length us, event | category | flops | bytes accessed | tf_op | source)
XLA Modules:
  0.0 107.2 jit_solution(1493074512742304700)
XLA Ops:
  0.6 2.3 %copy.7 = f32[8,8,8,512]{3,2,0,1:T(8,128)} copy(f32[8,8,8,512]{3,2,1,0:T(8,128)} %param.2) | data formatting | bytes 2097152 | tf_op args[0]
  3.0 7.0 %all-to-all-start = ((f32[8,8,8,512]{3,2,0,1:T(8,128)}), f32[8,8,8,512]{3,2,0,1:T(8,128)S(1)}, u32[]{:S(2)}, u32[]{:S(2)}) async-start(f32[8,8,8,512]{3,2,0,1:T(8,128)} %copy.7), calls=%async_computation | async-start | bytes 2097152 | tf_op jit(solution)/shard_map/all_to_all | solution.py:105
  10.0 1.5 %collective-permute-start.1 = (bf16[2,5,1,4,512]{4,3,2,1,0:T(4,128)(2,1)S(1)}, bf16[2,5,1,4,512]{4,3,2,1,0:T(4,128)(2,1)S(1)}, u32[]{:S(2)}, u32[]{:S(2)}) collective-permute-start(bf16[2,5,1,4,512]{4,3,2,1,0:T(4,128)(2,1)S(1)} %get-tuple-element.42), channel_id=1, source_target_pairs={{0,8},{8,16},{16,24},{24,32},{32,40},{40,48},{48,56},{56,64},{64,7... | collective-permute-start | bytes 122888 | tf_op jit(solution)/shard_map/ppermute | solution.py:16
  11.5 1.3 %collective-permute-start.2 = (bf16[2,5,1,4,512]{4,3,2,1,0:T(4,128)(2,1)S(1)}, bf16[2,5,1,4,512]{4,3,2,1,0:T(4,128)(2,1)S(1)}, u32[]{:S(2)}, u32[]{:S(2)}) collective-permute-start(bf16[2,5,1,4,512]{4,3,2,1,0:T(4,128)(2,1)S(1)} %get-tuple-element.43), channel_id=1, source_target_pairs={{8,0},{16,8},{24,16},{32,24},{40,32},{48,40},{56,48},{64,56},{72,6... | collective-permute-start | bytes 122888 | tf_op jit(solution)/shard_map/ppermute | solution.py:17
  12.8 14.4 %all-to-all-done = f32[8,8,8,512]{3,2,0,1:T(8,128)S(1)} async-done(((f32[8,8,8,512]{3,2,0,1:T(8,128)}), f32[8,8,8,512]{3,2,0,1:T(8,128)S(1)}, u32[]{:S(2)}, u32[]{:S(2)}) %all-to-all-start) | async-done | bytes 1048608 | tf_op jit(solution)/shard_map/all_to_all | solution.py:105
  27.2 0.6 copy.19
  27.8 0.1 fusion.33
  27.9 1.7 %collective-permute-start.3 = (f32[64,1,4,512]{3,0,2,1:T(8,128)S(1)}, f32[64,1,4,512]{3,0,2,1:T(8,128)S(1)}, u32[]{:S(2)}, u32[]{:S(2)}) collective-permute-start(f32[64,1,4,512]{3,0,2,1:T(8,128)S(1)} %get-tuple-element.30), channel_id=1, source_target_pairs={{0,8},{8,16},{16,24},{24,32},{32,40},{40,48},{48,56},{56,64},{64,7... | collective-permute-start | bytes 1572872 | tf_op jit(solution)/shard_map/ppermute | solution.py:16
  29.6 1.3 %collective-permute-start.4 = (f32[64,1,4,512]{3,0,2,1:T(8,128)S(1)}, f32[64,1,4,512]{3,0,2,1:T(8,128)S(1)}, u32[]{:S(2)}, u32[]{:S(2)}) collective-permute-start(f32[64,1,4,512]{3,0,2,1:T(8,128)S(1)} %get-tuple-element.31), channel_id=1, source_target_pairs={{8,0},{16,8},{24,16},{32,24},{40,32},{48,40},{56,48},{64,56},{72,6... | collective-permute-start | bytes 1572872 | tf_op jit(solution)/shard_map/ppermute | solution.py:17
  30.9 0.0 collective-permute-done.2
  30.9 0.1 maximum_convert_fusion
  31.0 2.1 %convolution_bitcast_fusion.3 = f32[64,64]{1,0:T(8,128)S(1)} fusion(f32[8,8,1,8,512]{4,3,1,0,2:T(8,128)S(1)} %bitcast.61), kind=kOutput, calls=%fused_computation.44 | convolution fusion | flops 201326592 | bytes 1064960 | tf_op jit(solution)/shard_map/alij,blij->ab/dot_general | solution.py:114
  33.1 0.6 collective-permute-start
  33.7 3.4 %collective-permute-done = f32[64,64]{1,0:T(8,128)S(1)} collective-permute-done((f32[64,64]{1,0:T(8,128)S(1)}, f32[64,64]{1,0:T(8,128)S(1)}, u32[]{:S(2)}, u32[]{:S(2)}) %collective-permute-start) | collective-permute-done | bytes 16416 | tf_op jit(solution)/shard_map/ppermute | solution.py:53
  37.1 0.0 collective-permute-done.3
  37.1 0.0 collective-permute-done.4
  37.1 0.2 pad_maximum_fusion
  37.3 1.3 %fusion.4 = f32[64,1,16,512]{3,0,2,1:T(8,128)S(1)} fusion(f32[64,1,16,512]{3,0,2,1:T(8,128)S(1)} %pad_maximum_fusion, f32[16,512]{1,0:T(8,128)S(1)} %get-tuple-element.37, f32[16,512]{1,0:T(8,128)S(1)} %get-tuple-element.38, f32[16,512]{1,0:T(8,128)S(1)} %get-tuple-element.39, f32[16,512]{1,0:T(8,128)S(1)} %get-tuple-element.40, ...), kind=kLoop, calls=%fused_computation.20 | loop fusion | flops 4718592 | bytes 4358144 | tf_op jit(solution)/shard_map/add | solution.py:33
  38.6 1.2 %collective-permute-start.5 = (f32[64,64]{1,0:T(8,128)S(1)}, f32[64,64]{1,0:T(8,128)S(1)}, u32[]{:S(2)}, u32[]{:S(2)}) collective-permute-start(f32[64,64]{1,0:T(8,128)S(1)} %add.107), channel_id=1, source_target_pairs={{0,2},{1,3},{2,0},{3,1},{4,6},{5,7},{6,4},{7,5},{8,10},{9,11},{10,... | collective-permute-start | bytes 49160 | tf_op jit(solution)/shard_map/ppermute | solution.py:53
  39.8 1.3 %fusion.10 = f32[64,1,16,512]{3,0,2,1:T(8,128)S(1)} fusion(f32[64,1,16,512]{3,0,2,1:T(8,128)S(1)} %fusion.4, f32[16,512]{1,0:T(8,128)S(1)} %get-tuple-element.33, f32[16,512]{1,0:T(8,128)S(1)} %get-tuple-element.34, f32[16,512]{1,0:T(8,128)S(1)} %get-tuple-element.35, f32[16,512]{1,0:T(8,128)S(1)} %get-tuple-element.36, f32[16,512]{1,0:T(8,128)S(1)} %get-tuple-element.32), kind=kLoop, calls=%fused_computation.26 | loop fusion | flops 4718592 | bytes 4358144 | tf_op jit(solution)/shard_map/add | solution.py:33
  41.1 3.0 %collective-permute-done.5 = f32[64,64]{1,0:T(8,128)S(1)} collective-permute-done((f32[64,64]{1,0:T(8,128)S(1)}, f32[64,64]{1,0:T(8,128)S(1)}, u32[]{:S(2)}, u32[]{:S(2)}) %collective-permute-start.5) | collective-permute-done | bytes 16416 | tf_op jit(solution)/shard_map/ppermute | solution.py:53
  44.1 1.2 %broadcast_multiply_fusion = (f32[64,1,16,512]{3,0,2,1:T(8,128)S(1)}, f32[64,1,16,512]{3,0,2,1:T(8,128)S(1)}, f32[64,1,16,512]{3,0,2,1:T(8,128)S(1)}, f32[64,1,16,512]{3,0,2,1:T(8,128)S(1)}) fusion(f32[64,1,16,512]{3,0,2,1:T(8,128)S(1)} %fusion.10, f32[16,512]{1,0:T(8,128)S(1)} %get-tuple-element.33, f32[16,512]{1,0:T(8,128)S(1)} %get-tuple-element.34, ...), kind=kLoop, calls=%fused_computation.51 | loop fusion | flops 2097152 | bytes 10616832 | tf_op jit(solution)/shard_map/mul | solution.py:38
  45.3 1.0 convolution_bitcast_fusion.2
  46.3 0.6 collective-permute-start.6
  47.0 1.5 %fusion.15 = f32[64,1,16,512]{3,0,2,1:T(8,128)S(1)} fusion(f32[64,1,16,512]{3,0,2,1:T(8,128)S(1)} %get-tuple-element.29, f32[64,1,16,512]{3,0,2,1:T(8,128)S(1)} %get-tuple-element.28, f32[64,1,16,512]{3,0,2,1:T(8,128)S(1)} %get-tuple-element.27, f32[64,1,16,512]{3,0,2,1:T(8,128)S(1)} %get-tuple-element.26, f32[64,1,16,512]{3,0,2,1:T(8,128)S(1)} %fusion.10, ...), kind=kLoop, calls=%fused_computation.31 | loop fusion | flops 2621440 | bytes 12615680 | tf_op jit(solution)/shard_map/add | solution.py:38
  48.5 3.7 %collective-permute-done.6 = f32[2,64,64]{2,1,0:T(8,128)S(1)} collective-permute-done((f32[2,64,64]{2,1,0:T(8,128)S(1)}, f32[2,64,64]{2,1,0:T(8,128)S(1)}, u32[]{:S(2)}, u32[]{:S(2)}) %collective-permute-start.6) | collective-permute-done | bytes 32800 | tf_op jit(solution)/shard_map/ppermute | solution.py:53
  52.2 1.2 %broadcast_multiply_fusion.4 = (f32[64,1,16,512]{3,0,2,1:T(8,128)S(1)}, f32[64,1,16,512]{3,0,2,1:T(8,128)S(1)}, f32[64,1,16,512]{3,0,2,1:T(8,128)S(1)}, f32[64,1,16,512]{3,0,2,1:T(8,128)S(1)}) fusion(f32[64,1,16,512]{3,0,2,1:T(8,128)S(1)} %fusion.15, f32[16,512]{1,0:T(8,128)S(1)} %get-tuple-element.37, f32[16,512]{1,0:T(8,128)S(1)} %get-tuple-element.38, ...), kind=kLoop, calls=%fused_computation.55 | loop fusion | flops 2097152 | bytes 10616832 | tf_op jit(solution)/shard_map/mul | solution.py:38
  53.4 3.2 %collective-permute-start.7 = (f32[2,64,64]{2,1,0:T(8,128)S(1)}, f32[2,64,64]{2,1,0:T(8,128)S(1)}, u32[]{:S(2)}, u32[]{:S(2)}) collective-permute-start(f32[2,64,64]{2,1,0:T(8,128)S(1)} %fusion.32), channel_id=1, source_target_pairs={{0,8},{8,0},{16,24},{24,16},{32,40},{40,32},{48,56},{56,48},{64,72... | collective-permute-start | bytes 98312 | tf_op jit(solution)/shard_map/ppermute | solution.py:53
  56.7 1.4 %fusion.19 = f32[64,1,16,512]{3,0,2,1:T(8,128)S(1)} fusion(f32[64,1,16,512]{3,0,2,1:T(8,128)S(1)} %get-tuple-element.25, f32[64,1,16,512]{3,0,2,1:T(8,128)S(1)} %get-tuple-element.24, f32[64,1,16,512]{3,0,2,1:T(8,128)S(1)} %get-tuple-element.23, f32[64,1,16,512]{3,0,2,1:T(8,128)S(1)} %get-tuple-element.22, f32[64,1,16,512]{3,0,2,1:T(8,128)S(1)} %fusion.15, ...), kind=kLoop, calls=%fused_computation.35 | loop fusion | flops 2621440 | bytes 12615680 | tf_op jit(solution)/shard_map/add | solution.py:38
  58.1 0.0 collective-permute-done.7
  58.1 2.8 %collective-permute-start.8 = (f32[2,64,64]{2,1,0:T(8,128)S(1)}, f32[2,64,64]{2,1,0:T(8,128)S(1)}, u32[]{:S(2)}, u32[]{:S(2)}) collective-permute-start(f32[2,64,64]{2,1,0:T(8,128)S(1)} %add.122), channel_id=1, source_target_pairs={{0,16},{8,24},{16,0},{24,8},{32,48},{40,56},{48,32},{56,40},{64,80... | collective-permute-start | bytes 98312 | tf_op jit(solution)/shard_map/ppermute | solution.py:53
  61.0 2.7 %collective-permute-done.8 = f32[2,64,64]{2,1,0:T(8,128)S(1)} collective-permute-done((f32[2,64,64]{2,1,0:T(8,128)S(1)}, f32[2,64,64]{2,1,0:T(8,128)S(1)}, u32[]{:S(2)}, u32[]{:S(2)}) %collective-permute-start.8) | collective-permute-done | bytes 32800 | tf_op jit(solution)/shard_map/ppermute | solution.py:53
  63.6 3.6 %collective-permute-start.9 = (f32[2,64,64]{2,1,0:T(8,128)S(1)}, f32[2,64,64]{2,1,0:T(8,128)S(1)}, u32[]{:S(2)}, u32[]{:S(2)}) collective-permute-start(f32[2,64,64]{2,1,0:T(8,128)S(1)} %add.127), channel_id=1, source_target_pairs={{0,32},{8,40},{16,48},{24,56},{32,0},{40,8},{48,16},{56,24},{64,96... | collective-permute-start | bytes 98312 | tf_op jit(solution)/shard_map/ppermute | solution.py:53
  67.3 2.2 %collective-permute-done.9 = f32[2,64,64]{2,1,0:T(8,128)S(1)} collective-permute-done((f32[2,64,64]{2,1,0:T(8,128)S(1)}, f32[2,64,64]{2,1,0:T(8,128)S(1)}, u32[]{:S(2)}, u32[]{:S(2)}) %collective-permute-start.9) | collective-permute-done | bytes 32800 | tf_op jit(solution)/shard_map/ppermute | solution.py:53
  69.5 2.3 %collective-permute-start.10 = (f32[2,64,64]{2,1,0:T(8,128)S(1)}, f32[2,64,64]{2,1,0:T(8,128)S(1)}, u32[]{:S(2)}, u32[]{:S(2)}) collective-permute-start(f32[2,64,64]{2,1,0:T(8,128)S(1)} %add.128), channel_id=1, source_target_pairs={{0,64},{8,72},{16,80},{24,88},{32,96},{40,104},{48,112},{56,120},{... | collective-permute-start | bytes 98312 | tf_op jit(solution)/shard_map/ppermute | solution.py:53
  71.9 2.2 %collective-permute-done.10 = f32[2,64,64]{2,1,0:T(8,128)S(1)} collective-permute-done((f32[2,64,64]{2,1,0:T(8,128)S(1)}, f32[2,64,64]{2,1,0:T(8,128)S(1)}, u32[]{:S(2)}, u32[]{:S(2)}) %collective-permute-start.10) | collective-permute-done | bytes 32800 | tf_op jit(solution)/shard_map/ppermute | solution.py:53
  74.1 0.6 slice_bitcast_fusion
  74.8 0.6 collective-permute-start.11
  75.4 8.2 %shard_map.41 = f32[64,64]{1,0:T(8,128)} custom-call(f32[64,64]{1,0:T(8,128)} %get-tuple-element.45.g_ref), custom_call_target="tpu_custom_call" | custom-call | tf_op jit(solution)/shard_map/pallas_call | solution.py:84
  83.5 1.1 convolution_bitcast_fusion.1
  84.6 1.0 convolution_bitcast_fusion
  85.6 1.6 %copy.10 = f32[64,1,8,512]{3,2,1,0:T(8,128)} copy(f32[64,1,8,512]{3,0,2,1:T(8,128)S(1)} %convolution_bitcast_fusion) | data formatting | bytes 2097152 | tf_op jit(solution)/shard_map/ab,blij->alij/dot_general | solution.py:139
  87.2 3.9 %all-to-all-start.1 = ((f32[64,1,8,512]{3,2,1,0:T(8,128)}), f32[64,1,8,512]{3,2,1,0:T(8,128)S(1)}, u32[]{:S(2)}, u32[]{:S(2)}) async-start(f32[64,1,8,512]{3,2,1,0:T(8,128)} %copy.10), calls=%async_computation.1 | async-start | bytes 2097152 | tf_op jit(solution)/shard_map/all_to_all | solution.py:143
  91.1 3.5 %collective-permute-start.12 = (f32[64,64]{1,0:T(8,128)S(1)}, f32[64,64]{1,0:T(8,128)S(1)}, u32[]{:S(2)}, u32[]{:S(2)}) collective-permute-start(f32[64,64]{1,0:T(8,128)S(1)} %fusion.31), channel_id=1, source_target_pairs={{0,2},{1,3},{2,0},{3,1},{4,6},{5,7},{6,4},{7,5},{8,10},{9,11},{10,... | collective-permute-start | bytes 49160 | tf_op jit(solution)/shard_map/ppermute | solution.py:53
  94.6 9.8 %collective-permute-done.12 = f32[64,64]{1,0:T(8,128)S(1)} collective-permute-done((f32[64,64]{1,0:T(8,128)S(1)}, f32[64,64]{1,0:T(8,128)S(1)}, u32[]{:S(2)}, u32[]{:S(2)}) %collective-permute-start.12) | collective-permute-done | bytes 16416 | tf_op jit(solution)/shard_map/ppermute | solution.py:53
  104.4 0.6 add_multiply_fusion
  105.1 1.1 %all-to-all-done.1 = f32[64,1,8,512]{3,2,1,0:T(8,128)S(1)} async-done(((f32[64,1,8,512]{3,2,1,0:T(8,128)}), f32[64,1,8,512]{3,2,1,0:T(8,128)S(1)}, u32[]{:S(2)}, u32[]{:S(2)}) %all-to-all-start.1) | async-done | bytes 1048608 | tf_op jit(solution)/shard_map/all_to_all | solution.py:143
  106.2 1.1 copy.18
  (15 shorter events, 0.1 us)
Async XLA Ops:
  0.6 9.4 %copy-start = (bf16[2,5,1,8,512]{4,3,2,1,0:T(8,128)(2,1)S(1)}, bf16[2,5,1,8,512]{4,3,2,1,0:T(8,128)(2,1)}, u32[]{:S(2)}) copy-start(bf16[2,5,1,8,512]{4,3,2,1,0:T(8,128)(2,1)} %param.3) | copy-start | bytes 245764
  3.0 24.2 %all-to-all-start = ((f32[8,8,8,512]{3,2,0,1:T(8,128)}), f32[8,8,8,512]{3,2,0,1:T(8,128)S(1)}, u32[]{:S(2)}, u32[]{:S(2)}) async-start(f32[8,8,8,512]{3,2,0,1:T(8,128)} %copy.7), calls=%async_computation | async-start | bytes 2097152 | tf_op jit(solution)/shard_map/all_to_all | solution.py:105
  10.0 20.8 %collective-permute-start.1 = (bf16[2,5,1,4,512]{4,3,2,1,0:T(4,128)(2,1)S(1)}, bf16[2,5,1,4,512]{4,3,2,1,0:T(4,128)(2,1)S(1)}, u32[]{:S(2)}, u32[]{:S(2)}) collective-permute-start(bf16[2,5,1,4,512]{4,3,2,1,0:T(4,128)(2,1)S(1)} %get-tuple-element.42), channel_id=1, source_target_pairs={{0,8},{8,16},{16,24},{24,32},{32,40},{40,48},{48,56},{56,64},{64,7... | collective-permute-start | bytes 122888 | tf_op jit(solution)/shard_map/ppermute | solution.py:16
  11.5 19.4 %collective-permute-start.2 = (bf16[2,5,1,4,512]{4,3,2,1,0:T(4,128)(2,1)S(1)}, bf16[2,5,1,4,512]{4,3,2,1,0:T(4,128)(2,1)S(1)}, u32[]{:S(2)}, u32[]{:S(2)}) collective-permute-start(bf16[2,5,1,4,512]{4,3,2,1,0:T(4,128)(2,1)S(1)} %get-tuple-element.43), channel_id=1, source_target_pairs={{8,0},{16,8},{24,16},{32,24},{40,32},{48,40},{56,48},{64,56},{72,6... | collective-permute-start | bytes 122888 | tf_op jit(solution)/shard_map/ppermute | solution.py:17
  27.9 9.2 %collective-permute-start.3 = (f32[64,1,4,512]{3,0,2,1:T(8,128)S(1)}, f32[64,1,4,512]{3,0,2,1:T(8,128)S(1)}, u32[]{:S(2)}, u32[]{:S(2)}) collective-permute-start(f32[64,1,4,512]{3,0,2,1:T(8,128)S(1)} %get-tuple-element.30), channel_id=1, source_target_pairs={{0,8},{8,16},{16,24},{24,32},{32,40},{40,48},{48,56},{56,64},{64,7... | collective-permute-start | bytes 1572872 | tf_op jit(solution)/shard_map/ppermute | solution.py:16
  29.6 7.5 %collective-permute-start.4 = (f32[64,1,4,512]{3,0,2,1:T(8,128)S(1)}, f32[64,1,4,512]{3,0,2,1:T(8,128)S(1)}, u32[]{:S(2)}, u32[]{:S(2)}) collective-permute-start(f32[64,1,4,512]{3,0,2,1:T(8,128)S(1)} %get-tuple-element.31), channel_id=1, source_target_pairs={{8,0},{16,8},{24,16},{32,24},{40,32},{48,40},{56,48},{64,56},{72,6... | collective-permute-start | bytes 1572872 | tf_op jit(solution)/shard_map/ppermute | solution.py:17
  33.1 4.0 %collective-permute-start = (f32[64,64]{1,0:T(8,128)S(1)}, f32[64,64]{1,0:T(8,128)S(1)}, u32[]{:S(2)}, u32[]{:S(2)}) collective-permute-start(f32[64,64]{1,0:T(8,128)S(1)} %convolution_bitcast_fusion.3), channel_id=1, source_target_pairs={{0,1},{1,0},{2,3},{3,2},{4,5},{5,4},{6,7},{7,6},{8,9},{9,8},{10,11... | collective-permute-start | bytes 49160 | tf_op jit(solution)/shard_map/ppermute | solution.py:53
  38.6 5.5 %collective-permute-start.5 = (f32[64,64]{1,0:T(8,128)S(1)}, f32[64,64]{1,0:T(8,128)S(1)}, u32[]{:S(2)}, u32[]{:S(2)}) collective-permute-start(f32[64,64]{1,0:T(8,128)S(1)} %add.107), channel_id=1, source_target_pairs={{0,2},{1,3},{2,0},{3,1},{4,6},{5,7},{6,4},{7,5},{8,10},{9,11},{10,... | collective-permute-start | bytes 49160 | tf_op jit(solution)/shard_map/ppermute | solution.py:53
  46.3 5.8 %collective-permute-start.6 = (f32[2,64,64]{2,1,0:T(8,128)S(1)}, f32[2,64,64]{2,1,0:T(8,128)S(1)}, u32[]{:S(2)}, u32[]{:S(2)}) collective-permute-start(f32[2,64,64]{2,1,0:T(8,128)S(1)} %pad_maximum_fusion.1), channel_id=1, source_target_pairs={{0,4},{1,5},{2,6},{3,7},{4,0},{5,1},{6,2},{7,3},{8,12},{9,13},{10,... | collective-permute-start | bytes 98312 | tf_op jit(solution)/shard_map/ppermute | solution.py:53
  53.4 4.7 %collective-permute-start.7 = (f32[2,64,64]{2,1,0:T(8,128)S(1)}, f32[2,64,64]{2,1,0:T(8,128)S(1)}, u32[]{:S(2)}, u32[]{:S(2)}) collective-permute-start(f32[2,64,64]{2,1,0:T(8,128)S(1)} %fusion.32), channel_id=1, source_target_pairs={{0,8},{8,0},{16,24},{24,16},{32,40},{40,32},{48,56},{56,48},{64,72... | collective-permute-start | bytes 98312 | tf_op jit(solution)/shard_map/ppermute | solution.py:53
  58.1 5.5 %collective-permute-start.8 = (f32[2,64,64]{2,1,0:T(8,128)S(1)}, f32[2,64,64]{2,1,0:T(8,128)S(1)}, u32[]{:S(2)}, u32[]{:S(2)}) collective-permute-start(f32[2,64,64]{2,1,0:T(8,128)S(1)} %add.122), channel_id=1, source_target_pairs={{0,16},{8,24},{16,0},{24,8},{32,48},{40,56},{48,32},{56,40},{64,80... | collective-permute-start | bytes 98312 | tf_op jit(solution)/shard_map/ppermute | solution.py:53
  63.6 5.9 %collective-permute-start.9 = (f32[2,64,64]{2,1,0:T(8,128)S(1)}, f32[2,64,64]{2,1,0:T(8,128)S(1)}, u32[]{:S(2)}, u32[]{:S(2)}) collective-permute-start(f32[2,64,64]{2,1,0:T(8,128)S(1)} %add.127), channel_id=1, source_target_pairs={{0,32},{8,40},{16,48},{24,56},{32,0},{40,8},{48,16},{56,24},{64,96... | collective-permute-start | bytes 98312 | tf_op jit(solution)/shard_map/ppermute | solution.py:53
  69.5 4.6 %collective-permute-start.10 = (f32[2,64,64]{2,1,0:T(8,128)S(1)}, f32[2,64,64]{2,1,0:T(8,128)S(1)}, u32[]{:S(2)}, u32[]{:S(2)}) collective-permute-start(f32[2,64,64]{2,1,0:T(8,128)S(1)} %add.128), channel_id=1, source_target_pairs={{0,64},{8,72},{16,80},{24,88},{32,96},{40,104},{48,112},{56,120},{... | collective-permute-start | bytes 98312 | tf_op jit(solution)/shard_map/ppermute | solution.py:53
  74.8 8.8 %collective-permute-start.11 = (f32[64,64]{1,0:T(8,128)S(1)}, f32[64,64]{1,0:T(8,128)S(1)}, u32[]{:S(2)}, u32[]{:S(2)}) collective-permute-start(f32[64,64]{1,0:T(8,128)S(1)} %get-tuple-element.44), channel_id=1, source_target_pairs={{0,1},{1,0},{2,3},{3,2},{4,5},{5,4},{6,7},{7,6},{8,9},{9,8},{10,11... | collective-permute-start | bytes 49160 | tf_op jit(solution)/shard_map/ppermute | solution.py:53
  87.2 18.9 %all-to-all-start.1 = ((f32[64,1,8,512]{3,2,1,0:T(8,128)}), f32[64,1,8,512]{3,2,1,0:T(8,128)S(1)}, u32[]{:S(2)}, u32[]{:S(2)}) async-start(f32[64,1,8,512]{3,2,1,0:T(8,128)} %copy.10), calls=%async_computation.1 | async-start | bytes 2097152 | tf_op jit(solution)/shard_map/all_to_all | solution.py:143
  91.1 13.3 %collective-permute-start.12 = (f32[64,64]{1,0:T(8,128)S(1)}, f32[64,64]{1,0:T(8,128)S(1)}, u32[]{:S(2)}, u32[]{:S(2)}) collective-permute-start(f32[64,64]{1,0:T(8,128)S(1)} %fusion.31), channel_id=1, source_target_pairs={{0,2},{1,3},{2,0},{3,1},{4,6},{5,7},{6,4},{7,5},{8,10},{9,11},{10,... | collective-permute-start | bytes 49160 | tf_op jit(solution)/shard_map/ppermute | solution.py:53

commit v13 on v12

--- a/solution.py
+++ b/solution.py
@@ -97,12 +97,32 @@
     return inverse, extra
 
 
+def regroup(x, split, concat):
+    count = lax.axis_size("mem")
+    me = lax.axis_index("mem")
+    size = x.shape[split] // count
+    pieces = []
+    for offset in range(count):
+        chunk = lax.dynamic_slice_in_dim(x, ((me + offset) % count) * size, size, split)
+        if offset:
+            pairs = [(i, (i + offset) % count) for i in range(count)]
+            chunk = lax.ppermute(chunk, "mem", pairs)
+        pieces.append(chunk)
+    order = (me - jnp.arange(count)) % count
+    stacked = jnp.take(jnp.stack(pieces), order, axis=0)
+    stacked = jnp.moveaxis(stacked, 0, concat)
+    shape = list(x.shape)
+    shape[split] = size
+    shape[concat] *= count
+    return stacked.reshape(shape)
+
+
 def body(perturbations, trajectory):
     width = 2 * STEPS
     rows = perturbations.shape[2]
     assert width <= rows
     coeffs = halo(trajectory, width, 3).astype(jnp.float32)
-    v = lax.all_to_all(perturbations, "mem", 1, 0, tiled=True)
+    v = regroup(perturbations, 1, 0)
     members = v.shape[0]
     ncells_all = (
         perturbations.shape[1]
@@ -140,7 +160,7 @@
     for axis, bit in cross_bits:
         cross = exchange(cross, axis, bit)
     projected = cross / ncells_all
-    ritz = lax.all_to_all(ritz, "mem", 0, 1, tiled=True)
+    ritz = regroup(ritz, 0, 1)
     return (ritz, projected)
 
 

time: 108 us -> 113 us (1.046)
  starting transfers between devices: 35.3 us -> 60.9 us
  waiting for transfers between devices: 42.5 us -> 19.9 us
    ppermute x0 -> x14, starting transfers between devices: none -> 34.7 us  [regroup(): chunk = lax.ppermute(chunk, 'mem', pairs)]
    all_to_all x2 -> x0, waiting for transfers between devices: 15.5 us -> none  [the longest x1 14.4 us: body(): v = lax.all_to_all(perturbations, 'mem', 1, 0, tiled=True)]
    all_to_all x2 -> x0, starting transfers between devices: 10.9 us -> none  [the longest x1 7.04 us: body(): v = lax.all_to_all(perturbations, 'mem', 1, 0, tiled=True)]
    ppermute x9, waiting for transfers between devices: 27 us -> 16.9 us  [exchange(): return x + lax.ppermute(x, axis, [(i, i ^ bit) for i in range(count)])]
    ppermute x0 -> x14, waiting for transfers between devices: none -> 3.03 us  [regroup(): chunk = lax.ppermute(chunk, 'mem', pairs)]
    ppermute x2, starting transfers between devices: 3.12 us -> 5.99 us  [halo(): lax.ppermute(lax.slice_in_dim(block, size - width, size, axis=dim), 'dom'...]
    all_to_all x2 -> x0, local copies, waits for them, and re-layouts: 1.67 us -> none  [the longest x1 1.06 us: body(): ritz = lax.all_to_all(ritz, 'mem', 0, 1, tiled=True)]
    dot_general x1 -> x0, local copies, waits for them, and re-layouts: 1.58 us -> none  [body(): ritz = jnp.einsum('ab,blij->alij', inverse, field, precision=hi)]
  transfers between devices with their start and end apart: 15 -> 27, of which waited for: 9 -> 8; matrix products, arithmetic and copies ran while one was open for 7% -> 11% of each run, Pallas kernels for 8% -> 7%
where the time goes in v13:
time: 113 us; the launch traced here: 112 us
  starting transfers between devices  60.9 us (54%)
  waiting for transfers between devices  19.9 us (18%)
  other arithmetic  10 us (9%)
  Pallas kernels  8.15 us (7%)
  local copies, waits for them, and re-layouts  6.19 us (5%)
  matrix products  5.15 us (5%)
  between operations  1.25 us (1%)
    ppermute x14, starting transfers between devices, regroup(): chunk = lax.ppermute(chunk, 'mem', pairs)  34.7 us
    ppermute x9, starting transfers between devices, exchange(): return x + lax.ppermute(x, axis, [(i, i ^ bit) for i in range(count)])  17.7 us
    ppermute x9, waiting for transfers between devices, exchange(): return x + lax.ppermute(x, axis, [(i, i ^ bit) for i in range(count)])  16.9 us
    pallas_call x1, Pallas kernels, lower_inverse(): pl.pallas_call(chol_inv_kernel, out_shape=jax.ShapeDtypeStruct((n, n), jn...  8.15 us
    ppermute x2, starting transfers between devices, halo(): lax.ppermute(lax.slice_in_dim(block, size - width, size, axis=dim), 'dom'...  5.99 us
    unnamed x18, local copies, waits for them, and re-layouts  3.53 us
    ppermute x14, waiting for transfers between devices, regroup(): chunk = lax.ppermute(chunk, 'mem', pairs)  3.03 us
    add x2, other arithmetic, adjoint_step(): result + shifted(coef[3] * field, 1, 3) + shifted(coef[4] * field, -1, 3)  2.94 us
  transfers between devices with their start and end apart: 27, of which 8 were waited for; matrix products, arithmetic and copies ran while one was open for 11% of the time, Pallas kernels for 7%

profile of v13, /device:TPU:0, one launch (start us, length us, event | category | flops | bytes accessed | tf_op | source)
XLA Modules:
  0.0 111.6 jit_solution(13741603868992625362)
XLA Ops:
  0.7 1.3 %dynamic-slice_bitcast_fusion.1 = (f32[8,1,8,512]{3,2,0,1:T(8,128)S(1)}, f32[8,1,8,512]{3,2,0,1:T(8,128)S(1)}, f32[8,1,8,512]{3,2,0,1:T(8,128)S(1)}, f32[8,1,8,5...) fusion(f32[8,8,8,512]{3,2,1,0:T(8,128)} %param.4, ...), kind=kLoop, calls=%fused_computation.89 | loop fusion | bytes 1835036
  2.1 1.7 %collective-permute-start = (f32[8,1,8,512]{3,2,0,1:T(8,128)S(1)}, f32[8,1,8,512]{3,2,0,1:T(8,128)S(1)}, u32[]{:S(2)}, u32[]{:S(2)}) collective-permute-start(f32[8,1,8,512]{3,2,0,1:T(8,128)S(1)} %get-tuple-element.50), channel_id=1, source_target_pairs={{0,1},{1,2},{2,3},{3,4},{4,5},{5,6},{6,7},{7,0},{8,9},{9,10},{10,1... | collective-permute-start | bytes 393224 | tf_op jit(solution)/shard_map/ppermute | solution.py:109
  3.8 2.7 %collective-permute-start.1 = (f32[8,1,8,512]{3,2,0,1:T(8,128)S(1)}, f32[8,1,8,512]{3,2,0,1:T(8,128)S(1)}, u32[]{:S(2)}, u32[]{:S(2)}) collective-permute-start(f32[8,1,8,512]{3,2,0,1:T(8,128)S(1)} %get-tuple-element.49), channel_id=1, source_target_pairs={{0,2},{1,3},{2,4},{3,5},{4,6},{5,7},{6,0},{7,1},{8,10},{9,11},{10,... | collective-permute-start | bytes 393224 | tf_op jit(solution)/shard_map/ppermute | solution.py:109
  6.5 4.1 %collective-permute-start.2 = (f32[8,1,8,512]{3,2,0,1:T(8,128)S(1)}, f32[8,1,8,512]{3,2,0,1:T(8,128)S(1)}, u32[]{:S(2)}, u32[]{:S(2)}) collective-permute-start(f32[8,1,8,512]{3,2,0,1:T(8,128)S(1)} %get-tuple-element.48), channel_id=1, source_target_pairs={{0,3},{1,4},{2,5},{3,6},{4,7},{5,0},{6,1},{7,2},{8,11},{9,12},{10,... | collective-permute-start | bytes 393224 | tf_op jit(solution)/shard_map/ppermute | solution.py:109
  10.9 3.2 %collective-permute-start.4 = (f32[8,1,8,512]{3,2,1,0:T(8,128)S(1)}, f32[8,1,8,512]{3,2,1,0:T(8,128)S(1)}, u32[]{:S(2)}, u32[]{:S(2)}) collective-permute-start(f32[8,1,8,512]{3,2,1,0:T(8,128)S(1)} %get-tuple-element.51), channel_id=1, source_target_pairs={{0,5},{1,6},{2,7},{3,0},{4,1},{5,2},{6,3},{7,4},{8,13},{9,14},{10,... | collective-permute-start | bytes 393224 | tf_op jit(solution)/shard_map/ppermute | solution.py:109
  14.2 0.9 bitcast_dynamic-update-slice_fusion.14
  15.1 3.3 %collective-permute-start.5 = (f32[8,1,8,512]{3,2,0,1:T(8,128)S(1)}, f32[8,1,8,512]{3,2,0,1:T(8,128)S(1)}, u32[]{:S(2)}, u32[]{:S(2)}) collective-permute-start(f32[8,1,8,512]{3,2,0,1:T(8,128)S(1)} %get-tuple-element.46), channel_id=1, source_target_pairs={{0,6},{1,7},{2,0},{3,1},{4,2},{5,3},{6,4},{7,5},{8,14},{9,15},{10,... | collective-permute-start | bytes 393224 | tf_op jit(solution)/shard_map/ppermute | solution.py:109
  18.4 1.8 %collective-permute-start.6 = (f32[8,1,8,512]{3,2,0,1:T(8,128)S(1)}, f32[8,1,8,512]{3,2,0,1:T(8,128)S(1)}, u32[]{:S(2)}, u32[]{:S(2)}) collective-permute-start(f32[8,1,8,512]{3,2,0,1:T(8,128)S(1)} %get-tuple-element.45), channel_id=1, source_target_pairs={{0,7},{1,0},{2,1},{3,2},{4,3},{5,4},{6,5},{7,6},{8,15},{9,8},{10,9... | collective-permute-start | bytes 393224 | tf_op jit(solution)/shard_map/ppermute | solution.py:109
  20.3 1.3 %collective-permute-start.8 = (bf16[2,5,1,4,512]{4,3,2,1,0:T(4,128)(2,1)S(1)}, bf16[2,5,1,4,512]{4,3,2,1,0:T(4,128)(2,1)S(1)}, u32[]{:S(2)}, u32[]{:S(2)}) collective-permute-start(bf16[2,5,1,4,512]{4,3,2,1,0:T(4,128)(2,1)S(1)} %get-tuple-element.62), channel_id=1, source_target_pairs={{0,8},{8,16},{16,24},{24,32},{32,40},{40,48},{48,56},{56,64},{64,7... | collective-permute-start | bytes 122888 | tf_op jit(solution)/shard_map/ppermute | solution.py:16
  21.6 1.3 %collective-permute-start.9 = (bf16[2,5,1,4,512]{4,3,2,1,0:T(4,128)(2,1)S(1)}, bf16[2,5,1,4,512]{4,3,2,1,0:T(4,128)(2,1)S(1)}, u32[]{:S(2)}, u32[]{:S(2)}) collective-permute-start(bf16[2,5,1,4,512]{4,3,2,1,0:T(4,128)(2,1)S(1)} %get-tuple-element.63), channel_id=1, source_target_pairs={{8,0},{16,8},{24,16},{32,24},{40,32},{48,40},{56,48},{64,56},{72,6... | collective-permute-start | bytes 122888 | tf_op jit(solution)/shard_map/ppermute | solution.py:17
  25.1 4.7 %collective-permute-start.10 = (f32[64,1,4,512]{3,0,2,1:T(8,128)S(1)}, f32[64,1,4,512]{3,0,2,1:T(8,128)S(1)}, u32[]{:S(2)}, u32[]{:S(2)}) collective-permute-start(f32[64,1,4,512]{3,0,2,1:T(8,128)S(1)} %get-tuple-element.43), channel_id=1, source_target_pairs={{0,8},{8,16},{16,24},{24,32},{32,40},{40,48},{48,56},{56,64},{64,7... | collective-permute-start | bytes 1572872 | tf_op jit(solution)/shard_map/ppermute | solution.py:16
  29.8 1.3 %collective-permute-start.11 = (f32[64,1,4,512]{3,0,2,1:T(8,128)S(1)}, f32[64,1,4,512]{3,0,2,1:T(8,128)S(1)}, u32[]{:S(2)}, u32[]{:S(2)}) collective-permute-start(f32[64,1,4,512]{3,0,2,1:T(8,128)S(1)} %get-tuple-element.44), channel_id=1, source_target_pairs={{8,0},{16,8},{24,16},{32,24},{40,32},{48,40},{56,48},{64,56},{72,6... | collective-permute-start | bytes 1572872 | tf_op jit(solution)/shard_map/ppermute | solution.py:17
  31.2 2.1 %convolution_bitcast_fusion.2 = f32[64,64]{1,0:T(8,128)S(1)} fusion(f32[64,8,512]{2,1,0:T(8,128)S(1)} %bitcast.124), kind=kOutput, calls=%fused_computation.45 | convolution fusion | flops 201326592 | bytes 1064960 | tf_op jit(solution)/shard_map/alij,blij->ab/dot_general | solution.py:134
  33.7 3.6 %collective-permute-done.7 = f32[64,64]{1,0:T(8,128)S(1)} collective-permute-done((f32[64,64]{1,0:T(8,128)S(1)}, f32[64,64]{1,0:T(8,128)S(1)}, u32[]{:S(2)}, u32[]{:S(2)}) %collective-permute-start.7) | collective-permute-done | bytes 16416 | tf_op jit(solution)/shard_map/ppermute | solution.py:53
  37.5 1.3 %fusion.4 = f32[64,1,16,512]{3,0,2,1:T(8,128)S(1)} fusion(f32[64,1,16,512]{3,0,2,1:T(8,128)S(1)} %pad_maximum_fusion, f32[16,512]{1,0:T(8,128)S(1)} %get-tuple-element.57, f32[16,512]{1,0:T(8,128)S(1)} %get-tuple-element.58, f32[16,512]{1,0:T(8,128)S(1)} %get-tuple-element.59, f32[16,512]{1,0:T(8,128)S(1)} %get-tuple-element.60, ...), kind=kLoop, calls=%fused_computation.22 | loop fusion | flops 4718592 | bytes 4358144 | tf_op jit(solution)/shard_map/add | solution.py:33
  38.8 1.6 %collective-permute-start.12 = (f32[64,64]{1,0:T(8,128)S(1)}, f32[64,64]{1,0:T(8,128)S(1)}, u32[]{:S(2)}, u32[]{:S(2)}) collective-permute-start(f32[64,64]{1,0:T(8,128)S(1)} %add.251), channel_id=1, source_target_pairs={{0,2},{1,3},{2,0},{3,1},{4,6},{5,7},{6,4},{7,5},{8,10},{9,11},{10,... | collective-permute-start | bytes 49160 | tf_op jit(solution)/shard_map/ppermute | solution.py:53
  40.4 1.3 %fusion.10 = f32[64,1,16,512]{3,0,2,1:T(8,128)S(1)} fusion(f32[64,1,16,512]{3,0,2,1:T(8,128)S(1)} %fusion.4, f32[16,512]{1,0:T(8,128)S(1)} %get-tuple-element.53, f32[16,512]{1,0:T(8,128)S(1)} %get-tuple-element.54, f32[16,512]{1,0:T(8,128)S(1)} %get-tuple-element.55, f32[16,512]{1,0:T(8,128)S(1)} %get-tuple-element.56, f32[16,512]{1,0:T(8,128)S(1)} %get-tuple-element.52), kind=kLoop, calls=%fused_computation.28 | loop fusion | flops 4718592 | bytes 4358144 | tf_op jit(solution)/shard_map/add | solution.py:33
  41.7 2.6 %collective-permute-done.12 = f32[64,64]{1,0:T(8,128)S(1)} collective-permute-done((f32[64,64]{1,0:T(8,128)S(1)}, f32[64,64]{1,0:T(8,128)S(1)}, u32[]{:S(2)}, u32[]{:S(2)}) %collective-permute-start.12) | collective-permute-done | bytes 16416 | tf_op jit(solution)/shard_map/ppermute | solution.py:53
  44.3 1.2 %broadcast_multiply_fusion = (f32[64,1,16,512]{3,0,2,1:T(8,128)S(1)}, f32[64,1,16,512]{3,0,2,1:T(8,128)S(1)}, f32[64,1,16,512]{3,0,2,1:T(8,128)S(1)}, f32[64,1,16,512]{3,0,2,1:T(8,128)S(1)}) fusion(f32[64,1,16,512]{3,0,2,1:T(8,128)S(1)} %fusion.10, f32[16,512]{1,0:T(8,128)S(1)} %get-tuple-element.53, f32[16,512]{1,0:T(8,128)S(1)} %get-tuple-element.54, ...), kind=kLoop, calls=%fused_computation.56 | loop fusion | flops 2097152 | bytes 10616832 | tf_op jit(solution)/shard_map/mul | solution.py:38
  45.6 1.0 convolution_bitcast_fusion.1
  46.6 1.0 collective-permute-start.13
  47.6 1.5 %fusion.15 = f32[64,1,16,512]{3,0,2,1:T(8,128)S(1)} fusion(f32[64,1,16,512]{3,0,2,1:T(8,128)S(1)} %get-tuple-element.34, f32[64,1,16,512]{3,0,2,1:T(8,128)S(1)} %get-tuple-element.33, f32[64,1,16,512]{3,0,2,1:T(8,128)S(1)} %get-tuple-element.32, f32[64,1,16,512]{3,0,2,1:T(8,128)S(1)} %get-tuple-element.31, f32[64,1,16,512]{3,0,2,1:T(8,128)S(1)} %fusion.10, ...), kind=kLoop, calls=%fused_computation.33 | loop fusion | flops 2621440 | bytes 12615680 | tf_op jit(solution)/shard_map/add | solution.py:38
  49.1 3.5 %collective-permute-done.13 = f32[2,64,64]{2,1,0:T(8,128)S(1)} collective-permute-done((f32[2,64,64]{2,1,0:T(8,128)S(1)}, f32[2,64,64]{2,1,0:T(8,128)S(1)}, u32[]{:S(2)}, u32[]{:S(2)}) %collective-permute-start.13) | collective-permute-done | bytes 32800 | tf_op jit(solution)/shard_map/ppermute | solution.py:53
  52.6 1.2 %broadcast_multiply_fusion.4 = (f32[64,1,16,512]{3,0,2,1:T(8,128)S(1)}, f32[64,1,16,512]{3,0,2,1:T(8,128)S(1)}, f32[64,1,16,512]{3,0,2,1:T(8,128)S(1)}, f32[64,1,16,512]{3,0,2,1:T(8,128)S(1)}) fusion(f32[64,1,16,512]{3,0,2,1:T(8,128)S(1)} %fusion.15, f32[16,512]{1,0:T(8,128)S(1)} %get-tuple-element.57, f32[16,512]{1,0:T(8,128)S(1)} %get-tuple-element.58, ...), kind=kLoop, calls=%fused_computation.60 | loop fusion | flops 2097152 | bytes 10616832 | tf_op jit(solution)/shard_map/mul | solution.py:38
  53.8 2.5 %collective-permute-start.14 = (f32[2,64,64]{2,1,0:T(8,128)S(1)}, f32[2,64,64]{2,1,0:T(8,128)S(1)}, u32[]{:S(2)}, u32[]{:S(2)}) collective-permute-start(f32[2,64,64]{2,1,0:T(8,128)S(1)} %fusion.34), channel_id=1, source_target_pairs={{0,8},{8,0},{16,24},{24,16},{32,40},{40,32},{48,56},{56,48},{64,72... | collective-permute-start | bytes 98312 | tf_op jit(solution)/shard_map/ppermute | solution.py:53
  56.3 1.4 %fusion.19 = f32[64,1,16,512]{3,0,2,1:T(8,128)S(1)} fusion(f32[64,1,16,512]{3,0,2,1:T(8,128)S(1)} %get-tuple-element.30, f32[64,1,16,512]{3,0,2,1:T(8,128)S(1)} %get-tuple-element.29, f32[64,1,16,512]{3,0,2,1:T(8,128)S(1)} %get-tuple-element.28, f32[64,1,16,512]{3,0,2,1:T(8,128)S(1)} %get-tuple-element.27, f32[64,1,16,512]{3,0,2,1:T(8,128)S(1)} %fusion.15, ...), kind=kLoop, calls=%fused_computation.37 | loop fusion | flops 2621440 | bytes 12615680 | tf_op jit(solution)/shard_map/add | solution.py:38
  57.8 2.8 %collective-permute-start.15 = (f32[2,64,64]{2,1,0:T(8,128)S(1)}, f32[2,64,64]{2,1,0:T(8,128)S(1)}, u32[]{:S(2)}, u32[]{:S(2)}) collective-permute-start(f32[2,64,64]{2,1,0:T(8,128)S(1)} %add.266), channel_id=1, source_target_pairs={{0,16},{8,24},{16,0},{24,8},{32,48},{40,56},{48,32},{56,40},{64,80... | collective-permute-start | bytes 98312 | tf_op jit(solution)/shard_map/ppermute | solution.py:53
  60.6 2.7 %collective-permute-done.15 = f32[2,64,64]{2,1,0:T(8,128)S(1)} collective-permute-done((f32[2,64,64]{2,1,0:T(8,128)S(1)}, f32[2,64,64]{2,1,0:T(8,128)S(1)}, u32[]{:S(2)}, u32[]{:S(2)}) %collective-permute-start.15) | collective-permute-done | bytes 32800 | tf_op jit(solution)/shard_map/ppermute | solution.py:53
  63.3 4.1 %collective-permute-start.16 = (f32[2,64,64]{2,1,0:T(8,128)S(1)}, f32[2,64,64]{2,1,0:T(8,128)S(1)}, u32[]{:S(2)}, u32[]{:S(2)}) collective-permute-start(f32[2,64,64]{2,1,0:T(8,128)S(1)} %add.271), channel_id=1, source_target_pairs={{0,32},{8,40},{16,48},{24,56},{32,0},{40,8},{48,16},{56,24},{64,96... | collective-permute-start | bytes 98312 | tf_op jit(solution)/shard_map/ppermute | solution.py:53
  67.3 2.2 %collective-permute-done.16 = f32[2,64,64]{2,1,0:T(8,128)S(1)} collective-permute-done((f32[2,64,64]{2,1,0:T(8,128)S(1)}, f32[2,64,64]{2,1,0:T(8,128)S(1)}, u32[]{:S(2)}, u32[]{:S(2)}) %collective-permute-start.16) | collective-permute-done | bytes 32800 | tf_op jit(solution)/shard_map/ppermute | solution.py:53
  69.6 3.7 %collective-permute-start.17 = (f32[2,64,64]{2,1,0:T(8,128)S(1)}, f32[2,64,64]{2,1,0:T(8,128)S(1)}, u32[]{:S(2)}, u32[]{:S(2)}) collective-permute-start(f32[2,64,64]{2,1,0:T(8,128)S(1)} %add.272), channel_id=1, source_target_pairs={{0,64},{8,72},{16,80},{24,88},{32,96},{40,104},{48,112},{56,120},{... | collective-permute-start | bytes 98312 | tf_op jit(solution)/shard_map/ppermute | solution.py:53
  73.3 2.2 %collective-permute-done.17 = f32[2,64,64]{2,1,0:T(8,128)S(1)} collective-permute-done((f32[2,64,64]{2,1,0:T(8,128)S(1)}, f32[2,64,64]{2,1,0:T(8,128)S(1)}, u32[]{:S(2)}, u32[]{:S(2)}) %collective-permute-start.17) | collective-permute-done | bytes 32800 | tf_op jit(solution)/shard_map/ppermute | solution.py:53
  75.6 0.6 slice_bitcast_fusion
  76.2 0.9 collective-permute-start.18
  77.1 8.2 %shard_map.41 = f32[64,64]{1,0:T(8,128)} custom-call(f32[64,64]{1,0:T(8,128)} %get-tuple-element.65.g_ref), custom_call_target="tpu_custom_call" | custom-call | tf_op jit(solution)/shard_map/pallas_call | solution.py:84
  85.3 0.7 collective-permute-start.26
  86.0 1.1 convolution_bitcast_fusion
  87.0 1.0 fusion.25
  88.4 1.5 %collective-permute-start.19 = (f32[8,1,8,512]{3,2,0,1:T(8,128)S(1)}, f32[8,1,8,512]{3,2,0,1:T(8,128)S(1)}, u32[]{:S(2)}, u32[]{:S(2)}) collective-permute-start(f32[8,1,8,512]{3,2,0,1:T(8,128)S(1)} %bitcast.137), channel_id=1, source_target_pairs={{0,1},{1,2},{2,3},{3,4},{4,5},{5,6},{6,7},{7,0},{8,9},{9,10},{10,1... | collective-permute-start | bytes 393224 | tf_op jit(solution)/shard_map/ppermute | solution.py:109
  89.9 3.3 %collective-permute-start.20 = (f32[8,1,8,512]{3,2,0,1:T(8,128)S(1)}, f32[8,1,8,512]{3,2,0,1:T(8,128)S(1)}, u32[]{:S(2)}, u32[]{:S(2)}) collective-permute-start(f32[8,1,8,512]{3,2,0,1:T(8,128)S(1)} %bitcast.136), channel_id=1, source_target_pairs={{0,2},{1,3},{2,4},{3,5},{4,6},{5,7},{6,0},{7,1},{8,10},{9,11},{10,... | collective-permute-start | bytes 393224 | tf_op jit(solution)/shard_map/ppermute | solution.py:109
  93.3 2.8 %collective-permute-start.21 = (f32[8,1,8,512]{3,2,0,1:T(8,128)S(1)}, f32[8,1,8,512]{3,2,0,1:T(8,128)S(1)}, u32[]{:S(2)}, u32[]{:S(2)}) collective-permute-start(f32[8,1,8,512]{3,2,0,1:T(8,128)S(1)} %bitcast.135), channel_id=1, source_target_pairs={{0,3},{1,4},{2,5},{3,6},{4,7},{5,0},{6,1},{7,2},{8,11},{9,12},{10,... | collective-permute-start | bytes 393224 | tf_op jit(solution)/shard_map/ppermute | solution.py:109
  96.2 1.2 %collective-permute-start.22 = (f32[8,1,8,512]{3,2,0,1:T(8,128)S(1)}, f32[8,1,8,512]{3,2,0,1:T(8,128)S(1)}, u32[]{:S(2)}, u32[]{:S(2)}) collective-permute-start(f32[8,1,8,512]{3,2,0,1:T(8,128)S(1)} %bitcast.134), channel_id=1, source_target_pairs={{0,4},{1,5},{2,6},{3,7},{4,0},{5,1},{6,2},{7,3},{8,12},{9,13},{10,... | collective-permute-start | bytes 393224 | tf_op jit(solution)/shard_map/ppermute | solution.py:109
  97.7 2.5 %collective-permute-start.23 = (f32[8,1,8,512]{3,2,0,1:T(8,128)S(1)}, f32[8,1,8,512]{3,2,0,1:T(8,128)S(1)}, u32[]{:S(2)}, u32[]{:S(2)}) collective-permute-start(f32[8,1,8,512]{3,2,0,1:T(8,128)S(1)} %bitcast.133), channel_id=1, source_target_pairs={{0,5},{1,6},{2,7},{3,0},{4,1},{5,2},{6,3},{7,4},{8,13},{9,14},{10,... | collective-permute-start | bytes 393224 | tf_op jit(solution)/shard_map/ppermute | solution.py:109
  100.1 0.6 add_multiply_fusion
  100.8 3.8 %collective-permute-start.24 = (f32[8,1,8,512]{3,2,0,1:T(8,128)S(1)}, f32[8,1,8,512]{3,2,0,1:T(8,128)S(1)}, u32[]{:S(2)}, u32[]{:S(2)}) collective-permute-start(f32[8,1,8,512]{3,2,0,1:T(8,128)S(1)} %bitcast.132), channel_id=1, source_target_pairs={{0,6},{1,7},{2,0},{3,1},{4,2},{5,3},{6,4},{7,5},{8,14},{9,15},{10,... | collective-permute-start | bytes 393224 | tf_op jit(solution)/shard_map/ppermute | solution.py:109
  104.6 2.4 %collective-permute-start.25 = (f32[8,1,8,512]{3,2,0,1:T(8,128)S(1)}, f32[8,1,8,512]{3,2,0,1:T(8,128)S(1)}, u32[]{:S(2)}, u32[]{:S(2)}) collective-permute-start(f32[8,1,8,512]{3,2,0,1:T(8,128)S(1)} %bitcast.131), channel_id=1, source_target_pairs={{0,7},{1,0},{2,1},{3,2},{4,3},{5,4},{6,5},{7,6},{8,15},{9,8},{10,9... | collective-permute-start | bytes 393224 | tf_op jit(solution)/shard_map/ppermute | solution.py:109
  107.2 2.4 %collective-permute-done.25 = f32[8,1,8,512]{3,2,0,1:T(8,128)S(1)} collective-permute-done((f32[8,1,8,512]{3,2,0,1:T(8,128)S(1)}, f32[8,1,8,512]{3,2,0,1:T(8,128)S(1)}, u32[]{:S(2)}, u32[]{:S(2)}) %collective-permute-start.25) | collective-permute-done | bytes 131104 | tf_op jit(solution)/shard_map/ppermute | solution.py:109
  110.5 1.1 copy.41
  (69 shorter events, 5.0 us)
Async XLA Ops:
  0.6 13.5 %copy-start = (bf16[2,5,1,8,512]{4,3,2,1,0:T(8,128)(2,1)S(1)}, bf16[2,5,1,8,512]{4,3,2,1,0:T(8,128)(2,1)}, u32[]{:S(2)}) copy-start(bf16[2,5,1,8,512]{4,3,2,1,0:T(8,128)(2,1)} %param.5) | copy-start | bytes 245764
  2.1 13.1 %collective-permute-start = (f32[8,1,8,512]{3,2,0,1:T(8,128)S(1)}, f32[8,1,8,512]{3,2,0,1:T(8,128)S(1)}, u32[]{:S(2)}, u32[]{:S(2)}) collective-permute-start(f32[8,1,8,512]{3,2,0,1:T(8,128)S(1)} %get-tuple-element.50), channel_id=1, source_target_pairs={{0,1},{1,2},{2,3},{3,4},{4,5},{5,6},{6,7},{7,0},{8,9},{9,10},{10,1... | collective-permute-start | bytes 393224 | tf_op jit(solution)/shard_map/ppermute | solution.py:109
  3.8 14.7 %collective-permute-start.1 = (f32[8,1,8,512]{3,2,0,1:T(8,128)S(1)}, f32[8,1,8,512]{3,2,0,1:T(8,128)S(1)}, u32[]{:S(2)}, u32[]{:S(2)}) collective-permute-start(f32[8,1,8,512]{3,2,0,1:T(8,128)S(1)} %get-tuple-element.49), channel_id=1, source_target_pairs={{0,2},{1,3},{2,4},{3,5},{4,6},{5,7},{6,0},{7,1},{8,10},{9,11},{10,... | collective-permute-start | bytes 393224 | tf_op jit(solution)/shard_map/ppermute | solution.py:109
  6.5 13.8 %collective-permute-start.2 = (f32[8,1,8,512]{3,2,0,1:T(8,128)S(1)}, f32[8,1,8,512]{3,2,0,1:T(8,128)S(1)}, u32[]{:S(2)}, u32[]{:S(2)}) collective-permute-start(f32[8,1,8,512]{3,2,0,1:T(8,128)S(1)} %get-tuple-element.48), channel_id=1, source_target_pairs={{0,3},{1,4},{2,5},{3,6},{4,7},{5,0},{6,1},{7,2},{8,11},{9,12},{10,... | collective-permute-start | bytes 393224 | tf_op jit(solution)/shard_map/ppermute | solution.py:109
  10.5 11.1 %collective-permute-start.3 = (f32[8,1,8,512]{3,2,0,1:T(8,128)S(1)}, f32[8,1,8,512]{3,2,0,1:T(8,128)S(1)}, u32[]{:S(2)}, u32[]{:S(2)}) collective-permute-start(f32[8,1,8,512]{3,2,0,1:T(8,128)S(1)} %get-tuple-element.47), channel_id=1, source_target_pairs={{0,4},{1,5},{2,6},{3,7},{4,0},{5,1},{6,2},{7,3},{8,12},{9,13},{10,... | collective-permute-start | bytes 393224 | tf_op jit(solution)/shard_map/ppermute | solution.py:109
  10.9 12.1 %collective-permute-start.4 = (f32[8,1,8,512]{3,2,1,0:T(8,128)S(1)}, f32[8,1,8,512]{3,2,1,0:T(8,128)S(1)}, u32[]{:S(2)}, u32[]{:S(2)}) collective-permute-start(f32[8,1,8,512]{3,2,1,0:T(8,128)S(1)} %get-tuple-element.51), channel_id=1, source_target_pairs={{0,5},{1,6},{2,7},{3,0},{4,1},{5,2},{6,3},{7,4},{8,13},{9,14},{10,... | collective-permute-start | bytes 393224 | tf_op jit(solution)/shard_map/ppermute | solution.py:109
  15.1 7.8 %collective-permute-start.5 = (f32[8,1,8,512]{3,2,0,1:T(8,128)S(1)}, f32[8,1,8,512]{3,2,0,1:T(8,128)S(1)}, u32[]{:S(2)}, u32[]{:S(2)}) collective-permute-start(f32[8,1,8,512]{3,2,0,1:T(8,128)S(1)} %get-tuple-element.46), channel_id=1, source_target_pairs={{0,6},{1,7},{2,0},{3,1},{4,2},{5,3},{6,4},{7,5},{8,14},{9,15},{10,... | collective-permute-start | bytes 393224 | tf_op jit(solution)/shard_map/ppermute | solution.py:109
  18.4 5.1 %collective-permute-start.6 = (f32[8,1,8,512]{3,2,0,1:T(8,128)S(1)}, f32[8,1,8,512]{3,2,0,1:T(8,128)S(1)}, u32[]{:S(2)}, u32[]{:S(2)}) collective-permute-start(f32[8,1,8,512]{3,2,0,1:T(8,128)S(1)} %get-tuple-element.45), channel_id=1, source_target_pairs={{0,7},{1,0},{2,1},{3,2},{4,3},{5,4},{6,5},{7,6},{8,15},{9,8},{10,9... | collective-permute-start | bytes 393224 | tf_op jit(solution)/shard_map/ppermute | solution.py:109
  20.3 10.8 %collective-permute-start.8 = (bf16[2,5,1,4,512]{4,3,2,1,0:T(4,128)(2,1)S(1)}, bf16[2,5,1,4,512]{4,3,2,1,0:T(4,128)(2,1)S(1)}, u32[]{:S(2)}, u32[]{:S(2)}) collective-permute-start(bf16[2,5,1,4,512]{4,3,2,1,0:T(4,128)(2,1)S(1)} %get-tuple-element.62), channel_id=1, source_target_pairs={{0,8},{8,16},{16,24},{24,32},{32,40},{40,48},{48,56},{56,64},{64,7... | collective-permute-start | bytes 122888 | tf_op jit(solution)/shard_map/ppermute | solution.py:16
  21.6 9.5 %collective-permute-start.9 = (bf16[2,5,1,4,512]{4,3,2,1,0:T(4,128)(2,1)S(1)}, bf16[2,5,1,4,512]{4,3,2,1,0:T(4,128)(2,1)S(1)}, u32[]{:S(2)}, u32[]{:S(2)}) collective-permute-start(bf16[2,5,1,4,512]{4,3,2,1,0:T(4,128)(2,1)S(1)} %get-tuple-element.63), channel_id=1, source_target_pairs={{8,0},{16,8},{24,16},{32,24},{40,32},{48,40},{56,48},{64,56},{72,6... | collective-permute-start | bytes 122888 | tf_op jit(solution)/shard_map/ppermute | solution.py:17
  25.1 12.2 %collective-permute-start.10 = (f32[64,1,4,512]{3,0,2,1:T(8,128)S(1)}, f32[64,1,4,512]{3,0,2,1:T(8,128)S(1)}, u32[]{:S(2)}, u32[]{:S(2)}) collective-permute-start(f32[64,1,4,512]{3,0,2,1:T(8,128)S(1)} %get-tuple-element.43), channel_id=1, source_target_pairs={{0,8},{8,16},{16,24},{24,32},{32,40},{40,48},{48,56},{56,64},{64,7... | collective-permute-start | bytes 1572872 | tf_op jit(solution)/shard_map/ppermute | solution.py:16
  29.8 7.5 %collective-permute-start.11 = (f32[64,1,4,512]{3,0,2,1:T(8,128)S(1)}, f32[64,1,4,512]{3,0,2,1:T(8,128)S(1)}, u32[]{:S(2)}, u32[]{:S(2)}) collective-permute-start(f32[64,1,4,512]{3,0,2,1:T(8,128)S(1)} %get-tuple-element.44), channel_id=1, source_target_pairs={{8,0},{16,8},{24,16},{32,24},{40,32},{48,40},{56,48},{64,56},{72,6... | collective-permute-start | bytes 1572872 | tf_op jit(solution)/shard_map/ppermute | solution.py:17
  33.3 4.0 %collective-permute-start.7 = (f32[64,64]{1,0:T(8,128)S(1)}, f32[64,64]{1,0:T(8,128)S(1)}, u32[]{:S(2)}, u32[]{:S(2)}) collective-permute-start(f32[64,64]{1,0:T(8,128)S(1)} %convolution_bitcast_fusion.2), channel_id=1, source_target_pairs={{0,1},{1,0},{2,3},{3,2},{4,5},{5,4},{6,7},{7,6},{8,9},{9,8},{10,11... | collective-permute-start | bytes 49160 | tf_op jit(solution)/shard_map/ppermute | solution.py:53
  38.8 5.5 %collective-permute-start.12 = (f32[64,64]{1,0:T(8,128)S(1)}, f32[64,64]{1,0:T(8,128)S(1)}, u32[]{:S(2)}, u32[]{:S(2)}) collective-permute-start(f32[64,64]{1,0:T(8,128)S(1)} %add.251), channel_id=1, source_target_pairs={{0,2},{1,3},{2,0},{3,1},{4,6},{5,7},{6,4},{7,5},{8,10},{9,11},{10,... | collective-permute-start | bytes 49160 | tf_op jit(solution)/shard_map/ppermute | solution.py:53
  46.6 6.0 %collective-permute-start.13 = (f32[2,64,64]{2,1,0:T(8,128)S(1)}, f32[2,64,64]{2,1,0:T(8,128)S(1)}, u32[]{:S(2)}, u32[]{:S(2)}) collective-permute-start(f32[2,64,64]{2,1,0:T(8,128)S(1)} %pad_maximum_fusion.1), channel_id=1, source_target_pairs={{0,4},{1,5},{2,6},{3,7},{4,0},{5,1},{6,2},{7,3},{8,12},{9,13},{10,... | collective-permute-start | bytes 98312 | tf_op jit(solution)/shard_map/ppermute | solution.py:53
  53.8 3.9 %collective-permute-start.14 = (f32[2,64,64]{2,1,0:T(8,128)S(1)}, f32[2,64,64]{2,1,0:T(8,128)S(1)}, u32[]{:S(2)}, u32[]{:S(2)}) collective-permute-start(f32[2,64,64]{2,1,0:T(8,128)S(1)} %fusion.34), channel_id=1, source_target_pairs={{0,8},{8,0},{16,24},{24,16},{32,40},{40,32},{48,56},{56,48},{64,72... | collective-permute-start | bytes 98312 | tf_op jit(solution)/shard_map/ppermute | solution.py:53
  57.8 5.5 %collective-permute-start.15 = (f32[2,64,64]{2,1,0:T(8,128)S(1)}, f32[2,64,64]{2,1,0:T(8,128)S(1)}, u32[]{:S(2)}, u32[]{:S(2)}) collective-permute-start(f32[2,64,64]{2,1,0:T(8,128)S(1)} %add.266), channel_id=1, source_target_pairs={{0,16},{8,24},{16,0},{24,8},{32,48},{40,56},{48,32},{56,40},{64,80... | collective-permute-start | bytes 98312 | tf_op jit(solution)/shard_map/ppermute | solution.py:53
  63.3 6.3 %collective-permute-start.16 = (f32[2,64,64]{2,1,0:T(8,128)S(1)}, f32[2,64,64]{2,1,0:T(8,128)S(1)}, u32[]{:S(2)}, u32[]{:S(2)}) collective-permute-start(f32[2,64,64]{2,1,0:T(8,128)S(1)} %add.271), channel_id=1, source_target_pairs={{0,32},{8,40},{16,48},{24,56},{32,0},{40,8},{48,16},{56,24},{64,96... | collective-permute-start | bytes 98312 | tf_op jit(solution)/shard_map/ppermute | solution.py:53
  69.6 6.0 %collective-permute-start.17 = (f32[2,64,64]{2,1,0:T(8,128)S(1)}, f32[2,64,64]{2,1,0:T(8,128)S(1)}, u32[]{:S(2)}, u32[]{:S(2)}) collective-permute-start(f32[2,64,64]{2,1,0:T(8,128)S(1)} %add.272), channel_id=1, source_target_pairs={{0,64},{8,72},{16,80},{24,88},{32,96},{40,104},{48,112},{56,120},{... | collective-permute-start | bytes 98312 | tf_op jit(solution)/shard_map/ppermute | solution.py:53
  76.2 9.0 %collective-permute-start.18 = (f32[64,64]{1,0:T(8,128)S(1)}, f32[64,64]{1,0:T(8,128)S(1)}, u32[]{:S(2)}, u32[]{:S(2)}) collective-permute-start(f32[64,64]{1,0:T(8,128)S(1)} %get-tuple-element.64), channel_id=1, source_target_pairs={{0,1},{1,0},{2,3},{3,2},{4,5},{5,4},{6,7},{7,6},{8,9},{9,8},{10,11... | collective-permute-start | bytes 49160 | tf_op jit(solution)/shard_map/ppermute | solution.py:53
  85.3 12.4 %collective-permute-start.26 = (f32[64,64]{1,0:T(8,128)S(1)}, f32[64,64]{1,0:T(8,128)S(1)}, u32[]{:S(2)}, u32[]{:S(2)}) collective-permute-start(f32[64,64]{1,0:T(8,128)S(1)} %fusion.33), channel_id=1, source_target_pairs={{0,2},{1,3},{2,0},{3,1},{4,6},{5,7},{6,4},{7,5},{8,10},{9,11},{10,... | collective-permute-start | bytes 49160 | tf_op jit(solution)/shard_map/ppermute | solution.py:53
  88.4 12.4 %collective-permute-start.19 = (f32[8,1,8,512]{3,2,0,1:T(8,128)S(1)}, f32[8,1,8,512]{3,2,0,1:T(8,128)S(1)}, u32[]{:S(2)}, u32[]{:S(2)}) collective-permute-start(f32[8,1,8,512]{3,2,0,1:T(8,128)S(1)} %bitcast.137), channel_id=1, source_target_pairs={{0,1},{1,2},{2,3},{3,4},{4,5},{5,6},{6,7},{7,0},{8,9},{9,10},{10,1... | collective-permute-start | bytes 393224 | tf_op jit(solution)/shard_map/ppermute | solution.py:109
  89.9 14.7 %collective-permute-start.20 = (f32[8,1,8,512]{3,2,0,1:T(8,128)S(1)}, f32[8,1,8,512]{3,2,0,1:T(8,128)S(1)}, u32[]{:S(2)}, u32[]{:S(2)}) collective-permute-start(f32[8,1,8,512]{3,2,0,1:T(8,128)S(1)} %bitcast.136), channel_id=1, source_target_pairs={{0,2},{1,3},{2,4},{3,5},{4,6},{5,7},{6,0},{7,1},{8,10},{9,11},{10,... | collective-permute-start | bytes 393224 | tf_op jit(solution)/shard_map/ppermute | solution.py:109
  93.3 13.8 %collective-permute-start.21 = (f32[8,1,8,512]{3,2,0,1:T(8,128)S(1)}, f32[8,1,8,512]{3,2,0,1:T(8,128)S(1)}, u32[]{:S(2)}, u32[]{:S(2)}) collective-permute-start(f32[8,1,8,512]{3,2,0,1:T(8,128)S(1)} %bitcast.135), channel_id=1, source_target_pairs={{0,3},{1,4},{2,5},{3,6},{4,7},{5,0},{6,1},{7,2},{8,11},{9,12},{10,... | collective-permute-start | bytes 393224 | tf_op jit(solution)/shard_map/ppermute | solution.py:109
  96.2 11.0 %collective-permute-start.22 = (f32[8,1,8,512]{3,2,0,1:T(8,128)S(1)}, f32[8,1,8,512]{3,2,0,1:T(8,128)S(1)}, u32[]{:S(2)}, u32[]{:S(2)}) collective-permute-start(f32[8,1,8,512]{3,2,0,1:T(8,128)S(1)} %bitcast.134), channel_id=1, source_target_pairs={{0,4},{1,5},{2,6},{3,7},{4,0},{5,1},{6,2},{7,3},{8,12},{9,13},{10,... | collective-permute-start | bytes 393224 | tf_op jit(solution)/shard_map/ppermute | solution.py:109
  97.7 9.5 %collective-permute-start.23 = (f32[8,1,8,512]{3,2,0,1:T(8,128)S(1)}, f32[8,1,8,512]{3,2,0,1:T(8,128)S(1)}, u32[]{:S(2)}, u32[]{:S(2)}) collective-permute-start(f32[8,1,8,512]{3,2,0,1:T(8,128)S(1)} %bitcast.133), channel_id=1, source_target_pairs={{0,5},{1,6},{2,7},{3,0},{4,1},{5,2},{6,3},{7,4},{8,13},{9,14},{10,... | collective-permute-start | bytes 393224 | tf_op jit(solution)/shard_map/ppermute | solution.py:109
  100.8 6.5 %collective-permute-start.24 = (f32[8,1,8,512]{3,2,0,1:T(8,128)S(1)}, f32[8,1,8,512]{3,2,0,1:T(8,128)S(1)}, u32[]{:S(2)}, u32[]{:S(2)}) collective-permute-start(f32[8,1,8,512]{3,2,0,1:T(8,128)S(1)} %bitcast.132), channel_id=1, source_target_pairs={{0,6},{1,7},{2,0},{3,1},{4,2},{5,3},{6,4},{7,5},{8,14},{9,15},{10,... | collective-permute-start | bytes 393224 | tf_op jit(solution)/shard_map/ppermute | solution.py:109
  104.6 5.0 %collective-permute-start.25 = (f32[8,1,8,512]{3,2,0,1:T(8,128)S(1)}, f32[8,1,8,512]{3,2,0,1:T(8,128)S(1)}, u32[]{:S(2)}, u32[]{:S(2)}) collective-permute-start(f32[8,1,8,512]{3,2,0,1:T(8,128)S(1)} %bitcast.131), channel_id=1, source_target_pairs={{0,7},{1,0},{2,1},{3,2},{4,3},{5,4},{6,5},{7,6},{8,15},{9,8},{10,9... | collective-permute-start | bytes 393224 | tf_op jit(solution)/shard_map/ppermute | solution.py:109

commit v14 on v9

--- a/solution.py
+++ b/solution.py
@@ -125,7 +125,7 @@
 
     field = halo(v, width, 2)
     for step in range(STEPS):
-        gram, field = tick(gram, forward_step(field, coeffs[step]))
+        field = forward_step(field, coeffs[step])
     flat_z = field[:, :, width : width + rows, :].reshape(members, -1)
     cross = jnp.dot(flat_z, flat_z.T, precision=hi)
     both = jnp.stack([gram, cross])

time: 108 us -> 110 us (1.019)
  waiting for transfers between devices: 42.5 us -> 48.8 us
  starting transfers between devices: 35.8 us -> 32.5 us
    all_to_all x1, waiting for transfers between devices: 1.09 us -> 14 us  [body(): ritz = lax.all_to_all(ritz.reshape(v.shape), 'mem', 0, 1, tiled=True)]
    ppermute x9 -> x7, waiting for transfers between devices: 27 us -> 17.9 us  [exchange(): return x + lax.ppermute(x, axis, [(i, i ^ bit) for i in range(count)])]
    ppermute x9 -> x7, starting transfers between devices: 19.2 us -> 16.2 us  [exchange(): return x + lax.ppermute(x, axis, [(i, i ^ bit) for i in range(count)])]
    ppermute x2, waiting for transfers between devices: 0.01 us -> 2.56 us  [halo(): lax.ppermute(lax.slice_in_dim(block, 0, width, axis=dim), 'dom', backward)]
    add x2 -> x1, other arithmetic: 2.56 us -> 1.29 us  [forward_step(): result + coef[3] * shifted(field, -1, 3) + coef[4] * shifted(field, 1, 3)]
  transfers between devices with their start and end apart: 15 -> 13, of which waited for: 9 -> 10; matrix products, arithmetic and copies ran while one was open for 7% -> 6% of each run, Pallas kernels for 8% -> 0%
where the time goes in v14:
time: 110 us
  waiting for transfers between devices  48.8 us (44%)
  starting transfers between devices  32.5 us (30%)
  other arithmetic  8.91 us (8%)
  Pallas kernels  8.15 us (7%)
  local copies, waits for them, and re-layouts  6.31 us (6%)
  matrix products  4.01 us (4%)
    ppermute x7, waiting for transfers between devices, exchange(): return x + lax.ppermute(x, axis, [(i, i ^ bit) for i in range(count)])  17.9 us
    ppermute x7, starting transfers between devices, exchange(): return x + lax.ppermute(x, axis, [(i, i ^ bit) for i in range(count)])  16.2 us
    all_to_all x1, waiting for transfers between devices, body(): v = lax.all_to_all(perturbations, 'mem', 1, 0, tiled=True)  14.4 us
    all_to_all x1, waiting for transfers between devices, body(): ritz = lax.all_to_all(ritz.reshape(v.shape), 'mem', 0, 1, tiled=True)  14 us
    pallas_call x1, Pallas kernels, lower_inverse(): pl.pallas_call(chol_inv_kernel, out_shape=jax.ShapeDtypeStruct((n, n), jn...  8.15 us
    all_to_all x1, starting transfers between devices, body(): v = lax.all_to_all(perturbations, 'mem', 1, 0, tiled=True)  7.04 us
    all_to_all x1, starting transfers between devices, body(): ritz = lax.all_to_all(ritz.reshape(v.shape), 'mem', 0, 1, tiled=True)  3.56 us
    ppermute x2, starting transfers between devices, halo(): lax.ppermute(lax.slice_in_dim(block, size - width, size, axis=dim), 'dom'...  3.12 us
  transfers between devices with their start and end apart: 13, of which 10 were waited for; matrix products, arithmetic and copies ran while one was open for 6% of the time, Pallas kernels for 0%

profile of v14, /device:TPU:0, one launch (start us, length us, event | category | flops | bytes accessed | tf_op | source)
XLA Modules:
  0.0 109.5 jit_solution(9399156069535397155)
XLA Ops:
  0.6 0.0 copy-start
  0.6 2.3 %copy.11 = f32[8,8,8,512]{3,2,0,1:T(8,128)} copy(f32[8,8,8,512]{3,2,1,0:T(8,128)} %param.2) | data formatting | bytes 2097152 | tf_op args[0]
  3.0 7.0 %all-to-all-start = ((f32[8,8,8,512]{3,2,0,1:T(8,128)}), f32[8,8,8,512]{3,2,0,1:T(8,128)S(1)}, u32[]{:S(2)}, u32[]{:S(2)}) async-start(f32[8,8,8,512]{3,2,0,1:T(8,128)} %copy.11), calls=%async_computation | async-start | bytes 2097152 | tf_op jit(solution)/shard_map/all_to_all | solution.py:105
  10.0 1.5 %collective-permute-start = (bf16[2,5,1,4,512]{4,3,2,1,0:T(4,128)(2,1)S(1)}, bf16[2,5,1,4,512]{4,3,2,1,0:T(4,128)(2,1)S(1)}, u32[]{:S(2)}, u32[]{:S(2)}) collective-permute-start(bf16[2,5,1,4,512]{4,3,2,1,0:T(4,128)(2,1)S(1)} %get-tuple-element.35), channel_id=1, source_target_pairs={{0,8},{8,16},{16,24},{24,32},{32,40},{40,48},{48,56},{56,64},{64,7... | collective-permute-start | bytes 122888 | tf_op jit(solution)/shard_map/ppermute | solution.py:16
  11.5 1.3 %collective-permute-start.1 = (bf16[2,5,1,4,512]{4,3,2,1,0:T(4,128)(2,1)S(1)}, bf16[2,5,1,4,512]{4,3,2,1,0:T(4,128)(2,1)S(1)}, u32[]{:S(2)}, u32[]{:S(2)}) collective-permute-start(bf16[2,5,1,4,512]{4,3,2,1,0:T(4,128)(2,1)S(1)} %get-tuple-element.36), channel_id=1, source_target_pairs={{8,0},{16,8},{24,16},{32,24},{40,32},{48,40},{56,48},{64,56},{72,6... | collective-permute-start | bytes 122888 | tf_op jit(solution)/shard_map/ppermute | solution.py:17
  12.8 14.4 %all-to-all-done = f32[8,8,8,512]{3,2,0,1:T(8,128)S(1)} async-done(((f32[8,8,8,512]{3,2,0,1:T(8,128)}), f32[8,8,8,512]{3,2,0,1:T(8,128)S(1)}, u32[]{:S(2)}, u32[]{:S(2)}) %all-to-all-start) | async-done | bytes 1048608 | tf_op jit(solution)/shard_map/all_to_all | solution.py:105
  27.2 0.6 copy.31
  27.8 0.1 fusion.29
  27.9 1.7 %collective-permute-start.2 = (f32[64,1,4,512]{3,0,2,1:T(8,128)S(1)}, f32[64,1,4,512]{3,0,2,1:T(8,128)S(1)}, u32[]{:S(2)}, u32[]{:S(2)}) collective-permute-start(f32[64,1,4,512]{3,0,2,1:T(8,128)S(1)} %get-tuple-element.23), channel_id=1, source_target_pairs={{0,8},{8,16},{16,24},{24,32},{32,40},{40,48},{48,56},{56,64},{64,7... | collective-permute-start | bytes 1572872 | tf_op jit(solution)/shard_map/ppermute | solution.py:16
  29.6 1.3 %collective-permute-start.3 = (f32[64,1,4,512]{3,0,2,1:T(8,128)S(1)}, f32[64,1,4,512]{3,0,2,1:T(8,128)S(1)}, u32[]{:S(2)}, u32[]{:S(2)}) collective-permute-start(f32[64,1,4,512]{3,0,2,1:T(8,128)S(1)} %get-tuple-element.24), channel_id=1, source_target_pairs={{8,0},{16,8},{24,16},{32,24},{40,32},{48,40},{56,48},{64,56},{72,6... | collective-permute-start | bytes 1572872 | tf_op jit(solution)/shard_map/ppermute | solution.py:17
  30.9 0.0 collective-permute-done
  30.9 0.0 collective-permute-done.1
  30.9 0.1 maximum_convert_fusion
  31.0 0.6 copy.18
  31.6 1.0 convolution_bitcast_fusion.3
  32.6 0.0 collective-permute-done.2
  32.6 2.6 %collective-permute-done.3 = f32[64,1,4,512]{3,0,2,1:T(8,128)S(1)} collective-permute-done((f32[64,1,4,512]{3,0,2,1:T(8,128)S(1)}, f32[64,1,4,512]{3,0,2,1:T(8,128)S(1)}, u32[]{:S(2)}, u32[]{:S(2)}) %collective-permute-start.3) | collective-permute-done | bytes 524320 | tf_op jit(solution)/shard_map/ppermute | solution.py:17
  35.2 0.2 pad_maximum_fusion
  35.4 1.3 %fusion.4 = f32[64,1,16,512]{3,0,2,1:T(8,128)S(1)} fusion(f32[64,1,16,512]{3,0,2,1:T(8,128)S(1)} %pad_maximum_fusion, f32[16,512]{1,0:T(8,128)S(1)} %get-tuple-element.30, f32[16,512]{1,0:T(8,128)S(1)} %get-tuple-element.31, f32[16,512]{1,0:T(8,128)S(1)} %get-tuple-element.32, f32[16,512]{1,0:T(8,128)S(1)} %get-tuple-element.33, ...), kind=kLoop, calls=%fused_computation.20 | loop fusion | flops 4718592 | bytes 4358144 | tf_op jit(solution)/shard_map/add | solution.py:33
  36.7 1.3 %broadcast_multiply_fusion = (f32[64,1,16,512]{3,0,2,1:T(8,128)S(1)}, f32[64,1,16,512]{3,0,2,1:T(8,128)S(1)}) fusion(f32[16,512]{1,0:T(8,128)S(1)} %get-tuple-element.26, f32[64,1,16,512]{3,0,2,1:T(8,128)S(1)} %fusion.4, f32[16,512]{1,0:T(8,128)S(1)} %get-tuple-element.27, f32[16,512]{1,0:T(8,128)S(1)} %get-tuple-element.28, ...), kind=kLoop, calls=%fused_computation.50 | loop fusion | flops 5242880 | bytes 6455296 | tf_op jit(solution)/shard_map/mul | solution.py:38
  38.0 1.0 convolution_bitcast_fusion.2
  39.0 0.6 broadcast_multiply_fusion.1
  39.6 0.9 collective-permute-start.4
  40.5 1.4 %fusion.15 = f32[64,1,16,512]{3,0,2,1:T(8,128)S(1)} fusion(f32[64,1,16,512]{3,0,2,1:T(8,128)S(1)} %get-tuple-element.22, f32[64,1,16,512]{3,0,2,1:T(8,128)S(1)} %get-tuple-element.21, f32[64,1,16,512]{3,0,2,1:T(8,128)S(1)} %get-tuple-element.20, f32[64,1,16,512]{3,0,2,1:T(8,128)S(1)} %get-tuple-element.14, f32[64,1,16,512]{3,0,2,1:T(8,128)S(1)} %get-tuple-element.15, ...), kind=kLoop, calls=%fused_computation.31 | loop fusion | flops 2621440 | bytes 12615680 | tf_op jit(solution)/shard_map/add | solution.py:38
  42.0 2.0 %collective-permute-done.4 = f32[2,64,64]{2,1,0:T(8,128)S(1)} collective-permute-done((f32[2,64,64]{2,1,0:T(8,128)S(1)}, f32[2,64,64]{2,1,0:T(8,128)S(1)}, u32[]{:S(2)}, u32[]{:S(2)}) %collective-permute-start.4) | collective-permute-done | bytes 32800 | tf_op jit(solution)/shard_map/ppermute | solution.py:53
  44.0 0.9 collective-permute-start.5
  44.9 1.2 %broadcast_multiply_fusion.4 = (f32[64,1,16,512]{3,0,2,1:T(8,128)S(1)}, f32[64,1,16,512]{3,0,2,1:T(8,128)S(1)}, f32[64,1,16,512]{3,0,2,1:T(8,128)S(1)}, f32[64,1,16,512]{3,0,2,1:T(8,128)S(1)}) fusion(f32[64,1,16,512]{3,0,2,1:T(8,128)S(1)} %fusion.15, f32[16,512]{1,0:T(8,128)S(1)} %get-tuple-element.30, f32[16,512]{1,0:T(8,128)S(1)} %get-tuple-element.31, ...), kind=kLoop, calls=%fused_computation.54 | loop fusion | flops 2097152 | bytes 10616832 | tf_op jit(solution)/shard_map/mul | solution.py:38
  46.1 1.4 %fusion.19 = f32[64,1,16,512]{3,0,2,1:T(8,128)S(1)} fusion(f32[64,1,16,512]{3,0,2,1:T(8,128)S(1)} %get-tuple-element.19, f32[64,1,16,512]{3,0,2,1:T(8,128)S(1)} %get-tuple-element.18, f32[64,1,16,512]{3,0,2,1:T(8,128)S(1)} %get-tuple-element.17, f32[64,1,16,512]{3,0,2,1:T(8,128)S(1)} %get-tuple-element.16, f32[64,1,16,512]{3,0,2,1:T(8,128)S(1)} %fusion.15, ...), kind=kLoop, calls=%fused_computation.35 | loop fusion | flops 2621440 | bytes 12615680 | tf_op jit(solution)/shard_map/add | solution.py:38
  47.6 2.6 %collective-permute-done.5 = f32[2,64,64]{2,1,0:T(8,128)S(1)} collective-permute-done((f32[2,64,64]{2,1,0:T(8,128)S(1)}, f32[2,64,64]{2,1,0:T(8,128)S(1)}, u32[]{:S(2)}, u32[]{:S(2)}) %collective-permute-start.5) | collective-permute-done | bytes 32800 | tf_op jit(solution)/shard_map/ppermute | solution.py:53
  50.2 0.3 collective-permute-start.6
  50.5 5.5 %collective-permute-done.6 = f32[2,64,64]{2,1,0:T(8,128)S(1)} collective-permute-done((f32[2,64,64]{2,1,0:T(8,128)S(1)}, f32[2,64,64]{2,1,0:T(8,128)S(1)}, u32[]{:S(2)}, u32[]{:S(2)}) %collective-permute-start.6) | collective-permute-done | bytes 32800 | tf_op jit(solution)/shard_map/ppermute | solution.py:53
  56.0 3.9 %collective-permute-start.7 = (f32[2,64,64]{2,1,0:T(8,128)S(1)}, f32[2,64,64]{2,1,0:T(8,128)S(1)}, u32[]{:S(2)}, u32[]{:S(2)}) collective-permute-start(f32[2,64,64]{2,1,0:T(8,128)S(1)} %add.119), channel_id=1, source_target_pairs={{0,8},{8,0},{16,24},{24,16},{32,40},{40,32},{48,56},{56,48},{64,72... | collective-permute-start | bytes 98312 | tf_op jit(solution)/shard_map/ppermute | solution.py:53
  60.0 0.9 collective-permute-done.7
  60.9 4.0 %collective-permute-start.8 = (f32[2,64,64]{2,1,0:T(8,128)S(1)}, f32[2,64,64]{2,1,0:T(8,128)S(1)}, u32[]{:S(2)}, u32[]{:S(2)}) collective-permute-start(f32[2,64,64]{2,1,0:T(8,128)S(1)} %add.120), channel_id=1, source_target_pairs={{0,16},{8,24},{16,0},{24,8},{32,48},{40,56},{48,32},{56,40},{64,80... | collective-permute-start | bytes 98312 | tf_op jit(solution)/shard_map/ppermute | solution.py:53
  64.8 2.4 %collective-permute-done.8 = f32[2,64,64]{2,1,0:T(8,128)S(1)} collective-permute-done((f32[2,64,64]{2,1,0:T(8,128)S(1)}, f32[2,64,64]{2,1,0:T(8,128)S(1)}, u32[]{:S(2)}, u32[]{:S(2)}) %collective-permute-start.8) | collective-permute-done | bytes 32800 | tf_op jit(solution)/shard_map/ppermute | solution.py:53
  67.3 3.8 %collective-permute-start.9 = (f32[2,64,64]{2,1,0:T(8,128)S(1)}, f32[2,64,64]{2,1,0:T(8,128)S(1)}, u32[]{:S(2)}, u32[]{:S(2)}) collective-permute-start(f32[2,64,64]{2,1,0:T(8,128)S(1)} %add.121), channel_id=1, source_target_pairs={{0,32},{8,40},{16,48},{24,56},{32,0},{40,8},{48,16},{56,24},{64,96... | collective-permute-start | bytes 98312 | tf_op jit(solution)/shard_map/ppermute | solution.py:53
  71.0 2.2 %collective-permute-done.9 = f32[2,64,64]{2,1,0:T(8,128)S(1)} collective-permute-done((f32[2,64,64]{2,1,0:T(8,128)S(1)}, f32[2,64,64]{2,1,0:T(8,128)S(1)}, u32[]{:S(2)}, u32[]{:S(2)}) %collective-permute-start.9) | collective-permute-done | bytes 32800 | tf_op jit(solution)/shard_map/ppermute | solution.py:53
  73.3 2.3 %collective-permute-start.10 = (f32[2,64,64]{2,1,0:T(8,128)S(1)}, f32[2,64,64]{2,1,0:T(8,128)S(1)}, u32[]{:S(2)}, u32[]{:S(2)}) collective-permute-start(f32[2,64,64]{2,1,0:T(8,128)S(1)} %add.122), channel_id=1, source_target_pairs={{0,64},{8,72},{16,80},{24,88},{32,96},{40,104},{48,112},{56,120},{... | collective-permute-start | bytes 98312 | tf_op jit(solution)/shard_map/ppermute | solution.py:53
  75.6 2.2 %collective-permute-done.10 = f32[2,64,64]{2,1,0:T(8,128)S(1)} collective-permute-done((f32[2,64,64]{2,1,0:T(8,128)S(1)}, f32[2,64,64]{2,1,0:T(8,128)S(1)}, u32[]{:S(2)}, u32[]{:S(2)}) %collective-permute-start.10) | collective-permute-done | bytes 32800 | tf_op jit(solution)/shard_map/ppermute | solution.py:53
  77.9 0.6 slice_bitcast_fusion.2
  78.5 8.2 %shard_map.41 = f32[64,64]{1,0:T(8,128)} custom-call(f32[64,64]{1,0:T(8,128)} %get-tuple-element.38.g_ref), custom_call_target="tpu_custom_call" | custom-call | tf_op jit(solution)/shard_map/pallas_call | solution.py:84
  86.6 1.1 convolution_bitcast_fusion.1
  87.7 1.0 convolution_bitcast_fusion
  88.7 1.6 %copy.15 = f32[64,1,8,512]{3,2,1,0:T(8,128)} copy(f32[64,1,8,512]{3,0,2,1:T(8,128)S(1)} %convolution_bitcast_fusion) | data formatting | bytes 2097152 | tf_op jit(solution)/shard_map/dot_general | solution.py:141
  90.3 3.6 %all-to-all-start.1 = ((f32[64,1,8,512]{3,2,1,0:T(8,128)}), f32[64,1,8,512]{3,2,1,0:T(8,128)S(1)}, u32[]{:S(2)}, u32[]{:S(2)}) async-start(f32[64,1,8,512]{3,2,1,0:T(8,128)} %copy.15), calls=%async_computation.1 | async-start | bytes 2097152 | tf_op jit(solution)/shard_map/all_to_all | solution.py:145
  93.9 0.6 broadcast_multiply_fusion.8
  94.5 14.0 %all-to-all-done.1 = f32[64,1,8,512]{3,2,1,0:T(8,128)S(1)} async-done(((f32[64,1,8,512]{3,2,1,0:T(8,128)}), f32[64,1,8,512]{3,2,1,0:T(8,128)S(1)}, u32[]{:S(2)}, u32[]{:S(2)}) %all-to-all-start.1) | async-done | bytes 1048608 | tf_op jit(solution)/shard_map/all_to_all | solution.py:145
  108.5 1.1 copy.30
  (11 shorter events, 0.1 us)
Async XLA Ops:
  0.6 9.4 %copy-start = (bf16[2,5,1,8,512]{4,3,2,1,0:T(8,128)(2,1)S(1)}, bf16[2,5,1,8,512]{4,3,2,1,0:T(8,128)(2,1)}, u32[]{:S(2)}) copy-start(bf16[2,5,1,8,512]{4,3,2,1,0:T(8,128)(2,1)} %param.3) | copy-start | bytes 245764
  3.0 24.2 %all-to-all-start = ((f32[8,8,8,512]{3,2,0,1:T(8,128)}), f32[8,8,8,512]{3,2,0,1:T(8,128)S(1)}, u32[]{:S(2)}, u32[]{:S(2)}) async-start(f32[8,8,8,512]{3,2,0,1:T(8,128)} %copy.11), calls=%async_computation | async-start | bytes 2097152 | tf_op jit(solution)/shard_map/all_to_all | solution.py:105
  10.0 20.8 %collective-permute-start = (bf16[2,5,1,4,512]{4,3,2,1,0:T(4,128)(2,1)S(1)}, bf16[2,5,1,4,512]{4,3,2,1,0:T(4,128)(2,1)S(1)}, u32[]{:S(2)}, u32[]{:S(2)}) collective-permute-start(bf16[2,5,1,4,512]{4,3,2,1,0:T(4,128)(2,1)S(1)} %get-tuple-element.35), channel_id=1, source_target_pairs={{0,8},{8,16},{16,24},{24,32},{32,40},{40,48},{48,56},{56,64},{64,7... | collective-permute-start | bytes 122888 | tf_op jit(solution)/shard_map/ppermute | solution.py:16
  11.5 19.4 %collective-permute-start.1 = (bf16[2,5,1,4,512]{4,3,2,1,0:T(4,128)(2,1)S(1)}, bf16[2,5,1,4,512]{4,3,2,1,0:T(4,128)(2,1)S(1)}, u32[]{:S(2)}, u32[]{:S(2)}) collective-permute-start(bf16[2,5,1,4,512]{4,3,2,1,0:T(4,128)(2,1)S(1)} %get-tuple-element.36), channel_id=1, source_target_pairs={{8,0},{16,8},{24,16},{32,24},{40,32},{48,40},{56,48},{64,56},{72,6... | collective-permute-start | bytes 122888 | tf_op jit(solution)/shard_map/ppermute | solution.py:17
  27.9 4.7 %collective-permute-start.2 = (f32[64,1,4,512]{3,0,2,1:T(8,128)S(1)}, f32[64,1,4,512]{3,0,2,1:T(8,128)S(1)}, u32[]{:S(2)}, u32[]{:S(2)}) collective-permute-start(f32[64,1,4,512]{3,0,2,1:T(8,128)S(1)} %get-tuple-element.23), channel_id=1, source_target_pairs={{0,8},{8,16},{16,24},{24,32},{32,40},{40,48},{48,56},{56,64},{64,7... | collective-permute-start | bytes 1572872 | tf_op jit(solution)/shard_map/ppermute | solution.py:16
  29.6 5.6 %collective-permute-start.3 = (f32[64,1,4,512]{3,0,2,1:T(8,128)S(1)}, f32[64,1,4,512]{3,0,2,1:T(8,128)S(1)}, u32[]{:S(2)}, u32[]{:S(2)}) collective-permute-start(f32[64,1,4,512]{3,0,2,1:T(8,128)S(1)} %get-tuple-element.24), channel_id=1, source_target_pairs={{8,0},{16,8},{24,16},{32,24},{40,32},{48,40},{56,48},{64,56},{72,6... | collective-permute-start | bytes 1572872 | tf_op jit(solution)/shard_map/ppermute | solution.py:17
  39.6 4.3 %collective-permute-start.4 = (f32[2,64,64]{2,1,0:T(8,128)S(1)}, f32[2,64,64]{2,1,0:T(8,128)S(1)}, u32[]{:S(2)}, u32[]{:S(2)}) collective-permute-start(f32[2,64,64]{2,1,0:T(8,128)S(1)} %pad_maximum_fusion.1), channel_id=1, source_target_pairs={{0,1},{1,0},{2,3},{3,2},{4,5},{5,4},{6,7},{7,6},{8,9},{9,8},{10,11... | collective-permute-start | bytes 98312 | tf_op jit(solution)/shard_map/ppermute | solution.py:53
  44.0 6.2 %collective-permute-start.5 = (f32[2,64,64]{2,1,0:T(8,128)S(1)}, f32[2,64,64]{2,1,0:T(8,128)S(1)}, u32[]{:S(2)}, u32[]{:S(2)}) collective-permute-start(f32[2,64,64]{2,1,0:T(8,128)S(1)} %fusion.27), channel_id=1, source_target_pairs={{0,2},{1,3},{2,0},{3,1},{4,6},{5,7},{6,4},{7,5},{8,10},{9,11},{10,... | collective-permute-start | bytes 98312 | tf_op jit(solution)/shard_map/ppermute | solution.py:53
  50.2 5.8 %collective-permute-start.6 = (f32[2,64,64]{2,1,0:T(8,128)S(1)}, f32[2,64,64]{2,1,0:T(8,128)S(1)}, u32[]{:S(2)}, u32[]{:S(2)}) collective-permute-start(f32[2,64,64]{2,1,0:T(8,128)S(1)} %add.114), channel_id=1, source_target_pairs={{0,4},{1,5},{2,6},{3,7},{4,0},{5,1},{6,2},{7,3},{8,12},{9,13},{10,... | collective-permute-start | bytes 98312 | tf_op jit(solution)/shard_map/ppermute | solution.py:53
  56.0 4.8 %collective-permute-start.7 = (f32[2,64,64]{2,1,0:T(8,128)S(1)}, f32[2,64,64]{2,1,0:T(8,128)S(1)}, u32[]{:S(2)}, u32[]{:S(2)}) collective-permute-start(f32[2,64,64]{2,1,0:T(8,128)S(1)} %add.119), channel_id=1, source_target_pairs={{0,8},{8,0},{16,24},{24,16},{32,40},{40,32},{48,56},{56,48},{64,72... | collective-permute-start | bytes 98312 | tf_op jit(solution)/shard_map/ppermute | solution.py:53
  60.9 6.4 %collective-permute-start.8 = (f32[2,64,64]{2,1,0:T(8,128)S(1)}, f32[2,64,64]{2,1,0:T(8,128)S(1)}, u32[]{:S(2)}, u32[]{:S(2)}) collective-permute-start(f32[2,64,64]{2,1,0:T(8,128)S(1)} %add.120), channel_id=1, source_target_pairs={{0,16},{8,24},{16,0},{24,8},{32,48},{40,56},{48,32},{56,40},{64,80... | collective-permute-start | bytes 98312 | tf_op jit(solution)/shard_map/ppermute | solution.py:53
  67.3 6.0 %collective-permute-start.9 = (f32[2,64,64]{2,1,0:T(8,128)S(1)}, f32[2,64,64]{2,1,0:T(8,128)S(1)}, u32[]{:S(2)}, u32[]{:S(2)}) collective-permute-start(f32[2,64,64]{2,1,0:T(8,128)S(1)} %add.121), channel_id=1, source_target_pairs={{0,32},{8,40},{16,48},{24,56},{32,0},{40,8},{48,16},{56,24},{64,96... | collective-permute-start | bytes 98312 | tf_op jit(solution)/shard_map/ppermute | solution.py:53
  73.3 4.6 %collective-permute-start.10 = (f32[2,64,64]{2,1,0:T(8,128)S(1)}, f32[2,64,64]{2,1,0:T(8,128)S(1)}, u32[]{:S(2)}, u32[]{:S(2)}) collective-permute-start(f32[2,64,64]{2,1,0:T(8,128)S(1)} %add.122), channel_id=1, source_target_pairs={{0,64},{8,72},{16,80},{24,88},{32,96},{40,104},{48,112},{56,120},{... | collective-permute-start | bytes 98312 | tf_op jit(solution)/shard_map/ppermute | solution.py:53
  90.3 18.1 %all-to-all-start.1 = ((f32[64,1,8,512]{3,2,1,0:T(8,128)}), f32[64,1,8,512]{3,2,1,0:T(8,128)S(1)}, u32[]{:S(2)}, u32[]{:S(2)}) async-start(f32[64,1,8,512]{3,2,1,0:T(8,128)} %copy.15), calls=%async_computation.1 | async-start | bytes 2097152 | tf_op jit(solution)/shard_map/all_to_all | solution.py:145

commit v15 on v9

--- a/solution.py
+++ b/solution.py
@@ -62,25 +62,40 @@
     lane = lax.broadcasted_iota(jnp.int32, (1, n), 1)
     sub = lax.broadcasted_iota(jnp.int32, (n, 1), 0)
 
-    def step(k, carry):
+    def pick(vec, index):
+        return jnp.sum(jnp.where(lane == index, vec, 0.0), axis=1, keepdims=True)
+
+    def step(half, carry):
+        k = 2 * half
         a = a_ref[...]
-        row = a_ref[pl.ds(k, 1), :]
-        pivot = jnp.sum(jnp.where(lane == k, row, 0.0), axis=1, keepdims=True)
-        scale = 1.0 / jnp.sqrt(pivot)
-        col = jnp.sum(jnp.where(cols == k, a, 0.0), axis=1, keepdims=True)
-        below = jnp.where(sub > k, col * scale, 0.0)
-        right = jnp.where(lane > k, row * scale, 0.0)
-        a_ref[...] = a - below * right
-        xrow = x_ref[pl.ds(k, 1), :] * scale
-        x_ref[pl.ds(k, 1), :] = xrow
-        x_ref[...] = x_ref[...] - below * xrow
+        row0 = a_ref[pl.ds(k, 1), :]
+        row1 = a_ref[pl.ds(k + 1, 1), :]
+        col0 = jnp.sum(jnp.where(cols == k, a, 0.0), axis=1, keepdims=True)
+        col1 = jnp.sum(jnp.where(cols == k + 1, a, 0.0), axis=1, keepdims=True)
+        scale0 = 1.0 / jnp.sqrt(pick(row0, k))
+        below0 = jnp.where(sub > k, col0 * scale0, 0.0)
+        right0 = jnp.where(lane > k, row0 * scale0, 0.0)
+        link = pick(right0, k + 1)
+        row1 = row1 - link * right0
+        col1 = col1 - below0 * link
+        scale1 = 1.0 / jnp.sqrt(pick(row1, k + 1))
+        below1 = jnp.where(sub > k + 1, col1 * scale1, 0.0)
+        right1 = jnp.where(lane > k + 1, row1 * scale1, 0.0)
+        a_ref[...] = a - below0 * right0 - below1 * right1
+        x = x_ref[...]
+        xrow0 = x_ref[pl.ds(k, 1), :] * scale0
+        xrow1 = (x_ref[pl.ds(k + 1, 1), :] - link * xrow0) * scale1
+        x = x - below0 * xrow0 - below1 * xrow1
+        x = jnp.where(rows == k, xrow0, jnp.where(rows == k + 1, xrow1, x))
+        x_ref[...] = x
         return carry
 
-    lax.fori_loop(0, n, step, 0)
+    lax.fori_loop(0, n // 2, step, 0)
 
 
 def lower_inverse(gram):
     n = gram.shape[0]
+    assert n % 2 == 0
     return pl.pallas_call(
         chol_inv_kernel,
         out_shape=jax.ShapeDtypeStruct((n, n), jnp.float32),

time: 108 us -> 110 us (1.019)
  Pallas kernels: 8.15 us -> 10.2 us
    pallas_call x1, Pallas kernels: 8.15 us -> 10.2 us  [lower_inverse(): pl.pallas_call(chol_inv_kernel, out_shape=jax.ShapeDtypeStruct((n, n), jn...]
  transfers between devices with their start and end apart: 15 -> 15, of which waited for: 9 -> 9; matrix products, arithmetic and copies ran while one was open for 7% -> 7% of each run, Pallas kernels for 8% -> 9%
where the time goes in v15:
time: 110 us; the launch traced here: 109 us
  waiting for transfers between devices  42.5 us (39%)
  starting transfers between devices  35.8 us (33%)
  Pallas kernels  10.2 us (9%)
  other arithmetic  9.57 us (9%)
  local copies, waits for them, and re-layouts  6.31 us (6%)
  matrix products  4.02 us (4%)
    ppermute x9, waiting for transfers between devices, exchange(): return x + lax.ppermute(x, axis, [(i, i ^ bit) for i in range(count)])  27 us
    ppermute x9, starting transfers between devices, exchange(): return x + lax.ppermute(x, axis, [(i, i ^ bit) for i in range(count)])  19.2 us
    all_to_all x1, waiting for transfers between devices, body(): v = lax.all_to_all(perturbations, 'mem', 1, 0, tiled=True)  14.4 us
    pallas_call x1, Pallas kernels, lower_inverse(): pl.pallas_call(chol_inv_kernel, out_shape=jax.ShapeDtypeStruct((n, n), jn...  10.2 us
    all_to_all x1, starting transfers between devices, body(): v = lax.all_to_all(perturbations, 'mem', 1, 0, tiled=True)  7.04 us
    all_to_all x1, starting transfers between devices, body(): ritz = lax.all_to_all(ritz.reshape(v.shape), 'mem', 0, 1, tiled=True)  3.87 us
    ppermute x2, starting transfers between devices, halo(): lax.ppermute(lax.slice_in_dim(block, size - width, size, axis=dim), 'dom'...  3.12 us
    add x2, other arithmetic, adjoint_step(): result + shifted(coef[3] * field, 1, 3) + shifted(coef[4] * field, -1, 3)  2.94 us
  transfers between devices with their start and end apart: 15, of which 9 were waited for; matrix products, arithmetic and copies ran while one was open for 7% of the time, Pallas kernels for 9%

profile of v15, /device:TPU:0, one launch (start us, length us, event | category | flops | bytes accessed | tf_op | source)
XLA Modules:
  0.0 109.3 jit_solution(14732898592720090518)
XLA Ops:
  0.6 2.3 %copy.11 = f32[8,8,8,512]{3,2,0,1:T(8,128)} copy(f32[8,8,8,512]{3,2,1,0:T(8,128)} %param.2) | data formatting | bytes 2097152 | tf_op args[0]
  3.0 7.0 %all-to-all-start = ((f32[8,8,8,512]{3,2,0,1:T(8,128)}), f32[8,8,8,512]{3,2,0,1:T(8,128)S(1)}, u32[]{:S(2)}, u32[]{:S(2)}) async-start(f32[8,8,8,512]{3,2,0,1:T(8,128)} %copy.11), calls=%async_computation | async-start | bytes 2097152 | tf_op jit(solution)/shard_map/all_to_all | solution.py:120
  10.0 1.5 %collective-permute-start.1 = (bf16[2,5,1,4,512]{4,3,2,1,0:T(4,128)(2,1)S(1)}, bf16[2,5,1,4,512]{4,3,2,1,0:T(4,128)(2,1)S(1)}, u32[]{:S(2)}, u32[]{:S(2)}) collective-permute-start(bf16[2,5,1,4,512]{4,3,2,1,0:T(4,128)(2,1)S(1)} %get-tuple-element.42), channel_id=1, source_target_pairs={{0,8},{8,16},{16,24},{24,32},{32,40},{40,48},{48,56},{56,64},{64,7... | collective-permute-start | bytes 122888 | tf_op jit(solution)/shard_map/ppermute | solution.py:16
  11.5 1.3 %collective-permute-start.2 = (bf16[2,5,1,4,512]{4,3,2,1,0:T(4,128)(2,1)S(1)}, bf16[2,5,1,4,512]{4,3,2,1,0:T(4,128)(2,1)S(1)}, u32[]{:S(2)}, u32[]{:S(2)}) collective-permute-start(bf16[2,5,1,4,512]{4,3,2,1,0:T(4,128)(2,1)S(1)} %get-tuple-element.43), channel_id=1, source_target_pairs={{8,0},{16,8},{24,16},{32,24},{40,32},{48,40},{56,48},{64,56},{72,6... | collective-permute-start | bytes 122888 | tf_op jit(solution)/shard_map/ppermute | solution.py:17
  12.8 14.4 %all-to-all-done = f32[8,8,8,512]{3,2,0,1:T(8,128)S(1)} async-done(((f32[8,8,8,512]{3,2,0,1:T(8,128)}), f32[8,8,8,512]{3,2,0,1:T(8,128)S(1)}, u32[]{:S(2)}, u32[]{:S(2)}) %all-to-all-start) | async-done | bytes 1048608 | tf_op jit(solution)/shard_map/all_to_all | solution.py:120
  27.2 0.6 copy.31
  27.8 0.1 fusion.31
  27.9 1.7 %collective-permute-start.3 = (f32[64,1,4,512]{3,0,2,1:T(8,128)S(1)}, f32[64,1,4,512]{3,0,2,1:T(8,128)S(1)}, u32[]{:S(2)}, u32[]{:S(2)}) collective-permute-start(f32[64,1,4,512]{3,0,2,1:T(8,128)S(1)} %get-tuple-element.30), channel_id=1, source_target_pairs={{0,8},{8,16},{16,24},{24,32},{32,40},{40,48},{48,56},{56,64},{64,7... | collective-permute-start | bytes 1572872 | tf_op jit(solution)/shard_map/ppermute | solution.py:16
  29.6 1.3 %collective-permute-start.4 = (f32[64,1,4,512]{3,0,2,1:T(8,128)S(1)}, f32[64,1,4,512]{3,0,2,1:T(8,128)S(1)}, u32[]{:S(2)}, u32[]{:S(2)}) collective-permute-start(f32[64,1,4,512]{3,0,2,1:T(8,128)S(1)} %get-tuple-element.31), channel_id=1, source_target_pairs={{8,0},{16,8},{24,16},{32,24},{40,32},{48,40},{56,48},{64,56},{72,6... | collective-permute-start | bytes 1572872 | tf_op jit(solution)/shard_map/ppermute | solution.py:17
  30.9 0.0 collective-permute-done.2
  30.9 0.1 maximum_convert_fusion
  31.0 0.6 copy.18
  31.6 1.0 fusion.33
  32.6 0.6 collective-permute-start
  33.2 3.4 %collective-permute-done = f32[64,64]{1,0:T(8,128)S(1)} collective-permute-done((f32[64,64]{1,0:T(8,128)S(1)}, f32[64,64]{1,0:T(8,128)S(1)}, u32[]{:S(2)}, u32[]{:S(2)}) %collective-permute-start) | collective-permute-done | bytes 16416 | tf_op jit(solution)/shard_map/ppermute | solution.py:53
  36.6 0.0 collective-permute-done.3
  36.6 0.0 collective-permute-done.4
  36.6 0.2 pad_maximum_fusion
  36.8 1.3 %fusion.4 = f32[64,1,16,512]{3,0,2,1:T(8,128)S(1)} fusion(f32[64,1,16,512]{3,0,2,1:T(8,128)S(1)} %pad_maximum_fusion, f32[16,512]{1,0:T(8,128)S(1)} %get-tuple-element.37, f32[16,512]{1,0:T(8,128)S(1)} %get-tuple-element.38, f32[16,512]{1,0:T(8,128)S(1)} %get-tuple-element.39, f32[16,512]{1,0:T(8,128)S(1)} %get-tuple-element.40, ...), kind=kLoop, calls=%fused_computation.20 | loop fusion | flops 4718592 | bytes 4358144 | tf_op jit(solution)/shard_map/add | solution.py:33
  38.1 1.2 %collective-permute-start.5 = (f32[64,64]{1,0:T(8,128)S(1)}, f32[64,64]{1,0:T(8,128)S(1)}, u32[]{:S(2)}, u32[]{:S(2)}) collective-permute-start(f32[64,64]{1,0:T(8,128)S(1)} %add.107), channel_id=1, source_target_pairs={{0,2},{1,3},{2,0},{3,1},{4,6},{5,7},{6,4},{7,5},{8,10},{9,11},{10,... | collective-permute-start | bytes 49160 | tf_op jit(solution)/shard_map/ppermute | solution.py:53
  39.3 1.3 %fusion.10 = f32[64,1,16,512]{3,0,2,1:T(8,128)S(1)} fusion(f32[64,1,16,512]{3,0,2,1:T(8,128)S(1)} %fusion.4, f32[16,512]{1,0:T(8,128)S(1)} %get-tuple-element.33, f32[16,512]{1,0:T(8,128)S(1)} %get-tuple-element.34, f32[16,512]{1,0:T(8,128)S(1)} %get-tuple-element.35, f32[16,512]{1,0:T(8,128)S(1)} %get-tuple-element.36, f32[16,512]{1,0:T(8,128)S(1)} %get-tuple-element.32), kind=kLoop, calls=%fused_computation.26 | loop fusion | flops 4718592 | bytes 4358144 | tf_op jit(solution)/shard_map/add | solution.py:33
  40.6 3.0 %collective-permute-done.5 = f32[64,64]{1,0:T(8,128)S(1)} collective-permute-done((f32[64,64]{1,0:T(8,128)S(1)}, f32[64,64]{1,0:T(8,128)S(1)}, u32[]{:S(2)}, u32[]{:S(2)}) %collective-permute-start.5) | collective-permute-done | bytes 16416 | tf_op jit(solution)/shard_map/ppermute | solution.py:53
  43.6 1.2 %broadcast_multiply_fusion = (f32[64,1,16,512]{3,0,2,1:T(8,128)S(1)}, f32[64,1,16,512]{3,0,2,1:T(8,128)S(1)}, f32[64,1,16,512]{3,0,2,1:T(8,128)S(1)}, f32[64,1,16,512]{3,0,2,1:T(8,128)S(1)}) fusion(f32[64,1,16,512]{3,0,2,1:T(8,128)S(1)} %fusion.10, f32[16,512]{1,0:T(8,128)S(1)} %get-tuple-element.33, f32[16,512]{1,0:T(8,128)S(1)} %get-tuple-element.34, ...), kind=kLoop, calls=%fused_computation.50 | loop fusion | flops 2097152 | bytes 10616832 | tf_op jit(solution)/shard_map/mul | solution.py:38
  44.8 1.0 convolution_bitcast_fusion.2
  45.8 0.6 collective-permute-start.6
  46.5 1.5 %fusion.15 = f32[64,1,16,512]{3,0,2,1:T(8,128)S(1)} fusion(f32[64,1,16,512]{3,0,2,1:T(8,128)S(1)} %get-tuple-element.29, f32[64,1,16,512]{3,0,2,1:T(8,128)S(1)} %get-tuple-element.28, f32[64,1,16,512]{3,0,2,1:T(8,128)S(1)} %get-tuple-element.27, f32[64,1,16,512]{3,0,2,1:T(8,128)S(1)} %get-tuple-element.26, f32[64,1,16,512]{3,0,2,1:T(8,128)S(1)} %fusion.10, ...), kind=kLoop, calls=%fused_computation.31 | loop fusion | flops 2621440 | bytes 12615680 | tf_op jit(solution)/shard_map/add | solution.py:38
  48.0 3.7 %collective-permute-done.6 = f32[2,64,64]{2,1,0:T(8,128)S(1)} collective-permute-done((f32[2,64,64]{2,1,0:T(8,128)S(1)}, f32[2,64,64]{2,1,0:T(8,128)S(1)}, u32[]{:S(2)}, u32[]{:S(2)}) %collective-permute-start.6) | collective-permute-done | bytes 32800 | tf_op jit(solution)/shard_map/ppermute | solution.py:53
  51.7 1.2 %broadcast_multiply_fusion.4 = (f32[64,1,16,512]{3,0,2,1:T(8,128)S(1)}, f32[64,1,16,512]{3,0,2,1:T(8,128)S(1)}, f32[64,1,16,512]{3,0,2,1:T(8,128)S(1)}, f32[64,1,16,512]{3,0,2,1:T(8,128)S(1)}) fusion(f32[64,1,16,512]{3,0,2,1:T(8,128)S(1)} %fusion.15, f32[16,512]{1,0:T(8,128)S(1)} %get-tuple-element.37, f32[16,512]{1,0:T(8,128)S(1)} %get-tuple-element.38, ...), kind=kLoop, calls=%fused_computation.54 | loop fusion | flops 2097152 | bytes 10616832 | tf_op jit(solution)/shard_map/mul | solution.py:38
  52.9 3.7 %collective-permute-start.7 = (f32[2,64,64]{2,1,0:T(8,128)S(1)}, f32[2,64,64]{2,1,0:T(8,128)S(1)}, u32[]{:S(2)}, u32[]{:S(2)}) collective-permute-start(f32[2,64,64]{2,1,0:T(8,128)S(1)} %fusion.30), channel_id=1, source_target_pairs={{0,8},{8,0},{16,24},{24,16},{32,40},{40,32},{48,56},{56,48},{64,72... | collective-permute-start | bytes 98312 | tf_op jit(solution)/shard_map/ppermute | solution.py:53
  56.7 1.4 %fusion.19 = f32[64,1,16,512]{3,0,2,1:T(8,128)S(1)} fusion(f32[64,1,16,512]{3,0,2,1:T(8,128)S(1)} %get-tuple-element.25, f32[64,1,16,512]{3,0,2,1:T(8,128)S(1)} %get-tuple-element.24, f32[64,1,16,512]{3,0,2,1:T(8,128)S(1)} %get-tuple-element.23, f32[64,1,16,512]{3,0,2,1:T(8,128)S(1)} %get-tuple-element.22, f32[64,1,16,512]{3,0,2,1:T(8,128)S(1)} %fusion.15, ...), kind=kLoop, calls=%fused_computation.35 | loop fusion | flops 2621440 | bytes 12615680 | tf_op jit(solution)/shard_map/add | solution.py:38
  58.1 2.8 %collective-permute-start.8 = (f32[2,64,64]{2,1,0:T(8,128)S(1)}, f32[2,64,64]{2,1,0:T(8,128)S(1)}, u32[]{:S(2)}, u32[]{:S(2)}) collective-permute-start(f32[2,64,64]{2,1,0:T(8,128)S(1)} %add.122), channel_id=1, source_target_pairs={{0,16},{8,24},{16,0},{24,8},{32,48},{40,56},{48,32},{56,40},{64,80... | collective-permute-start | bytes 98312 | tf_op jit(solution)/shard_map/ppermute | solution.py:53
  61.0 2.7 %collective-permute-done.8 = f32[2,64,64]{2,1,0:T(8,128)S(1)} collective-permute-done((f32[2,64,64]{2,1,0:T(8,128)S(1)}, f32[2,64,64]{2,1,0:T(8,128)S(1)}, u32[]{:S(2)}, u32[]{:S(2)}) %collective-permute-start.8) | collective-permute-done | bytes 32800 | tf_op jit(solution)/shard_map/ppermute | solution.py:53
  63.6 3.6 %collective-permute-start.9 = (f32[2,64,64]{2,1,0:T(8,128)S(1)}, f32[2,64,64]{2,1,0:T(8,128)S(1)}, u32[]{:S(2)}, u32[]{:S(2)}) collective-permute-start(f32[2,64,64]{2,1,0:T(8,128)S(1)} %add.127), channel_id=1, source_target_pairs={{0,32},{8,40},{16,48},{24,56},{32,0},{40,8},{48,16},{56,24},{64,96... | collective-permute-start | bytes 98312 | tf_op jit(solution)/shard_map/ppermute | solution.py:53
  67.3 2.2 %collective-permute-done.9 = f32[2,64,64]{2,1,0:T(8,128)S(1)} collective-permute-done((f32[2,64,64]{2,1,0:T(8,128)S(1)}, f32[2,64,64]{2,1,0:T(8,128)S(1)}, u32[]{:S(2)}, u32[]{:S(2)}) %collective-permute-start.9) | collective-permute-done | bytes 32800 | tf_op jit(solution)/shard_map/ppermute | solution.py:53
  69.5 2.3 %collective-permute-start.10 = (f32[2,64,64]{2,1,0:T(8,128)S(1)}, f32[2,64,64]{2,1,0:T(8,128)S(1)}, u32[]{:S(2)}, u32[]{:S(2)}) collective-permute-start(f32[2,64,64]{2,1,0:T(8,128)S(1)} %add.128), channel_id=1, source_target_pairs={{0,64},{8,72},{16,80},{24,88},{32,96},{40,104},{48,112},{56,120},{... | collective-permute-start | bytes 98312 | tf_op jit(solution)/shard_map/ppermute | solution.py:53
  71.9 2.2 %collective-permute-done.10 = f32[2,64,64]{2,1,0:T(8,128)S(1)} collective-permute-done((f32[2,64,64]{2,1,0:T(8,128)S(1)}, f32[2,64,64]{2,1,0:T(8,128)S(1)}, u32[]{:S(2)}, u32[]{:S(2)}) %collective-permute-start.10) | collective-permute-done | bytes 32800 | tf_op jit(solution)/shard_map/ppermute | solution.py:53
  74.1 0.6 slice_bitcast_fusion
  74.8 0.6 collective-permute-start.11
  75.4 10.2 %shard_map.41 = f32[64,64]{1,0:T(8,128)} custom-call(f32[64,64]{1,0:T(8,128)} %get-tuple-element.45.g_ref), custom_call_target="tpu_custom_call" | custom-call | tf_op jit(solution)/shard_map/pallas_call | solution.py:99
  85.6 1.1 convolution_bitcast_fusion.1
  86.7 1.0 convolution_bitcast_fusion
  87.7 1.6 %copy.15 = f32[64,1,8,512]{3,2,1,0:T(8,128)} copy(f32[64,1,8,512]{3,0,2,1:T(8,128)S(1)} %convolution_bitcast_fusion) | data formatting | bytes 2097152 | tf_op jit(solution)/shard_map/dot_general | solution.py:156
  89.3 3.9 %all-to-all-start.1 = ((f32[64,1,8,512]{3,2,1,0:T(8,128)}), f32[64,1,8,512]{3,2,1,0:T(8,128)S(1)}, u32[]{:S(2)}, u32[]{:S(2)}) async-start(f32[64,1,8,512]{3,2,1,0:T(8,128)} %copy.15), calls=%async_computation.1 | async-start | bytes 2097152 | tf_op jit(solution)/shard_map/all_to_all | solution.py:160
  93.1 3.5 %collective-permute-start.12 = (f32[64,64]{1,0:T(8,128)S(1)}, f32[64,64]{1,0:T(8,128)S(1)}, u32[]{:S(2)}, u32[]{:S(2)}) collective-permute-start(f32[64,64]{1,0:T(8,128)S(1)} %fusion.29), channel_id=1, source_target_pairs={{0,2},{1,3},{2,0},{3,1},{4,6},{5,7},{6,4},{7,5},{8,10},{9,11},{10,... | collective-permute-start | bytes 49160 | tf_op jit(solution)/shard_map/ppermute | solution.py:53
  96.7 9.8 %collective-permute-done.12 = f32[64,64]{1,0:T(8,128)S(1)} collective-permute-done((f32[64,64]{1,0:T(8,128)S(1)}, f32[64,64]{1,0:T(8,128)S(1)}, u32[]{:S(2)}, u32[]{:S(2)}) %collective-permute-start.12) | collective-permute-done | bytes 16416 | tf_op jit(solution)/shard_map/ppermute | solution.py:53
  106.5 0.6 add_multiply_fusion
  107.1 1.1 %all-to-all-done.1 = f32[64,1,8,512]{3,2,1,0:T(8,128)S(1)} async-done(((f32[64,1,8,512]{3,2,1,0:T(8,128)}), f32[64,1,8,512]{3,2,1,0:T(8,128)S(1)}, u32[]{:S(2)}, u32[]{:S(2)}) %all-to-all-start.1) | async-done | bytes 1048608 | tf_op jit(solution)/shard_map/all_to_all | solution.py:160
  108.2 1.1 copy.30
  (16 shorter events, 0.1 us)
Async XLA Ops:
  0.6 9.4 %copy-start = (bf16[2,5,1,8,512]{4,3,2,1,0:T(8,128)(2,1)S(1)}, bf16[2,5,1,8,512]{4,3,2,1,0:T(8,128)(2,1)}, u32[]{:S(2)}) copy-start(bf16[2,5,1,8,512]{4,3,2,1,0:T(8,128)(2,1)} %param.3) | copy-start | bytes 245764
  3.0 24.2 %all-to-all-start = ((f32[8,8,8,512]{3,2,0,1:T(8,128)}), f32[8,8,8,512]{3,2,0,1:T(8,128)S(1)}, u32[]{:S(2)}, u32[]{:S(2)}) async-start(f32[8,8,8,512]{3,2,0,1:T(8,128)} %copy.11), calls=%async_computation | async-start | bytes 2097152 | tf_op jit(solution)/shard_map/all_to_all | solution.py:120
  10.0 20.8 %collective-permute-start.1 = (bf16[2,5,1,4,512]{4,3,2,1,0:T(4,128)(2,1)S(1)}, bf16[2,5,1,4,512]{4,3,2,1,0:T(4,128)(2,1)S(1)}, u32[]{:S(2)}, u32[]{:S(2)}) collective-permute-start(bf16[2,5,1,4,512]{4,3,2,1,0:T(4,128)(2,1)S(1)} %get-tuple-element.42), channel_id=1, source_target_pairs={{0,8},{8,16},{16,24},{24,32},{32,40},{40,48},{48,56},{56,64},{64,7... | collective-permute-start | bytes 122888 | tf_op jit(solution)/shard_map/ppermute | solution.py:16
  11.5 19.4 %collective-permute-start.2 = (bf16[2,5,1,4,512]{4,3,2,1,0:T(4,128)(2,1)S(1)}, bf16[2,5,1,4,512]{4,3,2,1,0:T(4,128)(2,1)S(1)}, u32[]{:S(2)}, u32[]{:S(2)}) collective-permute-start(bf16[2,5,1,4,512]{4,3,2,1,0:T(4,128)(2,1)S(1)} %get-tuple-element.43), channel_id=1, source_target_pairs={{8,0},{16,8},{24,16},{32,24},{40,32},{48,40},{56,48},{64,56},{72,6... | collective-permute-start | bytes 122888 | tf_op jit(solution)/shard_map/ppermute | solution.py:17
  27.9 8.7 %collective-permute-start.3 = (f32[64,1,4,512]{3,0,2,1:T(8,128)S(1)}, f32[64,1,4,512]{3,0,2,1:T(8,128)S(1)}, u32[]{:S(2)}, u32[]{:S(2)}) collective-permute-start(f32[64,1,4,512]{3,0,2,1:T(8,128)S(1)} %get-tuple-element.30), channel_id=1, source_target_pairs={{0,8},{8,16},{16,24},{24,32},{32,40},{40,48},{48,56},{56,64},{64,7... | collective-permute-start | bytes 1572872 | tf_op jit(solution)/shard_map/ppermute | solution.py:16
  29.6 7.0 %collective-permute-start.4 = (f32[64,1,4,512]{3,0,2,1:T(8,128)S(1)}, f32[64,1,4,512]{3,0,2,1:T(8,128)S(1)}, u32[]{:S(2)}, u32[]{:S(2)}) collective-permute-start(f32[64,1,4,512]{3,0,2,1:T(8,128)S(1)} %get-tuple-element.31), channel_id=1, source_target_pairs={{8,0},{16,8},{24,16},{32,24},{40,32},{48,40},{56,48},{64,56},{72,6... | collective-permute-start | bytes 1572872 | tf_op jit(solution)/shard_map/ppermute | solution.py:17
  32.6 4.0 %collective-permute-start = (f32[64,64]{1,0:T(8,128)S(1)}, f32[64,64]{1,0:T(8,128)S(1)}, u32[]{:S(2)}, u32[]{:S(2)}) collective-permute-start(f32[64,64]{1,0:T(8,128)S(1)} %fusion.33), channel_id=1, source_target_pairs={{0,1},{1,0},{2,3},{3,2},{4,5},{5,4},{6,7},{7,6},{8,9},{9,8},{10,11... | collective-permute-start | bytes 49160 | tf_op jit(solution)/shard_map/ppermute | solution.py:53
  38.1 5.5 %collective-permute-start.5 = (f32[64,64]{1,0:T(8,128)S(1)}, f32[64,64]{1,0:T(8,128)S(1)}, u32[]{:S(2)}, u32[]{:S(2)}) collective-permute-start(f32[64,64]{1,0:T(8,128)S(1)} %add.107), channel_id=1, source_target_pairs={{0,2},{1,3},{2,0},{3,1},{4,6},{5,7},{6,4},{7,5},{8,10},{9,11},{10,... | collective-permute-start | bytes 49160 | tf_op jit(solution)/shard_map/ppermute | solution.py:53
  45.8 5.8 %collective-permute-start.6 = (f32[2,64,64]{2,1,0:T(8,128)S(1)}, f32[2,64,64]{2,1,0:T(8,128)S(1)}, u32[]{:S(2)}, u32[]{:S(2)}) collective-permute-start(f32[2,64,64]{2,1,0:T(8,128)S(1)} %pad_maximum_fusion.1), channel_id=1, source_target_pairs={{0,4},{1,5},{2,6},{3,7},{4,0},{5,1},{6,2},{7,3},{8,12},{9,13},{10,... | collective-permute-start | bytes 98312 | tf_op jit(solution)/shard_map/ppermute | solution.py:53
  52.9 5.2 %collective-permute-start.7 = (f32[2,64,64]{2,1,0:T(8,128)S(1)}, f32[2,64,64]{2,1,0:T(8,128)S(1)}, u32[]{:S(2)}, u32[]{:S(2)}) collective-permute-start(f32[2,64,64]{2,1,0:T(8,128)S(1)} %fusion.30), channel_id=1, source_target_pairs={{0,8},{8,0},{16,24},{24,16},{32,40},{40,32},{48,56},{56,48},{64,72... | collective-permute-start | bytes 98312 | tf_op jit(solution)/shard_map/ppermute | solution.py:53
  58.1 5.5 %collective-permute-start.8 = (f32[2,64,64]{2,1,0:T(8,128)S(1)}, f32[2,64,64]{2,1,0:T(8,128)S(1)}, u32[]{:S(2)}, u32[]{:S(2)}) collective-permute-start(f32[2,64,64]{2,1,0:T(8,128)S(1)} %add.122), channel_id=1, source_target_pairs={{0,16},{8,24},{16,0},{24,8},{32,48},{40,56},{48,32},{56,40},{64,80... | collective-permute-start | bytes 98312 | tf_op jit(solution)/shard_map/ppermute | solution.py:53
  63.6 5.9 %collective-permute-start.9 = (f32[2,64,64]{2,1,0:T(8,128)S(1)}, f32[2,64,64]{2,1,0:T(8,128)S(1)}, u32[]{:S(2)}, u32[]{:S(2)}) collective-permute-start(f32[2,64,64]{2,1,0:T(8,128)S(1)} %add.127), channel_id=1, source_target_pairs={{0,32},{8,40},{16,48},{24,56},{32,0},{40,8},{48,16},{56,24},{64,96... | collective-permute-start | bytes 98312 | tf_op jit(solution)/shard_map/ppermute | solution.py:53
  69.5 4.6 %collective-permute-start.10 = (f32[2,64,64]{2,1,0:T(8,128)S(1)}, f32[2,64,64]{2,1,0:T(8,128)S(1)}, u32[]{:S(2)}, u32[]{:S(2)}) collective-permute-start(f32[2,64,64]{2,1,0:T(8,128)S(1)} %add.128), channel_id=1, source_target_pairs={{0,64},{8,72},{16,80},{24,88},{32,96},{40,104},{48,112},{56,120},{... | collective-permute-start | bytes 98312 | tf_op jit(solution)/shard_map/ppermute | solution.py:53
  74.8 10.8 %collective-permute-start.11 = (f32[64,64]{1,0:T(8,128)S(1)}, f32[64,64]{1,0:T(8,128)S(1)}, u32[]{:S(2)}, u32[]{:S(2)}) collective-permute-start(f32[64,64]{1,0:T(8,128)S(1)} %get-tuple-element.44), channel_id=1, source_target_pairs={{0,1},{1,0},{2,3},{3,2},{4,5},{5,4},{6,7},{7,6},{8,9},{9,8},{10,11... | collective-permute-start | bytes 49160 | tf_op jit(solution)/shard_map/ppermute | solution.py:53
  89.3 18.9 %all-to-all-start.1 = ((f32[64,1,8,512]{3,2,1,0:T(8,128)}), f32[64,1,8,512]{3,2,1,0:T(8,128)S(1)}, u32[]{:S(2)}, u32[]{:S(2)}) async-start(f32[64,1,8,512]{3,2,1,0:T(8,128)} %copy.15), calls=%async_computation.1 | async-start | bytes 2097152 | tf_op jit(solution)/shard_map/all_to_all | solution.py:160
  93.1 13.3 %collective-permute-start.12 = (f32[64,64]{1,0:T(8,128)S(1)}, f32[64,64]{1,0:T(8,128)S(1)}, u32[]{:S(2)}, u32[]{:S(2)}) collective-permute-start(f32[64,64]{1,0:T(8,128)S(1)} %fusion.29), channel_id=1, source_target_pairs={{0,2},{1,3},{2,0},{3,1},{4,6},{5,7},{6,4},{7,5},{8,10},{9,11},{10,... | collective-permute-start | bytes 49160 | tf_op jit(solution)/shard_map/ppermute | solution.py:53

commit v16 on v9

--- a/solution.py
+++ b/solution.py
@@ -67,7 +67,7 @@
         row = a_ref[pl.ds(k, 1), :]
         pivot = jnp.sum(jnp.where(lane == k, row, 0.0), axis=1, keepdims=True)
         scale = 1.0 / jnp.sqrt(pivot)
-        col = jnp.sum(jnp.where(cols == k, a, 0.0), axis=1, keepdims=True)
+        col = jnp.transpose(row)
         below = jnp.where(sub > k, col * scale, 0.0)
         right = jnp.where(lane > k, row * scale, 0.0)
         a_ref[...] = a - below * right

time: 108 us -> 113 us (1.046)
  Pallas kernels: 8.15 us -> 13 us
    pallas_call x1, Pallas kernels: 8.15 us -> 13 us  [lower_inverse(): pl.pallas_call(chol_inv_kernel, out_shape=jax.ShapeDtypeStruct((n, n), jn...]
  transfers between devices with their start and end apart: 15 -> 15, of which waited for: 9 -> 9; matrix products, arithmetic and copies ran while one was open for 7% -> 6% of each run, Pallas kernels for 8% -> 12%
where the time goes in v16:
time: 113 us; the launch traced here: 112 us
  waiting for transfers between devices  42.5 us (38%)
  starting transfers between devices  35.8 us (32%)
  Pallas kernels  13 us (12%)
  other arithmetic  9.57 us (8%)
  local copies, waits for them, and re-layouts  6.31 us (6%)
  matrix products  4.02 us (4%)
    ppermute x9, waiting for transfers between devices, exchange(): return x + lax.ppermute(x, axis, [(i, i ^ bit) for i in range(count)])  27 us
    ppermute x9, starting transfers between devices, exchange(): return x + lax.ppermute(x, axis, [(i, i ^ bit) for i in range(count)])  19.2 us
    all_to_all x1, waiting for transfers between devices, body(): v = lax.all_to_all(perturbations, 'mem', 1, 0, tiled=True)  14.4 us
    pallas_call x1, Pallas kernels, lower_inverse(): pl.pallas_call(chol_inv_kernel, out_shape=jax.ShapeDtypeStruct((n, n), jn...  13 us
    all_to_all x1, starting transfers between devices, body(): v = lax.all_to_all(perturbations, 'mem', 1, 0, tiled=True)  7.04 us
    all_to_all x1, starting transfers between devices, body(): ritz = lax.all_to_all(ritz.reshape(v.shape), 'mem', 0, 1, tiled=True)  3.88 us
    ppermute x2, starting transfers between devices, halo(): lax.ppermute(lax.slice_in_dim(block, size - width, size, axis=dim), 'dom'...  3.12 us
    add x2, other arithmetic, adjoint_step(): result + shifted(coef[3] * field, 1, 3) + shifted(coef[4] * field, -1, 3)  2.94 us
  transfers between devices with their start and end apart: 15, of which 9 were waited for; matrix products, arithmetic and copies ran while one was open for 6% of the time, Pallas kernels for 12%

profile of v16, /device:TPU:0, one launch (start us, length us, event | category | flops | bytes accessed | tf_op | source)
XLA Modules:
  0.0 112.0 jit_solution(14383987442925195426)
XLA Ops:
  0.6 2.3 %copy.11 = f32[8,8,8,512]{3,2,0,1:T(8,128)} copy(f32[8,8,8,512]{3,2,1,0:T(8,128)} %param.2) | data formatting | bytes 2097152 | tf_op args[0]
  3.0 7.0 %all-to-all-start = ((f32[8,8,8,512]{3,2,0,1:T(8,128)}), f32[8,8,8,512]{3,2,0,1:T(8,128)S(1)}, u32[]{:S(2)}, u32[]{:S(2)}) async-start(f32[8,8,8,512]{3,2,0,1:T(8,128)} %copy.11), calls=%async_computation | async-start | bytes 2097152 | tf_op jit(solution)/shard_map/all_to_all | solution.py:105
  10.0 1.5 %collective-permute-start.1 = (bf16[2,5,1,4,512]{4,3,2,1,0:T(4,128)(2,1)S(1)}, bf16[2,5,1,4,512]{4,3,2,1,0:T(4,128)(2,1)S(1)}, u32[]{:S(2)}, u32[]{:S(2)}) collective-permute-start(bf16[2,5,1,4,512]{4,3,2,1,0:T(4,128)(2,1)S(1)} %get-tuple-element.42), channel_id=1, source_target_pairs={{0,8},{8,16},{16,24},{24,32},{32,40},{40,48},{48,56},{56,64},{64,7... | collective-permute-start | bytes 122888 | tf_op jit(solution)/shard_map/ppermute | solution.py:16
  11.5 1.3 %collective-permute-start.2 = (bf16[2,5,1,4,512]{4,3,2,1,0:T(4,128)(2,1)S(1)}, bf16[2,5,1,4,512]{4,3,2,1,0:T(4,128)(2,1)S(1)}, u32[]{:S(2)}, u32[]{:S(2)}) collective-permute-start(bf16[2,5,1,4,512]{4,3,2,1,0:T(4,128)(2,1)S(1)} %get-tuple-element.43), channel_id=1, source_target_pairs={{8,0},{16,8},{24,16},{32,24},{40,32},{48,40},{56,48},{64,56},{72,6... | collective-permute-start | bytes 122888 | tf_op jit(solution)/shard_map/ppermute | solution.py:17
  12.8 14.4 %all-to-all-done = f32[8,8,8,512]{3,2,0,1:T(8,128)S(1)} async-done(((f32[8,8,8,512]{3,2,0,1:T(8,128)}), f32[8,8,8,512]{3,2,0,1:T(8,128)S(1)}, u32[]{:S(2)}, u32[]{:S(2)}) %all-to-all-start) | async-done | bytes 1048608 | tf_op jit(solution)/shard_map/all_to_all | solution.py:105
  27.2 0.6 copy.31
  27.8 0.1 fusion.31
  27.9 1.7 %collective-permute-start.3 = (f32[64,1,4,512]{3,0,2,1:T(8,128)S(1)}, f32[64,1,4,512]{3,0,2,1:T(8,128)S(1)}, u32[]{:S(2)}, u32[]{:S(2)}) collective-permute-start(f32[64,1,4,512]{3,0,2,1:T(8,128)S(1)} %get-tuple-element.30), channel_id=1, source_target_pairs={{0,8},{8,16},{16,24},{24,32},{32,40},{40,48},{48,56},{56,64},{64,7... | collective-permute-start | bytes 1572872 | tf_op jit(solution)/shard_map/ppermute | solution.py:16
  29.6 1.3 %collective-permute-start.4 = (f32[64,1,4,512]{3,0,2,1:T(8,128)S(1)}, f32[64,1,4,512]{3,0,2,1:T(8,128)S(1)}, u32[]{:S(2)}, u32[]{:S(2)}) collective-permute-start(f32[64,1,4,512]{3,0,2,1:T(8,128)S(1)} %get-tuple-element.31), channel_id=1, source_target_pairs={{8,0},{16,8},{24,16},{32,24},{40,32},{48,40},{56,48},{64,56},{72,6... | collective-permute-start | bytes 1572872 | tf_op jit(solution)/shard_map/ppermute | solution.py:17
  30.9 0.0 collective-permute-done.1
  30.9 0.1 maximum_convert_fusion
  31.0 0.6 copy.18
  31.6 1.0 fusion.33
  32.6 0.6 collective-permute-start
  33.2 3.4 %collective-permute-done = f32[64,64]{1,0:T(8,128)S(1)} collective-permute-done((f32[64,64]{1,0:T(8,128)S(1)}, f32[64,64]{1,0:T(8,128)S(1)}, u32[]{:S(2)}, u32[]{:S(2)}) %collective-permute-start) | collective-permute-done | bytes 16416 | tf_op jit(solution)/shard_map/ppermute | solution.py:53
  36.6 0.0 collective-permute-done.3
  36.6 0.2 pad_maximum_fusion
  36.8 1.3 %fusion.4 = f32[64,1,16,512]{3,0,2,1:T(8,128)S(1)} fusion(f32[64,1,16,512]{3,0,2,1:T(8,128)S(1)} %pad_maximum_fusion, f32[16,512]{1,0:T(8,128)S(1)} %get-tuple-element.37, f32[16,512]{1,0:T(8,128)S(1)} %get-tuple-element.38, f32[16,512]{1,0:T(8,128)S(1)} %get-tuple-element.39, f32[16,512]{1,0:T(8,128)S(1)} %get-tuple-element.40, ...), kind=kLoop, calls=%fused_computation.20 | loop fusion | flops 4718592 | bytes 4358144 | tf_op jit(solution)/shard_map/add | solution.py:33
  38.1 1.2 %collective-permute-start.5 = (f32[64,64]{1,0:T(8,128)S(1)}, f32[64,64]{1,0:T(8,128)S(1)}, u32[]{:S(2)}, u32[]{:S(2)}) collective-permute-start(f32[64,64]{1,0:T(8,128)S(1)} %add.107), channel_id=1, source_target_pairs={{0,2},{1,3},{2,0},{3,1},{4,6},{5,7},{6,4},{7,5},{8,10},{9,11},{10,... | collective-permute-start | bytes 49160 | tf_op jit(solution)/shard_map/ppermute | solution.py:53
  39.3 1.3 %fusion.10 = f32[64,1,16,512]{3,0,2,1:T(8,128)S(1)} fusion(f32[64,1,16,512]{3,0,2,1:T(8,128)S(1)} %fusion.4, f32[16,512]{1,0:T(8,128)S(1)} %get-tuple-element.33, f32[16,512]{1,0:T(8,128)S(1)} %get-tuple-element.34, f32[16,512]{1,0:T(8,128)S(1)} %get-tuple-element.35, f32[16,512]{1,0:T(8,128)S(1)} %get-tuple-element.36, f32[16,512]{1,0:T(8,128)S(1)} %get-tuple-element.32), kind=kLoop, calls=%fused_computation.26 | loop fusion | flops 4718592 | bytes 4358144 | tf_op jit(solution)/shard_map/add | solution.py:33
  40.6 3.0 %collective-permute-done.5 = f32[64,64]{1,0:T(8,128)S(1)} collective-permute-done((f32[64,64]{1,0:T(8,128)S(1)}, f32[64,64]{1,0:T(8,128)S(1)}, u32[]{:S(2)}, u32[]{:S(2)}) %collective-permute-start.5) | collective-permute-done | bytes 16416 | tf_op jit(solution)/shard_map/ppermute | solution.py:53
  43.6 1.2 %broadcast_multiply_fusion = (f32[64,1,16,512]{3,0,2,1:T(8,128)S(1)}, f32[64,1,16,512]{3,0,2,1:T(8,128)S(1)}, f32[64,1,16,512]{3,0,2,1:T(8,128)S(1)}, f32[64,1,16,512]{3,0,2,1:T(8,128)S(1)}) fusion(f32[64,1,16,512]{3,0,2,1:T(8,128)S(1)} %fusion.10, f32[16,512]{1,0:T(8,128)S(1)} %get-tuple-element.33, f32[16,512]{1,0:T(8,128)S(1)} %get-tuple-element.34, ...), kind=kLoop, calls=%fused_computation.50 | loop fusion | flops 2097152 | bytes 10616832 | tf_op jit(solution)/shard_map/mul | solution.py:38
  44.8 1.0 convolution_bitcast_fusion.2
  45.8 0.6 collective-permute-start.6
  46.5 1.5 %fusion.15 = f32[64,1,16,512]{3,0,2,1:T(8,128)S(1)} fusion(f32[64,1,16,512]{3,0,2,1:T(8,128)S(1)} %get-tuple-element.29, f32[64,1,16,512]{3,0,2,1:T(8,128)S(1)} %get-tuple-element.28, f32[64,1,16,512]{3,0,2,1:T(8,128)S(1)} %get-tuple-element.27, f32[64,1,16,512]{3,0,2,1:T(8,128)S(1)} %get-tuple-element.26, f32[64,1,16,512]{3,0,2,1:T(8,128)S(1)} %fusion.10, ...), kind=kLoop, calls=%fused_computation.31 | loop fusion | flops 2621440 | bytes 12615680 | tf_op jit(solution)/shard_map/add | solution.py:38
  48.0 3.7 %collective-permute-done.6 = f32[2,64,64]{2,1,0:T(8,128)S(1)} collective-permute-done((f32[2,64,64]{2,1,0:T(8,128)S(1)}, f32[2,64,64]{2,1,0:T(8,128)S(1)}, u32[]{:S(2)}, u32[]{:S(2)}) %collective-permute-start.6) | collective-permute-done | bytes 32800 | tf_op jit(solution)/shard_map/ppermute | solution.py:53
  51.7 1.2 %broadcast_multiply_fusion.4 = (f32[64,1,16,512]{3,0,2,1:T(8,128)S(1)}, f32[64,1,16,512]{3,0,2,1:T(8,128)S(1)}, f32[64,1,16,512]{3,0,2,1:T(8,128)S(1)}, f32[64,1,16,512]{3,0,2,1:T(8,128)S(1)}) fusion(f32[64,1,16,512]{3,0,2,1:T(8,128)S(1)} %fusion.15, f32[16,512]{1,0:T(8,128)S(1)} %get-tuple-element.37, f32[16,512]{1,0:T(8,128)S(1)} %get-tuple-element.38, ...), kind=kLoop, calls=%fused_computation.54 | loop fusion | flops 2097152 | bytes 10616832 | tf_op jit(solution)/shard_map/mul | solution.py:38
  52.9 3.7 %collective-permute-start.7 = (f32[2,64,64]{2,1,0:T(8,128)S(1)}, f32[2,64,64]{2,1,0:T(8,128)S(1)}, u32[]{:S(2)}, u32[]{:S(2)}) collective-permute-start(f32[2,64,64]{2,1,0:T(8,128)S(1)} %fusion.30), channel_id=1, source_target_pairs={{0,8},{8,0},{16,24},{24,16},{32,40},{40,32},{48,56},{56,48},{64,72... | collective-permute-start | bytes 98312 | tf_op jit(solution)/shard_map/ppermute | solution.py:53
  56.7 1.4 %fusion.19 = f32[64,1,16,512]{3,0,2,1:T(8,128)S(1)} fusion(f32[64,1,16,512]{3,0,2,1:T(8,128)S(1)} %get-tuple-element.25, f32[64,1,16,512]{3,0,2,1:T(8,128)S(1)} %get-tuple-element.24, f32[64,1,16,512]{3,0,2,1:T(8,128)S(1)} %get-tuple-element.23, f32[64,1,16,512]{3,0,2,1:T(8,128)S(1)} %get-tuple-element.22, f32[64,1,16,512]{3,0,2,1:T(8,128)S(1)} %fusion.15, ...), kind=kLoop, calls=%fused_computation.35 | loop fusion | flops 2621440 | bytes 12615680 | tf_op jit(solution)/shard_map/add | solution.py:38
  58.1 2.8 %collective-permute-start.8 = (f32[2,64,64]{2,1,0:T(8,128)S(1)}, f32[2,64,64]{2,1,0:T(8,128)S(1)}, u32[]{:S(2)}, u32[]{:S(2)}) collective-permute-start(f32[2,64,64]{2,1,0:T(8,128)S(1)} %add.122), channel_id=1, source_target_pairs={{0,16},{8,24},{16,0},{24,8},{32,48},{40,56},{48,32},{56,40},{64,80... | collective-permute-start | bytes 98312 | tf_op jit(solution)/shard_map/ppermute | solution.py:53
  61.0 2.7 %collective-permute-done.8 = f32[2,64,64]{2,1,0:T(8,128)S(1)} collective-permute-done((f32[2,64,64]{2,1,0:T(8,128)S(1)}, f32[2,64,64]{2,1,0:T(8,128)S(1)}, u32[]{:S(2)}, u32[]{:S(2)}) %collective-permute-start.8) | collective-permute-done | bytes 32800 | tf_op jit(solution)/shard_map/ppermute | solution.py:53
  63.6 3.6 %collective-permute-start.9 = (f32[2,64,64]{2,1,0:T(8,128)S(1)}, f32[2,64,64]{2,1,0:T(8,128)S(1)}, u32[]{:S(2)}, u32[]{:S(2)}) collective-permute-start(f32[2,64,64]{2,1,0:T(8,128)S(1)} %add.127), channel_id=1, source_target_pairs={{0,32},{8,40},{16,48},{24,56},{32,0},{40,8},{48,16},{56,24},{64,96... | collective-permute-start | bytes 98312 | tf_op jit(solution)/shard_map/ppermute | solution.py:53
  67.3 2.2 %collective-permute-done.9 = f32[2,64,64]{2,1,0:T(8,128)S(1)} collective-permute-done((f32[2,64,64]{2,1,0:T(8,128)S(1)}, f32[2,64,64]{2,1,0:T(8,128)S(1)}, u32[]{:S(2)}, u32[]{:S(2)}) %collective-permute-start.9) | collective-permute-done | bytes 32800 | tf_op jit(solution)/shard_map/ppermute | solution.py:53
  69.5 2.3 %collective-permute-start.10 = (f32[2,64,64]{2,1,0:T(8,128)S(1)}, f32[2,64,64]{2,1,0:T(8,128)S(1)}, u32[]{:S(2)}, u32[]{:S(2)}) collective-permute-start(f32[2,64,64]{2,1,0:T(8,128)S(1)} %add.128), channel_id=1, source_target_pairs={{0,64},{8,72},{16,80},{24,88},{32,96},{40,104},{48,112},{56,120},{... | collective-permute-start | bytes 98312 | tf_op jit(solution)/shard_map/ppermute | solution.py:53
  71.9 2.2 %collective-permute-done.10 = f32[2,64,64]{2,1,0:T(8,128)S(1)} collective-permute-done((f32[2,64,64]{2,1,0:T(8,128)S(1)}, f32[2,64,64]{2,1,0:T(8,128)S(1)}, u32[]{:S(2)}, u32[]{:S(2)}) %collective-permute-start.10) | collective-permute-done | bytes 32800 | tf_op jit(solution)/shard_map/ppermute | solution.py:53
  74.1 0.6 slice_bitcast_fusion
  74.8 0.6 collective-permute-start.11
  75.4 13.0 %shard_map.41 = f32[64,64]{1,0:T(8,128)} custom-call(f32[64,64]{1,0:T(8,128)} %get-tuple-element.45.g_ref), custom_call_target="tpu_custom_call" | custom-call | tf_op jit(solution)/shard_map/pallas_call | solution.py:84
  88.4 0.0 collective-permute-done.11
  88.4 1.1 convolution_bitcast_fusion.1
  89.4 1.0 convolution_bitcast_fusion
  90.5 1.6 %copy.15 = f32[64,1,8,512]{3,2,1,0:T(8,128)} copy(f32[64,1,8,512]{3,0,2,1:T(8,128)S(1)} %convolution_bitcast_fusion) | data formatting | bytes 2097152 | tf_op jit(solution)/shard_map/dot_general | solution.py:141
  92.0 3.9 %all-to-all-start.1 = ((f32[64,1,8,512]{3,2,1,0:T(8,128)}), f32[64,1,8,512]{3,2,1,0:T(8,128)S(1)}, u32[]{:S(2)}, u32[]{:S(2)}) async-start(f32[64,1,8,512]{3,2,1,0:T(8,128)} %copy.15), calls=%async_computation.1 | async-start | bytes 2097152 | tf_op jit(solution)/shard_map/all_to_all | solution.py:145
  95.9 3.5 %collective-permute-start.12 = (f32[64,64]{1,0:T(8,128)S(1)}, f32[64,64]{1,0:T(8,128)S(1)}, u32[]{:S(2)}, u32[]{:S(2)}) collective-permute-start(f32[64,64]{1,0:T(8,128)S(1)} %fusion.29), channel_id=1, source_target_pairs={{0,2},{1,3},{2,0},{3,1},{4,6},{5,7},{6,4},{7,5},{8,10},{9,11},{10,... | collective-permute-start | bytes 49160 | tf_op jit(solution)/shard_map/ppermute | solution.py:53
  99.5 9.8 %collective-permute-done.12 = f32[64,64]{1,0:T(8,128)S(1)} collective-permute-done((f32[64,64]{1,0:T(8,128)S(1)}, f32[64,64]{1,0:T(8,128)S(1)}, u32[]{:S(2)}, u32[]{:S(2)}) %collective-permute-start.12) | collective-permute-done | bytes 16416 | tf_op jit(solution)/shard_map/ppermute | solution.py:53
  109.3 0.6 add_multiply_fusion
  109.9 1.1 all-to-all-done.1
  111.0 1.1 copy.30
  (16 shorter events, 0.1 us)
Async XLA Ops:
  0.6 9.4 %copy-start = (bf16[2,5,1,8,512]{4,3,2,1,0:T(8,128)(2,1)S(1)}, bf16[2,5,1,8,512]{4,3,2,1,0:T(8,128)(2,1)}, u32[]{:S(2)}) copy-start(bf16[2,5,1,8,512]{4,3,2,1,0:T(8,128)(2,1)} %param.3) | copy-start | bytes 245764
  3.0 24.2 %all-to-all-start = ((f32[8,8,8,512]{3,2,0,1:T(8,128)}), f32[8,8,8,512]{3,2,0,1:T(8,128)S(1)}, u32[]{:S(2)}, u32[]{:S(2)}) async-start(f32[8,8,8,512]{3,2,0,1:T(8,128)} %copy.11), calls=%async_computation | async-start | bytes 2097152 | tf_op jit(solution)/shard_map/all_to_all | solution.py:105
  10.0 20.8 %collective-permute-start.1 = (bf16[2,5,1,4,512]{4,3,2,1,0:T(4,128)(2,1)S(1)}, bf16[2,5,1,4,512]{4,3,2,1,0:T(4,128)(2,1)S(1)}, u32[]{:S(2)}, u32[]{:S(2)}) collective-permute-start(bf16[2,5,1,4,512]{4,3,2,1,0:T(4,128)(2,1)S(1)} %get-tuple-element.42), channel_id=1, source_target_pairs={{0,8},{8,16},{16,24},{24,32},{32,40},{40,48},{48,56},{56,64},{64,7... | collective-permute-start | bytes 122888 | tf_op jit(solution)/shard_map/ppermute | solution.py:16
  11.5 19.4 %collective-permute-start.2 = (bf16[2,5,1,4,512]{4,3,2,1,0:T(4,128)(2,1)S(1)}, bf16[2,5,1,4,512]{4,3,2,1,0:T(4,128)(2,1)S(1)}, u32[]{:S(2)}, u32[]{:S(2)}) collective-permute-start(bf16[2,5,1,4,512]{4,3,2,1,0:T(4,128)(2,1)S(1)} %get-tuple-element.43), channel_id=1, source_target_pairs={{8,0},{16,8},{24,16},{32,24},{40,32},{48,40},{56,48},{64,56},{72,6... | collective-permute-start | bytes 122888 | tf_op jit(solution)/shard_map/ppermute | solution.py:17
  27.9 8.7 %collective-permute-start.3 = (f32[64,1,4,512]{3,0,2,1:T(8,128)S(1)}, f32[64,1,4,512]{3,0,2,1:T(8,128)S(1)}, u32[]{:S(2)}, u32[]{:S(2)}) collective-permute-start(f32[64,1,4,512]{3,0,2,1:T(8,128)S(1)} %get-tuple-element.30), channel_id=1, source_target_pairs={{0,8},{8,16},{16,24},{24,32},{32,40},{40,48},{48,56},{56,64},{64,7... | collective-permute-start | bytes 1572872 | tf_op jit(solution)/shard_map/ppermute | solution.py:16
  29.6 7.0 %collective-permute-start.4 = (f32[64,1,4,512]{3,0,2,1:T(8,128)S(1)}, f32[64,1,4,512]{3,0,2,1:T(8,128)S(1)}, u32[]{:S(2)}, u32[]{:S(2)}) collective-permute-start(f32[64,1,4,512]{3,0,2,1:T(8,128)S(1)} %get-tuple-element.31), channel_id=1, source_target_pairs={{8,0},{16,8},{24,16},{32,24},{40,32},{48,40},{56,48},{64,56},{72,6... | collective-permute-start | bytes 1572872 | tf_op jit(solution)/shard_map/ppermute | solution.py:17
  32.6 4.0 %collective-permute-start = (f32[64,64]{1,0:T(8,128)S(1)}, f32[64,64]{1,0:T(8,128)S(1)}, u32[]{:S(2)}, u32[]{:S(2)}) collective-permute-start(f32[64,64]{1,0:T(8,128)S(1)} %fusion.33), channel_id=1, source_target_pairs={{0,1},{1,0},{2,3},{3,2},{4,5},{5,4},{6,7},{7,6},{8,9},{9,8},{10,11... | collective-permute-start | bytes 49160 | tf_op jit(solution)/shard_map/ppermute | solution.py:53
  38.1 5.5 %collective-permute-start.5 = (f32[64,64]{1,0:T(8,128)S(1)}, f32[64,64]{1,0:T(8,128)S(1)}, u32[]{:S(2)}, u32[]{:S(2)}) collective-permute-start(f32[64,64]{1,0:T(8,128)S(1)} %add.107), channel_id=1, source_target_pairs={{0,2},{1,3},{2,0},{3,1},{4,6},{5,7},{6,4},{7,5},{8,10},{9,11},{10,... | collective-permute-start | bytes 49160 | tf_op jit(solution)/shard_map/ppermute | solution.py:53
  45.8 5.8 %collective-permute-start.6 = (f32[2,64,64]{2,1,0:T(8,128)S(1)}, f32[2,64,64]{2,1,0:T(8,128)S(1)}, u32[]{:S(2)}, u32[]{:S(2)}) collective-permute-start(f32[2,64,64]{2,1,0:T(8,128)S(1)} %pad_maximum_fusion.1), channel_id=1, source_target_pairs={{0,4},{1,5},{2,6},{3,7},{4,0},{5,1},{6,2},{7,3},{8,12},{9,13},{10,... | collective-permute-start | bytes 98312 | tf_op jit(solution)/shard_map/ppermute | solution.py:53
  52.9 5.2 %collective-permute-start.7 = (f32[2,64,64]{2,1,0:T(8,128)S(1)}, f32[2,64,64]{2,1,0:T(8,128)S(1)}, u32[]{:S(2)}, u32[]{:S(2)}) collective-permute-start(f32[2,64,64]{2,1,0:T(8,128)S(1)} %fusion.30), channel_id=1, source_target_pairs={{0,8},{8,0},{16,24},{24,16},{32,40},{40,32},{48,56},{56,48},{64,72... | collective-permute-start | bytes 98312 | tf_op jit(solution)/shard_map/ppermute | solution.py:53
  58.1 5.5 %collective-permute-start.8 = (f32[2,64,64]{2,1,0:T(8,128)S(1)}, f32[2,64,64]{2,1,0:T(8,128)S(1)}, u32[]{:S(2)}, u32[]{:S(2)}) collective-permute-start(f32[2,64,64]{2,1,0:T(8,128)S(1)} %add.122), channel_id=1, source_target_pairs={{0,16},{8,24},{16,0},{24,8},{32,48},{40,56},{48,32},{56,40},{64,80... | collective-permute-start | bytes 98312 | tf_op jit(solution)/shard_map/ppermute | solution.py:53
  63.6 5.9 %collective-permute-start.9 = (f32[2,64,64]{2,1,0:T(8,128)S(1)}, f32[2,64,64]{2,1,0:T(8,128)S(1)}, u32[]{:S(2)}, u32[]{:S(2)}) collective-permute-start(f32[2,64,64]{2,1,0:T(8,128)S(1)} %add.127), channel_id=1, source_target_pairs={{0,32},{8,40},{16,48},{24,56},{32,0},{40,8},{48,16},{56,24},{64,96... | collective-permute-start | bytes 98312 | tf_op jit(solution)/shard_map/ppermute | solution.py:53
  69.5 4.6 %collective-permute-start.10 = (f32[2,64,64]{2,1,0:T(8,128)S(1)}, f32[2,64,64]{2,1,0:T(8,128)S(1)}, u32[]{:S(2)}, u32[]{:S(2)}) collective-permute-start(f32[2,64,64]{2,1,0:T(8,128)S(1)} %add.128), channel_id=1, source_target_pairs={{0,64},{8,72},{16,80},{24,88},{32,96},{40,104},{48,112},{56,120},{... | collective-permute-start | bytes 98312 | tf_op jit(solution)/shard_map/ppermute | solution.py:53
  74.8 13.6 %collective-permute-start.11 = (f32[64,64]{1,0:T(8,128)S(1)}, f32[64,64]{1,0:T(8,128)S(1)}, u32[]{:S(2)}, u32[]{:S(2)}) collective-permute-start(f32[64,64]{1,0:T(8,128)S(1)} %get-tuple-element.44), channel_id=1, source_target_pairs={{0,1},{1,0},{2,3},{3,2},{4,5},{5,4},{6,7},{7,6},{8,9},{9,8},{10,11... | collective-permute-start | bytes 49160 | tf_op jit(solution)/shard_map/ppermute | solution.py:53
  92.0 18.9 %all-to-all-start.1 = ((f32[64,1,8,512]{3,2,1,0:T(8,128)}), f32[64,1,8,512]{3,2,1,0:T(8,128)S(1)}, u32[]{:S(2)}, u32[]{:S(2)}) async-start(f32[64,1,8,512]{3,2,1,0:T(8,128)} %copy.15), calls=%async_computation.1 | async-start | bytes 2097152 | tf_op jit(solution)/shard_map/all_to_all | solution.py:145
  95.9 13.3 %collective-permute-start.12 = (f32[64,64]{1,0:T(8,128)S(1)}, f32[64,64]{1,0:T(8,128)S(1)}, u32[]{:S(2)}, u32[]{:S(2)}) collective-permute-start(f32[64,64]{1,0:T(8,128)S(1)} %fusion.29), channel_id=1, source_target_pairs={{0,2},{1,3},{2,0},{3,1},{4,6},{5,7},{6,4},{7,5},{8,10},{9,11},{10,... | collective-permute-start | bytes 49160 | tf_op jit(solution)/shard_map/ppermute | solution.py:53

commit v17 on v9

--- a/solution.py
+++ b/solution.py
@@ -79,21 +79,25 @@
     lax.fori_loop(0, n, step, 0)
 
 
-def lower_inverse(gram):
-    n = gram.shape[0]
-    return pl.pallas_call(
-        chol_inv_kernel,
-        out_shape=jax.ShapeDtypeStruct((n, n), jnp.float32),
-        scratch_shapes=[pltpu.VMEM((n, n), jnp.float32)],
-    )(gram)
+def inverse_kernel(g_ref, o_ref, x_ref, a_ref):
+    chol_inv_kernel(g_ref, x_ref, a_ref)
+    x = x_ref[...]
+    o_ref[...] = lax.dot_general(
+        x, x, (((0,), (0,)), ((), ())), precision=lax.Precision.HIGHEST,
+        preferred_element_type=jnp.float32,
+    )
 
 
 def invert_beside(gram, extra, bits):
-    solved = lower_inverse(gram)
+    n = gram.shape[0]
+    inverse = pl.pallas_call(
+        inverse_kernel,
+        out_shape=jax.ShapeDtypeStruct((n, n), jnp.float32),
+        scratch_shapes=[pltpu.VMEM((n, n), jnp.float32), pltpu.VMEM((n, n), jnp.float32)],
+    )(gram)
     if bits:
         extra = exchange(extra, *bits.pop(0))
-    solved, extra = lax.optimization_barrier((solved, extra))
-    inverse = jnp.dot(solved.T, solved, precision=lax.Precision.HIGHEST)
+    inverse, extra = lax.optimization_barrier((inverse, extra))
     return inverse, extra
 
 

time: 108 us -> 108 us (level)
  no operation moved by 1% of the time
where the time goes in v17:
time: 108 us; the launch traced here: 107 us
  waiting for transfers between devices  42.5 us (39%)
  starting transfers between devices  35.8 us (33%)
  other arithmetic  9.57 us (9%)
  Pallas kernels  8.38 us (8%)
  local copies, waits for them, and re-layouts  6.31 us (6%)
  matrix products  3.73 us (3%)
    ppermute x9, waiting for transfers between devices, exchange(): return x + lax.ppermute(x, axis, [(i, i ^ bit) for i in range(count)])  27 us
    ppermute x9, starting transfers between devices, exchange(): return x + lax.ppermute(x, axis, [(i, i ^ bit) for i in range(count)])  19.2 us
    all_to_all x1, waiting for transfers between devices, body(): v = lax.all_to_all(perturbations, 'mem', 1, 0, tiled=True)  14.4 us
    pallas_call x1, Pallas kernels, invert_beside(): pl.pallas_call(inverse_kernel, out_shape=jax.ShapeDtypeStruct((n, n), jnp...  8.38 us
    all_to_all x1, starting transfers between devices, body(): v = lax.all_to_all(perturbations, 'mem', 1, 0, tiled=True)  7.04 us
    all_to_all x1, starting transfers between devices, body(): ritz = lax.all_to_all(ritz.reshape(v.shape), 'mem', 0, 1, tiled=True)  3.88 us
    ppermute x2, starting transfers between devices, halo(): lax.ppermute(lax.slice_in_dim(block, size - width, size, axis=dim), 'dom'...  3.12 us
    add x2, other arithmetic, adjoint_step(): result + shifted(coef[3] * field, 1, 3) + shifted(coef[4] * field, -1, 3)  2.94 us
  transfers between devices with their start and end apart: 15, of which 9 were waited for; matrix products, arithmetic and copies ran while one was open for 7% of the time, Pallas kernels for 8%

profile of v17, /device:TPU:0, one launch (start us, length us, event | category | flops | bytes accessed | tf_op | source)
XLA Modules:
  0.0 107.2 jit_solution(5967243709324447525)
XLA Ops:
  0.6 2.3 %copy.11 = f32[8,8,8,512]{3,2,0,1:T(8,128)} copy(f32[8,8,8,512]{3,2,1,0:T(8,128)} %param.2) | data formatting | bytes 2097152 | tf_op args[0]
  3.0 7.0 %all-to-all-start = ((f32[8,8,8,512]{3,2,0,1:T(8,128)}), f32[8,8,8,512]{3,2,0,1:T(8,128)S(1)}, u32[]{:S(2)}, u32[]{:S(2)}) async-start(f32[8,8,8,512]{3,2,0,1:T(8,128)} %copy.11), calls=%async_computation | async-start | bytes 2097152 | tf_op jit(solution)/shard_map/all_to_all | solution.py:109
  10.0 1.5 %collective-permute-start.1 = (bf16[2,5,1,4,512]{4,3,2,1,0:T(4,128)(2,1)S(1)}, bf16[2,5,1,4,512]{4,3,2,1,0:T(4,128)(2,1)S(1)}, u32[]{:S(2)}, u32[]{:S(2)}) collective-permute-start(bf16[2,5,1,4,512]{4,3,2,1,0:T(4,128)(2,1)S(1)} %get-tuple-element.42), channel_id=1, source_target_pairs={{0,8},{8,16},{16,24},{24,32},{32,40},{40,48},{48,56},{56,64},{64,7... | collective-permute-start | bytes 122888 | tf_op jit(solution)/shard_map/ppermute | solution.py:16
  11.5 1.3 %collective-permute-start.2 = (bf16[2,5,1,4,512]{4,3,2,1,0:T(4,128)(2,1)S(1)}, bf16[2,5,1,4,512]{4,3,2,1,0:T(4,128)(2,1)S(1)}, u32[]{:S(2)}, u32[]{:S(2)}) collective-permute-start(bf16[2,5,1,4,512]{4,3,2,1,0:T(4,128)(2,1)S(1)} %get-tuple-element.43), channel_id=1, source_target_pairs={{8,0},{16,8},{24,16},{32,24},{40,32},{48,40},{56,48},{64,56},{72,6... | collective-permute-start | bytes 122888 | tf_op jit(solution)/shard_map/ppermute | solution.py:17
  12.8 14.4 %all-to-all-done = f32[8,8,8,512]{3,2,0,1:T(8,128)S(1)} async-done(((f32[8,8,8,512]{3,2,0,1:T(8,128)}), f32[8,8,8,512]{3,2,0,1:T(8,128)S(1)}, u32[]{:S(2)}, u32[]{:S(2)}) %all-to-all-start) | async-done | bytes 1048608 | tf_op jit(solution)/shard_map/all_to_all | solution.py:109
  27.2 0.6 copy.31
  27.8 0.1 fusion.32
  27.9 1.7 %collective-permute-start.3 = (f32[64,1,4,512]{3,0,2,1:T(8,128)S(1)}, f32[64,1,4,512]{3,0,2,1:T(8,128)S(1)}, u32[]{:S(2)}, u32[]{:S(2)}) collective-permute-start(f32[64,1,4,512]{3,0,2,1:T(8,128)S(1)} %get-tuple-element.30), channel_id=1, source_target_pairs={{0,8},{8,16},{16,24},{24,32},{32,40},{40,48},{48,56},{56,64},{64,7... | collective-permute-start | bytes 1572872 | tf_op jit(solution)/shard_map/ppermute | solution.py:16
  29.6 1.3 %collective-permute-start.4 = (f32[64,1,4,512]{3,0,2,1:T(8,128)S(1)}, f32[64,1,4,512]{3,0,2,1:T(8,128)S(1)}, u32[]{:S(2)}, u32[]{:S(2)}) collective-permute-start(f32[64,1,4,512]{3,0,2,1:T(8,128)S(1)} %get-tuple-element.31), channel_id=1, source_target_pairs={{8,0},{16,8},{24,16},{32,24},{40,32},{48,40},{56,48},{64,56},{72,6... | collective-permute-start | bytes 1572872 | tf_op jit(solution)/shard_map/ppermute | solution.py:17
  30.9 0.0 collective-permute-done.2
  30.9 0.1 maximum_convert_fusion
  31.0 0.6 copy.18
  31.6 1.0 fusion.34
  32.6 0.6 collective-permute-start
  33.2 3.4 %collective-permute-done = f32[64,64]{1,0:T(8,128)S(1)} collective-permute-done((f32[64,64]{1,0:T(8,128)S(1)}, f32[64,64]{1,0:T(8,128)S(1)}, u32[]{:S(2)}, u32[]{:S(2)}) %collective-permute-start) | collective-permute-done | bytes 16416 | tf_op jit(solution)/shard_map/ppermute | solution.py:53
  36.6 0.0 collective-permute-done.3
  36.6 0.0 collective-permute-done.4
  36.6 0.2 pad_maximum_fusion
  36.8 1.3 %fusion.4 = f32[64,1,16,512]{3,0,2,1:T(8,128)S(1)} fusion(f32[64,1,16,512]{3,0,2,1:T(8,128)S(1)} %pad_maximum_fusion, f32[16,512]{1,0:T(8,128)S(1)} %get-tuple-element.37, f32[16,512]{1,0:T(8,128)S(1)} %get-tuple-element.38, f32[16,512]{1,0:T(8,128)S(1)} %get-tuple-element.39, f32[16,512]{1,0:T(8,128)S(1)} %get-tuple-element.40, ...), kind=kLoop, calls=%fused_computation.20 | loop fusion | flops 4718592 | bytes 4358144 | tf_op jit(solution)/shard_map/add | solution.py:33
  38.1 1.2 %collective-permute-start.5 = (f32[64,64]{1,0:T(8,128)S(1)}, f32[64,64]{1,0:T(8,128)S(1)}, u32[]{:S(2)}, u32[]{:S(2)}) collective-permute-start(f32[64,64]{1,0:T(8,128)S(1)} %add.107), channel_id=1, source_target_pairs={{0,2},{1,3},{2,0},{3,1},{4,6},{5,7},{6,4},{7,5},{8,10},{9,11},{10,... | collective-permute-start | bytes 49160 | tf_op jit(solution)/shard_map/ppermute | solution.py:53
  39.3 1.3 %fusion.10 = f32[64,1,16,512]{3,0,2,1:T(8,128)S(1)} fusion(f32[64,1,16,512]{3,0,2,1:T(8,128)S(1)} %fusion.4, f32[16,512]{1,0:T(8,128)S(1)} %get-tuple-element.33, f32[16,512]{1,0:T(8,128)S(1)} %get-tuple-element.34, f32[16,512]{1,0:T(8,128)S(1)} %get-tuple-element.35, f32[16,512]{1,0:T(8,128)S(1)} %get-tuple-element.36, f32[16,512]{1,0:T(8,128)S(1)} %get-tuple-element.32), kind=kLoop, calls=%fused_computation.26 | loop fusion | flops 4718592 | bytes 4358144 | tf_op jit(solution)/shard_map/add | solution.py:33
  40.6 3.0 %collective-permute-done.5 = f32[64,64]{1,0:T(8,128)S(1)} collective-permute-done((f32[64,64]{1,0:T(8,128)S(1)}, f32[64,64]{1,0:T(8,128)S(1)}, u32[]{:S(2)}, u32[]{:S(2)}) %collective-permute-start.5) | collective-permute-done | bytes 16416 | tf_op jit(solution)/shard_map/ppermute | solution.py:53
  43.6 1.2 %broadcast_multiply_fusion = (f32[64,1,16,512]{3,0,2,1:T(8,128)S(1)}, f32[64,1,16,512]{3,0,2,1:T(8,128)S(1)}, f32[64,1,16,512]{3,0,2,1:T(8,128)S(1)}, f32[64,1,16,512]{3,0,2,1:T(8,128)S(1)}) fusion(f32[64,1,16,512]{3,0,2,1:T(8,128)S(1)} %fusion.10, f32[16,512]{1,0:T(8,128)S(1)} %get-tuple-element.33, f32[16,512]{1,0:T(8,128)S(1)} %get-tuple-element.34, ...), kind=kLoop, calls=%fused_computation.49 | loop fusion | flops 2097152 | bytes 10616832 | tf_op jit(solution)/shard_map/mul | solution.py:38
  44.8 1.0 convolution_bitcast_fusion.1
  45.8 0.6 collective-permute-start.6
  46.5 1.5 %fusion.15 = f32[64,1,16,512]{3,0,2,1:T(8,128)S(1)} fusion(f32[64,1,16,512]{3,0,2,1:T(8,128)S(1)} %get-tuple-element.29, f32[64,1,16,512]{3,0,2,1:T(8,128)S(1)} %get-tuple-element.28, f32[64,1,16,512]{3,0,2,1:T(8,128)S(1)} %get-tuple-element.27, f32[64,1,16,512]{3,0,2,1:T(8,128)S(1)} %get-tuple-element.26, f32[64,1,16,512]{3,0,2,1:T(8,128)S(1)} %fusion.10, ...), kind=kLoop, calls=%fused_computation.31 | loop fusion | flops 2621440 | bytes 12615680 | tf_op jit(solution)/shard_map/add | solution.py:38
  48.0 3.7 %collective-permute-done.6 = f32[2,64,64]{2,1,0:T(8,128)S(1)} collective-permute-done((f32[2,64,64]{2,1,0:T(8,128)S(1)}, f32[2,64,64]{2,1,0:T(8,128)S(1)}, u32[]{:S(2)}, u32[]{:S(2)}) %collective-permute-start.6) | collective-permute-done | bytes 32800 | tf_op jit(solution)/shard_map/ppermute | solution.py:53
  51.7 1.2 %broadcast_multiply_fusion.4 = (f32[64,1,16,512]{3,0,2,1:T(8,128)S(1)}, f32[64,1,16,512]{3,0,2,1:T(8,128)S(1)}, f32[64,1,16,512]{3,0,2,1:T(8,128)S(1)}, f32[64,1,16,512]{3,0,2,1:T(8,128)S(1)}) fusion(f32[64,1,16,512]{3,0,2,1:T(8,128)S(1)} %fusion.15, f32[16,512]{1,0:T(8,128)S(1)} %get-tuple-element.37, f32[16,512]{1,0:T(8,128)S(1)} %get-tuple-element.38, ...), kind=kLoop, calls=%fused_computation.53 | loop fusion | flops 2097152 | bytes 10616832 | tf_op jit(solution)/shard_map/mul | solution.py:38
  52.9 3.7 %collective-permute-start.7 = (f32[2,64,64]{2,1,0:T(8,128)S(1)}, f32[2,64,64]{2,1,0:T(8,128)S(1)}, u32[]{:S(2)}, u32[]{:S(2)}) collective-permute-start(f32[2,64,64]{2,1,0:T(8,128)S(1)} %fusion.31), channel_id=1, source_target_pairs={{0,8},{8,0},{16,24},{24,16},{32,40},{40,32},{48,56},{56,48},{64,72... | collective-permute-start | bytes 98312 | tf_op jit(solution)/shard_map/ppermute | solution.py:53
  56.7 1.4 %fusion.19 = f32[64,1,16,512]{3,0,2,1:T(8,128)S(1)} fusion(f32[64,1,16,512]{3,0,2,1:T(8,128)S(1)} %get-tuple-element.25, f32[64,1,16,512]{3,0,2,1:T(8,128)S(1)} %get-tuple-element.24, f32[64,1,16,512]{3,0,2,1:T(8,128)S(1)} %get-tuple-element.23, f32[64,1,16,512]{3,0,2,1:T(8,128)S(1)} %get-tuple-element.22, f32[64,1,16,512]{3,0,2,1:T(8,128)S(1)} %fusion.15, ...), kind=kLoop, calls=%fused_computation.35 | loop fusion | flops 2621440 | bytes 12615680 | tf_op jit(solution)/shard_map/add | solution.py:38
  58.1 0.0 collective-permute-done.7
  58.1 2.8 %collective-permute-start.8 = (f32[2,64,64]{2,1,0:T(8,128)S(1)}, f32[2,64,64]{2,1,0:T(8,128)S(1)}, u32[]{:S(2)}, u32[]{:S(2)}) collective-permute-start(f32[2,64,64]{2,1,0:T(8,128)S(1)} %add.122), channel_id=1, source_target_pairs={{0,16},{8,24},{16,0},{24,8},{32,48},{40,56},{48,32},{56,40},{64,80... | collective-permute-start | bytes 98312 | tf_op jit(solution)/shard_map/ppermute | solution.py:53
  61.0 2.7 %collective-permute-done.8 = f32[2,64,64]{2,1,0:T(8,128)S(1)} collective-permute-done((f32[2,64,64]{2,1,0:T(8,128)S(1)}, f32[2,64,64]{2,1,0:T(8,128)S(1)}, u32[]{:S(2)}, u32[]{:S(2)}) %collective-permute-start.8) | collective-permute-done | bytes 32800 | tf_op jit(solution)/shard_map/ppermute | solution.py:53
  63.6 3.6 %collective-permute-start.9 = (f32[2,64,64]{2,1,0:T(8,128)S(1)}, f32[2,64,64]{2,1,0:T(8,128)S(1)}, u32[]{:S(2)}, u32[]{:S(2)}) collective-permute-start(f32[2,64,64]{2,1,0:T(8,128)S(1)} %add.127), channel_id=1, source_target_pairs={{0,32},{8,40},{16,48},{24,56},{32,0},{40,8},{48,16},{56,24},{64,96... | collective-permute-start | bytes 98312 | tf_op jit(solution)/shard_map/ppermute | solution.py:53
  67.3 2.2 %collective-permute-done.9 = f32[2,64,64]{2,1,0:T(8,128)S(1)} collective-permute-done((f32[2,64,64]{2,1,0:T(8,128)S(1)}, f32[2,64,64]{2,1,0:T(8,128)S(1)}, u32[]{:S(2)}, u32[]{:S(2)}) %collective-permute-start.9) | collective-permute-done | bytes 32800 | tf_op jit(solution)/shard_map/ppermute | solution.py:53
  69.5 2.3 %collective-permute-start.10 = (f32[2,64,64]{2,1,0:T(8,128)S(1)}, f32[2,64,64]{2,1,0:T(8,128)S(1)}, u32[]{:S(2)}, u32[]{:S(2)}) collective-permute-start(f32[2,64,64]{2,1,0:T(8,128)S(1)} %add.128), channel_id=1, source_target_pairs={{0,64},{8,72},{16,80},{24,88},{32,96},{40,104},{48,112},{56,120},{... | collective-permute-start | bytes 98312 | tf_op jit(solution)/shard_map/ppermute | solution.py:53
  71.9 2.2 %collective-permute-done.10 = f32[2,64,64]{2,1,0:T(8,128)S(1)} collective-permute-done((f32[2,64,64]{2,1,0:T(8,128)S(1)}, f32[2,64,64]{2,1,0:T(8,128)S(1)}, u32[]{:S(2)}, u32[]{:S(2)}) %collective-permute-start.10) | collective-permute-done | bytes 32800 | tf_op jit(solution)/shard_map/ppermute | solution.py:53
  74.1 0.6 slice_bitcast_fusion
  74.8 0.6 collective-permute-start.11
  75.4 8.4 %shard_map.41 = f32[64,64]{1,0:T(8,128)} custom-call(f32[64,64]{1,0:T(8,128)} %get-tuple-element.45.g_ref), custom_call_target="tpu_custom_call" | custom-call | tf_op jit(solution)/shard_map/pallas_call | solution.py:93
  83.8 1.8 %convolution_bitcast_fusion = f32[64,1,8,512]{3,0,2,1:T(8,128)S(1)} fusion(f32[64,64]{1,0:T(8,128)} %shard_map.41, f32[64,1,16,512]{3,0,2,1:T(8,128)S(1)} %fusion.19), kind=kOutput, calls=%fused_computation.41 | convolution fusion | flops 201326592 | bytes 2113536 | tf_op jit(solution)/shard_map/dot_general | solution.py:145
  85.6 1.6 %copy.15 = f32[64,1,8,512]{3,2,1,0:T(8,128)} copy(f32[64,1,8,512]{3,0,2,1:T(8,128)S(1)} %convolution_bitcast_fusion) | data formatting | bytes 2097152 | tf_op jit(solution)/shard_map/dot_general | solution.py:145
  87.2 3.9 %all-to-all-start.1 = ((f32[64,1,8,512]{3,2,1,0:T(8,128)}), f32[64,1,8,512]{3,2,1,0:T(8,128)S(1)}, u32[]{:S(2)}, u32[]{:S(2)}) async-start(f32[64,1,8,512]{3,2,1,0:T(8,128)} %copy.15), calls=%async_computation.1 | async-start | bytes 2097152 | tf_op jit(solution)/shard_map/all_to_all | solution.py:149
  91.0 3.5 %collective-permute-start.12 = (f32[64,64]{1,0:T(8,128)S(1)}, f32[64,64]{1,0:T(8,128)S(1)}, u32[]{:S(2)}, u32[]{:S(2)}) collective-permute-start(f32[64,64]{1,0:T(8,128)S(1)} %fusion.30), channel_id=1, source_target_pairs={{0,2},{1,3},{2,0},{3,1},{4,6},{5,7},{6,4},{7,5},{8,10},{9,11},{10,... | collective-permute-start | bytes 49160 | tf_op jit(solution)/shard_map/ppermute | solution.py:53
  94.6 9.8 %collective-permute-done.12 = f32[64,64]{1,0:T(8,128)S(1)} collective-permute-done((f32[64,64]{1,0:T(8,128)S(1)}, f32[64,64]{1,0:T(8,128)S(1)}, u32[]{:S(2)}, u32[]{:S(2)}) %collective-permute-start.12) | collective-permute-done | bytes 16416 | tf_op jit(solution)/shard_map/ppermute | solution.py:53
  104.4 0.6 add_multiply_fusion
  105.0 1.1 %all-to-all-done.1 = f32[64,1,8,512]{3,2,1,0:T(8,128)S(1)} async-done(((f32[64,1,8,512]{3,2,1,0:T(8,128)}), f32[64,1,8,512]{3,2,1,0:T(8,128)S(1)}, u32[]{:S(2)}, u32[]{:S(2)}) %all-to-all-start.1) | async-done | bytes 1048608 | tf_op jit(solution)/shard_map/all_to_all | solution.py:149
  106.1 1.1 copy.30
  (15 shorter events, 0.1 us)
Async XLA Ops:
  0.6 9.4 %copy-start = (bf16[2,5,1,8,512]{4,3,2,1,0:T(8,128)(2,1)S(1)}, bf16[2,5,1,8,512]{4,3,2,1,0:T(8,128)(2,1)}, u32[]{:S(2)}) copy-start(bf16[2,5,1,8,512]{4,3,2,1,0:T(8,128)(2,1)} %param.3) | copy-start | bytes 245764
  3.0 24.2 %all-to-all-start = ((f32[8,8,8,512]{3,2,0,1:T(8,128)}), f32[8,8,8,512]{3,2,0,1:T(8,128)S(1)}, u32[]{:S(2)}, u32[]{:S(2)}) async-start(f32[8,8,8,512]{3,2,0,1:T(8,128)} %copy.11), calls=%async_computation | async-start | bytes 2097152 | tf_op jit(solution)/shard_map/all_to_all | solution.py:109
  10.0 20.8 %collective-permute-start.1 = (bf16[2,5,1,4,512]{4,3,2,1,0:T(4,128)(2,1)S(1)}, bf16[2,5,1,4,512]{4,3,2,1,0:T(4,128)(2,1)S(1)}, u32[]{:S(2)}, u32[]{:S(2)}) collective-permute-start(bf16[2,5,1,4,512]{4,3,2,1,0:T(4,128)(2,1)S(1)} %get-tuple-element.42), channel_id=1, source_target_pairs={{0,8},{8,16},{16,24},{24,32},{32,40},{40,48},{48,56},{56,64},{64,7... | collective-permute-start | bytes 122888 | tf_op jit(solution)/shard_map/ppermute | solution.py:16
  11.5 19.4 %collective-permute-start.2 = (bf16[2,5,1,4,512]{4,3,2,1,0:T(4,128)(2,1)S(1)}, bf16[2,5,1,4,512]{4,3,2,1,0:T(4,128)(2,1)S(1)}, u32[]{:S(2)}, u32[]{:S(2)}) collective-permute-start(bf16[2,5,1,4,512]{4,3,2,1,0:T(4,128)(2,1)S(1)} %get-tuple-element.43), channel_id=1, source_target_pairs={{8,0},{16,8},{24,16},{32,24},{40,32},{48,40},{56,48},{64,56},{72,6... | collective-permute-start | bytes 122888 | tf_op jit(solution)/shard_map/ppermute | solution.py:17
  27.9 8.7 %collective-permute-start.3 = (f32[64,1,4,512]{3,0,2,1:T(8,128)S(1)}, f32[64,1,4,512]{3,0,2,1:T(8,128)S(1)}, u32[]{:S(2)}, u32[]{:S(2)}) collective-permute-start(f32[64,1,4,512]{3,0,2,1:T(8,128)S(1)} %get-tuple-element.30), channel_id=1, source_target_pairs={{0,8},{8,16},{16,24},{24,32},{32,40},{40,48},{48,56},{56,64},{64,7... | collective-permute-start | bytes 1572872 | tf_op jit(solution)/shard_map/ppermute | solution.py:16
  29.6 7.0 %collective-permute-start.4 = (f32[64,1,4,512]{3,0,2,1:T(8,128)S(1)}, f32[64,1,4,512]{3,0,2,1:T(8,128)S(1)}, u32[]{:S(2)}, u32[]{:S(2)}) collective-permute-start(f32[64,1,4,512]{3,0,2,1:T(8,128)S(1)} %get-tuple-element.31), channel_id=1, source_target_pairs={{8,0},{16,8},{24,16},{32,24},{40,32},{48,40},{56,48},{64,56},{72,6... | collective-permute-start | bytes 1572872 | tf_op jit(solution)/shard_map/ppermute | solution.py:17
  32.6 4.0 %collective-permute-start = (f32[64,64]{1,0:T(8,128)S(1)}, f32[64,64]{1,0:T(8,128)S(1)}, u32[]{:S(2)}, u32[]{:S(2)}) collective-permute-start(f32[64,64]{1,0:T(8,128)S(1)} %fusion.34), channel_id=1, source_target_pairs={{0,1},{1,0},{2,3},{3,2},{4,5},{5,4},{6,7},{7,6},{8,9},{9,8},{10,11... | collective-permute-start | bytes 49160 | tf_op jit(solution)/shard_map/ppermute | solution.py:53
  38.1 5.5 %collective-permute-start.5 = (f32[64,64]{1,0:T(8,128)S(1)}, f32[64,64]{1,0:T(8,128)S(1)}, u32[]{:S(2)}, u32[]{:S(2)}) collective-permute-start(f32[64,64]{1,0:T(8,128)S(1)} %add.107), channel_id=1, source_target_pairs={{0,2},{1,3},{2,0},{3,1},{4,6},{5,7},{6,4},{7,5},{8,10},{9,11},{10,... | collective-permute-start | bytes 49160 | tf_op jit(solution)/shard_map/ppermute | solution.py:53
  45.8 5.8 %collective-permute-start.6 = (f32[2,64,64]{2,1,0:T(8,128)S(1)}, f32[2,64,64]{2,1,0:T(8,128)S(1)}, u32[]{:S(2)}, u32[]{:S(2)}) collective-permute-start(f32[2,64,64]{2,1,0:T(8,128)S(1)} %pad_maximum_fusion.1), channel_id=1, source_target_pairs={{0,4},{1,5},{2,6},{3,7},{4,0},{5,1},{6,2},{7,3},{8,12},{9,13},{10,... | collective-permute-start | bytes 98312 | tf_op jit(solution)/shard_map/ppermute | solution.py:53
  52.9 5.2 %collective-permute-start.7 = (f32[2,64,64]{2,1,0:T(8,128)S(1)}, f32[2,64,64]{2,1,0:T(8,128)S(1)}, u32[]{:S(2)}, u32[]{:S(2)}) collective-permute-start(f32[2,64,64]{2,1,0:T(8,128)S(1)} %fusion.31), channel_id=1, source_target_pairs={{0,8},{8,0},{16,24},{24,16},{32,40},{40,32},{48,56},{56,48},{64,72... | collective-permute-start | bytes 98312 | tf_op jit(solution)/shard_map/ppermute | solution.py:53
  58.1 5.5 %collective-permute-start.8 = (f32[2,64,64]{2,1,0:T(8,128)S(1)}, f32[2,64,64]{2,1,0:T(8,128)S(1)}, u32[]{:S(2)}, u32[]{:S(2)}) collective-permute-start(f32[2,64,64]{2,1,0:T(8,128)S(1)} %add.122), channel_id=1, source_target_pairs={{0,16},{8,24},{16,0},{24,8},{32,48},{40,56},{48,32},{56,40},{64,80... | collective-permute-start | bytes 98312 | tf_op jit(solution)/shard_map/ppermute | solution.py:53
  63.6 5.9 %collective-permute-start.9 = (f32[2,64,64]{2,1,0:T(8,128)S(1)}, f32[2,64,64]{2,1,0:T(8,128)S(1)}, u32[]{:S(2)}, u32[]{:S(2)}) collective-permute-start(f32[2,64,64]{2,1,0:T(8,128)S(1)} %add.127), channel_id=1, source_target_pairs={{0,32},{8,40},{16,48},{24,56},{32,0},{40,8},{48,16},{56,24},{64,96... | collective-permute-start | bytes 98312 | tf_op jit(solution)/shard_map/ppermute | solution.py:53
  69.5 4.6 %collective-permute-start.10 = (f32[2,64,64]{2,1,0:T(8,128)S(1)}, f32[2,64,64]{2,1,0:T(8,128)S(1)}, u32[]{:S(2)}, u32[]{:S(2)}) collective-permute-start(f32[2,64,64]{2,1,0:T(8,128)S(1)} %add.128), channel_id=1, source_target_pairs={{0,64},{8,72},{16,80},{24,88},{32,96},{40,104},{48,112},{56,120},{... | collective-permute-start | bytes 98312 | tf_op jit(solution)/shard_map/ppermute | solution.py:53
  74.8 9.0 %collective-permute-start.11 = (f32[64,64]{1,0:T(8,128)S(1)}, f32[64,64]{1,0:T(8,128)S(1)}, u32[]{:S(2)}, u32[]{:S(2)}) collective-permute-start(f32[64,64]{1,0:T(8,128)S(1)} %get-tuple-element.44), channel_id=1, source_target_pairs={{0,1},{1,0},{2,3},{3,2},{4,5},{5,4},{6,7},{7,6},{8,9},{9,8},{10,11... | collective-permute-start | bytes 49160 | tf_op jit(solution)/shard_map/ppermute | solution.py:53
  87.2 18.9 %all-to-all-start.1 = ((f32[64,1,8,512]{3,2,1,0:T(8,128)}), f32[64,1,8,512]{3,2,1,0:T(8,128)S(1)}, u32[]{:S(2)}, u32[]{:S(2)}) async-start(f32[64,1,8,512]{3,2,1,0:T(8,128)} %copy.15), calls=%async_computation.1 | async-start | bytes 2097152 | tf_op jit(solution)/shard_map/all_to_all | solution.py:149
  91.0 13.3 %collective-permute-start.12 = (f32[64,64]{1,0:T(8,128)S(1)}, f32[64,64]{1,0:T(8,128)S(1)}, u32[]{:S(2)}, u32[]{:S(2)}) collective-permute-start(f32[64,64]{1,0:T(8,128)S(1)} %fusion.30), channel_id=1, source_target_pairs={{0,2},{1,3},{2,0},{3,1},{4,6},{5,7},{6,4},{7,5},{8,10},{9,11},{10,... | collective-permute-start | bytes 49160 | tf_op jit(solution)/shard_map/ppermute | solution.py:53

commit v18 on v9

--- a/solution.py
+++ b/solution.py
@@ -39,11 +39,13 @@
 
 
 def butterfly_bits():
+    rings = {"mem": (2,), "dom": (4,)}
     bits = []
     for axis in ("mem", "dom"):
         bit = 1
         while bit < lax.axis_size(axis):
-            bits.append((axis, bit))
+            mask = bit | (bit // 2) if bit in rings[axis] else bit
+            bits.append((axis, mask))
             bit *= 2
     return bits
 

time: 108 us -> 107 us (level)
  starting transfers between devices: 35.8 us -> 34.6 us
    ppermute x9, starting transfers between devices: 19.2 us -> 17.7 us  [exchange(): return x + lax.ppermute(x, axis, [(i, i ^ bit) for i in range(count)])]
where the time goes in v18:
time: 107 us
  waiting for transfers between devices  43.1 us (40%)
  starting transfers between devices  34.6 us (32%)
  other arithmetic  9.57 us (9%)
  Pallas kernels  8.15 us (8%)
  local copies, waits for them, and re-layouts  6.31 us (6%)
  matrix products  4.02 us (4%)
    ppermute x9, waiting for transfers between devices, exchange(): return x + lax.ppermute(x, axis, [(i, i ^ bit) for i in range(count)])  27.3 us
    ppermute x9, starting transfers between devices, exchange(): return x + lax.ppermute(x, axis, [(i, i ^ bit) for i in range(count)])  17.7 us
    all_to_all x1, waiting for transfers between devices, body(): v = lax.all_to_all(perturbations, 'mem', 1, 0, tiled=True)  14.4 us
    pallas_call x1, Pallas kernels, lower_inverse(): pl.pallas_call(chol_inv_kernel, out_shape=jax.ShapeDtypeStruct((n, n), jn...  8.15 us
    all_to_all x1, starting transfers between devices, body(): v = lax.all_to_all(perturbations, 'mem', 1, 0, tiled=True)  7.04 us
    all_to_all x1, starting transfers between devices, body(): ritz = lax.all_to_all(ritz.reshape(v.shape), 'mem', 0, 1, tiled=True)  4.17 us
    ppermute x2, starting transfers between devices, halo(): lax.ppermute(lax.slice_in_dim(block, size - width, size, axis=dim), 'dom'...  3.12 us
    add x2, other arithmetic, adjoint_step(): result + shifted(coef[3] * field, 1, 3) + shifted(coef[4] * field, -1, 3)  2.94 us
  transfers between devices with their start and end apart: 15, of which 9 were waited for; matrix products, arithmetic and copies ran while one was open for 7% of the time, Pallas kernels for 8%

profile of v18, /device:TPU:0, one launch (start us, length us, event | category | flops | bytes accessed | tf_op | source)
XLA Modules:
  0.0 106.6 jit_solution(8700017962774901343)
XLA Ops:
  0.6 2.3 %copy.11 = f32[8,8,8,512]{3,2,0,1:T(8,128)} copy(f32[8,8,8,512]{3,2,1,0:T(8,128)} %param.2) | data formatting | bytes 2097152 | tf_op args[0]
  3.0 7.0 %all-to-all-start = ((f32[8,8,8,512]{3,2,0,1:T(8,128)}), f32[8,8,8,512]{3,2,0,1:T(8,128)S(1)}, u32[]{:S(2)}, u32[]{:S(2)}) async-start(f32[8,8,8,512]{3,2,0,1:T(8,128)} %copy.11), calls=%async_computation | async-start | bytes 2097152 | tf_op jit(solution)/shard_map/all_to_all | solution.py:107
  10.0 1.5 %collective-permute-start.1 = (bf16[2,5,1,4,512]{4,3,2,1,0:T(4,128)(2,1)S(1)}, bf16[2,5,1,4,512]{4,3,2,1,0:T(4,128)(2,1)S(1)}, u32[]{:S(2)}, u32[]{:S(2)}) collective-permute-start(bf16[2,5,1,4,512]{4,3,2,1,0:T(4,128)(2,1)S(1)} %get-tuple-element.42), channel_id=1, source_target_pairs={{0,8},{8,16},{16,24},{24,32},{32,40},{40,48},{48,56},{56,64},{64,7... | collective-permute-start | bytes 122888 | tf_op jit(solution)/shard_map/ppermute | solution.py:16
  11.5 1.3 %collective-permute-start.2 = (bf16[2,5,1,4,512]{4,3,2,1,0:T(4,128)(2,1)S(1)}, bf16[2,5,1,4,512]{4,3,2,1,0:T(4,128)(2,1)S(1)}, u32[]{:S(2)}, u32[]{:S(2)}) collective-permute-start(bf16[2,5,1,4,512]{4,3,2,1,0:T(4,128)(2,1)S(1)} %get-tuple-element.43), channel_id=1, source_target_pairs={{8,0},{16,8},{24,16},{32,24},{40,32},{48,40},{56,48},{64,56},{72,6... | collective-permute-start | bytes 122888 | tf_op jit(solution)/shard_map/ppermute | solution.py:17
  12.8 14.4 %all-to-all-done = f32[8,8,8,512]{3,2,0,1:T(8,128)S(1)} async-done(((f32[8,8,8,512]{3,2,0,1:T(8,128)}), f32[8,8,8,512]{3,2,0,1:T(8,128)S(1)}, u32[]{:S(2)}, u32[]{:S(2)}) %all-to-all-start) | async-done | bytes 1048608 | tf_op jit(solution)/shard_map/all_to_all | solution.py:107
  27.2 0.6 copy.31
  27.8 0.1 fusion.31
  27.9 1.7 %collective-permute-start.3 = (f32[64,1,4,512]{3,0,2,1:T(8,128)S(1)}, f32[64,1,4,512]{3,0,2,1:T(8,128)S(1)}, u32[]{:S(2)}, u32[]{:S(2)}) collective-permute-start(f32[64,1,4,512]{3,0,2,1:T(8,128)S(1)} %get-tuple-element.30), channel_id=1, source_target_pairs={{0,8},{8,16},{16,24},{24,32},{32,40},{40,48},{48,56},{56,64},{64,7... | collective-permute-start | bytes 1572872 | tf_op jit(solution)/shard_map/ppermute | solution.py:16
  29.6 1.3 %collective-permute-start.4 = (f32[64,1,4,512]{3,0,2,1:T(8,128)S(1)}, f32[64,1,4,512]{3,0,2,1:T(8,128)S(1)}, u32[]{:S(2)}, u32[]{:S(2)}) collective-permute-start(f32[64,1,4,512]{3,0,2,1:T(8,128)S(1)} %get-tuple-element.31), channel_id=1, source_target_pairs={{8,0},{16,8},{24,16},{32,24},{40,32},{48,40},{56,48},{64,56},{72,6... | collective-permute-start | bytes 1572872 | tf_op jit(solution)/shard_map/ppermute | solution.py:17
  30.9 0.0 collective-permute-done.1
  30.9 0.0 collective-permute-done.2
  30.9 0.1 maximum_convert_fusion
  31.0 0.6 copy.18
  31.6 1.0 fusion.33
  32.6 0.6 collective-permute-start
  33.2 3.4 %collective-permute-done = f32[64,64]{1,0:T(8,128)S(1)} collective-permute-done((f32[64,64]{1,0:T(8,128)S(1)}, f32[64,64]{1,0:T(8,128)S(1)}, u32[]{:S(2)}, u32[]{:S(2)}) %collective-permute-start) | collective-permute-done | bytes 16416 | tf_op jit(solution)/shard_map/ppermute | solution.py:55
  36.6 0.2 pad_maximum_fusion
  36.8 1.3 %fusion.4 = f32[64,1,16,512]{3,0,2,1:T(8,128)S(1)} fusion(f32[64,1,16,512]{3,0,2,1:T(8,128)S(1)} %pad_maximum_fusion, f32[16,512]{1,0:T(8,128)S(1)} %get-tuple-element.37, f32[16,512]{1,0:T(8,128)S(1)} %get-tuple-element.38, f32[16,512]{1,0:T(8,128)S(1)} %get-tuple-element.39, f32[16,512]{1,0:T(8,128)S(1)} %get-tuple-element.40, ...), kind=kLoop, calls=%fused_computation.20 | loop fusion | flops 4718592 | bytes 4358144 | tf_op jit(solution)/shard_map/add | solution.py:33
  38.1 0.9 collective-permute-start.5
  39.0 1.3 %fusion.10 = f32[64,1,16,512]{3,0,2,1:T(8,128)S(1)} fusion(f32[64,1,16,512]{3,0,2,1:T(8,128)S(1)} %fusion.4, f32[16,512]{1,0:T(8,128)S(1)} %get-tuple-element.33, f32[16,512]{1,0:T(8,128)S(1)} %get-tuple-element.34, f32[16,512]{1,0:T(8,128)S(1)} %get-tuple-element.35, f32[16,512]{1,0:T(8,128)S(1)} %get-tuple-element.36, f32[16,512]{1,0:T(8,128)S(1)} %get-tuple-element.32), kind=kLoop, calls=%fused_computation.26 | loop fusion | flops 4718592 | bytes 4358144 | tf_op jit(solution)/shard_map/add | solution.py:33
  40.3 3.0 %collective-permute-done.5 = f32[64,64]{1,0:T(8,128)S(1)} collective-permute-done((f32[64,64]{1,0:T(8,128)S(1)}, f32[64,64]{1,0:T(8,128)S(1)}, u32[]{:S(2)}, u32[]{:S(2)}) %collective-permute-start.5) | collective-permute-done | bytes 16416 | tf_op jit(solution)/shard_map/ppermute | solution.py:55
  43.3 1.2 %broadcast_multiply_fusion = (f32[64,1,16,512]{3,0,2,1:T(8,128)S(1)}, f32[64,1,16,512]{3,0,2,1:T(8,128)S(1)}, f32[64,1,16,512]{3,0,2,1:T(8,128)S(1)}, f32[64,1,16,512]{3,0,2,1:T(8,128)S(1)}) fusion(f32[64,1,16,512]{3,0,2,1:T(8,128)S(1)} %fusion.10, f32[16,512]{1,0:T(8,128)S(1)} %get-tuple-element.33, f32[16,512]{1,0:T(8,128)S(1)} %get-tuple-element.34, ...), kind=kLoop, calls=%fused_computation.50 | loop fusion | flops 2097152 | bytes 10616832 | tf_op jit(solution)/shard_map/mul | solution.py:38
  44.5 1.0 convolution_bitcast_fusion.2
  45.5 0.6 collective-permute-start.6
  46.2 1.5 %fusion.15 = f32[64,1,16,512]{3,0,2,1:T(8,128)S(1)} fusion(f32[64,1,16,512]{3,0,2,1:T(8,128)S(1)} %get-tuple-element.29, f32[64,1,16,512]{3,0,2,1:T(8,128)S(1)} %get-tuple-element.28, f32[64,1,16,512]{3,0,2,1:T(8,128)S(1)} %get-tuple-element.27, f32[64,1,16,512]{3,0,2,1:T(8,128)S(1)} %get-tuple-element.26, f32[64,1,16,512]{3,0,2,1:T(8,128)S(1)} %fusion.10, ...), kind=kLoop, calls=%fused_computation.31 | loop fusion | flops 2621440 | bytes 12615680 | tf_op jit(solution)/shard_map/add | solution.py:38
  47.7 3.7 %collective-permute-done.6 = f32[2,64,64]{2,1,0:T(8,128)S(1)} collective-permute-done((f32[2,64,64]{2,1,0:T(8,128)S(1)}, f32[2,64,64]{2,1,0:T(8,128)S(1)}, u32[]{:S(2)}, u32[]{:S(2)}) %collective-permute-start.6) | collective-permute-done | bytes 32800 | tf_op jit(solution)/shard_map/ppermute | solution.py:55
  51.4 1.2 %broadcast_multiply_fusion.4 = (f32[64,1,16,512]{3,0,2,1:T(8,128)S(1)}, f32[64,1,16,512]{3,0,2,1:T(8,128)S(1)}, f32[64,1,16,512]{3,0,2,1:T(8,128)S(1)}, f32[64,1,16,512]{3,0,2,1:T(8,128)S(1)}) fusion(f32[64,1,16,512]{3,0,2,1:T(8,128)S(1)} %fusion.15, f32[16,512]{1,0:T(8,128)S(1)} %get-tuple-element.37, f32[16,512]{1,0:T(8,128)S(1)} %get-tuple-element.38, ...), kind=kLoop, calls=%fused_computation.54 | loop fusion | flops 2097152 | bytes 10616832 | tf_op jit(solution)/shard_map/mul | solution.py:38
  52.6 3.7 %collective-permute-start.7 = (f32[2,64,64]{2,1,0:T(8,128)S(1)}, f32[2,64,64]{2,1,0:T(8,128)S(1)}, u32[]{:S(2)}, u32[]{:S(2)}) collective-permute-start(f32[2,64,64]{2,1,0:T(8,128)S(1)} %fusion.30), channel_id=1, source_target_pairs={{0,8},{8,0},{16,24},{24,16},{32,40},{40,32},{48,56},{56,48},{64,72... | collective-permute-start | bytes 98312 | tf_op jit(solution)/shard_map/ppermute | solution.py:55
  56.4 1.4 %fusion.19 = f32[64,1,16,512]{3,0,2,1:T(8,128)S(1)} fusion(f32[64,1,16,512]{3,0,2,1:T(8,128)S(1)} %get-tuple-element.25, f32[64,1,16,512]{3,0,2,1:T(8,128)S(1)} %get-tuple-element.24, f32[64,1,16,512]{3,0,2,1:T(8,128)S(1)} %get-tuple-element.23, f32[64,1,16,512]{3,0,2,1:T(8,128)S(1)} %get-tuple-element.22, f32[64,1,16,512]{3,0,2,1:T(8,128)S(1)} %fusion.15, ...), kind=kLoop, calls=%fused_computation.35 | loop fusion | flops 2621440 | bytes 12615680 | tf_op jit(solution)/shard_map/add | solution.py:38
  57.8 0.0 collective-permute-done.7
  57.8 2.8 %collective-permute-start.8 = (f32[2,64,64]{2,1,0:T(8,128)S(1)}, f32[2,64,64]{2,1,0:T(8,128)S(1)}, u32[]{:S(2)}, u32[]{:S(2)}) collective-permute-start(f32[2,64,64]{2,1,0:T(8,128)S(1)} %add.122), channel_id=1, source_target_pairs={{0,16},{8,24},{16,0},{24,8},{32,48},{40,56},{48,32},{56,40},{64,80... | collective-permute-start | bytes 98312 | tf_op jit(solution)/shard_map/ppermute | solution.py:55
  60.7 2.7 %collective-permute-done.8 = f32[2,64,64]{2,1,0:T(8,128)S(1)} collective-permute-done((f32[2,64,64]{2,1,0:T(8,128)S(1)}, f32[2,64,64]{2,1,0:T(8,128)S(1)}, u32[]{:S(2)}, u32[]{:S(2)}) %collective-permute-start.8) | collective-permute-done | bytes 32800 | tf_op jit(solution)/shard_map/ppermute | solution.py:55
  63.3 3.9 %collective-permute-start.9 = (f32[2,64,64]{2,1,0:T(8,128)S(1)}, f32[2,64,64]{2,1,0:T(8,128)S(1)}, u32[]{:S(2)}, u32[]{:S(2)}) collective-permute-start(f32[2,64,64]{2,1,0:T(8,128)S(1)} %add.127), channel_id=1, source_target_pairs={{0,48},{8,56},{16,32},{24,40},{32,16},{40,24},{48,0},{56,8},{64,11... | collective-permute-start | bytes 98312 | tf_op jit(solution)/shard_map/ppermute | solution.py:55
  67.3 2.2 %collective-permute-done.9 = f32[2,64,64]{2,1,0:T(8,128)S(1)} collective-permute-done((f32[2,64,64]{2,1,0:T(8,128)S(1)}, f32[2,64,64]{2,1,0:T(8,128)S(1)}, u32[]{:S(2)}, u32[]{:S(2)}) %collective-permute-start.9) | collective-permute-done | bytes 32800 | tf_op jit(solution)/shard_map/ppermute | solution.py:55
  69.5 1.8 %collective-permute-start.10 = (f32[2,64,64]{2,1,0:T(8,128)S(1)}, f32[2,64,64]{2,1,0:T(8,128)S(1)}, u32[]{:S(2)}, u32[]{:S(2)}) collective-permute-start(f32[2,64,64]{2,1,0:T(8,128)S(1)} %add.128), channel_id=1, source_target_pairs={{0,64},{8,72},{16,80},{24,88},{32,96},{40,104},{48,112},{56,120},{... | collective-permute-start | bytes 98312 | tf_op jit(solution)/shard_map/ppermute | solution.py:55
  71.3 2.6 %collective-permute-done.10 = f32[2,64,64]{2,1,0:T(8,128)S(1)} collective-permute-done((f32[2,64,64]{2,1,0:T(8,128)S(1)}, f32[2,64,64]{2,1,0:T(8,128)S(1)}, u32[]{:S(2)}, u32[]{:S(2)}) %collective-permute-start.10) | collective-permute-done | bytes 32800 | tf_op jit(solution)/shard_map/ppermute | solution.py:55
  73.9 0.6 slice_bitcast_fusion
  74.5 8.2 %shard_map.41 = f32[64,64]{1,0:T(8,128)} custom-call(f32[64,64]{1,0:T(8,128)} %get-tuple-element.45.g_ref), custom_call_target="tpu_custom_call" | custom-call | tf_op jit(solution)/shard_map/pallas_call | solution.py:86
  82.7 0.0 collective-permute-done.11
  82.7 1.1 %convolution_bitcast_fusion.1 = f32[64,64,1]{1,0,2:T(8,128)S(1)} fusion(f32[64,64]{1,0:T(8,128)} %shard_map.41), kind=kOutput, calls=%fused_computation.42 | convolution fusion | flops 3145728 | bytes 32768 | tf_op jit(solution)/shard_map/dot_general | solution.py:98
  83.7 1.0 convolution_bitcast_fusion
  84.8 1.6 %copy.15 = f32[64,1,8,512]{3,2,1,0:T(8,128)} copy(f32[64,1,8,512]{3,0,2,1:T(8,128)S(1)} %convolution_bitcast_fusion) | data formatting | bytes 2097152 | tf_op jit(solution)/shard_map/dot_general | solution.py:143
  86.3 4.2 %all-to-all-start.1 = ((f32[64,1,8,512]{3,2,1,0:T(8,128)}), f32[64,1,8,512]{3,2,1,0:T(8,128)S(1)}, u32[]{:S(2)}, u32[]{:S(2)}) async-start(f32[64,1,8,512]{3,2,1,0:T(8,128)} %copy.15), calls=%async_computation.1 | async-start | bytes 2097152 | tf_op jit(solution)/shard_map/all_to_all | solution.py:147
  90.5 3.2 %collective-permute-start.12 = (f32[64,64]{1,0:T(8,128)S(1)}, f32[64,64]{1,0:T(8,128)S(1)}, u32[]{:S(2)}, u32[]{:S(2)}) collective-permute-start(f32[64,64]{1,0:T(8,128)S(1)} %fusion.29), channel_id=1, source_target_pairs={{0,3},{1,2},{2,1},{3,0},{4,7},{5,6},{6,5},{7,4},{8,11},{9,10},{10,... | collective-permute-start | bytes 49160 | tf_op jit(solution)/shard_map/ppermute | solution.py:55
  93.7 9.8 %collective-permute-done.12 = f32[64,64]{1,0:T(8,128)S(1)} collective-permute-done((f32[64,64]{1,0:T(8,128)S(1)}, f32[64,64]{1,0:T(8,128)S(1)}, u32[]{:S(2)}, u32[]{:S(2)}) %collective-permute-start.12) | collective-permute-done | bytes 16416 | tf_op jit(solution)/shard_map/ppermute | solution.py:55
  103.5 0.6 add_multiply_fusion
  104.1 1.4 %all-to-all-done.1 = f32[64,1,8,512]{3,2,1,0:T(8,128)S(1)} async-done(((f32[64,1,8,512]{3,2,1,0:T(8,128)}), f32[64,1,8,512]{3,2,1,0:T(8,128)S(1)}, u32[]{:S(2)}, u32[]{:S(2)}) %all-to-all-start.1) | async-done | bytes 1048608 | tf_op jit(solution)/shard_map/all_to_all | solution.py:147
  105.6 1.1 copy.30
  (16 shorter events, 0.1 us)
Async XLA Ops:
  0.6 9.4 %copy-start = (bf16[2,5,1,8,512]{4,3,2,1,0:T(8,128)(2,1)S(1)}, bf16[2,5,1,8,512]{4,3,2,1,0:T(8,128)(2,1)}, u32[]{:S(2)}) copy-start(bf16[2,5,1,8,512]{4,3,2,1,0:T(8,128)(2,1)} %param.3) | copy-start | bytes 245764
  3.0 24.2 %all-to-all-start = ((f32[8,8,8,512]{3,2,0,1:T(8,128)}), f32[8,8,8,512]{3,2,0,1:T(8,128)S(1)}, u32[]{:S(2)}, u32[]{:S(2)}) async-start(f32[8,8,8,512]{3,2,0,1:T(8,128)} %copy.11), calls=%async_computation | async-start | bytes 2097152 | tf_op jit(solution)/shard_map/all_to_all | solution.py:107
  10.0 20.8 %collective-permute-start.1 = (bf16[2,5,1,4,512]{4,3,2,1,0:T(4,128)(2,1)S(1)}, bf16[2,5,1,4,512]{4,3,2,1,0:T(4,128)(2,1)S(1)}, u32[]{:S(2)}, u32[]{:S(2)}) collective-permute-start(bf16[2,5,1,4,512]{4,3,2,1,0:T(4,128)(2,1)S(1)} %get-tuple-element.42), channel_id=1, source_target_pairs={{0,8},{8,16},{16,24},{24,32},{32,40},{40,48},{48,56},{56,64},{64,7... | collective-permute-start | bytes 122888 | tf_op jit(solution)/shard_map/ppermute | solution.py:16
  11.5 19.4 %collective-permute-start.2 = (bf16[2,5,1,4,512]{4,3,2,1,0:T(4,128)(2,1)S(1)}, bf16[2,5,1,4,512]{4,3,2,1,0:T(4,128)(2,1)S(1)}, u32[]{:S(2)}, u32[]{:S(2)}) collective-permute-start(bf16[2,5,1,4,512]{4,3,2,1,0:T(4,128)(2,1)S(1)} %get-tuple-element.43), channel_id=1, source_target_pairs={{8,0},{16,8},{24,16},{32,24},{40,32},{48,40},{56,48},{64,56},{72,6... | collective-permute-start | bytes 122888 | tf_op jit(solution)/shard_map/ppermute | solution.py:17
  27.9 8.7 %collective-permute-start.3 = (f32[64,1,4,512]{3,0,2,1:T(8,128)S(1)}, f32[64,1,4,512]{3,0,2,1:T(8,128)S(1)}, u32[]{:S(2)}, u32[]{:S(2)}) collective-permute-start(f32[64,1,4,512]{3,0,2,1:T(8,128)S(1)} %get-tuple-element.30), channel_id=1, source_target_pairs={{0,8},{8,16},{16,24},{24,32},{32,40},{40,48},{48,56},{56,64},{64,7... | collective-permute-start | bytes 1572872 | tf_op jit(solution)/shard_map/ppermute | solution.py:16
  29.6 7.0 %collective-permute-start.4 = (f32[64,1,4,512]{3,0,2,1:T(8,128)S(1)}, f32[64,1,4,512]{3,0,2,1:T(8,128)S(1)}, u32[]{:S(2)}, u32[]{:S(2)}) collective-permute-start(f32[64,1,4,512]{3,0,2,1:T(8,128)S(1)} %get-tuple-element.31), channel_id=1, source_target_pairs={{8,0},{16,8},{24,16},{32,24},{40,32},{48,40},{56,48},{64,56},{72,6... | collective-permute-start | bytes 1572872 | tf_op jit(solution)/shard_map/ppermute | solution.py:17
  32.6 4.0 %collective-permute-start = (f32[64,64]{1,0:T(8,128)S(1)}, f32[64,64]{1,0:T(8,128)S(1)}, u32[]{:S(2)}, u32[]{:S(2)}) collective-permute-start(f32[64,64]{1,0:T(8,128)S(1)} %fusion.33), channel_id=1, source_target_pairs={{0,1},{1,0},{2,3},{3,2},{4,5},{5,4},{6,7},{7,6},{8,9},{9,8},{10,11... | collective-permute-start | bytes 49160 | tf_op jit(solution)/shard_map/ppermute | solution.py:55
  38.1 5.2 %collective-permute-start.5 = (f32[64,64]{1,0:T(8,128)S(1)}, f32[64,64]{1,0:T(8,128)S(1)}, u32[]{:S(2)}, u32[]{:S(2)}) collective-permute-start(f32[64,64]{1,0:T(8,128)S(1)} %add.107), channel_id=1, source_target_pairs={{0,3},{1,2},{2,1},{3,0},{4,7},{5,6},{6,5},{7,4},{8,11},{9,10},{10,... | collective-permute-start | bytes 49160 | tf_op jit(solution)/shard_map/ppermute | solution.py:55
  45.5 5.8 %collective-permute-start.6 = (f32[2,64,64]{2,1,0:T(8,128)S(1)}, f32[2,64,64]{2,1,0:T(8,128)S(1)}, u32[]{:S(2)}, u32[]{:S(2)}) collective-permute-start(f32[2,64,64]{2,1,0:T(8,128)S(1)} %pad_maximum_fusion.1), channel_id=1, source_target_pairs={{0,4},{1,5},{2,6},{3,7},{4,0},{5,1},{6,2},{7,3},{8,12},{9,13},{10,... | collective-permute-start | bytes 98312 | tf_op jit(solution)/shard_map/ppermute | solution.py:55
  52.6 5.2 %collective-permute-start.7 = (f32[2,64,64]{2,1,0:T(8,128)S(1)}, f32[2,64,64]{2,1,0:T(8,128)S(1)}, u32[]{:S(2)}, u32[]{:S(2)}) collective-permute-start(f32[2,64,64]{2,1,0:T(8,128)S(1)} %fusion.30), channel_id=1, source_target_pairs={{0,8},{8,0},{16,24},{24,16},{32,40},{40,32},{48,56},{56,48},{64,72... | collective-permute-start | bytes 98312 | tf_op jit(solution)/shard_map/ppermute | solution.py:55
  57.8 5.5 %collective-permute-start.8 = (f32[2,64,64]{2,1,0:T(8,128)S(1)}, f32[2,64,64]{2,1,0:T(8,128)S(1)}, u32[]{:S(2)}, u32[]{:S(2)}) collective-permute-start(f32[2,64,64]{2,1,0:T(8,128)S(1)} %add.122), channel_id=1, source_target_pairs={{0,16},{8,24},{16,0},{24,8},{32,48},{40,56},{48,32},{56,40},{64,80... | collective-permute-start | bytes 98312 | tf_op jit(solution)/shard_map/ppermute | solution.py:55
  63.3 6.2 %collective-permute-start.9 = (f32[2,64,64]{2,1,0:T(8,128)S(1)}, f32[2,64,64]{2,1,0:T(8,128)S(1)}, u32[]{:S(2)}, u32[]{:S(2)}) collective-permute-start(f32[2,64,64]{2,1,0:T(8,128)S(1)} %add.127), channel_id=1, source_target_pairs={{0,48},{8,56},{16,32},{24,40},{32,16},{40,24},{48,0},{56,8},{64,11... | collective-permute-start | bytes 98312 | tf_op jit(solution)/shard_map/ppermute | solution.py:55
  69.5 4.3 %collective-permute-start.10 = (f32[2,64,64]{2,1,0:T(8,128)S(1)}, f32[2,64,64]{2,1,0:T(8,128)S(1)}, u32[]{:S(2)}, u32[]{:S(2)}) collective-permute-start(f32[2,64,64]{2,1,0:T(8,128)S(1)} %add.128), channel_id=1, source_target_pairs={{0,64},{8,72},{16,80},{24,88},{32,96},{40,104},{48,112},{56,120},{... | collective-permute-start | bytes 98312 | tf_op jit(solution)/shard_map/ppermute | solution.py:55
  74.5 8.2 %collective-permute-start.11 = (f32[64,64]{1,0:T(8,128)S(1)}, f32[64,64]{1,0:T(8,128)S(1)}, u32[]{:S(2)}, u32[]{:S(2)}) collective-permute-start(f32[64,64]{1,0:T(8,128)S(1)} %get-tuple-element.44), channel_id=1, source_target_pairs={{0,1},{1,0},{2,3},{3,2},{4,5},{5,4},{6,7},{7,6},{8,9},{9,8},{10,11... | collective-permute-start | bytes 49160 | tf_op jit(solution)/shard_map/ppermute | solution.py:55
  86.3 19.2 %all-to-all-start.1 = ((f32[64,1,8,512]{3,2,1,0:T(8,128)}), f32[64,1,8,512]{3,2,1,0:T(8,128)S(1)}, u32[]{:S(2)}, u32[]{:S(2)}) async-start(f32[64,1,8,512]{3,2,1,0:T(8,128)} %copy.15), calls=%async_computation.1 | async-start | bytes 2097152 | tf_op jit(solution)/shard_map/all_to_all | solution.py:147
  90.5 13.0 %collective-permute-start.12 = (f32[64,64]{1,0:T(8,128)S(1)}, f32[64,64]{1,0:T(8,128)S(1)}, u32[]{:S(2)}, u32[]{:S(2)}) collective-permute-start(f32[64,64]{1,0:T(8,128)S(1)} %fusion.29), channel_id=1, source_target_pairs={{0,3},{1,2},{2,1},{3,0},{4,7},{5,6},{6,5},{7,4},{8,11},{9,10},{10,... | collective-permute-start | bytes 49160 | tf_op jit(solution)/shard_map/ppermute | solution.py:55

commit v19 on v18

--- a/solution.py
+++ b/solution.py
@@ -62,23 +62,27 @@
     cols = lax.broadcasted_iota(jnp.int32, (n, n), 1)
     x_ref[...] = jnp.where(rows == cols, 1.0, 0.0).astype(jnp.float32)
     lane = lax.broadcasted_iota(jnp.int32, (1, n), 1)
-    sub = lax.broadcasted_iota(jnp.int32, (n, 1), 0)
+    phase = 16 if n % 16 == 0 else n
 
-    def step(k, carry):
-        a = a_ref[...]
-        row = a_ref[pl.ds(k, 1), :]
-        pivot = jnp.sum(jnp.where(lane == k, row, 0.0), axis=1, keepdims=True)
-        scale = 1.0 / jnp.sqrt(pivot)
-        col = jnp.sum(jnp.where(cols == k, a, 0.0), axis=1, keepdims=True)
-        below = jnp.where(sub > k, col * scale, 0.0)
-        right = jnp.where(lane > k, row * scale, 0.0)
-        a_ref[...] = a - below * right
-        xrow = x_ref[pl.ds(k, 1), :] * scale
-        x_ref[pl.ds(k, 1), :] = xrow
-        x_ref[...] = x_ref[...] - below * xrow
-        return carry
+    for lo in range(0, n, phase):
+        cols_lo = lax.broadcasted_iota(jnp.int32, (n - lo, n), 1)
+        sub = lo + lax.broadcasted_iota(jnp.int32, (n - lo, 1), 0)
 
-    lax.fori_loop(0, n, step, 0)
+        def step(k, carry):
+            a = a_ref[lo:, :]
+            row = a_ref[pl.ds(k, 1), :]
+            pivot = jnp.sum(jnp.where(lane == k, row, 0.0), axis=1, keepdims=True)
+            scale = 1.0 / jnp.sqrt(pivot)
+            col = jnp.sum(jnp.where(cols_lo == k, a, 0.0), axis=1, keepdims=True)
+            below = jnp.where(sub > k, col * scale, 0.0)
+            right = jnp.where(lane > k, row * scale, 0.0)
+            a_ref[lo:, :] = a - below * right
+            xrow = x_ref[pl.ds(k, 1), :] * scale
+            x_ref[pl.ds(k, 1), :] = xrow
+            x_ref[lo:, :] = x_ref[lo:, :] - below * xrow
+            return carry
+
+        lax.fori_loop(lo, min(lo + phase, n), step, 0)
 
 
 def lower_inverse(gram):

time: 107 us -> 107 us (level)
  no operation moved by 1% of the time
where the time goes in v19:
time: 107 us
  waiting for transfers between devices  43.1 us (40%)
  starting transfers between devices  34.6 us (32%)
  other arithmetic  9.57 us (9%)
  Pallas kernels  8.06 us (8%)
  local copies, waits for them, and re-layouts  6.31 us (6%)
  matrix products  4.02 us (4%)
    ppermute x9, waiting for transfers between devices, exchange(): return x + lax.ppermute(x, axis, [(i, i ^ bit) for i in range(count)])  27.3 us
    ppermute x9, starting transfers between devices, exchange(): return x + lax.ppermute(x, axis, [(i, i ^ bit) for i in range(count)])  17.7 us
    all_to_all x1, waiting for transfers between devices, body(): v = lax.all_to_all(perturbations, 'mem', 1, 0, tiled=True)  14.4 us
    pallas_call x1, Pallas kernels, lower_inverse(): pl.pallas_call(chol_inv_kernel, out_shape=jax.ShapeDtypeStruct((n, n), jn...  8.06 us
    all_to_all x1, starting transfers between devices, body(): v = lax.all_to_all(perturbations, 'mem', 1, 0, tiled=True)  7.04 us
    all_to_all x1, starting transfers between devices, body(): ritz = lax.all_to_all(ritz.reshape(v.shape), 'mem', 0, 1, tiled=True)  4.18 us
    ppermute x2, starting transfers between devices, halo(): lax.ppermute(lax.slice_in_dim(block, size - width, size, axis=dim), 'dom'...  3.12 us
    add x2, other arithmetic, adjoint_step(): result + shifted(coef[3] * field, 1, 3) + shifted(coef[4] * field, -1, 3)  2.94 us
  transfers between devices with their start and end apart: 15, of which 9 were waited for; matrix products, arithmetic and copies ran while one was open for 7% of the time, Pallas kernels for 8%

profile of v19, /device:TPU:0, one launch (start us, length us, event | category | flops | bytes accessed | tf_op | source)
XLA Modules:
  0.0 106.5 jit_solution(15709137763489122074)
XLA Ops:
  0.6 2.3 %copy.11 = f32[8,8,8,512]{3,2,0,1:T(8,128)} copy(f32[8,8,8,512]{3,2,1,0:T(8,128)} %param.2) | data formatting | bytes 2097152 | tf_op args[0]
  3.0 7.0 %all-to-all-start = ((f32[8,8,8,512]{3,2,0,1:T(8,128)}), f32[8,8,8,512]{3,2,0,1:T(8,128)S(1)}, u32[]{:S(2)}, u32[]{:S(2)}) async-start(f32[8,8,8,512]{3,2,0,1:T(8,128)} %copy.11), calls=%async_computation | async-start | bytes 2097152 | tf_op jit(solution)/shard_map/all_to_all | solution.py:111
  10.0 1.5 %collective-permute-start.1 = (bf16[2,5,1,4,512]{4,3,2,1,0:T(4,128)(2,1)S(1)}, bf16[2,5,1,4,512]{4,3,2,1,0:T(4,128)(2,1)S(1)}, u32[]{:S(2)}, u32[]{:S(2)}) collective-permute-start(bf16[2,5,1,4,512]{4,3,2,1,0:T(4,128)(2,1)S(1)} %get-tuple-element.42), channel_id=1, source_target_pairs={{0,8},{8,16},{16,24},{24,32},{32,40},{40,48},{48,56},{56,64},{64,7... | collective-permute-start | bytes 122888 | tf_op jit(solution)/shard_map/ppermute | solution.py:16
  11.5 1.3 %collective-permute-start.2 = (bf16[2,5,1,4,512]{4,3,2,1,0:T(4,128)(2,1)S(1)}, bf16[2,5,1,4,512]{4,3,2,1,0:T(4,128)(2,1)S(1)}, u32[]{:S(2)}, u32[]{:S(2)}) collective-permute-start(bf16[2,5,1,4,512]{4,3,2,1,0:T(4,128)(2,1)S(1)} %get-tuple-element.43), channel_id=1, source_target_pairs={{8,0},{16,8},{24,16},{32,24},{40,32},{48,40},{56,48},{64,56},{72,6... | collective-permute-start | bytes 122888 | tf_op jit(solution)/shard_map/ppermute | solution.py:17
  12.8 14.4 %all-to-all-done = f32[8,8,8,512]{3,2,0,1:T(8,128)S(1)} async-done(((f32[8,8,8,512]{3,2,0,1:T(8,128)}), f32[8,8,8,512]{3,2,0,1:T(8,128)S(1)}, u32[]{:S(2)}, u32[]{:S(2)}) %all-to-all-start) | async-done | bytes 1048608 | tf_op jit(solution)/shard_map/all_to_all | solution.py:111
  27.2 0.6 copy.31
  27.8 0.1 fusion.31
  27.9 1.7 %collective-permute-start.3 = (f32[64,1,4,512]{3,0,2,1:T(8,128)S(1)}, f32[64,1,4,512]{3,0,2,1:T(8,128)S(1)}, u32[]{:S(2)}, u32[]{:S(2)}) collective-permute-start(f32[64,1,4,512]{3,0,2,1:T(8,128)S(1)} %get-tuple-element.30), channel_id=1, source_target_pairs={{0,8},{8,16},{16,24},{24,32},{32,40},{40,48},{48,56},{56,64},{64,7... | collective-permute-start | bytes 1572872 | tf_op jit(solution)/shard_map/ppermute | solution.py:16
  29.6 1.3 %collective-permute-start.4 = (f32[64,1,4,512]{3,0,2,1:T(8,128)S(1)}, f32[64,1,4,512]{3,0,2,1:T(8,128)S(1)}, u32[]{:S(2)}, u32[]{:S(2)}) collective-permute-start(f32[64,1,4,512]{3,0,2,1:T(8,128)S(1)} %get-tuple-element.31), channel_id=1, source_target_pairs={{8,0},{16,8},{24,16},{32,24},{40,32},{48,40},{56,48},{64,56},{72,6... | collective-permute-start | bytes 1572872 | tf_op jit(solution)/shard_map/ppermute | solution.py:17
  30.9 0.0 collective-permute-done.1
  30.9 0.0 collective-permute-done.2
  30.9 0.1 maximum_convert_fusion
  31.0 0.6 copy.18
  31.6 1.0 fusion.33
  32.6 0.6 collective-permute-start
  33.2 3.4 %collective-permute-done = f32[64,64]{1,0:T(8,128)S(1)} collective-permute-done((f32[64,64]{1,0:T(8,128)S(1)}, f32[64,64]{1,0:T(8,128)S(1)}, u32[]{:S(2)}, u32[]{:S(2)}) %collective-permute-start) | collective-permute-done | bytes 16416 | tf_op jit(solution)/shard_map/ppermute | solution.py:55
  36.6 0.0 collective-permute-done.3
  36.6 0.2 pad_maximum_fusion
  36.8 1.3 %fusion.4 = f32[64,1,16,512]{3,0,2,1:T(8,128)S(1)} fusion(f32[64,1,16,512]{3,0,2,1:T(8,128)S(1)} %pad_maximum_fusion, f32[16,512]{1,0:T(8,128)S(1)} %get-tuple-element.37, f32[16,512]{1,0:T(8,128)S(1)} %get-tuple-element.38, f32[16,512]{1,0:T(8,128)S(1)} %get-tuple-element.39, f32[16,512]{1,0:T(8,128)S(1)} %get-tuple-element.40, ...), kind=kLoop, calls=%fused_computation.20 | loop fusion | flops 4718592 | bytes 4358144 | tf_op jit(solution)/shard_map/add | solution.py:33
  38.1 0.9 collective-permute-start.5
  39.0 1.3 %fusion.10 = f32[64,1,16,512]{3,0,2,1:T(8,128)S(1)} fusion(f32[64,1,16,512]{3,0,2,1:T(8,128)S(1)} %fusion.4, f32[16,512]{1,0:T(8,128)S(1)} %get-tuple-element.33, f32[16,512]{1,0:T(8,128)S(1)} %get-tuple-element.34, f32[16,512]{1,0:T(8,128)S(1)} %get-tuple-element.35, f32[16,512]{1,0:T(8,128)S(1)} %get-tuple-element.36, f32[16,512]{1,0:T(8,128)S(1)} %get-tuple-element.32), kind=kLoop, calls=%fused_computation.26 | loop fusion | flops 4718592 | bytes 4358144 | tf_op jit(solution)/shard_map/add | solution.py:33
  40.3 3.0 %collective-permute-done.5 = f32[64,64]{1,0:T(8,128)S(1)} collective-permute-done((f32[64,64]{1,0:T(8,128)S(1)}, f32[64,64]{1,0:T(8,128)S(1)}, u32[]{:S(2)}, u32[]{:S(2)}) %collective-permute-start.5) | collective-permute-done | bytes 16416 | tf_op jit(solution)/shard_map/ppermute | solution.py:55
  43.3 1.2 %broadcast_multiply_fusion = (f32[64,1,16,512]{3,0,2,1:T(8,128)S(1)}, f32[64,1,16,512]{3,0,2,1:T(8,128)S(1)}, f32[64,1,16,512]{3,0,2,1:T(8,128)S(1)}, f32[64,1,16,512]{3,0,2,1:T(8,128)S(1)}) fusion(f32[64,1,16,512]{3,0,2,1:T(8,128)S(1)} %fusion.10, f32[16,512]{1,0:T(8,128)S(1)} %get-tuple-element.33, f32[16,512]{1,0:T(8,128)S(1)} %get-tuple-element.34, ...), kind=kLoop, calls=%fused_computation.50 | loop fusion | flops 2097152 | bytes 10616832 | tf_op jit(solution)/shard_map/mul | solution.py:38
  44.5 1.0 convolution_bitcast_fusion.2
  45.5 0.6 collective-permute-start.6
  46.2 1.5 %fusion.15 = f32[64,1,16,512]{3,0,2,1:T(8,128)S(1)} fusion(f32[64,1,16,512]{3,0,2,1:T(8,128)S(1)} %get-tuple-element.29, f32[64,1,16,512]{3,0,2,1:T(8,128)S(1)} %get-tuple-element.28, f32[64,1,16,512]{3,0,2,1:T(8,128)S(1)} %get-tuple-element.27, f32[64,1,16,512]{3,0,2,1:T(8,128)S(1)} %get-tuple-element.26, f32[64,1,16,512]{3,0,2,1:T(8,128)S(1)} %fusion.10, ...), kind=kLoop, calls=%fused_computation.31 | loop fusion | flops 2621440 | bytes 12615680 | tf_op jit(solution)/shard_map/add | solution.py:38
  47.7 3.7 %collective-permute-done.6 = f32[2,64,64]{2,1,0:T(8,128)S(1)} collective-permute-done((f32[2,64,64]{2,1,0:T(8,128)S(1)}, f32[2,64,64]{2,1,0:T(8,128)S(1)}, u32[]{:S(2)}, u32[]{:S(2)}) %collective-permute-start.6) | collective-permute-done | bytes 32800 | tf_op jit(solution)/shard_map/ppermute | solution.py:55
  51.4 1.2 %broadcast_multiply_fusion.4 = (f32[64,1,16,512]{3,0,2,1:T(8,128)S(1)}, f32[64,1,16,512]{3,0,2,1:T(8,128)S(1)}, f32[64,1,16,512]{3,0,2,1:T(8,128)S(1)}, f32[64,1,16,512]{3,0,2,1:T(8,128)S(1)}) fusion(f32[64,1,16,512]{3,0,2,1:T(8,128)S(1)} %fusion.15, f32[16,512]{1,0:T(8,128)S(1)} %get-tuple-element.37, f32[16,512]{1,0:T(8,128)S(1)} %get-tuple-element.38, ...), kind=kLoop, calls=%fused_computation.54 | loop fusion | flops 2097152 | bytes 10616832 | tf_op jit(solution)/shard_map/mul | solution.py:38
  52.6 3.7 %collective-permute-start.7 = (f32[2,64,64]{2,1,0:T(8,128)S(1)}, f32[2,64,64]{2,1,0:T(8,128)S(1)}, u32[]{:S(2)}, u32[]{:S(2)}) collective-permute-start(f32[2,64,64]{2,1,0:T(8,128)S(1)} %fusion.30), channel_id=1, source_target_pairs={{0,8},{8,0},{16,24},{24,16},{32,40},{40,32},{48,56},{56,48},{64,72... | collective-permute-start | bytes 98312 | tf_op jit(solution)/shard_map/ppermute | solution.py:55
  56.4 1.4 %fusion.19 = f32[64,1,16,512]{3,0,2,1:T(8,128)S(1)} fusion(f32[64,1,16,512]{3,0,2,1:T(8,128)S(1)} %get-tuple-element.25, f32[64,1,16,512]{3,0,2,1:T(8,128)S(1)} %get-tuple-element.24, f32[64,1,16,512]{3,0,2,1:T(8,128)S(1)} %get-tuple-element.23, f32[64,1,16,512]{3,0,2,1:T(8,128)S(1)} %get-tuple-element.22, f32[64,1,16,512]{3,0,2,1:T(8,128)S(1)} %fusion.15, ...), kind=kLoop, calls=%fused_computation.35 | loop fusion | flops 2621440 | bytes 12615680 | tf_op jit(solution)/shard_map/add | solution.py:38
  57.8 0.0 collective-permute-done.7
  57.8 2.8 %collective-permute-start.8 = (f32[2,64,64]{2,1,0:T(8,128)S(1)}, f32[2,64,64]{2,1,0:T(8,128)S(1)}, u32[]{:S(2)}, u32[]{:S(2)}) collective-permute-start(f32[2,64,64]{2,1,0:T(8,128)S(1)} %add.122), channel_id=1, source_target_pairs={{0,16},{8,24},{16,0},{24,8},{32,48},{40,56},{48,32},{56,40},{64,80... | collective-permute-start | bytes 98312 | tf_op jit(solution)/shard_map/ppermute | solution.py:55
  60.7 2.7 %collective-permute-done.8 = f32[2,64,64]{2,1,0:T(8,128)S(1)} collective-permute-done((f32[2,64,64]{2,1,0:T(8,128)S(1)}, f32[2,64,64]{2,1,0:T(8,128)S(1)}, u32[]{:S(2)}, u32[]{:S(2)}) %collective-permute-start.8) | collective-permute-done | bytes 32800 | tf_op jit(solution)/shard_map/ppermute | solution.py:55
  63.3 3.9 %collective-permute-start.9 = (f32[2,64,64]{2,1,0:T(8,128)S(1)}, f32[2,64,64]{2,1,0:T(8,128)S(1)}, u32[]{:S(2)}, u32[]{:S(2)}) collective-permute-start(f32[2,64,64]{2,1,0:T(8,128)S(1)} %add.127), channel_id=1, source_target_pairs={{0,48},{8,56},{16,32},{24,40},{32,16},{40,24},{48,0},{56,8},{64,11... | collective-permute-start | bytes 98312 | tf_op jit(solution)/shard_map/ppermute | solution.py:55
  67.3 2.2 %collective-permute-done.9 = f32[2,64,64]{2,1,0:T(8,128)S(1)} collective-permute-done((f32[2,64,64]{2,1,0:T(8,128)S(1)}, f32[2,64,64]{2,1,0:T(8,128)S(1)}, u32[]{:S(2)}, u32[]{:S(2)}) %collective-permute-start.9) | collective-permute-done | bytes 32800 | tf_op jit(solution)/shard_map/ppermute | solution.py:55
  69.5 1.8 %collective-permute-start.10 = (f32[2,64,64]{2,1,0:T(8,128)S(1)}, f32[2,64,64]{2,1,0:T(8,128)S(1)}, u32[]{:S(2)}, u32[]{:S(2)}) collective-permute-start(f32[2,64,64]{2,1,0:T(8,128)S(1)} %add.128), channel_id=1, source_target_pairs={{0,64},{8,72},{16,80},{24,88},{32,96},{40,104},{48,112},{56,120},{... | collective-permute-start | bytes 98312 | tf_op jit(solution)/shard_map/ppermute | solution.py:55
  71.3 2.6 %collective-permute-done.10 = f32[2,64,64]{2,1,0:T(8,128)S(1)} collective-permute-done((f32[2,64,64]{2,1,0:T(8,128)S(1)}, f32[2,64,64]{2,1,0:T(8,128)S(1)}, u32[]{:S(2)}, u32[]{:S(2)}) %collective-permute-start.10) | collective-permute-done | bytes 32800 | tf_op jit(solution)/shard_map/ppermute | solution.py:55
  73.9 0.6 slice_bitcast_fusion
  74.5 8.1 %shard_map.41 = f32[64,64]{1,0:T(8,128)} custom-call(f32[64,64]{1,0:T(8,128)} %get-tuple-element.45.g_ref), custom_call_target="tpu_custom_call" | custom-call | tf_op jit(solution)/shard_map/pallas_call | solution.py:90
  82.6 1.1 %convolution_bitcast_fusion.1 = f32[64,64,1]{1,0,2:T(8,128)S(1)} fusion(f32[64,64]{1,0:T(8,128)} %shard_map.41), kind=kOutput, calls=%fused_computation.42 | convolution fusion | flops 3145728 | bytes 32768 | tf_op jit(solution)/shard_map/dot_general | solution.py:102
  83.7 1.0 convolution_bitcast_fusion
  84.7 1.6 %copy.15 = f32[64,1,8,512]{3,2,1,0:T(8,128)} copy(f32[64,1,8,512]{3,0,2,1:T(8,128)S(1)} %convolution_bitcast_fusion) | data formatting | bytes 2097152 | tf_op jit(solution)/shard_map/dot_general | solution.py:147
  86.3 4.2 %all-to-all-start.1 = ((f32[64,1,8,512]{3,2,1,0:T(8,128)}), f32[64,1,8,512]{3,2,1,0:T(8,128)S(1)}, u32[]{:S(2)}, u32[]{:S(2)}) async-start(f32[64,1,8,512]{3,2,1,0:T(8,128)} %copy.15), calls=%async_computation.1 | async-start | bytes 2097152 | tf_op jit(solution)/shard_map/all_to_all | solution.py:151
  90.4 3.2 %collective-permute-start.12 = (f32[64,64]{1,0:T(8,128)S(1)}, f32[64,64]{1,0:T(8,128)S(1)}, u32[]{:S(2)}, u32[]{:S(2)}) collective-permute-start(f32[64,64]{1,0:T(8,128)S(1)} %fusion.29), channel_id=1, source_target_pairs={{0,3},{1,2},{2,1},{3,0},{4,7},{5,6},{6,5},{7,4},{8,11},{9,10},{10,... | collective-permute-start | bytes 49160 | tf_op jit(solution)/shard_map/ppermute | solution.py:55
  93.7 9.8 %collective-permute-done.12 = f32[64,64]{1,0:T(8,128)S(1)} collective-permute-done((f32[64,64]{1,0:T(8,128)S(1)}, f32[64,64]{1,0:T(8,128)S(1)}, u32[]{:S(2)}, u32[]{:S(2)}) %collective-permute-start.12) | collective-permute-done | bytes 16416 | tf_op jit(solution)/shard_map/ppermute | solution.py:55
  103.4 0.6 add_multiply_fusion
  104.1 1.4 %all-to-all-done.1 = f32[64,1,8,512]{3,2,1,0:T(8,128)S(1)} async-done(((f32[64,1,8,512]{3,2,1,0:T(8,128)}), f32[64,1,8,512]{3,2,1,0:T(8,128)S(1)}, u32[]{:S(2)}, u32[]{:S(2)}) %all-to-all-start.1) | async-done | bytes 1048608 | tf_op jit(solution)/shard_map/all_to_all | solution.py:151
  105.5 1.1 copy.30
  (16 shorter events, 0.1 us)
Async XLA Ops:
  0.6 9.4 %copy-start = (bf16[2,5,1,8,512]{4,3,2,1,0:T(8,128)(2,1)S(1)}, bf16[2,5,1,8,512]{4,3,2,1,0:T(8,128)(2,1)}, u32[]{:S(2)}) copy-start(bf16[2,5,1,8,512]{4,3,2,1,0:T(8,128)(2,1)} %param.3) | copy-start | bytes 245764
  3.0 24.2 %all-to-all-start = ((f32[8,8,8,512]{3,2,0,1:T(8,128)}), f32[8,8,8,512]{3,2,0,1:T(8,128)S(1)}, u32[]{:S(2)}, u32[]{:S(2)}) async-start(f32[8,8,8,512]{3,2,0,1:T(8,128)} %copy.11), calls=%async_computation | async-start | bytes 2097152 | tf_op jit(solution)/shard_map/all_to_all | solution.py:111
  10.0 20.8 %collective-permute-start.1 = (bf16[2,5,1,4,512]{4,3,2,1,0:T(4,128)(2,1)S(1)}, bf16[2,5,1,4,512]{4,3,2,1,0:T(4,128)(2,1)S(1)}, u32[]{:S(2)}, u32[]{:S(2)}) collective-permute-start(bf16[2,5,1,4,512]{4,3,2,1,0:T(4,128)(2,1)S(1)} %get-tuple-element.42), channel_id=1, source_target_pairs={{0,8},{8,16},{16,24},{24,32},{32,40},{40,48},{48,56},{56,64},{64,7... | collective-permute-start | bytes 122888 | tf_op jit(solution)/shard_map/ppermute | solution.py:16
  11.5 19.4 %collective-permute-start.2 = (bf16[2,5,1,4,512]{4,3,2,1,0:T(4,128)(2,1)S(1)}, bf16[2,5,1,4,512]{4,3,2,1,0:T(4,128)(2,1)S(1)}, u32[]{:S(2)}, u32[]{:S(2)}) collective-permute-start(bf16[2,5,1,4,512]{4,3,2,1,0:T(4,128)(2,1)S(1)} %get-tuple-element.43), channel_id=1, source_target_pairs={{8,0},{16,8},{24,16},{32,24},{40,32},{48,40},{56,48},{64,56},{72,6... | collective-permute-start | bytes 122888 | tf_op jit(solution)/shard_map/ppermute | solution.py:17
  27.9 8.7 %collective-permute-start.3 = (f32[64,1,4,512]{3,0,2,1:T(8,128)S(1)}, f32[64,1,4,512]{3,0,2,1:T(8,128)S(1)}, u32[]{:S(2)}, u32[]{:S(2)}) collective-permute-start(f32[64,1,4,512]{3,0,2,1:T(8,128)S(1)} %get-tuple-element.30), channel_id=1, source_target_pairs={{0,8},{8,16},{16,24},{24,32},{32,40},{40,48},{48,56},{56,64},{64,7... | collective-permute-start | bytes 1572872 | tf_op jit(solution)/shard_map/ppermute | solution.py:16
  29.6 7.0 %collective-permute-start.4 = (f32[64,1,4,512]{3,0,2,1:T(8,128)S(1)}, f32[64,1,4,512]{3,0,2,1:T(8,128)S(1)}, u32[]{:S(2)}, u32[]{:S(2)}) collective-permute-start(f32[64,1,4,512]{3,0,2,1:T(8,128)S(1)} %get-tuple-element.31), channel_id=1, source_target_pairs={{8,0},{16,8},{24,16},{32,24},{40,32},{48,40},{56,48},{64,56},{72,6... | collective-permute-start | bytes 1572872 | tf_op jit(solution)/shard_map/ppermute | solution.py:17
  32.6 4.0 %collective-permute-start = (f32[64,64]{1,0:T(8,128)S(1)}, f32[64,64]{1,0:T(8,128)S(1)}, u32[]{:S(2)}, u32[]{:S(2)}) collective-permute-start(f32[64,64]{1,0:T(8,128)S(1)} %fusion.33), channel_id=1, source_target_pairs={{0,1},{1,0},{2,3},{3,2},{4,5},{5,4},{6,7},{7,6},{8,9},{9,8},{10,11... | collective-permute-start | bytes 49160 | tf_op jit(solution)/shard_map/ppermute | solution.py:55
  38.1 5.2 %collective-permute-start.5 = (f32[64,64]{1,0:T(8,128)S(1)}, f32[64,64]{1,0:T(8,128)S(1)}, u32[]{:S(2)}, u32[]{:S(2)}) collective-permute-start(f32[64,64]{1,0:T(8,128)S(1)} %add.107), channel_id=1, source_target_pairs={{0,3},{1,2},{2,1},{3,0},{4,7},{5,6},{6,5},{7,4},{8,11},{9,10},{10,... | collective-permute-start | bytes 49160 | tf_op jit(solution)/shard_map/ppermute | solution.py:55
  45.5 5.8 %collective-permute-start.6 = (f32[2,64,64]{2,1,0:T(8,128)S(1)}, f32[2,64,64]{2,1,0:T(8,128)S(1)}, u32[]{:S(2)}, u32[]{:S(2)}) collective-permute-start(f32[2,64,64]{2,1,0:T(8,128)S(1)} %pad_maximum_fusion.1), channel_id=1, source_target_pairs={{0,4},{1,5},{2,6},{3,7},{4,0},{5,1},{6,2},{7,3},{8,12},{9,13},{10,... | collective-permute-start | bytes 98312 | tf_op jit(solution)/shard_map/ppermute | solution.py:55
  52.6 5.2 %collective-permute-start.7 = (f32[2,64,64]{2,1,0:T(8,128)S(1)}, f32[2,64,64]{2,1,0:T(8,128)S(1)}, u32[]{:S(2)}, u32[]{:S(2)}) collective-permute-start(f32[2,64,64]{2,1,0:T(8,128)S(1)} %fusion.30), channel_id=1, source_target_pairs={{0,8},{8,0},{16,24},{24,16},{32,40},{40,32},{48,56},{56,48},{64,72... | collective-permute-start | bytes 98312 | tf_op jit(solution)/shard_map/ppermute | solution.py:55
  57.8 5.5 %collective-permute-start.8 = (f32[2,64,64]{2,1,0:T(8,128)S(1)}, f32[2,64,64]{2,1,0:T(8,128)S(1)}, u32[]{:S(2)}, u32[]{:S(2)}) collective-permute-start(f32[2,64,64]{2,1,0:T(8,128)S(1)} %add.122), channel_id=1, source_target_pairs={{0,16},{8,24},{16,0},{24,8},{32,48},{40,56},{48,32},{56,40},{64,80... | collective-permute-start | bytes 98312 | tf_op jit(solution)/shard_map/ppermute | solution.py:55
  63.3 6.2 %collective-permute-start.9 = (f32[2,64,64]{2,1,0:T(8,128)S(1)}, f32[2,64,64]{2,1,0:T(8,128)S(1)}, u32[]{:S(2)}, u32[]{:S(2)}) collective-permute-start(f32[2,64,64]{2,1,0:T(8,128)S(1)} %add.127), channel_id=1, source_target_pairs={{0,48},{8,56},{16,32},{24,40},{32,16},{40,24},{48,0},{56,8},{64,11... | collective-permute-start | bytes 98312 | tf_op jit(solution)/shard_map/ppermute | solution.py:55
  69.5 4.3 %collective-permute-start.10 = (f32[2,64,64]{2,1,0:T(8,128)S(1)}, f32[2,64,64]{2,1,0:T(8,128)S(1)}, u32[]{:S(2)}, u32[]{:S(2)}) collective-permute-start(f32[2,64,64]{2,1,0:T(8,128)S(1)} %add.128), channel_id=1, source_target_pairs={{0,64},{8,72},{16,80},{24,88},{32,96},{40,104},{48,112},{56,120},{... | collective-permute-start | bytes 98312 | tf_op jit(solution)/shard_map/ppermute | solution.py:55
  74.5 8.1 %collective-permute-start.11 = (f32[64,64]{1,0:T(8,128)S(1)}, f32[64,64]{1,0:T(8,128)S(1)}, u32[]{:S(2)}, u32[]{:S(2)}) collective-permute-start(f32[64,64]{1,0:T(8,128)S(1)} %get-tuple-element.44), channel_id=1, source_target_pairs={{0,1},{1,0},{2,3},{3,2},{4,5},{5,4},{6,7},{7,6},{8,9},{9,8},{10,11... | collective-permute-start | bytes 49160 | tf_op jit(solution)/shard_map/ppermute | solution.py:55
  86.3 19.2 %all-to-all-start.1 = ((f32[64,1,8,512]{3,2,1,0:T(8,128)}), f32[64,1,8,512]{3,2,1,0:T(8,128)S(1)}, u32[]{:S(2)}, u32[]{:S(2)}) async-start(f32[64,1,8,512]{3,2,1,0:T(8,128)} %copy.15), calls=%async_computation.1 | async-start | bytes 2097152 | tf_op jit(solution)/shard_map/all_to_all | solution.py:151
  90.4 13.0 %collective-permute-start.12 = (f32[64,64]{1,0:T(8,128)S(1)}, f32[64,64]{1,0:T(8,128)S(1)}, u32[]{:S(2)}, u32[]{:S(2)}) collective-permute-start(f32[64,64]{1,0:T(8,128)S(1)} %fusion.29), channel_id=1, source_target_pairs={{0,3},{1,2},{2,1},{3,0},{4,7},{5,6},{6,5},{7,4},{8,11},{9,10},{10,... | collective-permute-start | bytes 49160 | tf_op jit(solution)/shard_map/ppermute | solution.py:55

commit v20 on v19

--- a/solution.py
+++ b/solution.py
@@ -70,19 +70,20 @@
 
         def step(k, carry):
             a = a_ref[lo:, :]
-            row = a_ref[pl.ds(k, 1), :]
+            row = a_ref[k : k + 1, :]
             pivot = jnp.sum(jnp.where(lane == k, row, 0.0), axis=1, keepdims=True)
             scale = 1.0 / jnp.sqrt(pivot)
             col = jnp.sum(jnp.where(cols_lo == k, a, 0.0), axis=1, keepdims=True)
             below = jnp.where(sub > k, col * scale, 0.0)
             right = jnp.where(lane > k, row * scale, 0.0)
             a_ref[lo:, :] = a - below * right
-            xrow = x_ref[pl.ds(k, 1), :] * scale
-            x_ref[pl.ds(k, 1), :] = xrow
+            xrow = x_ref[k : k + 1, :] * scale
+            x_ref[k : k + 1, :] = xrow
             x_ref[lo:, :] = x_ref[lo:, :] - below * xrow
             return carry
 
-        lax.fori_loop(lo, min(lo + phase, n), step, 0)
+        for k in range(lo, min(lo + phase, n)):
+            step(k, 0)
 
 
 def lower_inverse(gram):

time: 107 us -> 107 us (level)
  no operation moved by 1% of the time
where the time goes in v20:
time: 107 us
  waiting for transfers between devices  43.1 us (40%)
  starting transfers between devices  34.6 us (32%)
  other arithmetic  9.57 us (9%)
  Pallas kernels  8.41 us (8%)
  local copies, waits for them, and re-layouts  6.31 us (6%)
  matrix products  4.02 us (4%)
    ppermute x9, waiting for transfers between devices, exchange(): return x + lax.ppermute(x, axis, [(i, i ^ bit) for i in range(count)])  27.3 us
    ppermute x9, starting transfers between devices, exchange(): return x + lax.ppermute(x, axis, [(i, i ^ bit) for i in range(count)])  17.7 us
    all_to_all x1, waiting for transfers between devices, body(): v = lax.all_to_all(perturbations, 'mem', 1, 0, tiled=True)  14.4 us
    pallas_call x1, Pallas kernels, lower_inverse(): pl.pallas_call(chol_inv_kernel, out_shape=jax.ShapeDtypeStruct((n, n), jn...  8.41 us
    all_to_all x1, starting transfers between devices, body(): v = lax.all_to_all(perturbations, 'mem', 1, 0, tiled=True)  7.04 us
    all_to_all x1, starting transfers between devices, body(): ritz = lax.all_to_all(ritz.reshape(v.shape), 'mem', 0, 1, tiled=True)  4.17 us
    ppermute x2, starting transfers between devices, halo(): lax.ppermute(lax.slice_in_dim(block, size - width, size, axis=dim), 'dom'...  3.12 us
    add x2, other arithmetic, adjoint_step(): result + shifted(coef[3] * field, 1, 3) + shifted(coef[4] * field, -1, 3)  2.94 us
  transfers between devices with their start and end apart: 15, of which 9 were waited for; matrix products, arithmetic and copies ran while one was open for 7% of the time, Pallas kernels for 8%

profile of v20, /device:TPU:0, one launch (start us, length us, event | category | flops | bytes accessed | tf_op | source)
XLA Modules:
  0.0 106.9 jit_solution(8593047451647787998)
XLA Ops:
  0.6 2.3 %copy.11 = f32[8,8,8,512]{3,2,0,1:T(8,128)} copy(f32[8,8,8,512]{3,2,1,0:T(8,128)} %param.2) | data formatting | bytes 2097152 | tf_op args[0]
  3.0 7.0 %all-to-all-start = ((f32[8,8,8,512]{3,2,0,1:T(8,128)}), f32[8,8,8,512]{3,2,0,1:T(8,128)S(1)}, u32[]{:S(2)}, u32[]{:S(2)}) async-start(f32[8,8,8,512]{3,2,0,1:T(8,128)} %copy.11), calls=%async_computation | async-start | bytes 2097152 | tf_op jit(solution)/shard_map/all_to_all | solution.py:112
  10.0 1.5 %collective-permute-start.1 = (bf16[2,5,1,4,512]{4,3,2,1,0:T(4,128)(2,1)S(1)}, bf16[2,5,1,4,512]{4,3,2,1,0:T(4,128)(2,1)S(1)}, u32[]{:S(2)}, u32[]{:S(2)}) collective-permute-start(bf16[2,5,1,4,512]{4,3,2,1,0:T(4,128)(2,1)S(1)} %get-tuple-element.42), channel_id=1, source_target_pairs={{0,8},{8,16},{16,24},{24,32},{32,40},{40,48},{48,56},{56,64},{64,7... | collective-permute-start | bytes 122888 | tf_op jit(solution)/shard_map/ppermute | solution.py:16
  11.5 1.3 %collective-permute-start.2 = (bf16[2,5,1,4,512]{4,3,2,1,0:T(4,128)(2,1)S(1)}, bf16[2,5,1,4,512]{4,3,2,1,0:T(4,128)(2,1)S(1)}, u32[]{:S(2)}, u32[]{:S(2)}) collective-permute-start(bf16[2,5,1,4,512]{4,3,2,1,0:T(4,128)(2,1)S(1)} %get-tuple-element.43), channel_id=1, source_target_pairs={{8,0},{16,8},{24,16},{32,24},{40,32},{48,40},{56,48},{64,56},{72,6... | collective-permute-start | bytes 122888 | tf_op jit(solution)/shard_map/ppermute | solution.py:17
  12.8 14.4 %all-to-all-done = f32[8,8,8,512]{3,2,0,1:T(8,128)S(1)} async-done(((f32[8,8,8,512]{3,2,0,1:T(8,128)}), f32[8,8,8,512]{3,2,0,1:T(8,128)S(1)}, u32[]{:S(2)}, u32[]{:S(2)}) %all-to-all-start) | async-done | bytes 1048608 | tf_op jit(solution)/shard_map/all_to_all | solution.py:112
  27.2 0.6 copy.31
  27.8 0.1 fusion.31
  27.9 1.7 %collective-permute-start.3 = (f32[64,1,4,512]{3,0,2,1:T(8,128)S(1)}, f32[64,1,4,512]{3,0,2,1:T(8,128)S(1)}, u32[]{:S(2)}, u32[]{:S(2)}) collective-permute-start(f32[64,1,4,512]{3,0,2,1:T(8,128)S(1)} %get-tuple-element.30), channel_id=1, source_target_pairs={{0,8},{8,16},{16,24},{24,32},{32,40},{40,48},{48,56},{56,64},{64,7... | collective-permute-start | bytes 1572872 | tf_op jit(solution)/shard_map/ppermute | solution.py:16
  29.6 1.3 %collective-permute-start.4 = (f32[64,1,4,512]{3,0,2,1:T(8,128)S(1)}, f32[64,1,4,512]{3,0,2,1:T(8,128)S(1)}, u32[]{:S(2)}, u32[]{:S(2)}) collective-permute-start(f32[64,1,4,512]{3,0,2,1:T(8,128)S(1)} %get-tuple-element.31), channel_id=1, source_target_pairs={{8,0},{16,8},{24,16},{32,24},{40,32},{48,40},{56,48},{64,56},{72,6... | collective-permute-start | bytes 1572872 | tf_op jit(solution)/shard_map/ppermute | solution.py:17
  30.9 0.0 collective-permute-done.2
  30.9 0.1 maximum_convert_fusion
  31.0 0.6 copy.18
  31.6 1.0 fusion.33
  32.6 0.6 collective-permute-start
  33.2 3.4 %collective-permute-done = f32[64,64]{1,0:T(8,128)S(1)} collective-permute-done((f32[64,64]{1,0:T(8,128)S(1)}, f32[64,64]{1,0:T(8,128)S(1)}, u32[]{:S(2)}, u32[]{:S(2)}) %collective-permute-start) | collective-permute-done | bytes 16416 | tf_op jit(solution)/shard_map/ppermute | solution.py:55
  36.6 0.0 collective-permute-done.3
  36.6 0.0 collective-permute-done.4
  36.6 0.2 pad_maximum_fusion
  36.8 1.3 %fusion.4 = f32[64,1,16,512]{3,0,2,1:T(8,128)S(1)} fusion(f32[64,1,16,512]{3,0,2,1:T(8,128)S(1)} %pad_maximum_fusion, f32[16,512]{1,0:T(8,128)S(1)} %get-tuple-element.37, f32[16,512]{1,0:T(8,128)S(1)} %get-tuple-element.38, f32[16,512]{1,0:T(8,128)S(1)} %get-tuple-element.39, f32[16,512]{1,0:T(8,128)S(1)} %get-tuple-element.40, ...), kind=kLoop, calls=%fused_computation.20 | loop fusion | flops 4718592 | bytes 4358144 | tf_op jit(solution)/shard_map/add | solution.py:33
  38.1 0.9 collective-permute-start.5
  39.0 1.3 %fusion.10 = f32[64,1,16,512]{3,0,2,1:T(8,128)S(1)} fusion(f32[64,1,16,512]{3,0,2,1:T(8,128)S(1)} %fusion.4, f32[16,512]{1,0:T(8,128)S(1)} %get-tuple-element.33, f32[16,512]{1,0:T(8,128)S(1)} %get-tuple-element.34, f32[16,512]{1,0:T(8,128)S(1)} %get-tuple-element.35, f32[16,512]{1,0:T(8,128)S(1)} %get-tuple-element.36, f32[16,512]{1,0:T(8,128)S(1)} %get-tuple-element.32), kind=kLoop, calls=%fused_computation.26 | loop fusion | flops 4718592 | bytes 4358144 | tf_op jit(solution)/shard_map/add | solution.py:33
  40.3 3.0 %collective-permute-done.5 = f32[64,64]{1,0:T(8,128)S(1)} collective-permute-done((f32[64,64]{1,0:T(8,128)S(1)}, f32[64,64]{1,0:T(8,128)S(1)}, u32[]{:S(2)}, u32[]{:S(2)}) %collective-permute-start.5) | collective-permute-done | bytes 16416 | tf_op jit(solution)/shard_map/ppermute | solution.py:55
  43.3 1.2 %broadcast_multiply_fusion = (f32[64,1,16,512]{3,0,2,1:T(8,128)S(1)}, f32[64,1,16,512]{3,0,2,1:T(8,128)S(1)}, f32[64,1,16,512]{3,0,2,1:T(8,128)S(1)}, f32[64,1,16,512]{3,0,2,1:T(8,128)S(1)}) fusion(f32[64,1,16,512]{3,0,2,1:T(8,128)S(1)} %fusion.10, f32[16,512]{1,0:T(8,128)S(1)} %get-tuple-element.33, f32[16,512]{1,0:T(8,128)S(1)} %get-tuple-element.34, ...), kind=kLoop, calls=%fused_computation.50 | loop fusion | flops 2097152 | bytes 10616832 | tf_op jit(solution)/shard_map/mul | solution.py:38
  44.5 1.0 convolution_bitcast_fusion.2
  45.5 0.6 collective-permute-start.6
  46.2 1.5 %fusion.15 = f32[64,1,16,512]{3,0,2,1:T(8,128)S(1)} fusion(f32[64,1,16,512]{3,0,2,1:T(8,128)S(1)} %get-tuple-element.29, f32[64,1,16,512]{3,0,2,1:T(8,128)S(1)} %get-tuple-element.28, f32[64,1,16,512]{3,0,2,1:T(8,128)S(1)} %get-tuple-element.27, f32[64,1,16,512]{3,0,2,1:T(8,128)S(1)} %get-tuple-element.26, f32[64,1,16,512]{3,0,2,1:T(8,128)S(1)} %fusion.10, ...), kind=kLoop, calls=%fused_computation.31 | loop fusion | flops 2621440 | bytes 12615680 | tf_op jit(solution)/shard_map/add | solution.py:38
  47.7 3.7 %collective-permute-done.6 = f32[2,64,64]{2,1,0:T(8,128)S(1)} collective-permute-done((f32[2,64,64]{2,1,0:T(8,128)S(1)}, f32[2,64,64]{2,1,0:T(8,128)S(1)}, u32[]{:S(2)}, u32[]{:S(2)}) %collective-permute-start.6) | collective-permute-done | bytes 32800 | tf_op jit(solution)/shard_map/ppermute | solution.py:55
  51.4 1.2 %broadcast_multiply_fusion.4 = (f32[64,1,16,512]{3,0,2,1:T(8,128)S(1)}, f32[64,1,16,512]{3,0,2,1:T(8,128)S(1)}, f32[64,1,16,512]{3,0,2,1:T(8,128)S(1)}, f32[64,1,16,512]{3,0,2,1:T(8,128)S(1)}) fusion(f32[64,1,16,512]{3,0,2,1:T(8,128)S(1)} %fusion.15, f32[16,512]{1,0:T(8,128)S(1)} %get-tuple-element.37, f32[16,512]{1,0:T(8,128)S(1)} %get-tuple-element.38, ...), kind=kLoop, calls=%fused_computation.54 | loop fusion | flops 2097152 | bytes 10616832 | tf_op jit(solution)/shard_map/mul | solution.py:38
  52.6 3.7 %collective-permute-start.7 = (f32[2,64,64]{2,1,0:T(8,128)S(1)}, f32[2,64,64]{2,1,0:T(8,128)S(1)}, u32[]{:S(2)}, u32[]{:S(2)}) collective-permute-start(f32[2,64,64]{2,1,0:T(8,128)S(1)} %fusion.30), channel_id=1, source_target_pairs={{0,8},{8,0},{16,24},{24,16},{32,40},{40,32},{48,56},{56,48},{64,72... | collective-permute-start | bytes 98312 | tf_op jit(solution)/shard_map/ppermute | solution.py:55
  56.4 1.4 %fusion.19 = f32[64,1,16,512]{3,0,2,1:T(8,128)S(1)} fusion(f32[64,1,16,512]{3,0,2,1:T(8,128)S(1)} %get-tuple-element.25, f32[64,1,16,512]{3,0,2,1:T(8,128)S(1)} %get-tuple-element.24, f32[64,1,16,512]{3,0,2,1:T(8,128)S(1)} %get-tuple-element.23, f32[64,1,16,512]{3,0,2,1:T(8,128)S(1)} %get-tuple-element.22, f32[64,1,16,512]{3,0,2,1:T(8,128)S(1)} %fusion.15, ...), kind=kLoop, calls=%fused_computation.35 | loop fusion | flops 2621440 | bytes 12615680 | tf_op jit(solution)/shard_map/add | solution.py:38
  57.8 2.8 %collective-permute-start.8 = (f32[2,64,64]{2,1,0:T(8,128)S(1)}, f32[2,64,64]{2,1,0:T(8,128)S(1)}, u32[]{:S(2)}, u32[]{:S(2)}) collective-permute-start(f32[2,64,64]{2,1,0:T(8,128)S(1)} %add.122), channel_id=1, source_target_pairs={{0,16},{8,24},{16,0},{24,8},{32,48},{40,56},{48,32},{56,40},{64,80... | collective-permute-start | bytes 98312 | tf_op jit(solution)/shard_map/ppermute | solution.py:55
  60.7 2.7 %collective-permute-done.8 = f32[2,64,64]{2,1,0:T(8,128)S(1)} collective-permute-done((f32[2,64,64]{2,1,0:T(8,128)S(1)}, f32[2,64,64]{2,1,0:T(8,128)S(1)}, u32[]{:S(2)}, u32[]{:S(2)}) %collective-permute-start.8) | collective-permute-done | bytes 32800 | tf_op jit(solution)/shard_map/ppermute | solution.py:55
  63.3 3.9 %collective-permute-start.9 = (f32[2,64,64]{2,1,0:T(8,128)S(1)}, f32[2,64,64]{2,1,0:T(8,128)S(1)}, u32[]{:S(2)}, u32[]{:S(2)}) collective-permute-start(f32[2,64,64]{2,1,0:T(8,128)S(1)} %add.127), channel_id=1, source_target_pairs={{0,48},{8,56},{16,32},{24,40},{32,16},{40,24},{48,0},{56,8},{64,11... | collective-permute-start | bytes 98312 | tf_op jit(solution)/shard_map/ppermute | solution.py:55
  67.3 2.2 %collective-permute-done.9 = f32[2,64,64]{2,1,0:T(8,128)S(1)} collective-permute-done((f32[2,64,64]{2,1,0:T(8,128)S(1)}, f32[2,64,64]{2,1,0:T(8,128)S(1)}, u32[]{:S(2)}, u32[]{:S(2)}) %collective-permute-start.9) | collective-permute-done | bytes 32800 | tf_op jit(solution)/shard_map/ppermute | solution.py:55
  69.5 1.8 %collective-permute-start.10 = (f32[2,64,64]{2,1,0:T(8,128)S(1)}, f32[2,64,64]{2,1,0:T(8,128)S(1)}, u32[]{:S(2)}, u32[]{:S(2)}) collective-permute-start(f32[2,64,64]{2,1,0:T(8,128)S(1)} %add.128), channel_id=1, source_target_pairs={{0,64},{8,72},{16,80},{24,88},{32,96},{40,104},{48,112},{56,120},{... | collective-permute-start | bytes 98312 | tf_op jit(solution)/shard_map/ppermute | solution.py:55
  71.3 2.6 %collective-permute-done.10 = f32[2,64,64]{2,1,0:T(8,128)S(1)} collective-permute-done((f32[2,64,64]{2,1,0:T(8,128)S(1)}, f32[2,64,64]{2,1,0:T(8,128)S(1)}, u32[]{:S(2)}, u32[]{:S(2)}) %collective-permute-start.10) | collective-permute-done | bytes 32800 | tf_op jit(solution)/shard_map/ppermute | solution.py:55
  73.9 0.6 slice_bitcast_fusion
  74.5 0.0 collective-permute-start.11
  74.5 8.4 %shard_map.41 = f32[64,64]{1,0:T(8,128)} custom-call(f32[64,64]{1,0:T(8,128)} %get-tuple-element.45.g_ref), custom_call_target="tpu_custom_call" | custom-call | tf_op jit(solution)/shard_map/pallas_call | solution.py:91
  82.9 1.1 convolution_bitcast_fusion.1
  84.0 1.0 convolution_bitcast_fusion
  85.0 1.6 %copy.15 = f32[64,1,8,512]{3,2,1,0:T(8,128)} copy(f32[64,1,8,512]{3,0,2,1:T(8,128)S(1)} %convolution_bitcast_fusion) | data formatting | bytes 2097152 | tf_op jit(solution)/shard_map/dot_general | solution.py:148
  86.6 4.2 %all-to-all-start.1 = ((f32[64,1,8,512]{3,2,1,0:T(8,128)}), f32[64,1,8,512]{3,2,1,0:T(8,128)S(1)}, u32[]{:S(2)}, u32[]{:S(2)}) async-start(f32[64,1,8,512]{3,2,1,0:T(8,128)} %copy.15), calls=%async_computation.1 | async-start | bytes 2097152 | tf_op jit(solution)/shard_map/all_to_all | solution.py:152
  90.8 3.2 %collective-permute-start.12 = (f32[64,64]{1,0:T(8,128)S(1)}, f32[64,64]{1,0:T(8,128)S(1)}, u32[]{:S(2)}, u32[]{:S(2)}) collective-permute-start(f32[64,64]{1,0:T(8,128)S(1)} %fusion.29), channel_id=1, source_target_pairs={{0,3},{1,2},{2,1},{3,0},{4,7},{5,6},{6,5},{7,4},{8,11},{9,10},{10,... | collective-permute-start | bytes 49160 | tf_op jit(solution)/shard_map/ppermute | solution.py:55
  94.0 9.8 %collective-permute-done.12 = f32[64,64]{1,0:T(8,128)S(1)} collective-permute-done((f32[64,64]{1,0:T(8,128)S(1)}, f32[64,64]{1,0:T(8,128)S(1)}, u32[]{:S(2)}, u32[]{:S(2)}) %collective-permute-start.12) | collective-permute-done | bytes 16416 | tf_op jit(solution)/shard_map/ppermute | solution.py:55
  103.8 0.6 add_multiply_fusion
  104.4 1.4 %all-to-all-done.1 = f32[64,1,8,512]{3,2,1,0:T(8,128)S(1)} async-done(((f32[64,1,8,512]{3,2,1,0:T(8,128)}), f32[64,1,8,512]{3,2,1,0:T(8,128)S(1)}, u32[]{:S(2)}, u32[]{:S(2)}) %all-to-all-start.1) | async-done | bytes 1048608 | tf_op jit(solution)/shard_map/all_to_all | solution.py:152
  105.8 1.1 copy.30
  (16 shorter events, 0.1 us)
Async XLA Ops:
  0.6 9.4 %copy-start = (bf16[2,5,1,8,512]{4,3,2,1,0:T(8,128)(2,1)S(1)}, bf16[2,5,1,8,512]{4,3,2,1,0:T(8,128)(2,1)}, u32[]{:S(2)}) copy-start(bf16[2,5,1,8,512]{4,3,2,1,0:T(8,128)(2,1)} %param.3) | copy-start | bytes 245764
  3.0 24.2 %all-to-all-start = ((f32[8,8,8,512]{3,2,0,1:T(8,128)}), f32[8,8,8,512]{3,2,0,1:T(8,128)S(1)}, u32[]{:S(2)}, u32[]{:S(2)}) async-start(f32[8,8,8,512]{3,2,0,1:T(8,128)} %copy.11), calls=%async_computation | async-start | bytes 2097152 | tf_op jit(solution)/shard_map/all_to_all | solution.py:112
  10.0 20.8 %collective-permute-start.1 = (bf16[2,5,1,4,512]{4,3,2,1,0:T(4,128)(2,1)S(1)}, bf16[2,5,1,4,512]{4,3,2,1,0:T(4,128)(2,1)S(1)}, u32[]{:S(2)}, u32[]{:S(2)}) collective-permute-start(bf16[2,5,1,4,512]{4,3,2,1,0:T(4,128)(2,1)S(1)} %get-tuple-element.42), channel_id=1, source_target_pairs={{0,8},{8,16},{16,24},{24,32},{32,40},{40,48},{48,56},{56,64},{64,7... | collective-permute-start | bytes 122888 | tf_op jit(solution)/shard_map/ppermute | solution.py:16
  11.5 19.4 %collective-permute-start.2 = (bf16[2,5,1,4,512]{4,3,2,1,0:T(4,128)(2,1)S(1)}, bf16[2,5,1,4,512]{4,3,2,1,0:T(4,128)(2,1)S(1)}, u32[]{:S(2)}, u32[]{:S(2)}) collective-permute-start(bf16[2,5,1,4,512]{4,3,2,1,0:T(4,128)(2,1)S(1)} %get-tuple-element.43), channel_id=1, source_target_pairs={{8,0},{16,8},{24,16},{32,24},{40,32},{48,40},{56,48},{64,56},{72,6... | collective-permute-start | bytes 122888 | tf_op jit(solution)/shard_map/ppermute | solution.py:17
  27.9 8.7 %collective-permute-start.3 = (f32[64,1,4,512]{3,0,2,1:T(8,128)S(1)}, f32[64,1,4,512]{3,0,2,1:T(8,128)S(1)}, u32[]{:S(2)}, u32[]{:S(2)}) collective-permute-start(f32[64,1,4,512]{3,0,2,1:T(8,128)S(1)} %get-tuple-element.30), channel_id=1, source_target_pairs={{0,8},{8,16},{16,24},{24,32},{32,40},{40,48},{48,56},{56,64},{64,7... | collective-permute-start | bytes 1572872 | tf_op jit(solution)/shard_map/ppermute | solution.py:16
  29.6 7.0 %collective-permute-start.4 = (f32[64,1,4,512]{3,0,2,1:T(8,128)S(1)}, f32[64,1,4,512]{3,0,2,1:T(8,128)S(1)}, u32[]{:S(2)}, u32[]{:S(2)}) collective-permute-start(f32[64,1,4,512]{3,0,2,1:T(8,128)S(1)} %get-tuple-element.31), channel_id=1, source_target_pairs={{8,0},{16,8},{24,16},{32,24},{40,32},{48,40},{56,48},{64,56},{72,6... | collective-permute-start | bytes 1572872 | tf_op jit(solution)/shard_map/ppermute | solution.py:17
  32.6 4.0 %collective-permute-start = (f32[64,64]{1,0:T(8,128)S(1)}, f32[64,64]{1,0:T(8,128)S(1)}, u32[]{:S(2)}, u32[]{:S(2)}) collective-permute-start(f32[64,64]{1,0:T(8,128)S(1)} %fusion.33), channel_id=1, source_target_pairs={{0,1},{1,0},{2,3},{3,2},{4,5},{5,4},{6,7},{7,6},{8,9},{9,8},{10,11... | collective-permute-start | bytes 49160 | tf_op jit(solution)/shard_map/ppermute | solution.py:55
  38.1 5.2 %collective-permute-start.5 = (f32[64,64]{1,0:T(8,128)S(1)}, f32[64,64]{1,0:T(8,128)S(1)}, u32[]{:S(2)}, u32[]{:S(2)}) collective-permute-start(f32[64,64]{1,0:T(8,128)S(1)} %add.107), channel_id=1, source_target_pairs={{0,3},{1,2},{2,1},{3,0},{4,7},{5,6},{6,5},{7,4},{8,11},{9,10},{10,... | collective-permute-start | bytes 49160 | tf_op jit(solution)/shard_map/ppermute | solution.py:55
  45.5 5.8 %collective-permute-start.6 = (f32[2,64,64]{2,1,0:T(8,128)S(1)}, f32[2,64,64]{2,1,0:T(8,128)S(1)}, u32[]{:S(2)}, u32[]{:S(2)}) collective-permute-start(f32[2,64,64]{2,1,0:T(8,128)S(1)} %pad_maximum_fusion.1), channel_id=1, source_target_pairs={{0,4},{1,5},{2,6},{3,7},{4,0},{5,1},{6,2},{7,3},{8,12},{9,13},{10,... | collective-permute-start | bytes 98312 | tf_op jit(solution)/shard_map/ppermute | solution.py:55
  52.6 5.2 %collective-permute-start.7 = (f32[2,64,64]{2,1,0:T(8,128)S(1)}, f32[2,64,64]{2,1,0:T(8,128)S(1)}, u32[]{:S(2)}, u32[]{:S(2)}) collective-permute-start(f32[2,64,64]{2,1,0:T(8,128)S(1)} %fusion.30), channel_id=1, source_target_pairs={{0,8},{8,0},{16,24},{24,16},{32,40},{40,32},{48,56},{56,48},{64,72... | collective-permute-start | bytes 98312 | tf_op jit(solution)/shard_map/ppermute | solution.py:55
  57.8 5.5 %collective-permute-start.8 = (f32[2,64,64]{2,1,0:T(8,128)S(1)}, f32[2,64,64]{2,1,0:T(8,128)S(1)}, u32[]{:S(2)}, u32[]{:S(2)}) collective-permute-start(f32[2,64,64]{2,1,0:T(8,128)S(1)} %add.122), channel_id=1, source_target_pairs={{0,16},{8,24},{16,0},{24,8},{32,48},{40,56},{48,32},{56,40},{64,80... | collective-permute-start | bytes 98312 | tf_op jit(solution)/shard_map/ppermute | solution.py:55
  63.3 6.2 %collective-permute-start.9 = (f32[2,64,64]{2,1,0:T(8,128)S(1)}, f32[2,64,64]{2,1,0:T(8,128)S(1)}, u32[]{:S(2)}, u32[]{:S(2)}) collective-permute-start(f32[2,64,64]{2,1,0:T(8,128)S(1)} %add.127), channel_id=1, source_target_pairs={{0,48},{8,56},{16,32},{24,40},{32,16},{40,24},{48,0},{56,8},{64,11... | collective-permute-start | bytes 98312 | tf_op jit(solution)/shard_map/ppermute | solution.py:55
  69.5 4.3 %collective-permute-start.10 = (f32[2,64,64]{2,1,0:T(8,128)S(1)}, f32[2,64,64]{2,1,0:T(8,128)S(1)}, u32[]{:S(2)}, u32[]{:S(2)}) collective-permute-start(f32[2,64,64]{2,1,0:T(8,128)S(1)} %add.128), channel_id=1, source_target_pairs={{0,64},{8,72},{16,80},{24,88},{32,96},{40,104},{48,112},{56,120},{... | collective-permute-start | bytes 98312 | tf_op jit(solution)/shard_map/ppermute | solution.py:55
  74.5 8.4 %collective-permute-start.11 = (f32[64,64]{1,0:T(8,128)S(1)}, f32[64,64]{1,0:T(8,128)S(1)}, u32[]{:S(2)}, u32[]{:S(2)}) collective-permute-start(f32[64,64]{1,0:T(8,128)S(1)} %get-tuple-element.44), channel_id=1, source_target_pairs={{0,1},{1,0},{2,3},{3,2},{4,5},{5,4},{6,7},{7,6},{8,9},{9,8},{10,11... | collective-permute-start | bytes 49160 | tf_op jit(solution)/shard_map/ppermute | solution.py:55
  86.6 19.2 %all-to-all-start.1 = ((f32[64,1,8,512]{3,2,1,0:T(8,128)}), f32[64,1,8,512]{3,2,1,0:T(8,128)S(1)}, u32[]{:S(2)}, u32[]{:S(2)}) async-start(f32[64,1,8,512]{3,2,1,0:T(8,128)} %copy.15), calls=%async_computation.1 | async-start | bytes 2097152 | tf_op jit(solution)/shard_map/all_to_all | solution.py:152
  90.8 13.0 %collective-permute-start.12 = (f32[64,64]{1,0:T(8,128)S(1)}, f32[64,64]{1,0:T(8,128)S(1)}, u32[]{:S(2)}, u32[]{:S(2)}) collective-permute-start(f32[64,64]{1,0:T(8,128)S(1)} %fusion.29), channel_id=1, source_target_pairs={{0,3},{1,2},{2,1},{3,0},{4,7},{5,6},{6,5},{7,4},{8,11},{9,10},{10,... | collective-permute-start | bytes 49160 | tf_op jit(solution)/shard_map/ppermute | solution.py:55

commit v21 on v20

--- a/solution.py
+++ b/solution.py
@@ -72,7 +72,7 @@
             a = a_ref[lo:, :]
             row = a_ref[k : k + 1, :]
             pivot = jnp.sum(jnp.where(lane == k, row, 0.0), axis=1, keepdims=True)
-            scale = 1.0 / jnp.sqrt(pivot)
+            scale = lax.rsqrt(pivot)
             col = jnp.sum(jnp.where(cols_lo == k, a, 0.0), axis=1, keepdims=True)
             below = jnp.where(sub > k, col * scale, 0.0)
             right = jnp.where(lane > k, row * scale, 0.0)

time: 107 us -> 107 us (level)
  transfers between devices with their start and end apart: 15 -> 15, of which waited for: 9 -> 9; matrix products, arithmetic and copies ran while one was open for 7% -> 7% of each run, Pallas kernels for 8% -> 7%
where the time goes in v21:
time: 107 us; the launch traced here: 106 us
  waiting for transfers between devices  43.1 us (40%)
  starting transfers between devices  34.6 us (32%)
  other arithmetic  9.57 us (9%)
  Pallas kernels  7.62 us (7%)
  local copies, waits for them, and re-layouts  6.31 us (6%)
  matrix products  4.02 us (4%)
    ppermute x9, waiting for transfers between devices, exchange(): return x + lax.ppermute(x, axis, [(i, i ^ bit) for i in range(count)])  27.3 us
    ppermute x9, starting transfers between devices, exchange(): return x + lax.ppermute(x, axis, [(i, i ^ bit) for i in range(count)])  17.7 us
    all_to_all x1, waiting for transfers between devices, body(): v = lax.all_to_all(perturbations, 'mem', 1, 0, tiled=True)  14.4 us
    pallas_call x1, Pallas kernels, lower_inverse(): pl.pallas_call(chol_inv_kernel, out_shape=jax.ShapeDtypeStruct((n, n), jn...  7.62 us
    all_to_all x1, starting transfers between devices, body(): v = lax.all_to_all(perturbations, 'mem', 1, 0, tiled=True)  7.04 us
    all_to_all x1, starting transfers between devices, body(): ritz = lax.all_to_all(ritz.reshape(v.shape), 'mem', 0, 1, tiled=True)  4.17 us
    ppermute x2, starting transfers between devices, halo(): lax.ppermute(lax.slice_in_dim(block, size - width, size, axis=dim), 'dom'...  3.12 us
    add x2, other arithmetic, adjoint_step(): result + shifted(coef[3] * field, 1, 3) + shifted(coef[4] * field, -1, 3)  2.94 us
  transfers between devices with their start and end apart: 15, of which 9 were waited for; matrix products, arithmetic and copies ran while one was open for 7% of the time, Pallas kernels for 7%

profile of v21, /device:TPU:0, one launch (start us, length us, event | category | flops | bytes accessed | tf_op | source)
XLA Modules:
  0.0 106.1 jit_solution(6975147852879631778)
XLA Ops:
  0.6 2.3 %copy.11 = f32[8,8,8,512]{3,2,0,1:T(8,128)} copy(f32[8,8,8,512]{3,2,1,0:T(8,128)} %param.2) | data formatting | bytes 2097152 | tf_op args[0]
  3.0 7.0 %all-to-all-start = ((f32[8,8,8,512]{3,2,0,1:T(8,128)}), f32[8,8,8,512]{3,2,0,1:T(8,128)S(1)}, u32[]{:S(2)}, u32[]{:S(2)}) async-start(f32[8,8,8,512]{3,2,0,1:T(8,128)} %copy.11), calls=%async_computation | async-start | bytes 2097152 | tf_op jit(solution)/shard_map/all_to_all | solution.py:112
  10.0 1.5 %collective-permute-start.1 = (bf16[2,5,1,4,512]{4,3,2,1,0:T(4,128)(2,1)S(1)}, bf16[2,5,1,4,512]{4,3,2,1,0:T(4,128)(2,1)S(1)}, u32[]{:S(2)}, u32[]{:S(2)}) collective-permute-start(bf16[2,5,1,4,512]{4,3,2,1,0:T(4,128)(2,1)S(1)} %get-tuple-element.42), channel_id=1, source_target_pairs={{0,8},{8,16},{16,24},{24,32},{32,40},{40,48},{48,56},{56,64},{64,7... | collective-permute-start | bytes 122888 | tf_op jit(solution)/shard_map/ppermute | solution.py:16
  11.5 1.3 %collective-permute-start.2 = (bf16[2,5,1,4,512]{4,3,2,1,0:T(4,128)(2,1)S(1)}, bf16[2,5,1,4,512]{4,3,2,1,0:T(4,128)(2,1)S(1)}, u32[]{:S(2)}, u32[]{:S(2)}) collective-permute-start(bf16[2,5,1,4,512]{4,3,2,1,0:T(4,128)(2,1)S(1)} %get-tuple-element.43), channel_id=1, source_target_pairs={{8,0},{16,8},{24,16},{32,24},{40,32},{48,40},{56,48},{64,56},{72,6... | collective-permute-start | bytes 122888 | tf_op jit(solution)/shard_map/ppermute | solution.py:17
  12.8 14.4 %all-to-all-done = f32[8,8,8,512]{3,2,0,1:T(8,128)S(1)} async-done(((f32[8,8,8,512]{3,2,0,1:T(8,128)}), f32[8,8,8,512]{3,2,0,1:T(8,128)S(1)}, u32[]{:S(2)}, u32[]{:S(2)}) %all-to-all-start) | async-done | bytes 1048608 | tf_op jit(solution)/shard_map/all_to_all | solution.py:112
  27.2 0.6 copy.31
  27.8 0.1 fusion.31
  27.9 1.7 %collective-permute-start.3 = (f32[64,1,4,512]{3,0,2,1:T(8,128)S(1)}, f32[64,1,4,512]{3,0,2,1:T(8,128)S(1)}, u32[]{:S(2)}, u32[]{:S(2)}) collective-permute-start(f32[64,1,4,512]{3,0,2,1:T(8,128)S(1)} %get-tuple-element.30), channel_id=1, source_target_pairs={{0,8},{8,16},{16,24},{24,32},{32,40},{40,48},{48,56},{56,64},{64,7... | collective-permute-start | bytes 1572872 | tf_op jit(solution)/shard_map/ppermute | solution.py:16
  29.6 1.3 %collective-permute-start.4 = (f32[64,1,4,512]{3,0,2,1:T(8,128)S(1)}, f32[64,1,4,512]{3,0,2,1:T(8,128)S(1)}, u32[]{:S(2)}, u32[]{:S(2)}) collective-permute-start(f32[64,1,4,512]{3,0,2,1:T(8,128)S(1)} %get-tuple-element.31), channel_id=1, source_target_pairs={{8,0},{16,8},{24,16},{32,24},{40,32},{48,40},{56,48},{64,56},{72,6... | collective-permute-start | bytes 1572872 | tf_op jit(solution)/shard_map/ppermute | solution.py:17
  30.9 0.0 collective-permute-done.1
  30.9 0.0 collective-permute-done.2
  30.9 0.1 maximum_convert_fusion
  31.0 0.6 copy.18
  31.6 1.0 fusion.33
  32.6 0.6 collective-permute-start
  33.2 3.4 %collective-permute-done = f32[64,64]{1,0:T(8,128)S(1)} collective-permute-done((f32[64,64]{1,0:T(8,128)S(1)}, f32[64,64]{1,0:T(8,128)S(1)}, u32[]{:S(2)}, u32[]{:S(2)}) %collective-permute-start) | collective-permute-done | bytes 16416 | tf_op jit(solution)/shard_map/ppermute | solution.py:55
  36.6 0.0 collective-permute-done.3
  36.6 0.2 pad_maximum_fusion
  36.8 1.3 %fusion.4 = f32[64,1,16,512]{3,0,2,1:T(8,128)S(1)} fusion(f32[64,1,16,512]{3,0,2,1:T(8,128)S(1)} %pad_maximum_fusion, f32[16,512]{1,0:T(8,128)S(1)} %get-tuple-element.37, f32[16,512]{1,0:T(8,128)S(1)} %get-tuple-element.38, f32[16,512]{1,0:T(8,128)S(1)} %get-tuple-element.39, f32[16,512]{1,0:T(8,128)S(1)} %get-tuple-element.40, ...), kind=kLoop, calls=%fused_computation.20 | loop fusion | flops 4718592 | bytes 4358144 | tf_op jit(solution)/shard_map/add | solution.py:33
  38.1 0.9 collective-permute-start.5
  39.0 1.3 %fusion.10 = f32[64,1,16,512]{3,0,2,1:T(8,128)S(1)} fusion(f32[64,1,16,512]{3,0,2,1:T(8,128)S(1)} %fusion.4, f32[16,512]{1,0:T(8,128)S(1)} %get-tuple-element.33, f32[16,512]{1,0:T(8,128)S(1)} %get-tuple-element.34, f32[16,512]{1,0:T(8,128)S(1)} %get-tuple-element.35, f32[16,512]{1,0:T(8,128)S(1)} %get-tuple-element.36, f32[16,512]{1,0:T(8,128)S(1)} %get-tuple-element.32), kind=kLoop, calls=%fused_computation.26 | loop fusion | flops 4718592 | bytes 4358144 | tf_op jit(solution)/shard_map/add | solution.py:33
  40.3 3.0 %collective-permute-done.5 = f32[64,64]{1,0:T(8,128)S(1)} collective-permute-done((f32[64,64]{1,0:T(8,128)S(1)}, f32[64,64]{1,0:T(8,128)S(1)}, u32[]{:S(2)}, u32[]{:S(2)}) %collective-permute-start.5) | collective-permute-done | bytes 16416 | tf_op jit(solution)/shard_map/ppermute | solution.py:55
  43.3 1.2 %broadcast_multiply_fusion = (f32[64,1,16,512]{3,0,2,1:T(8,128)S(1)}, f32[64,1,16,512]{3,0,2,1:T(8,128)S(1)}, f32[64,1,16,512]{3,0,2,1:T(8,128)S(1)}, f32[64,1,16,512]{3,0,2,1:T(8,128)S(1)}) fusion(f32[64,1,16,512]{3,0,2,1:T(8,128)S(1)} %fusion.10, f32[16,512]{1,0:T(8,128)S(1)} %get-tuple-element.33, f32[16,512]{1,0:T(8,128)S(1)} %get-tuple-element.34, ...), kind=kLoop, calls=%fused_computation.50 | loop fusion | flops 2097152 | bytes 10616832 | tf_op jit(solution)/shard_map/mul | solution.py:38
  44.5 1.0 convolution_bitcast_fusion.2
  45.5 0.6 collective-permute-start.6
  46.2 1.5 %fusion.15 = f32[64,1,16,512]{3,0,2,1:T(8,128)S(1)} fusion(f32[64,1,16,512]{3,0,2,1:T(8,128)S(1)} %get-tuple-element.29, f32[64,1,16,512]{3,0,2,1:T(8,128)S(1)} %get-tuple-element.28, f32[64,1,16,512]{3,0,2,1:T(8,128)S(1)} %get-tuple-element.27, f32[64,1,16,512]{3,0,2,1:T(8,128)S(1)} %get-tuple-element.26, f32[64,1,16,512]{3,0,2,1:T(8,128)S(1)} %fusion.10, ...), kind=kLoop, calls=%fused_computation.31 | loop fusion | flops 2621440 | bytes 12615680 | tf_op jit(solution)/shard_map/add | solution.py:38
  47.7 3.7 %collective-permute-done.6 = f32[2,64,64]{2,1,0:T(8,128)S(1)} collective-permute-done((f32[2,64,64]{2,1,0:T(8,128)S(1)}, f32[2,64,64]{2,1,0:T(8,128)S(1)}, u32[]{:S(2)}, u32[]{:S(2)}) %collective-permute-start.6) | collective-permute-done | bytes 32800 | tf_op jit(solution)/shard_map/ppermute | solution.py:55
  51.4 1.2 %broadcast_multiply_fusion.4 = (f32[64,1,16,512]{3,0,2,1:T(8,128)S(1)}, f32[64,1,16,512]{3,0,2,1:T(8,128)S(1)}, f32[64,1,16,512]{3,0,2,1:T(8,128)S(1)}, f32[64,1,16,512]{3,0,2,1:T(8,128)S(1)}) fusion(f32[64,1,16,512]{3,0,2,1:T(8,128)S(1)} %fusion.15, f32[16,512]{1,0:T(8,128)S(1)} %get-tuple-element.37, f32[16,512]{1,0:T(8,128)S(1)} %get-tuple-element.38, ...), kind=kLoop, calls=%fused_computation.54 | loop fusion | flops 2097152 | bytes 10616832 | tf_op jit(solution)/shard_map/mul | solution.py:38
  52.6 3.7 %collective-permute-start.7 = (f32[2,64,64]{2,1,0:T(8,128)S(1)}, f32[2,64,64]{2,1,0:T(8,128)S(1)}, u32[]{:S(2)}, u32[]{:S(2)}) collective-permute-start(f32[2,64,64]{2,1,0:T(8,128)S(1)} %fusion.30), channel_id=1, source_target_pairs={{0,8},{8,0},{16,24},{24,16},{32,40},{40,32},{48,56},{56,48},{64,72... | collective-permute-start | bytes 98312 | tf_op jit(solution)/shard_map/ppermute | solution.py:55
  56.4 1.4 %fusion.19 = f32[64,1,16,512]{3,0,2,1:T(8,128)S(1)} fusion(f32[64,1,16,512]{3,0,2,1:T(8,128)S(1)} %get-tuple-element.25, f32[64,1,16,512]{3,0,2,1:T(8,128)S(1)} %get-tuple-element.24, f32[64,1,16,512]{3,0,2,1:T(8,128)S(1)} %get-tuple-element.23, f32[64,1,16,512]{3,0,2,1:T(8,128)S(1)} %get-tuple-element.22, f32[64,1,16,512]{3,0,2,1:T(8,128)S(1)} %fusion.15, ...), kind=kLoop, calls=%fused_computation.35 | loop fusion | flops 2621440 | bytes 12615680 | tf_op jit(solution)/shard_map/add | solution.py:38
  57.8 0.0 collective-permute-done.7
  57.8 2.8 %collective-permute-start.8 = (f32[2,64,64]{2,1,0:T(8,128)S(1)}, f32[2,64,64]{2,1,0:T(8,128)S(1)}, u32[]{:S(2)}, u32[]{:S(2)}) collective-permute-start(f32[2,64,64]{2,1,0:T(8,128)S(1)} %add.122), channel_id=1, source_target_pairs={{0,16},{8,24},{16,0},{24,8},{32,48},{40,56},{48,32},{56,40},{64,80... | collective-permute-start | bytes 98312 | tf_op jit(solution)/shard_map/ppermute | solution.py:55
  60.7 2.7 %collective-permute-done.8 = f32[2,64,64]{2,1,0:T(8,128)S(1)} collective-permute-done((f32[2,64,64]{2,1,0:T(8,128)S(1)}, f32[2,64,64]{2,1,0:T(8,128)S(1)}, u32[]{:S(2)}, u32[]{:S(2)}) %collective-permute-start.8) | collective-permute-done | bytes 32800 | tf_op jit(solution)/shard_map/ppermute | solution.py:55
  63.3 3.9 %collective-permute-start.9 = (f32[2,64,64]{2,1,0:T(8,128)S(1)}, f32[2,64,64]{2,1,0:T(8,128)S(1)}, u32[]{:S(2)}, u32[]{:S(2)}) collective-permute-start(f32[2,64,64]{2,1,0:T(8,128)S(1)} %add.127), channel_id=1, source_target_pairs={{0,48},{8,56},{16,32},{24,40},{32,16},{40,24},{48,0},{56,8},{64,11... | collective-permute-start | bytes 98312 | tf_op jit(solution)/shard_map/ppermute | solution.py:55
  67.3 2.2 %collective-permute-done.9 = f32[2,64,64]{2,1,0:T(8,128)S(1)} collective-permute-done((f32[2,64,64]{2,1,0:T(8,128)S(1)}, f32[2,64,64]{2,1,0:T(8,128)S(1)}, u32[]{:S(2)}, u32[]{:S(2)}) %collective-permute-start.9) | collective-permute-done | bytes 32800 | tf_op jit(solution)/shard_map/ppermute | solution.py:55
  69.5 1.8 %collective-permute-start.10 = (f32[2,64,64]{2,1,0:T(8,128)S(1)}, f32[2,64,64]{2,1,0:T(8,128)S(1)}, u32[]{:S(2)}, u32[]{:S(2)}) collective-permute-start(f32[2,64,64]{2,1,0:T(8,128)S(1)} %add.128), channel_id=1, source_target_pairs={{0,64},{8,72},{16,80},{24,88},{32,96},{40,104},{48,112},{56,120},{... | collective-permute-start | bytes 98312 | tf_op jit(solution)/shard_map/ppermute | solution.py:55
  71.3 2.6 %collective-permute-done.10 = f32[2,64,64]{2,1,0:T(8,128)S(1)} collective-permute-done((f32[2,64,64]{2,1,0:T(8,128)S(1)}, f32[2,64,64]{2,1,0:T(8,128)S(1)}, u32[]{:S(2)}, u32[]{:S(2)}) %collective-permute-start.10) | collective-permute-done | bytes 32800 | tf_op jit(solution)/shard_map/ppermute | solution.py:55
  73.9 0.6 slice_bitcast_fusion
  74.5 7.6 %shard_map.41 = f32[64,64]{1,0:T(8,128)} custom-call(f32[64,64]{1,0:T(8,128)} %get-tuple-element.45.g_ref), custom_call_target="tpu_custom_call" | custom-call | tf_op jit(solution)/shard_map/pallas_call | solution.py:91
  82.1 1.1 %convolution_bitcast_fusion.1 = f32[64,64,1]{1,0,2:T(8,128)S(1)} fusion(f32[64,64]{1,0:T(8,128)} %shard_map.41), kind=kOutput, calls=%fused_computation.42 | convolution fusion | flops 3145728 | bytes 32768 | tf_op jit(solution)/shard_map/dot_general | solution.py:103
  83.2 1.0 convolution_bitcast_fusion
  84.2 1.6 %copy.15 = f32[64,1,8,512]{3,2,1,0:T(8,128)} copy(f32[64,1,8,512]{3,0,2,1:T(8,128)S(1)} %convolution_bitcast_fusion) | data formatting | bytes 2097152 | tf_op jit(solution)/shard_map/dot_general | solution.py:148
  85.8 4.2 %all-to-all-start.1 = ((f32[64,1,8,512]{3,2,1,0:T(8,128)}), f32[64,1,8,512]{3,2,1,0:T(8,128)S(1)}, u32[]{:S(2)}, u32[]{:S(2)}) async-start(f32[64,1,8,512]{3,2,1,0:T(8,128)} %copy.15), calls=%async_computation.1 | async-start | bytes 2097152 | tf_op jit(solution)/shard_map/all_to_all | solution.py:152
  90.0 3.2 %collective-permute-start.12 = (f32[64,64]{1,0:T(8,128)S(1)}, f32[64,64]{1,0:T(8,128)S(1)}, u32[]{:S(2)}, u32[]{:S(2)}) collective-permute-start(f32[64,64]{1,0:T(8,128)S(1)} %fusion.29), channel_id=1, source_target_pairs={{0,3},{1,2},{2,1},{3,0},{4,7},{5,6},{6,5},{7,4},{8,11},{9,10},{10,... | collective-permute-start | bytes 49160 | tf_op jit(solution)/shard_map/ppermute | solution.py:55
  93.2 9.8 %collective-permute-done.12 = f32[64,64]{1,0:T(8,128)S(1)} collective-permute-done((f32[64,64]{1,0:T(8,128)S(1)}, f32[64,64]{1,0:T(8,128)S(1)}, u32[]{:S(2)}, u32[]{:S(2)}) %collective-permute-start.12) | collective-permute-done | bytes 16416 | tf_op jit(solution)/shard_map/ppermute | solution.py:55
  103.0 0.6 add_multiply_fusion
  103.6 1.4 %all-to-all-done.1 = f32[64,1,8,512]{3,2,1,0:T(8,128)S(1)} async-done(((f32[64,1,8,512]{3,2,1,0:T(8,128)}), f32[64,1,8,512]{3,2,1,0:T(8,128)S(1)}, u32[]{:S(2)}, u32[]{:S(2)}) %all-to-all-start.1) | async-done | bytes 1048608 | tf_op jit(solution)/shard_map/all_to_all | solution.py:152
  105.0 1.1 %copy.30 = f32[8,8,1,8,512]{4,3,0,1,2:T(8,128)} copy(f32[8,8,1,8,512]{4,3,1,0,2:T(8,128)S(1)} %bitcast.81) | data formatting | bytes 2097152 | tf_op jit(solution)/shard_map/all_to_all | solution.py:152
  (16 shorter events, 0.1 us)
Async XLA Ops:
  0.6 9.4 %copy-start = (bf16[2,5,1,8,512]{4,3,2,1,0:T(8,128)(2,1)S(1)}, bf16[2,5,1,8,512]{4,3,2,1,0:T(8,128)(2,1)}, u32[]{:S(2)}) copy-start(bf16[2,5,1,8,512]{4,3,2,1,0:T(8,128)(2,1)} %param.3) | copy-start | bytes 245764
  3.0 24.2 %all-to-all-start = ((f32[8,8,8,512]{3,2,0,1:T(8,128)}), f32[8,8,8,512]{3,2,0,1:T(8,128)S(1)}, u32[]{:S(2)}, u32[]{:S(2)}) async-start(f32[8,8,8,512]{3,2,0,1:T(8,128)} %copy.11), calls=%async_computation | async-start | bytes 2097152 | tf_op jit(solution)/shard_map/all_to_all | solution.py:112
  10.0 20.8 %collective-permute-start.1 = (bf16[2,5,1,4,512]{4,3,2,1,0:T(4,128)(2,1)S(1)}, bf16[2,5,1,4,512]{4,3,2,1,0:T(4,128)(2,1)S(1)}, u32[]{:S(2)}, u32[]{:S(2)}) collective-permute-start(bf16[2,5,1,4,512]{4,3,2,1,0:T(4,128)(2,1)S(1)} %get-tuple-element.42), channel_id=1, source_target_pairs={{0,8},{8,16},{16,24},{24,32},{32,40},{40,48},{48,56},{56,64},{64,7... | collective-permute-start | bytes 122888 | tf_op jit(solution)/shard_map/ppermute | solution.py:16
  11.5 19.4 %collective-permute-start.2 = (bf16[2,5,1,4,512]{4,3,2,1,0:T(4,128)(2,1)S(1)}, bf16[2,5,1,4,512]{4,3,2,1,0:T(4,128)(2,1)S(1)}, u32[]{:S(2)}, u32[]{:S(2)}) collective-permute-start(bf16[2,5,1,4,512]{4,3,2,1,0:T(4,128)(2,1)S(1)} %get-tuple-element.43), channel_id=1, source_target_pairs={{8,0},{16,8},{24,16},{32,24},{40,32},{48,40},{56,48},{64,56},{72,6... | collective-permute-start | bytes 122888 | tf_op jit(solution)/shard_map/ppermute | solution.py:17
  27.9 8.7 %collective-permute-start.3 = (f32[64,1,4,512]{3,0,2,1:T(8,128)S(1)}, f32[64,1,4,512]{3,0,2,1:T(8,128)S(1)}, u32[]{:S(2)}, u32[]{:S(2)}) collective-permute-start(f32[64,1,4,512]{3,0,2,1:T(8,128)S(1)} %get-tuple-element.30), channel_id=1, source_target_pairs={{0,8},{8,16},{16,24},{24,32},{32,40},{40,48},{48,56},{56,64},{64,7... | collective-permute-start | bytes 1572872 | tf_op jit(solution)/shard_map/ppermute | solution.py:16
  29.6 7.0 %collective-permute-start.4 = (f32[64,1,4,512]{3,0,2,1:T(8,128)S(1)}, f32[64,1,4,512]{3,0,2,1:T(8,128)S(1)}, u32[]{:S(2)}, u32[]{:S(2)}) collective-permute-start(f32[64,1,4,512]{3,0,2,1:T(8,128)S(1)} %get-tuple-element.31), channel_id=1, source_target_pairs={{8,0},{16,8},{24,16},{32,24},{40,32},{48,40},{56,48},{64,56},{72,6... | collective-permute-start | bytes 1572872 | tf_op jit(solution)/shard_map/ppermute | solution.py:17
  32.6 4.0 %collective-permute-start = (f32[64,64]{1,0:T(8,128)S(1)}, f32[64,64]{1,0:T(8,128)S(1)}, u32[]{:S(2)}, u32[]{:S(2)}) collective-permute-start(f32[64,64]{1,0:T(8,128)S(1)} %fusion.33), channel_id=1, source_target_pairs={{0,1},{1,0},{2,3},{3,2},{4,5},{5,4},{6,7},{7,6},{8,9},{9,8},{10,11... | collective-permute-start | bytes 49160 | tf_op jit(solution)/shard_map/ppermute | solution.py:55
  38.1 5.2 %collective-permute-start.5 = (f32[64,64]{1,0:T(8,128)S(1)}, f32[64,64]{1,0:T(8,128)S(1)}, u32[]{:S(2)}, u32[]{:S(2)}) collective-permute-start(f32[64,64]{1,0:T(8,128)S(1)} %add.107), channel_id=1, source_target_pairs={{0,3},{1,2},{2,1},{3,0},{4,7},{5,6},{6,5},{7,4},{8,11},{9,10},{10,... | collective-permute-start | bytes 49160 | tf_op jit(solution)/shard_map/ppermute | solution.py:55
  45.5 5.8 %collective-permute-start.6 = (f32[2,64,64]{2,1,0:T(8,128)S(1)}, f32[2,64,64]{2,1,0:T(8,128)S(1)}, u32[]{:S(2)}, u32[]{:S(2)}) collective-permute-start(f32[2,64,64]{2,1,0:T(8,128)S(1)} %pad_maximum_fusion.1), channel_id=1, source_target_pairs={{0,4},{1,5},{2,6},{3,7},{4,0},{5,1},{6,2},{7,3},{8,12},{9,13},{10,... | collective-permute-start | bytes 98312 | tf_op jit(solution)/shard_map/ppermute | solution.py:55
  52.6 5.2 %collective-permute-start.7 = (f32[2,64,64]{2,1,0:T(8,128)S(1)}, f32[2,64,64]{2,1,0:T(8,128)S(1)}, u32[]{:S(2)}, u32[]{:S(2)}) collective-permute-start(f32[2,64,64]{2,1,0:T(8,128)S(1)} %fusion.30), channel_id=1, source_target_pairs={{0,8},{8,0},{16,24},{24,16},{32,40},{40,32},{48,56},{56,48},{64,72... | collective-permute-start | bytes 98312 | tf_op jit(solution)/shard_map/ppermute | solution.py:55
  57.8 5.5 %collective-permute-start.8 = (f32[2,64,64]{2,1,0:T(8,128)S(1)}, f32[2,64,64]{2,1,0:T(8,128)S(1)}, u32[]{:S(2)}, u32[]{:S(2)}) collective-permute-start(f32[2,64,64]{2,1,0:T(8,128)S(1)} %add.122), channel_id=1, source_target_pairs={{0,16},{8,24},{16,0},{24,8},{32,48},{40,56},{48,32},{56,40},{64,80... | collective-permute-start | bytes 98312 | tf_op jit(solution)/shard_map/ppermute | solution.py:55
  63.3 6.2 %collective-permute-start.9 = (f32[2,64,64]{2,1,0:T(8,128)S(1)}, f32[2,64,64]{2,1,0:T(8,128)S(1)}, u32[]{:S(2)}, u32[]{:S(2)}) collective-permute-start(f32[2,64,64]{2,1,0:T(8,128)S(1)} %add.127), channel_id=1, source_target_pairs={{0,48},{8,56},{16,32},{24,40},{32,16},{40,24},{48,0},{56,8},{64,11... | collective-permute-start | bytes 98312 | tf_op jit(solution)/shard_map/ppermute | solution.py:55
  69.5 4.3 %collective-permute-start.10 = (f32[2,64,64]{2,1,0:T(8,128)S(1)}, f32[2,64,64]{2,1,0:T(8,128)S(1)}, u32[]{:S(2)}, u32[]{:S(2)}) collective-permute-start(f32[2,64,64]{2,1,0:T(8,128)S(1)} %add.128), channel_id=1, source_target_pairs={{0,64},{8,72},{16,80},{24,88},{32,96},{40,104},{48,112},{56,120},{... | collective-permute-start | bytes 98312 | tf_op jit(solution)/shard_map/ppermute | solution.py:55
  74.5 7.6 %collective-permute-start.11 = (f32[64,64]{1,0:T(8,128)S(1)}, f32[64,64]{1,0:T(8,128)S(1)}, u32[]{:S(2)}, u32[]{:S(2)}) collective-permute-start(f32[64,64]{1,0:T(8,128)S(1)} %get-tuple-element.44), channel_id=1, source_target_pairs={{0,1},{1,0},{2,3},{3,2},{4,5},{5,4},{6,7},{7,6},{8,9},{9,8},{10,11... | collective-permute-start | bytes 49160 | tf_op jit(solution)/shard_map/ppermute | solution.py:55
  85.8 19.2 %all-to-all-start.1 = ((f32[64,1,8,512]{3,2,1,0:T(8,128)}), f32[64,1,8,512]{3,2,1,0:T(8,128)S(1)}, u32[]{:S(2)}, u32[]{:S(2)}) async-start(f32[64,1,8,512]{3,2,1,0:T(8,128)} %copy.15), calls=%async_computation.1 | async-start | bytes 2097152 | tf_op jit(solution)/shard_map/all_to_all | solution.py:152
  90.0 13.0 %collective-permute-start.12 = (f32[64,64]{1,0:T(8,128)S(1)}, f32[64,64]{1,0:T(8,128)S(1)}, u32[]{:S(2)}, u32[]{:S(2)}) collective-permute-start(f32[64,64]{1,0:T(8,128)S(1)} %fusion.29), channel_id=1, source_target_pairs={{0,3},{1,2},{2,1},{3,0},{4,7},{5,6},{6,5},{7,4},{8,11},{9,10},{10,... | collective-permute-start | bytes 49160 | tf_op jit(solution)/shard_map/ppermute | solution.py:55

commit v22 on v21

--- a/solution.py
+++ b/solution.py
@@ -73,13 +73,13 @@
             row = a_ref[k : k + 1, :]
             pivot = jnp.sum(jnp.where(lane == k, row, 0.0), axis=1, keepdims=True)
             scale = lax.rsqrt(pivot)
+            inv_pivot = scale * scale
             col = jnp.sum(jnp.where(cols_lo == k, a, 0.0), axis=1, keepdims=True)
-            below = jnp.where(sub > k, col * scale, 0.0)
-            right = jnp.where(lane > k, row * scale, 0.0)
-            a_ref[lo:, :] = a - below * right
-            xrow = x_ref[k : k + 1, :] * scale
-            x_ref[k : k + 1, :] = xrow
-            x_ref[lo:, :] = x_ref[lo:, :] - below * xrow
+            below = jnp.where(sub > k, col, 0.0)
+            a_ref[lo:, :] = a - (col * row) * inv_pivot
+            xrow = x_ref[k : k + 1, :]
+            x_ref[lo:, :] = x_ref[lo:, :] - (below * xrow) * inv_pivot
+            x_ref[k : k + 1, :] = xrow * scale
             return carry
 
         for k in range(lo, min(lo + phase, n)):

time: 107 us -> 106 us (level)
  no operation moved by 1% of the time
where the time goes in v22:
time: 106 us
  waiting for transfers between devices  43.1 us (41%)
  starting transfers between devices  34.6 us (33%)
  other arithmetic  9.57 us (9%)
  Pallas kernels  7.53 us (7%)
  local copies, waits for them, and re-layouts  6.31 us (6%)
  matrix products  4.02 us (4%)
    ppermute x9, waiting for transfers between devices, exchange(): return x + lax.ppermute(x, axis, [(i, i ^ bit) for i in range(count)])  27.3 us
    ppermute x9, starting transfers between devices, exchange(): return x + lax.ppermute(x, axis, [(i, i ^ bit) for i in range(count)])  17.7 us
    all_to_all x1, waiting for transfers between devices, body(): v = lax.all_to_all(perturbations, 'mem', 1, 0, tiled=True)  14.4 us
    pallas_call x1, Pallas kernels, lower_inverse(): pl.pallas_call(chol_inv_kernel, out_shape=jax.ShapeDtypeStruct((n, n), jn...  7.53 us
    all_to_all x1, starting transfers between devices, body(): v = lax.all_to_all(perturbations, 'mem', 1, 0, tiled=True)  7.04 us
    all_to_all x1, starting transfers between devices, body(): ritz = lax.all_to_all(ritz.reshape(v.shape), 'mem', 0, 1, tiled=True)  4.18 us
    ppermute x2, starting transfers between devices, halo(): lax.ppermute(lax.slice_in_dim(block, size - width, size, axis=dim), 'dom'...  3.12 us
    add x2, other arithmetic, adjoint_step(): result + shifted(coef[3] * field, 1, 3) + shifted(coef[4] * field, -1, 3)  2.94 us
  transfers between devices with their start and end apart: 15, of which 9 were waited for; matrix products, arithmetic and copies ran while one was open for 7% of the time, Pallas kernels for 7%

profile of v22, /device:TPU:0, one launch (start us, length us, event | category | flops | bytes accessed | tf_op | source)
XLA Modules:
  0.0 106.0 jit_solution(14531971470096396193)
XLA Ops:
  0.6 2.3 %copy.11 = f32[8,8,8,512]{3,2,0,1:T(8,128)} copy(f32[8,8,8,512]{3,2,1,0:T(8,128)} %param.2) | data formatting | bytes 2097152 | tf_op args[0]
  3.0 7.0 %all-to-all-start = ((f32[8,8,8,512]{3,2,0,1:T(8,128)}), f32[8,8,8,512]{3,2,0,1:T(8,128)S(1)}, u32[]{:S(2)}, u32[]{:S(2)}) async-start(f32[8,8,8,512]{3,2,0,1:T(8,128)} %copy.11), calls=%async_computation | async-start | bytes 2097152 | tf_op jit(solution)/shard_map/all_to_all | solution.py:112
  10.0 1.5 %collective-permute-start.1 = (bf16[2,5,1,4,512]{4,3,2,1,0:T(4,128)(2,1)S(1)}, bf16[2,5,1,4,512]{4,3,2,1,0:T(4,128)(2,1)S(1)}, u32[]{:S(2)}, u32[]{:S(2)}) collective-permute-start(bf16[2,5,1,4,512]{4,3,2,1,0:T(4,128)(2,1)S(1)} %get-tuple-element.42), channel_id=1, source_target_pairs={{0,8},{8,16},{16,24},{24,32},{32,40},{40,48},{48,56},{56,64},{64,7... | collective-permute-start | bytes 122888 | tf_op jit(solution)/shard_map/ppermute | solution.py:16
  11.5 1.3 %collective-permute-start.2 = (bf16[2,5,1,4,512]{4,3,2,1,0:T(4,128)(2,1)S(1)}, bf16[2,5,1,4,512]{4,3,2,1,0:T(4,128)(2,1)S(1)}, u32[]{:S(2)}, u32[]{:S(2)}) collective-permute-start(bf16[2,5,1,4,512]{4,3,2,1,0:T(4,128)(2,1)S(1)} %get-tuple-element.43), channel_id=1, source_target_pairs={{8,0},{16,8},{24,16},{32,24},{40,32},{48,40},{56,48},{64,56},{72,6... | collective-permute-start | bytes 122888 | tf_op jit(solution)/shard_map/ppermute | solution.py:17
  12.8 14.4 %all-to-all-done = f32[8,8,8,512]{3,2,0,1:T(8,128)S(1)} async-done(((f32[8,8,8,512]{3,2,0,1:T(8,128)}), f32[8,8,8,512]{3,2,0,1:T(8,128)S(1)}, u32[]{:S(2)}, u32[]{:S(2)}) %all-to-all-start) | async-done | bytes 1048608 | tf_op jit(solution)/shard_map/all_to_all | solution.py:112
  27.2 0.6 copy.31
  27.8 0.1 fusion.31
  27.9 1.7 %collective-permute-start.3 = (f32[64,1,4,512]{3,0,2,1:T(8,128)S(1)}, f32[64,1,4,512]{3,0,2,1:T(8,128)S(1)}, u32[]{:S(2)}, u32[]{:S(2)}) collective-permute-start(f32[64,1,4,512]{3,0,2,1:T(8,128)S(1)} %get-tuple-element.30), channel_id=1, source_target_pairs={{0,8},{8,16},{16,24},{24,32},{32,40},{40,48},{48,56},{56,64},{64,7... | collective-permute-start | bytes 1572872 | tf_op jit(solution)/shard_map/ppermute | solution.py:16
  29.6 1.3 %collective-permute-start.4 = (f32[64,1,4,512]{3,0,2,1:T(8,128)S(1)}, f32[64,1,4,512]{3,0,2,1:T(8,128)S(1)}, u32[]{:S(2)}, u32[]{:S(2)}) collective-permute-start(f32[64,1,4,512]{3,0,2,1:T(8,128)S(1)} %get-tuple-element.31), channel_id=1, source_target_pairs={{8,0},{16,8},{24,16},{32,24},{40,32},{48,40},{56,48},{64,56},{72,6... | collective-permute-start | bytes 1572872 | tf_op jit(solution)/shard_map/ppermute | solution.py:17
  30.9 0.0 collective-permute-done.1
  30.9 0.1 maximum_convert_fusion
  31.0 0.6 copy.18
  31.6 1.0 fusion.33
  32.6 0.6 collective-permute-start
  33.2 3.4 %collective-permute-done = f32[64,64]{1,0:T(8,128)S(1)} collective-permute-done((f32[64,64]{1,0:T(8,128)S(1)}, f32[64,64]{1,0:T(8,128)S(1)}, u32[]{:S(2)}, u32[]{:S(2)}) %collective-permute-start) | collective-permute-done | bytes 16416 | tf_op jit(solution)/shard_map/ppermute | solution.py:55
  36.6 0.0 collective-permute-done.3
  36.6 0.2 pad_maximum_fusion
  36.8 1.3 %fusion.4 = f32[64,1,16,512]{3,0,2,1:T(8,128)S(1)} fusion(f32[64,1,16,512]{3,0,2,1:T(8,128)S(1)} %pad_maximum_fusion, f32[16,512]{1,0:T(8,128)S(1)} %get-tuple-element.37, f32[16,512]{1,0:T(8,128)S(1)} %get-tuple-element.38, f32[16,512]{1,0:T(8,128)S(1)} %get-tuple-element.39, f32[16,512]{1,0:T(8,128)S(1)} %get-tuple-element.40, ...), kind=kLoop, calls=%fused_computation.20 | loop fusion | flops 4718592 | bytes 4358144 | tf_op jit(solution)/shard_map/add | solution.py:33
  38.1 0.9 collective-permute-start.5
  39.0 1.3 %fusion.10 = f32[64,1,16,512]{3,0,2,1:T(8,128)S(1)} fusion(f32[64,1,16,512]{3,0,2,1:T(8,128)S(1)} %fusion.4, f32[16,512]{1,0:T(8,128)S(1)} %get-tuple-element.33, f32[16,512]{1,0:T(8,128)S(1)} %get-tuple-element.34, f32[16,512]{1,0:T(8,128)S(1)} %get-tuple-element.35, f32[16,512]{1,0:T(8,128)S(1)} %get-tuple-element.36, f32[16,512]{1,0:T(8,128)S(1)} %get-tuple-element.32), kind=kLoop, calls=%fused_computation.26 | loop fusion | flops 4718592 | bytes 4358144 | tf_op jit(solution)/shard_map/add | solution.py:33
  40.3 3.0 %collective-permute-done.5 = f32[64,64]{1,0:T(8,128)S(1)} collective-permute-done((f32[64,64]{1,0:T(8,128)S(1)}, f32[64,64]{1,0:T(8,128)S(1)}, u32[]{:S(2)}, u32[]{:S(2)}) %collective-permute-start.5) | collective-permute-done | bytes 16416 | tf_op jit(solution)/shard_map/ppermute | solution.py:55
  43.3 1.2 %broadcast_multiply_fusion = (f32[64,1,16,512]{3,0,2,1:T(8,128)S(1)}, f32[64,1,16,512]{3,0,2,1:T(8,128)S(1)}, f32[64,1,16,512]{3,0,2,1:T(8,128)S(1)}, f32[64,1,16,512]{3,0,2,1:T(8,128)S(1)}) fusion(f32[64,1,16,512]{3,0,2,1:T(8,128)S(1)} %fusion.10, f32[16,512]{1,0:T(8,128)S(1)} %get-tuple-element.33, f32[16,512]{1,0:T(8,128)S(1)} %get-tuple-element.34, ...), kind=kLoop, calls=%fused_computation.50 | loop fusion | flops 2097152 | bytes 10616832 | tf_op jit(solution)/shard_map/mul | solution.py:38
  44.5 1.0 convolution_bitcast_fusion.2
  45.5 0.6 collective-permute-start.6
  46.2 1.5 %fusion.15 = f32[64,1,16,512]{3,0,2,1:T(8,128)S(1)} fusion(f32[64,1,16,512]{3,0,2,1:T(8,128)S(1)} %get-tuple-element.29, f32[64,1,16,512]{3,0,2,1:T(8,128)S(1)} %get-tuple-element.28, f32[64,1,16,512]{3,0,2,1:T(8,128)S(1)} %get-tuple-element.27, f32[64,1,16,512]{3,0,2,1:T(8,128)S(1)} %get-tuple-element.26, f32[64,1,16,512]{3,0,2,1:T(8,128)S(1)} %fusion.10, ...), kind=kLoop, calls=%fused_computation.31 | loop fusion | flops 2621440 | bytes 12615680 | tf_op jit(solution)/shard_map/add | solution.py:38
  47.7 3.7 %collective-permute-done.6 = f32[2,64,64]{2,1,0:T(8,128)S(1)} collective-permute-done((f32[2,64,64]{2,1,0:T(8,128)S(1)}, f32[2,64,64]{2,1,0:T(8,128)S(1)}, u32[]{:S(2)}, u32[]{:S(2)}) %collective-permute-start.6) | collective-permute-done | bytes 32800 | tf_op jit(solution)/shard_map/ppermute | solution.py:55
  51.4 1.2 %broadcast_multiply_fusion.4 = (f32[64,1,16,512]{3,0,2,1:T(8,128)S(1)}, f32[64,1,16,512]{3,0,2,1:T(8,128)S(1)}, f32[64,1,16,512]{3,0,2,1:T(8,128)S(1)}, f32[64,1,16,512]{3,0,2,1:T(8,128)S(1)}) fusion(f32[64,1,16,512]{3,0,2,1:T(8,128)S(1)} %fusion.15, f32[16,512]{1,0:T(8,128)S(1)} %get-tuple-element.37, f32[16,512]{1,0:T(8,128)S(1)} %get-tuple-element.38, ...), kind=kLoop, calls=%fused_computation.54 | loop fusion | flops 2097152 | bytes 10616832 | tf_op jit(solution)/shard_map/mul | solution.py:38
  52.6 3.7 %collective-permute-start.7 = (f32[2,64,64]{2,1,0:T(8,128)S(1)}, f32[2,64,64]{2,1,0:T(8,128)S(1)}, u32[]{:S(2)}, u32[]{:S(2)}) collective-permute-start(f32[2,64,64]{2,1,0:T(8,128)S(1)} %fusion.30), channel_id=1, source_target_pairs={{0,8},{8,0},{16,24},{24,16},{32,40},{40,32},{48,56},{56,48},{64,72... | collective-permute-start | bytes 98312 | tf_op jit(solution)/shard_map/ppermute | solution.py:55
  56.4 1.4 %fusion.19 = f32[64,1,16,512]{3,0,2,1:T(8,128)S(1)} fusion(f32[64,1,16,512]{3,0,2,1:T(8,128)S(1)} %get-tuple-element.25, f32[64,1,16,512]{3,0,2,1:T(8,128)S(1)} %get-tuple-element.24, f32[64,1,16,512]{3,0,2,1:T(8,128)S(1)} %get-tuple-element.23, f32[64,1,16,512]{3,0,2,1:T(8,128)S(1)} %get-tuple-element.22, f32[64,1,16,512]{3,0,2,1:T(8,128)S(1)} %fusion.15, ...), kind=kLoop, calls=%fused_computation.35 | loop fusion | flops 2621440 | bytes 12615680 | tf_op jit(solution)/shard_map/add | solution.py:38
  57.8 0.0 collective-permute-done.7
  57.8 2.8 %collective-permute-start.8 = (f32[2,64,64]{2,1,0:T(8,128)S(1)}, f32[2,64,64]{2,1,0:T(8,128)S(1)}, u32[]{:S(2)}, u32[]{:S(2)}) collective-permute-start(f32[2,64,64]{2,1,0:T(8,128)S(1)} %add.122), channel_id=1, source_target_pairs={{0,16},{8,24},{16,0},{24,8},{32,48},{40,56},{48,32},{56,40},{64,80... | collective-permute-start | bytes 98312 | tf_op jit(solution)/shard_map/ppermute | solution.py:55
  60.7 2.7 %collective-permute-done.8 = f32[2,64,64]{2,1,0:T(8,128)S(1)} collective-permute-done((f32[2,64,64]{2,1,0:T(8,128)S(1)}, f32[2,64,64]{2,1,0:T(8,128)S(1)}, u32[]{:S(2)}, u32[]{:S(2)}) %collective-permute-start.8) | collective-permute-done | bytes 32800 | tf_op jit(solution)/shard_map/ppermute | solution.py:55
  63.3 3.9 %collective-permute-start.9 = (f32[2,64,64]{2,1,0:T(8,128)S(1)}, f32[2,64,64]{2,1,0:T(8,128)S(1)}, u32[]{:S(2)}, u32[]{:S(2)}) collective-permute-start(f32[2,64,64]{2,1,0:T(8,128)S(1)} %add.127), channel_id=1, source_target_pairs={{0,48},{8,56},{16,32},{24,40},{32,16},{40,24},{48,0},{56,8},{64,11... | collective-permute-start | bytes 98312 | tf_op jit(solution)/shard_map/ppermute | solution.py:55
  67.3 2.2 %collective-permute-done.9 = f32[2,64,64]{2,1,0:T(8,128)S(1)} collective-permute-done((f32[2,64,64]{2,1,0:T(8,128)S(1)}, f32[2,64,64]{2,1,0:T(8,128)S(1)}, u32[]{:S(2)}, u32[]{:S(2)}) %collective-permute-start.9) | collective-permute-done | bytes 32800 | tf_op jit(solution)/shard_map/ppermute | solution.py:55
  69.5 1.8 %collective-permute-start.10 = (f32[2,64,64]{2,1,0:T(8,128)S(1)}, f32[2,64,64]{2,1,0:T(8,128)S(1)}, u32[]{:S(2)}, u32[]{:S(2)}) collective-permute-start(f32[2,64,64]{2,1,0:T(8,128)S(1)} %add.128), channel_id=1, source_target_pairs={{0,64},{8,72},{16,80},{24,88},{32,96},{40,104},{48,112},{56,120},{... | collective-permute-start | bytes 98312 | tf_op jit(solution)/shard_map/ppermute | solution.py:55
  71.3 2.6 %collective-permute-done.10 = f32[2,64,64]{2,1,0:T(8,128)S(1)} collective-permute-done((f32[2,64,64]{2,1,0:T(8,128)S(1)}, f32[2,64,64]{2,1,0:T(8,128)S(1)}, u32[]{:S(2)}, u32[]{:S(2)}) %collective-permute-start.10) | collective-permute-done | bytes 32800 | tf_op jit(solution)/shard_map/ppermute | solution.py:55
  73.9 0.6 slice_bitcast_fusion
  74.5 0.0 collective-permute-start.11
  74.5 7.5 %shard_map.41 = f32[64,64]{1,0:T(8,128)} custom-call(f32[64,64]{1,0:T(8,128)} %get-tuple-element.45.g_ref), custom_call_target="tpu_custom_call" | custom-call | tf_op jit(solution)/shard_map/pallas_call | solution.py:91
  82.0 1.1 %convolution_bitcast_fusion.1 = f32[64,64,1]{1,0,2:T(8,128)S(1)} fusion(f32[64,64]{1,0:T(8,128)} %shard_map.41), kind=kOutput, calls=%fused_computation.42 | convolution fusion | flops 3145728 | bytes 32768 | tf_op jit(solution)/shard_map/dot_general | solution.py:103
  83.1 1.0 convolution_bitcast_fusion
  84.1 1.6 %copy.15 = f32[64,1,8,512]{3,2,1,0:T(8,128)} copy(f32[64,1,8,512]{3,0,2,1:T(8,128)S(1)} %convolution_bitcast_fusion) | data formatting | bytes 2097152 | tf_op jit(solution)/shard_map/dot_general | solution.py:148
  85.7 4.2 %all-to-all-start.1 = ((f32[64,1,8,512]{3,2,1,0:T(8,128)}), f32[64,1,8,512]{3,2,1,0:T(8,128)S(1)}, u32[]{:S(2)}, u32[]{:S(2)}) async-start(f32[64,1,8,512]{3,2,1,0:T(8,128)} %copy.15), calls=%async_computation.1 | async-start | bytes 2097152 | tf_op jit(solution)/shard_map/all_to_all | solution.py:152
  89.9 3.2 %collective-permute-start.12 = (f32[64,64]{1,0:T(8,128)S(1)}, f32[64,64]{1,0:T(8,128)S(1)}, u32[]{:S(2)}, u32[]{:S(2)}) collective-permute-start(f32[64,64]{1,0:T(8,128)S(1)} %fusion.29), channel_id=1, source_target_pairs={{0,3},{1,2},{2,1},{3,0},{4,7},{5,6},{6,5},{7,4},{8,11},{9,10},{10,... | collective-permute-start | bytes 49160 | tf_op jit(solution)/shard_map/ppermute | solution.py:55
  93.1 9.8 %collective-permute-done.12 = f32[64,64]{1,0:T(8,128)S(1)} collective-permute-done((f32[64,64]{1,0:T(8,128)S(1)}, f32[64,64]{1,0:T(8,128)S(1)}, u32[]{:S(2)}, u32[]{:S(2)}) %collective-permute-start.12) | collective-permute-done | bytes 16416 | tf_op jit(solution)/shard_map/ppermute | solution.py:55
  102.9 0.6 add_multiply_fusion
  103.5 1.4 %all-to-all-done.1 = f32[64,1,8,512]{3,2,1,0:T(8,128)S(1)} async-done(((f32[64,1,8,512]{3,2,1,0:T(8,128)}), f32[64,1,8,512]{3,2,1,0:T(8,128)S(1)}, u32[]{:S(2)}, u32[]{:S(2)}) %all-to-all-start.1) | async-done | bytes 1048608 | tf_op jit(solution)/shard_map/all_to_all | solution.py:152
  104.9 1.1 %copy.30 = f32[8,8,1,8,512]{4,3,0,1,2:T(8,128)} copy(f32[8,8,1,8,512]{4,3,1,0,2:T(8,128)S(1)} %bitcast.81) | data formatting | bytes 2097152 | tf_op jit(solution)/shard_map/all_to_all | solution.py:152
  (16 shorter events, 0.1 us)
Async XLA Ops:
  0.6 9.4 %copy-start = (bf16[2,5,1,8,512]{4,3,2,1,0:T(8,128)(2,1)S(1)}, bf16[2,5,1,8,512]{4,3,2,1,0:T(8,128)(2,1)}, u32[]{:S(2)}) copy-start(bf16[2,5,1,8,512]{4,3,2,1,0:T(8,128)(2,1)} %param.3) | copy-start | bytes 245764
  3.0 24.2 %all-to-all-start = ((f32[8,8,8,512]{3,2,0,1:T(8,128)}), f32[8,8,8,512]{3,2,0,1:T(8,128)S(1)}, u32[]{:S(2)}, u32[]{:S(2)}) async-start(f32[8,8,8,512]{3,2,0,1:T(8,128)} %copy.11), calls=%async_computation | async-start | bytes 2097152 | tf_op jit(solution)/shard_map/all_to_all | solution.py:112
  10.0 20.8 %collective-permute-start.1 = (bf16[2,5,1,4,512]{4,3,2,1,0:T(4,128)(2,1)S(1)}, bf16[2,5,1,4,512]{4,3,2,1,0:T(4,128)(2,1)S(1)}, u32[]{:S(2)}, u32[]{:S(2)}) collective-permute-start(bf16[2,5,1,4,512]{4,3,2,1,0:T(4,128)(2,1)S(1)} %get-tuple-element.42), channel_id=1, source_target_pairs={{0,8},{8,16},{16,24},{24,32},{32,40},{40,48},{48,56},{56,64},{64,7... | collective-permute-start | bytes 122888 | tf_op jit(solution)/shard_map/ppermute | solution.py:16
  11.5 19.4 %collective-permute-start.2 = (bf16[2,5,1,4,512]{4,3,2,1,0:T(4,128)(2,1)S(1)}, bf16[2,5,1,4,512]{4,3,2,1,0:T(4,128)(2,1)S(1)}, u32[]{:S(2)}, u32[]{:S(2)}) collective-permute-start(bf16[2,5,1,4,512]{4,3,2,1,0:T(4,128)(2,1)S(1)} %get-tuple-element.43), channel_id=1, source_target_pairs={{8,0},{16,8},{24,16},{32,24},{40,32},{48,40},{56,48},{64,56},{72,6... | collective-permute-start | bytes 122888 | tf_op jit(solution)/shard_map/ppermute | solution.py:17
  27.9 8.7 %collective-permute-start.3 = (f32[64,1,4,512]{3,0,2,1:T(8,128)S(1)}, f32[64,1,4,512]{3,0,2,1:T(8,128)S(1)}, u32[]{:S(2)}, u32[]{:S(2)}) collective-permute-start(f32[64,1,4,512]{3,0,2,1:T(8,128)S(1)} %get-tuple-element.30), channel_id=1, source_target_pairs={{0,8},{8,16},{16,24},{24,32},{32,40},{40,48},{48,56},{56,64},{64,7... | collective-permute-start | bytes 1572872 | tf_op jit(solution)/shard_map/ppermute | solution.py:16
  29.6 7.0 %collective-permute-start.4 = (f32[64,1,4,512]{3,0,2,1:T(8,128)S(1)}, f32[64,1,4,512]{3,0,2,1:T(8,128)S(1)}, u32[]{:S(2)}, u32[]{:S(2)}) collective-permute-start(f32[64,1,4,512]{3,0,2,1:T(8,128)S(1)} %get-tuple-element.31), channel_id=1, source_target_pairs={{8,0},{16,8},{24,16},{32,24},{40,32},{48,40},{56,48},{64,56},{72,6... | collective-permute-start | bytes 1572872 | tf_op jit(solution)/shard_map/ppermute | solution.py:17
  32.6 4.0 %collective-permute-start = (f32[64,64]{1,0:T(8,128)S(1)}, f32[64,64]{1,0:T(8,128)S(1)}, u32[]{:S(2)}, u32[]{:S(2)}) collective-permute-start(f32[64,64]{1,0:T(8,128)S(1)} %fusion.33), channel_id=1, source_target_pairs={{0,1},{1,0},{2,3},{3,2},{4,5},{5,4},{6,7},{7,6},{8,9},{9,8},{10,11... | collective-permute-start | bytes 49160 | tf_op jit(solution)/shard_map/ppermute | solution.py:55
  38.1 5.2 %collective-permute-start.5 = (f32[64,64]{1,0:T(8,128)S(1)}, f32[64,64]{1,0:T(8,128)S(1)}, u32[]{:S(2)}, u32[]{:S(2)}) collective-permute-start(f32[64,64]{1,0:T(8,128)S(1)} %add.107), channel_id=1, source_target_pairs={{0,3},{1,2},{2,1},{3,0},{4,7},{5,6},{6,5},{7,4},{8,11},{9,10},{10,... | collective-permute-start | bytes 49160 | tf_op jit(solution)/shard_map/ppermute | solution.py:55
  45.5 5.8 %collective-permute-start.6 = (f32[2,64,64]{2,1,0:T(8,128)S(1)}, f32[2,64,64]{2,1,0:T(8,128)S(1)}, u32[]{:S(2)}, u32[]{:S(2)}) collective-permute-start(f32[2,64,64]{2,1,0:T(8,128)S(1)} %pad_maximum_fusion.1), channel_id=1, source_target_pairs={{0,4},{1,5},{2,6},{3,7},{4,0},{5,1},{6,2},{7,3},{8,12},{9,13},{10,... | collective-permute-start | bytes 98312 | tf_op jit(solution)/shard_map/ppermute | solution.py:55
  52.6 5.2 %collective-permute-start.7 = (f32[2,64,64]{2,1,0:T(8,128)S(1)}, f32[2,64,64]{2,1,0:T(8,128)S(1)}, u32[]{:S(2)}, u32[]{:S(2)}) collective-permute-start(f32[2,64,64]{2,1,0:T(8,128)S(1)} %fusion.30), channel_id=1, source_target_pairs={{0,8},{8,0},{16,24},{24,16},{32,40},{40,32},{48,56},{56,48},{64,72... | collective-permute-start | bytes 98312 | tf_op jit(solution)/shard_map/ppermute | solution.py:55
  57.8 5.5 %collective-permute-start.8 = (f32[2,64,64]{2,1,0:T(8,128)S(1)}, f32[2,64,64]{2,1,0:T(8,128)S(1)}, u32[]{:S(2)}, u32[]{:S(2)}) collective-permute-start(f32[2,64,64]{2,1,0:T(8,128)S(1)} %add.122), channel_id=1, source_target_pairs={{0,16},{8,24},{16,0},{24,8},{32,48},{40,56},{48,32},{56,40},{64,80... | collective-permute-start | bytes 98312 | tf_op jit(solution)/shard_map/ppermute | solution.py:55
  63.3 6.2 %collective-permute-start.9 = (f32[2,64,64]{2,1,0:T(8,128)S(1)}, f32[2,64,64]{2,1,0:T(8,128)S(1)}, u32[]{:S(2)}, u32[]{:S(2)}) collective-permute-start(f32[2,64,64]{2,1,0:T(8,128)S(1)} %add.127), channel_id=1, source_target_pairs={{0,48},{8,56},{16,32},{24,40},{32,16},{40,24},{48,0},{56,8},{64,11... | collective-permute-start | bytes 98312 | tf_op jit(solution)/shard_map/ppermute | solution.py:55
  69.5 4.3 %collective-permute-start.10 = (f32[2,64,64]{2,1,0:T(8,128)S(1)}, f32[2,64,64]{2,1,0:T(8,128)S(1)}, u32[]{:S(2)}, u32[]{:S(2)}) collective-permute-start(f32[2,64,64]{2,1,0:T(8,128)S(1)} %add.128), channel_id=1, source_target_pairs={{0,64},{8,72},{16,80},{24,88},{32,96},{40,104},{48,112},{56,120},{... | collective-permute-start | bytes 98312 | tf_op jit(solution)/shard_map/ppermute | solution.py:55
  74.5 7.5 %collective-permute-start.11 = (f32[64,64]{1,0:T(8,128)S(1)}, f32[64,64]{1,0:T(8,128)S(1)}, u32[]{:S(2)}, u32[]{:S(2)}) collective-permute-start(f32[64,64]{1,0:T(8,128)S(1)} %get-tuple-element.44), channel_id=1, source_target_pairs={{0,1},{1,0},{2,3},{3,2},{4,5},{5,4},{6,7},{7,6},{8,9},{9,8},{10,11... | collective-permute-start | bytes 49160 | tf_op jit(solution)/shard_map/ppermute | solution.py:55
  85.7 19.2 %all-to-all-start.1 = ((f32[64,1,8,512]{3,2,1,0:T(8,128)}), f32[64,1,8,512]{3,2,1,0:T(8,128)S(1)}, u32[]{:S(2)}, u32[]{:S(2)}) async-start(f32[64,1,8,512]{3,2,1,0:T(8,128)} %copy.15), calls=%async_computation.1 | async-start | bytes 2097152 | tf_op jit(solution)/shard_map/all_to_all | solution.py:152
  89.9 13.0 %collective-permute-start.12 = (f32[64,64]{1,0:T(8,128)S(1)}, f32[64,64]{1,0:T(8,128)S(1)}, u32[]{:S(2)}, u32[]{:S(2)}) collective-permute-start(f32[64,64]{1,0:T(8,128)S(1)} %fusion.29), channel_id=1, source_target_pairs={{0,3},{1,2},{2,1},{3,0},{4,7},{5,6},{6,5},{7,4},{8,11},{9,10},{10,... | collective-permute-start | bytes 49160 | tf_op jit(solution)/shard_map/ppermute | solution.py:55

commit v23 on v21

--- a/solution.py
+++ b/solution.py
@@ -86,21 +86,25 @@
             step(k, 0)
 
 
-def lower_inverse(gram):
-    n = gram.shape[0]
-    return pl.pallas_call(
-        chol_inv_kernel,
-        out_shape=jax.ShapeDtypeStruct((n, n), jnp.float32),
-        scratch_shapes=[pltpu.VMEM((n, n), jnp.float32)],
-    )(gram)
+def inverse_kernel(g_ref, o_ref, x_ref, a_ref):
+    chol_inv_kernel(g_ref, x_ref, a_ref)
+    x = x_ref[...]
+    o_ref[...] = lax.dot_general(
+        x, x, (((0,), (0,)), ((), ())), precision=lax.Precision.HIGHEST,
+        preferred_element_type=jnp.float32,
+    )
 
 
 def invert_beside(gram, extra, bits):
-    solved = lower_inverse(gram)
+    n = gram.shape[0]
+    inverse = pl.pallas_call(
+        inverse_kernel,
+        out_shape=jax.ShapeDtypeStruct((n, n), jnp.float32),
+        scratch_shapes=[pltpu.VMEM((n, n), jnp.float32), pltpu.VMEM((n, n), jnp.float32)],
+    )(gram)
     if bits:
         extra = exchange(extra, *bits.pop(0))
-    solved, extra = lax.optimization_barrier((solved, extra))
-    inverse = jnp.dot(solved.T, solved, precision=lax.Precision.HIGHEST)
+    inverse, extra = lax.optimization_barrier((inverse, extra))
     return inverse, extra
 
 

time: 107 us -> 106 us (level)
  no operation moved by 1% of the time
where the time goes in v23:
time: 106 us
  waiting for transfers between devices  43.1 us (41%)
  starting transfers between devices  34.6 us (33%)
  other arithmetic  9.57 us (9%)
  Pallas kernels  7.84 us (7%)
  local copies, waits for them, and re-layouts  6.31 us (6%)
  matrix products  3.73 us (4%)
    ppermute x9, waiting for transfers between devices, exchange(): return x + lax.ppermute(x, axis, [(i, i ^ bit) for i in range(count)])  27.3 us
    ppermute x9, starting transfers between devices, exchange(): return x + lax.ppermute(x, axis, [(i, i ^ bit) for i in range(count)])  17.7 us
    all_to_all x1, waiting for transfers between devices, body(): v = lax.all_to_all(perturbations, 'mem', 1, 0, tiled=True)  14.4 us
    pallas_call x1, Pallas kernels, invert_beside(): pl.pallas_call(inverse_kernel, out_shape=jax.ShapeDtypeStruct((n, n), jnp...  7.84 us
    all_to_all x1, starting transfers between devices, body(): v = lax.all_to_all(perturbations, 'mem', 1, 0, tiled=True)  7.04 us
    all_to_all x1, starting transfers between devices, body(): ritz = lax.all_to_all(ritz.reshape(v.shape), 'mem', 0, 1, tiled=True)  4.18 us
    ppermute x2, starting transfers between devices, halo(): lax.ppermute(lax.slice_in_dim(block, size - width, size, axis=dim), 'dom'...  3.12 us
    add x2, other arithmetic, adjoint_step(): result + shifted(coef[3] * field, 1, 3) + shifted(coef[4] * field, -1, 3)  2.94 us
  transfers between devices with their start and end apart: 15, of which 9 were waited for; matrix products, arithmetic and copies ran while one was open for 7% of the time, Pallas kernels for 7%

profile of v23, /device:TPU:0, one launch (start us, length us, event | category | flops | bytes accessed | tf_op | source)
XLA Modules:
  0.0 106.0 jit_solution(14542920876552970541)
XLA Ops:
  0.6 2.3 %copy.11 = f32[8,8,8,512]{3,2,0,1:T(8,128)} copy(f32[8,8,8,512]{3,2,1,0:T(8,128)} %param.2) | data formatting | bytes 2097152 | tf_op args[0]
  3.0 7.0 %all-to-all-start = ((f32[8,8,8,512]{3,2,0,1:T(8,128)}), f32[8,8,8,512]{3,2,0,1:T(8,128)S(1)}, u32[]{:S(2)}, u32[]{:S(2)}) async-start(f32[8,8,8,512]{3,2,0,1:T(8,128)} %copy.11), calls=%async_computation | async-start | bytes 2097152 | tf_op jit(solution)/shard_map/all_to_all | solution.py:116
  10.0 1.5 %collective-permute-start.1 = (bf16[2,5,1,4,512]{4,3,2,1,0:T(4,128)(2,1)S(1)}, bf16[2,5,1,4,512]{4,3,2,1,0:T(4,128)(2,1)S(1)}, u32[]{:S(2)}, u32[]{:S(2)}) collective-permute-start(bf16[2,5,1,4,512]{4,3,2,1,0:T(4,128)(2,1)S(1)} %get-tuple-element.42), channel_id=1, source_target_pairs={{0,8},{8,16},{16,24},{24,32},{32,40},{40,48},{48,56},{56,64},{64,7... | collective-permute-start | bytes 122888 | tf_op jit(solution)/shard_map/ppermute | solution.py:16
  11.5 1.3 %collective-permute-start.2 = (bf16[2,5,1,4,512]{4,3,2,1,0:T(4,128)(2,1)S(1)}, bf16[2,5,1,4,512]{4,3,2,1,0:T(4,128)(2,1)S(1)}, u32[]{:S(2)}, u32[]{:S(2)}) collective-permute-start(bf16[2,5,1,4,512]{4,3,2,1,0:T(4,128)(2,1)S(1)} %get-tuple-element.43), channel_id=1, source_target_pairs={{8,0},{16,8},{24,16},{32,24},{40,32},{48,40},{56,48},{64,56},{72,6... | collective-permute-start | bytes 122888 | tf_op jit(solution)/shard_map/ppermute | solution.py:17
  12.8 14.4 %all-to-all-done = f32[8,8,8,512]{3,2,0,1:T(8,128)S(1)} async-done(((f32[8,8,8,512]{3,2,0,1:T(8,128)}), f32[8,8,8,512]{3,2,0,1:T(8,128)S(1)}, u32[]{:S(2)}, u32[]{:S(2)}) %all-to-all-start) | async-done | bytes 1048608 | tf_op jit(solution)/shard_map/all_to_all | solution.py:116
  27.2 0.6 copy.31
  27.8 0.1 fusion.32
  27.9 1.7 %collective-permute-start.3 = (f32[64,1,4,512]{3,0,2,1:T(8,128)S(1)}, f32[64,1,4,512]{3,0,2,1:T(8,128)S(1)}, u32[]{:S(2)}, u32[]{:S(2)}) collective-permute-start(f32[64,1,4,512]{3,0,2,1:T(8,128)S(1)} %get-tuple-element.30), channel_id=1, source_target_pairs={{0,8},{8,16},{16,24},{24,32},{32,40},{40,48},{48,56},{56,64},{64,7... | collective-permute-start | bytes 1572872 | tf_op jit(solution)/shard_map/ppermute | solution.py:16
  29.6 1.3 %collective-permute-start.4 = (f32[64,1,4,512]{3,0,2,1:T(8,128)S(1)}, f32[64,1,4,512]{3,0,2,1:T(8,128)S(1)}, u32[]{:S(2)}, u32[]{:S(2)}) collective-permute-start(f32[64,1,4,512]{3,0,2,1:T(8,128)S(1)} %get-tuple-element.31), channel_id=1, source_target_pairs={{8,0},{16,8},{24,16},{32,24},{40,32},{48,40},{56,48},{64,56},{72,6... | collective-permute-start | bytes 1572872 | tf_op jit(solution)/shard_map/ppermute | solution.py:17
  30.9 0.0 collective-permute-done.2
  30.9 0.1 maximum_convert_fusion
  31.0 0.6 copy.18
  31.6 1.0 fusion.34
  32.6 0.6 collective-permute-start
  33.2 3.4 %collective-permute-done = f32[64,64]{1,0:T(8,128)S(1)} collective-permute-done((f32[64,64]{1,0:T(8,128)S(1)}, f32[64,64]{1,0:T(8,128)S(1)}, u32[]{:S(2)}, u32[]{:S(2)}) %collective-permute-start) | collective-permute-done | bytes 16416 | tf_op jit(solution)/shard_map/ppermute | solution.py:55
  36.6 0.0 collective-permute-done.3
  36.6 0.0 collective-permute-done.4
  36.6 0.2 pad_maximum_fusion
  36.8 1.3 %fusion.4 = f32[64,1,16,512]{3,0,2,1:T(8,128)S(1)} fusion(f32[64,1,16,512]{3,0,2,1:T(8,128)S(1)} %pad_maximum_fusion, f32[16,512]{1,0:T(8,128)S(1)} %get-tuple-element.37, f32[16,512]{1,0:T(8,128)S(1)} %get-tuple-element.38, f32[16,512]{1,0:T(8,128)S(1)} %get-tuple-element.39, f32[16,512]{1,0:T(8,128)S(1)} %get-tuple-element.40, ...), kind=kLoop, calls=%fused_computation.20 | loop fusion | flops 4718592 | bytes 4358144 | tf_op jit(solution)/shard_map/add | solution.py:33
  38.1 0.9 collective-permute-start.5
  39.0 1.3 %fusion.10 = f32[64,1,16,512]{3,0,2,1:T(8,128)S(1)} fusion(f32[64,1,16,512]{3,0,2,1:T(8,128)S(1)} %fusion.4, f32[16,512]{1,0:T(8,128)S(1)} %get-tuple-element.33, f32[16,512]{1,0:T(8,128)S(1)} %get-tuple-element.34, f32[16,512]{1,0:T(8,128)S(1)} %get-tuple-element.35, f32[16,512]{1,0:T(8,128)S(1)} %get-tuple-element.36, f32[16,512]{1,0:T(8,128)S(1)} %get-tuple-element.32), kind=kLoop, calls=%fused_computation.26 | loop fusion | flops 4718592 | bytes 4358144 | tf_op jit(solution)/shard_map/add | solution.py:33
  40.3 3.0 %collective-permute-done.5 = f32[64,64]{1,0:T(8,128)S(1)} collective-permute-done((f32[64,64]{1,0:T(8,128)S(1)}, f32[64,64]{1,0:T(8,128)S(1)}, u32[]{:S(2)}, u32[]{:S(2)}) %collective-permute-start.5) | collective-permute-done | bytes 16416 | tf_op jit(solution)/shard_map/ppermute | solution.py:55
  43.3 1.2 %broadcast_multiply_fusion = (f32[64,1,16,512]{3,0,2,1:T(8,128)S(1)}, f32[64,1,16,512]{3,0,2,1:T(8,128)S(1)}, f32[64,1,16,512]{3,0,2,1:T(8,128)S(1)}, f32[64,1,16,512]{3,0,2,1:T(8,128)S(1)}) fusion(f32[64,1,16,512]{3,0,2,1:T(8,128)S(1)} %fusion.10, f32[16,512]{1,0:T(8,128)S(1)} %get-tuple-element.33, f32[16,512]{1,0:T(8,128)S(1)} %get-tuple-element.34, ...), kind=kLoop, calls=%fused_computation.49 | loop fusion | flops 2097152 | bytes 10616832 | tf_op jit(solution)/shard_map/mul | solution.py:38
  44.5 1.0 convolution_bitcast_fusion.1
  45.5 0.6 collective-permute-start.6
  46.2 1.5 %fusion.15 = f32[64,1,16,512]{3,0,2,1:T(8,128)S(1)} fusion(f32[64,1,16,512]{3,0,2,1:T(8,128)S(1)} %get-tuple-element.29, f32[64,1,16,512]{3,0,2,1:T(8,128)S(1)} %get-tuple-element.28, f32[64,1,16,512]{3,0,2,1:T(8,128)S(1)} %get-tuple-element.27, f32[64,1,16,512]{3,0,2,1:T(8,128)S(1)} %get-tuple-element.26, f32[64,1,16,512]{3,0,2,1:T(8,128)S(1)} %fusion.10, ...), kind=kLoop, calls=%fused_computation.31 | loop fusion | flops 2621440 | bytes 12615680 | tf_op jit(solution)/shard_map/add | solution.py:38
  47.7 3.7 %collective-permute-done.6 = f32[2,64,64]{2,1,0:T(8,128)S(1)} collective-permute-done((f32[2,64,64]{2,1,0:T(8,128)S(1)}, f32[2,64,64]{2,1,0:T(8,128)S(1)}, u32[]{:S(2)}, u32[]{:S(2)}) %collective-permute-start.6) | collective-permute-done | bytes 32800 | tf_op jit(solution)/shard_map/ppermute | solution.py:55
  51.4 1.2 %broadcast_multiply_fusion.4 = (f32[64,1,16,512]{3,0,2,1:T(8,128)S(1)}, f32[64,1,16,512]{3,0,2,1:T(8,128)S(1)}, f32[64,1,16,512]{3,0,2,1:T(8,128)S(1)}, f32[64,1,16,512]{3,0,2,1:T(8,128)S(1)}) fusion(f32[64,1,16,512]{3,0,2,1:T(8,128)S(1)} %fusion.15, f32[16,512]{1,0:T(8,128)S(1)} %get-tuple-element.37, f32[16,512]{1,0:T(8,128)S(1)} %get-tuple-element.38, ...), kind=kLoop, calls=%fused_computation.53 | loop fusion | flops 2097152 | bytes 10616832 | tf_op jit(solution)/shard_map/mul | solution.py:38
  52.6 3.7 %collective-permute-start.7 = (f32[2,64,64]{2,1,0:T(8,128)S(1)}, f32[2,64,64]{2,1,0:T(8,128)S(1)}, u32[]{:S(2)}, u32[]{:S(2)}) collective-permute-start(f32[2,64,64]{2,1,0:T(8,128)S(1)} %fusion.31), channel_id=1, source_target_pairs={{0,8},{8,0},{16,24},{24,16},{32,40},{40,32},{48,56},{56,48},{64,72... | collective-permute-start | bytes 98312 | tf_op jit(solution)/shard_map/ppermute | solution.py:55
  56.4 1.4 %fusion.19 = f32[64,1,16,512]{3,0,2,1:T(8,128)S(1)} fusion(f32[64,1,16,512]{3,0,2,1:T(8,128)S(1)} %get-tuple-element.25, f32[64,1,16,512]{3,0,2,1:T(8,128)S(1)} %get-tuple-element.24, f32[64,1,16,512]{3,0,2,1:T(8,128)S(1)} %get-tuple-element.23, f32[64,1,16,512]{3,0,2,1:T(8,128)S(1)} %get-tuple-element.22, f32[64,1,16,512]{3,0,2,1:T(8,128)S(1)} %fusion.15, ...), kind=kLoop, calls=%fused_computation.35 | loop fusion | flops 2621440 | bytes 12615680 | tf_op jit(solution)/shard_map/add | solution.py:38
  57.8 0.0 collective-permute-done.7
  57.8 2.8 %collective-permute-start.8 = (f32[2,64,64]{2,1,0:T(8,128)S(1)}, f32[2,64,64]{2,1,0:T(8,128)S(1)}, u32[]{:S(2)}, u32[]{:S(2)}) collective-permute-start(f32[2,64,64]{2,1,0:T(8,128)S(1)} %add.122), channel_id=1, source_target_pairs={{0,16},{8,24},{16,0},{24,8},{32,48},{40,56},{48,32},{56,40},{64,80... | collective-permute-start | bytes 98312 | tf_op jit(solution)/shard_map/ppermute | solution.py:55
  60.7 2.7 %collective-permute-done.8 = f32[2,64,64]{2,1,0:T(8,128)S(1)} collective-permute-done((f32[2,64,64]{2,1,0:T(8,128)S(1)}, f32[2,64,64]{2,1,0:T(8,128)S(1)}, u32[]{:S(2)}, u32[]{:S(2)}) %collective-permute-start.8) | collective-permute-done | bytes 32800 | tf_op jit(solution)/shard_map/ppermute | solution.py:55
  63.3 3.9 %collective-permute-start.9 = (f32[2,64,64]{2,1,0:T(8,128)S(1)}, f32[2,64,64]{2,1,0:T(8,128)S(1)}, u32[]{:S(2)}, u32[]{:S(2)}) collective-permute-start(f32[2,64,64]{2,1,0:T(8,128)S(1)} %add.127), channel_id=1, source_target_pairs={{0,48},{8,56},{16,32},{24,40},{32,16},{40,24},{48,0},{56,8},{64,11... | collective-permute-start | bytes 98312 | tf_op jit(solution)/shard_map/ppermute | solution.py:55
  67.3 2.2 %collective-permute-done.9 = f32[2,64,64]{2,1,0:T(8,128)S(1)} collective-permute-done((f32[2,64,64]{2,1,0:T(8,128)S(1)}, f32[2,64,64]{2,1,0:T(8,128)S(1)}, u32[]{:S(2)}, u32[]{:S(2)}) %collective-permute-start.9) | collective-permute-done | bytes 32800 | tf_op jit(solution)/shard_map/ppermute | solution.py:55
  69.5 1.8 %collective-permute-start.10 = (f32[2,64,64]{2,1,0:T(8,128)S(1)}, f32[2,64,64]{2,1,0:T(8,128)S(1)}, u32[]{:S(2)}, u32[]{:S(2)}) collective-permute-start(f32[2,64,64]{2,1,0:T(8,128)S(1)} %add.128), channel_id=1, source_target_pairs={{0,64},{8,72},{16,80},{24,88},{32,96},{40,104},{48,112},{56,120},{... | collective-permute-start | bytes 98312 | tf_op jit(solution)/shard_map/ppermute | solution.py:55
  71.3 2.6 %collective-permute-done.10 = f32[2,64,64]{2,1,0:T(8,128)S(1)} collective-permute-done((f32[2,64,64]{2,1,0:T(8,128)S(1)}, f32[2,64,64]{2,1,0:T(8,128)S(1)}, u32[]{:S(2)}, u32[]{:S(2)}) %collective-permute-start.10) | collective-permute-done | bytes 32800 | tf_op jit(solution)/shard_map/ppermute | solution.py:55
  73.9 0.6 slice_bitcast_fusion
  74.5 0.0 collective-permute-start.11
  74.5 7.8 %shard_map.41 = f32[64,64]{1,0:T(8,128)} custom-call(f32[64,64]{1,0:T(8,128)} %get-tuple-element.45.g_ref), custom_call_target="tpu_custom_call" | custom-call | tf_op jit(solution)/shard_map/pallas_call | solution.py:100
  82.4 1.8 %convolution_bitcast_fusion = f32[64,1,8,512]{3,0,2,1:T(8,128)S(1)} fusion(f32[64,64]{1,0:T(8,128)} %shard_map.41, f32[64,1,16,512]{3,0,2,1:T(8,128)S(1)} %fusion.19), kind=kOutput, calls=%fused_computation.41 | convolution fusion | flops 201326592 | bytes 2113536 | tf_op jit(solution)/shard_map/dot_general | solution.py:152
  84.2 1.6 %copy.15 = f32[64,1,8,512]{3,2,1,0:T(8,128)} copy(f32[64,1,8,512]{3,0,2,1:T(8,128)S(1)} %convolution_bitcast_fusion) | data formatting | bytes 2097152 | tf_op jit(solution)/shard_map/dot_general | solution.py:152
  85.7 4.2 %all-to-all-start.1 = ((f32[64,1,8,512]{3,2,1,0:T(8,128)}), f32[64,1,8,512]{3,2,1,0:T(8,128)S(1)}, u32[]{:S(2)}, u32[]{:S(2)}) async-start(f32[64,1,8,512]{3,2,1,0:T(8,128)} %copy.15), calls=%async_computation.1 | async-start | bytes 2097152 | tf_op jit(solution)/shard_map/all_to_all | solution.py:156
  89.9 3.2 %collective-permute-start.12 = (f32[64,64]{1,0:T(8,128)S(1)}, f32[64,64]{1,0:T(8,128)S(1)}, u32[]{:S(2)}, u32[]{:S(2)}) collective-permute-start(f32[64,64]{1,0:T(8,128)S(1)} %fusion.30), channel_id=1, source_target_pairs={{0,3},{1,2},{2,1},{3,0},{4,7},{5,6},{6,5},{7,4},{8,11},{9,10},{10,... | collective-permute-start | bytes 49160 | tf_op jit(solution)/shard_map/ppermute | solution.py:55
  93.1 9.8 %collective-permute-done.12 = f32[64,64]{1,0:T(8,128)S(1)} collective-permute-done((f32[64,64]{1,0:T(8,128)S(1)}, f32[64,64]{1,0:T(8,128)S(1)}, u32[]{:S(2)}, u32[]{:S(2)}) %collective-permute-start.12) | collective-permute-done | bytes 16416 | tf_op jit(solution)/shard_map/ppermute | solution.py:55
  102.9 0.6 add_multiply_fusion
  103.5 1.4 %all-to-all-done.1 = f32[64,1,8,512]{3,2,1,0:T(8,128)S(1)} async-done(((f32[64,1,8,512]{3,2,1,0:T(8,128)}), f32[64,1,8,512]{3,2,1,0:T(8,128)S(1)}, u32[]{:S(2)}, u32[]{:S(2)}) %all-to-all-start.1) | async-done | bytes 1048608 | tf_op jit(solution)/shard_map/all_to_all | solution.py:156
  105.0 1.1 %copy.30 = f32[8,8,1,8,512]{4,3,0,1,2:T(8,128)} copy(f32[8,8,1,8,512]{4,3,1,0,2:T(8,128)S(1)} %bitcast.79) | data formatting | bytes 2097152 | tf_op jit(solution)/shard_map/all_to_all | solution.py:156
  (15 shorter events, 0.1 us)
Async XLA Ops:
  0.6 9.4 %copy-start = (bf16[2,5,1,8,512]{4,3,2,1,0:T(8,128)(2,1)S(1)}, bf16[2,5,1,8,512]{4,3,2,1,0:T(8,128)(2,1)}, u32[]{:S(2)}) copy-start(bf16[2,5,1,8,512]{4,3,2,1,0:T(8,128)(2,1)} %param.3) | copy-start | bytes 245764
  3.0 24.2 %all-to-all-start = ((f32[8,8,8,512]{3,2,0,1:T(8,128)}), f32[8,8,8,512]{3,2,0,1:T(8,128)S(1)}, u32[]{:S(2)}, u32[]{:S(2)}) async-start(f32[8,8,8,512]{3,2,0,1:T(8,128)} %copy.11), calls=%async_computation | async-start | bytes 2097152 | tf_op jit(solution)/shard_map/all_to_all | solution.py:116
  10.0 20.8 %collective-permute-start.1 = (bf16[2,5,1,4,512]{4,3,2,1,0:T(4,128)(2,1)S(1)}, bf16[2,5,1,4,512]{4,3,2,1,0:T(4,128)(2,1)S(1)}, u32[]{:S(2)}, u32[]{:S(2)}) collective-permute-start(bf16[2,5,1,4,512]{4,3,2,1,0:T(4,128)(2,1)S(1)} %get-tuple-element.42), channel_id=1, source_target_pairs={{0,8},{8,16},{16,24},{24,32},{32,40},{40,48},{48,56},{56,64},{64,7... | collective-permute-start | bytes 122888 | tf_op jit(solution)/shard_map/ppermute | solution.py:16
  11.5 19.4 %collective-permute-start.2 = (bf16[2,5,1,4,512]{4,3,2,1,0:T(4,128)(2,1)S(1)}, bf16[2,5,1,4,512]{4,3,2,1,0:T(4,128)(2,1)S(1)}, u32[]{:S(2)}, u32[]{:S(2)}) collective-permute-start(bf16[2,5,1,4,512]{4,3,2,1,0:T(4,128)(2,1)S(1)} %get-tuple-element.43), channel_id=1, source_target_pairs={{8,0},{16,8},{24,16},{32,24},{40,32},{48,40},{56,48},{64,56},{72,6... | collective-permute-start | bytes 122888 | tf_op jit(solution)/shard_map/ppermute | solution.py:17
  27.9 8.7 %collective-permute-start.3 = (f32[64,1,4,512]{3,0,2,1:T(8,128)S(1)}, f32[64,1,4,512]{3,0,2,1:T(8,128)S(1)}, u32[]{:S(2)}, u32[]{:S(2)}) collective-permute-start(f32[64,1,4,512]{3,0,2,1:T(8,128)S(1)} %get-tuple-element.30), channel_id=1, source_target_pairs={{0,8},{8,16},{16,24},{24,32},{32,40},{40,48},{48,56},{56,64},{64,7... | collective-permute-start | bytes 1572872 | tf_op jit(solution)/shard_map/ppermute | solution.py:16
  29.6 7.0 %collective-permute-start.4 = (f32[64,1,4,512]{3,0,2,1:T(8,128)S(1)}, f32[64,1,4,512]{3,0,2,1:T(8,128)S(1)}, u32[]{:S(2)}, u32[]{:S(2)}) collective-permute-start(f32[64,1,4,512]{3,0,2,1:T(8,128)S(1)} %get-tuple-element.31), channel_id=1, source_target_pairs={{8,0},{16,8},{24,16},{32,24},{40,32},{48,40},{56,48},{64,56},{72,6... | collective-permute-start | bytes 1572872 | tf_op jit(solution)/shard_map/ppermute | solution.py:17
  32.6 4.0 %collective-permute-start = (f32[64,64]{1,0:T(8,128)S(1)}, f32[64,64]{1,0:T(8,128)S(1)}, u32[]{:S(2)}, u32[]{:S(2)}) collective-permute-start(f32[64,64]{1,0:T(8,128)S(1)} %fusion.34), channel_id=1, source_target_pairs={{0,1},{1,0},{2,3},{3,2},{4,5},{5,4},{6,7},{7,6},{8,9},{9,8},{10,11... | collective-permute-start | bytes 49160 | tf_op jit(solution)/shard_map/ppermute | solution.py:55
  38.1 5.2 %collective-permute-start.5 = (f32[64,64]{1,0:T(8,128)S(1)}, f32[64,64]{1,0:T(8,128)S(1)}, u32[]{:S(2)}, u32[]{:S(2)}) collective-permute-start(f32[64,64]{1,0:T(8,128)S(1)} %add.107), channel_id=1, source_target_pairs={{0,3},{1,2},{2,1},{3,0},{4,7},{5,6},{6,5},{7,4},{8,11},{9,10},{10,... | collective-permute-start | bytes 49160 | tf_op jit(solution)/shard_map/ppermute | solution.py:55
  45.5 5.8 %collective-permute-start.6 = (f32[2,64,64]{2,1,0:T(8,128)S(1)}, f32[2,64,64]{2,1,0:T(8,128)S(1)}, u32[]{:S(2)}, u32[]{:S(2)}) collective-permute-start(f32[2,64,64]{2,1,0:T(8,128)S(1)} %pad_maximum_fusion.1), channel_id=1, source_target_pairs={{0,4},{1,5},{2,6},{3,7},{4,0},{5,1},{6,2},{7,3},{8,12},{9,13},{10,... | collective-permute-start | bytes 98312 | tf_op jit(solution)/shard_map/ppermute | solution.py:55
  52.6 5.2 %collective-permute-start.7 = (f32[2,64,64]{2,1,0:T(8,128)S(1)}, f32[2,64,64]{2,1,0:T(8,128)S(1)}, u32[]{:S(2)}, u32[]{:S(2)}) collective-permute-start(f32[2,64,64]{2,1,0:T(8,128)S(1)} %fusion.31), channel_id=1, source_target_pairs={{0,8},{8,0},{16,24},{24,16},{32,40},{40,32},{48,56},{56,48},{64,72... | collective-permute-start | bytes 98312 | tf_op jit(solution)/shard_map/ppermute | solution.py:55
  57.8 5.5 %collective-permute-start.8 = (f32[2,64,64]{2,1,0:T(8,128)S(1)}, f32[2,64,64]{2,1,0:T(8,128)S(1)}, u32[]{:S(2)}, u32[]{:S(2)}) collective-permute-start(f32[2,64,64]{2,1,0:T(8,128)S(1)} %add.122), channel_id=1, source_target_pairs={{0,16},{8,24},{16,0},{24,8},{32,48},{40,56},{48,32},{56,40},{64,80... | collective-permute-start | bytes 98312 | tf_op jit(solution)/shard_map/ppermute | solution.py:55
  63.3 6.2 %collective-permute-start.9 = (f32[2,64,64]{2,1,0:T(8,128)S(1)}, f32[2,64,64]{2,1,0:T(8,128)S(1)}, u32[]{:S(2)}, u32[]{:S(2)}) collective-permute-start(f32[2,64,64]{2,1,0:T(8,128)S(1)} %add.127), channel_id=1, source_target_pairs={{0,48},{8,56},{16,32},{24,40},{32,16},{40,24},{48,0},{56,8},{64,11... | collective-permute-start | bytes 98312 | tf_op jit(solution)/shard_map/ppermute | solution.py:55
  69.5 4.3 %collective-permute-start.10 = (f32[2,64,64]{2,1,0:T(8,128)S(1)}, f32[2,64,64]{2,1,0:T(8,128)S(1)}, u32[]{:S(2)}, u32[]{:S(2)}) collective-permute-start(f32[2,64,64]{2,1,0:T(8,128)S(1)} %add.128), channel_id=1, source_target_pairs={{0,64},{8,72},{16,80},{24,88},{32,96},{40,104},{48,112},{56,120},{... | collective-permute-start | bytes 98312 | tf_op jit(solution)/shard_map/ppermute | solution.py:55
  74.5 7.8 %collective-permute-start.11 = (f32[64,64]{1,0:T(8,128)S(1)}, f32[64,64]{1,0:T(8,128)S(1)}, u32[]{:S(2)}, u32[]{:S(2)}) collective-permute-start(f32[64,64]{1,0:T(8,128)S(1)} %get-tuple-element.44), channel_id=1, source_target_pairs={{0,1},{1,0},{2,3},{3,2},{4,5},{5,4},{6,7},{7,6},{8,9},{9,8},{10,11... | collective-permute-start | bytes 49160 | tf_op jit(solution)/shard_map/ppermute | solution.py:55
  85.7 19.2 %all-to-all-start.1 = ((f32[64,1,8,512]{3,2,1,0:T(8,128)}), f32[64,1,8,512]{3,2,1,0:T(8,128)S(1)}, u32[]{:S(2)}, u32[]{:S(2)}) async-start(f32[64,1,8,512]{3,2,1,0:T(8,128)} %copy.15), calls=%async_computation.1 | async-start | bytes 2097152 | tf_op jit(solution)/shard_map/all_to_all | solution.py:156
  89.9 13.0 %collective-permute-start.12 = (f32[64,64]{1,0:T(8,128)S(1)}, f32[64,64]{1,0:T(8,128)S(1)}, u32[]{:S(2)}, u32[]{:S(2)}) collective-permute-start(f32[64,64]{1,0:T(8,128)S(1)} %fusion.30), channel_id=1, source_target_pairs={{0,3},{1,2},{2,1},{3,0},{4,7},{5,6},{6,5},{7,4},{8,11},{9,10},{10,... | collective-permute-start | bytes 49160 | tf_op jit(solution)/shard_map/ppermute | solution.py:55

commit v24 on v23

--- a/solution.py
+++ b/solution.py
@@ -122,8 +122,7 @@
         * lax.axis_size("dom")
     )
     hi = lax.Precision.HIGHEST
-    flat_v = v.reshape(members, -1)
-    gram = jnp.dot(flat_v, flat_v.T, precision=hi)
+    gram = jnp.einsum("alij,blij->ab", v, v, precision=hi)
     pending = butterfly_bits()
     done = []
 
@@ -137,8 +136,8 @@
     field = halo(v, width, 2)
     for step in range(STEPS):
         gram, field = tick(gram, forward_step(field, coeffs[step]))
-    flat_z = field[:, :, width : width + rows, :].reshape(members, -1)
-    cross = jnp.dot(flat_z, flat_z.T, precision=hi)
+    own = field[:, :, width : width + rows, :]
+    cross = jnp.einsum("alij,blij->ab", own, own, precision=hi)
     both = jnp.stack([gram, cross])
     cross_bits = list(done)
     for step in reversed(range(STEPS)):
@@ -147,13 +146,12 @@
         both = exchange(both, *pending.pop(0))
     gram, cross = both[0], both[1]
     field = field[:, :, width : width + rows, :]
-    flat_w = field.reshape(members, -1)
     inverse, cross = invert_beside(gram / ncells_all, cross, cross_bits)
-    ritz = jnp.dot(inverse, flat_w, precision=hi)
+    ritz = jnp.einsum("ab,blij->alij", inverse, field, precision=hi)
     for axis, bit in cross_bits:
         cross = exchange(cross, axis, bit)
     projected = cross / ncells_all
-    ritz = lax.all_to_all(ritz.reshape(v.shape), "mem", 0, 1, tiled=True)
+    ritz = lax.all_to_all(ritz, "mem", 0, 1, tiled=True)
     return (ritz, projected)
 
 

time: 106 us -> 106 us (level)
  matrix products: 3.73 us -> 4.86 us
    dot_general x3, matrix products: 3.73 us -> 4.86 us  [the longest x1 2.1 us: body(): gram = jnp.einsum('alij,blij->ab', v, v, precision=hi)]
    unnamed x4 -> x3, local copies, waits for them, and re-layouts: 2.93 us -> 2.32 us
where the time goes in v24:
time: 106 us
  waiting for transfers between devices  43.1 us (41%)
  starting transfers between devices  34.1 us (32%)
  other arithmetic  9.57 us (9%)
  Pallas kernels  7.84 us (7%)
  local copies, waits for them, and re-layouts  5.7 us (5%)
  matrix products  4.86 us (5%)
    ppermute x9, waiting for transfers between devices, exchange(): return x + lax.ppermute(x, axis, [(i, i ^ bit) for i in range(count)])  27.3 us
    ppermute x9, starting transfers between devices, exchange(): return x + lax.ppermute(x, axis, [(i, i ^ bit) for i in range(count)])  17.2 us
    all_to_all x1, waiting for transfers between devices, body(): v = lax.all_to_all(perturbations, 'mem', 1, 0, tiled=True)  14.4 us
    pallas_call x1, Pallas kernels, invert_beside(): pl.pallas_call(inverse_kernel, out_shape=jax.ShapeDtypeStruct((n, n), jnp...  7.84 us
    all_to_all x1, starting transfers between devices, body(): v = lax.all_to_all(perturbations, 'mem', 1, 0, tiled=True)  7.04 us
    all_to_all x1, starting transfers between devices, body(): ritz = lax.all_to_all(ritz, 'mem', 0, 1, tiled=True)  4.18 us
    ppermute x2, starting transfers between devices, halo(): lax.ppermute(lax.slice_in_dim(block, size - width, size, axis=dim), 'dom'...  3.12 us
    add x2, other arithmetic, adjoint_step(): result + shifted(coef[3] * field, 1, 3) + shifted(coef[4] * field, -1, 3)  2.94 us
  transfers between devices with their start and end apart: 15, of which 9 were waited for; matrix products, arithmetic and copies ran while one was open for 7% of the time, Pallas kernels for 7%

profile of v24, /device:TPU:0, one launch (start us, length us, event | category | flops | bytes accessed | tf_op | source)
XLA Modules:
  0.0 106.0 jit_solution(17380467830152927558)
XLA Ops:
  0.6 2.3 %copy.7 = f32[8,8,8,512]{3,2,0,1:T(8,128)} copy(f32[8,8,8,512]{3,2,1,0:T(8,128)} %param.2) | data formatting | bytes 2097152 | tf_op args[0]
  3.0 7.0 %all-to-all-start = ((f32[8,8,8,512]{3,2,0,1:T(8,128)}), f32[8,8,8,512]{3,2,0,1:T(8,128)S(1)}, u32[]{:S(2)}, u32[]{:S(2)}) async-start(f32[8,8,8,512]{3,2,0,1:T(8,128)} %copy.7), calls=%async_computation | async-start | bytes 2097152 | tf_op jit(solution)/shard_map/all_to_all | solution.py:116
  10.0 1.5 %collective-permute-start.1 = (bf16[2,5,1,4,512]{4,3,2,1,0:T(4,128)(2,1)S(1)}, bf16[2,5,1,4,512]{4,3,2,1,0:T(4,128)(2,1)S(1)}, u32[]{:S(2)}, u32[]{:S(2)}) collective-permute-start(bf16[2,5,1,4,512]{4,3,2,1,0:T(4,128)(2,1)S(1)} %get-tuple-element.42), channel_id=1, source_target_pairs={{0,8},{8,16},{16,24},{24,32},{32,40},{40,48},{48,56},{56,64},{64,7... | collective-permute-start | bytes 122888 | tf_op jit(solution)/shard_map/ppermute | solution.py:16
  11.5 1.3 %collective-permute-start.2 = (bf16[2,5,1,4,512]{4,3,2,1,0:T(4,128)(2,1)S(1)}, bf16[2,5,1,4,512]{4,3,2,1,0:T(4,128)(2,1)S(1)}, u32[]{:S(2)}, u32[]{:S(2)}) collective-permute-start(bf16[2,5,1,4,512]{4,3,2,1,0:T(4,128)(2,1)S(1)} %get-tuple-element.43), channel_id=1, source_target_pairs={{8,0},{16,8},{24,16},{32,24},{40,32},{48,40},{56,48},{64,56},{72,6... | collective-permute-start | bytes 122888 | tf_op jit(solution)/shard_map/ppermute | solution.py:17
  12.8 14.4 %all-to-all-done = f32[8,8,8,512]{3,2,0,1:T(8,128)S(1)} async-done(((f32[8,8,8,512]{3,2,0,1:T(8,128)}), f32[8,8,8,512]{3,2,0,1:T(8,128)S(1)}, u32[]{:S(2)}, u32[]{:S(2)}) %all-to-all-start) | async-done | bytes 1048608 | tf_op jit(solution)/shard_map/all_to_all | solution.py:116
  27.2 0.6 copy.19
  27.8 0.1 fusion.34
  27.9 1.7 %collective-permute-start.3 = (f32[64,1,4,512]{3,0,2,1:T(8,128)S(1)}, f32[64,1,4,512]{3,0,2,1:T(8,128)S(1)}, u32[]{:S(2)}, u32[]{:S(2)}) collective-permute-start(f32[64,1,4,512]{3,0,2,1:T(8,128)S(1)} %get-tuple-element.30), channel_id=1, source_target_pairs={{0,8},{8,16},{16,24},{24,32},{32,40},{40,48},{48,56},{56,64},{64,7... | collective-permute-start | bytes 1572872 | tf_op jit(solution)/shard_map/ppermute | solution.py:16
  29.6 1.3 %collective-permute-start.4 = (f32[64,1,4,512]{3,0,2,1:T(8,128)S(1)}, f32[64,1,4,512]{3,0,2,1:T(8,128)S(1)}, u32[]{:S(2)}, u32[]{:S(2)}) collective-permute-start(f32[64,1,4,512]{3,0,2,1:T(8,128)S(1)} %get-tuple-element.31), channel_id=1, source_target_pairs={{8,0},{16,8},{24,16},{32,24},{40,32},{48,40},{56,48},{64,56},{72,6... | collective-permute-start | bytes 1572872 | tf_op jit(solution)/shard_map/ppermute | solution.py:17
  30.9 0.0 collective-permute-done.2
  30.9 0.1 maximum_convert_fusion
  31.0 2.1 %convolution_bitcast_fusion.2 = f32[64,64]{1,0:T(8,128)S(1)} fusion(f32[8,8,1,8,512]{4,3,1,0,2:T(8,128)S(1)} %bitcast.59), kind=kOutput, calls=%fused_computation.43 | convolution fusion | flops 201326592 | bytes 1064960 | tf_op jit(solution)/shard_map/alij,blij->ab/dot_general | solution.py:125
  33.1 0.6 collective-permute-start
  33.7 3.4 %collective-permute-done = f32[64,64]{1,0:T(8,128)S(1)} collective-permute-done((f32[64,64]{1,0:T(8,128)S(1)}, f32[64,64]{1,0:T(8,128)S(1)}, u32[]{:S(2)}, u32[]{:S(2)}) %collective-permute-start) | collective-permute-done | bytes 16416 | tf_op jit(solution)/shard_map/ppermute | solution.py:55
  37.1 0.0 collective-permute-done.3
  37.1 0.0 collective-permute-done.4
  37.1 0.2 pad_maximum_fusion
  37.3 1.3 %fusion.4 = f32[64,1,16,512]{3,0,2,1:T(8,128)S(1)} fusion(f32[64,1,16,512]{3,0,2,1:T(8,128)S(1)} %pad_maximum_fusion, f32[16,512]{1,0:T(8,128)S(1)} %get-tuple-element.37, f32[16,512]{1,0:T(8,128)S(1)} %get-tuple-element.38, f32[16,512]{1,0:T(8,128)S(1)} %get-tuple-element.39, f32[16,512]{1,0:T(8,128)S(1)} %get-tuple-element.40, ...), kind=kLoop, calls=%fused_computation.20 | loop fusion | flops 4718592 | bytes 4358144 | tf_op jit(solution)/shard_map/add | solution.py:33
  38.6 0.9 collective-permute-start.5
  39.5 1.3 %fusion.10 = f32[64,1,16,512]{3,0,2,1:T(8,128)S(1)} fusion(f32[64,1,16,512]{3,0,2,1:T(8,128)S(1)} %fusion.4, f32[16,512]{1,0:T(8,128)S(1)} %get-tuple-element.33, f32[16,512]{1,0:T(8,128)S(1)} %get-tuple-element.34, f32[16,512]{1,0:T(8,128)S(1)} %get-tuple-element.35, f32[16,512]{1,0:T(8,128)S(1)} %get-tuple-element.36, f32[16,512]{1,0:T(8,128)S(1)} %get-tuple-element.32), kind=kLoop, calls=%fused_computation.26 | loop fusion | flops 4718592 | bytes 4358144 | tf_op jit(solution)/shard_map/add | solution.py:33
  40.8 3.0 %collective-permute-done.5 = f32[64,64]{1,0:T(8,128)S(1)} collective-permute-done((f32[64,64]{1,0:T(8,128)S(1)}, f32[64,64]{1,0:T(8,128)S(1)}, u32[]{:S(2)}, u32[]{:S(2)}) %collective-permute-start.5) | collective-permute-done | bytes 16416 | tf_op jit(solution)/shard_map/ppermute | solution.py:55
  43.8 1.2 %broadcast_multiply_fusion = (f32[64,1,16,512]{3,0,2,1:T(8,128)S(1)}, f32[64,1,16,512]{3,0,2,1:T(8,128)S(1)}, f32[64,1,16,512]{3,0,2,1:T(8,128)S(1)}, f32[64,1,16,512]{3,0,2,1:T(8,128)S(1)}) fusion(f32[64,1,16,512]{3,0,2,1:T(8,128)S(1)} %fusion.10, f32[16,512]{1,0:T(8,128)S(1)} %get-tuple-element.33, f32[16,512]{1,0:T(8,128)S(1)} %get-tuple-element.34, ...), kind=kLoop, calls=%fused_computation.50 | loop fusion | flops 2097152 | bytes 10616832 | tf_op jit(solution)/shard_map/mul | solution.py:38
  45.1 1.0 convolution_bitcast_fusion.1
  46.0 0.6 collective-permute-start.6
  46.7 1.5 %fusion.15 = f32[64,1,16,512]{3,0,2,1:T(8,128)S(1)} fusion(f32[64,1,16,512]{3,0,2,1:T(8,128)S(1)} %get-tuple-element.29, f32[64,1,16,512]{3,0,2,1:T(8,128)S(1)} %get-tuple-element.28, f32[64,1,16,512]{3,0,2,1:T(8,128)S(1)} %get-tuple-element.27, f32[64,1,16,512]{3,0,2,1:T(8,128)S(1)} %get-tuple-element.26, f32[64,1,16,512]{3,0,2,1:T(8,128)S(1)} %fusion.10, ...), kind=kLoop, calls=%fused_computation.31 | loop fusion | flops 2621440 | bytes 12615680 | tf_op jit(solution)/shard_map/add | solution.py:38
  48.2 3.7 %collective-permute-done.6 = f32[2,64,64]{2,1,0:T(8,128)S(1)} collective-permute-done((f32[2,64,64]{2,1,0:T(8,128)S(1)}, f32[2,64,64]{2,1,0:T(8,128)S(1)}, u32[]{:S(2)}, u32[]{:S(2)}) %collective-permute-start.6) | collective-permute-done | bytes 32800 | tf_op jit(solution)/shard_map/ppermute | solution.py:55
  51.9 1.2 %broadcast_multiply_fusion.4 = (f32[64,1,16,512]{3,0,2,1:T(8,128)S(1)}, f32[64,1,16,512]{3,0,2,1:T(8,128)S(1)}, f32[64,1,16,512]{3,0,2,1:T(8,128)S(1)}, f32[64,1,16,512]{3,0,2,1:T(8,128)S(1)}) fusion(f32[64,1,16,512]{3,0,2,1:T(8,128)S(1)} %fusion.15, f32[16,512]{1,0:T(8,128)S(1)} %get-tuple-element.37, f32[16,512]{1,0:T(8,128)S(1)} %get-tuple-element.38, ...), kind=kLoop, calls=%fused_computation.54 | loop fusion | flops 2097152 | bytes 10616832 | tf_op jit(solution)/shard_map/mul | solution.py:38
  53.2 3.2 %collective-permute-start.7 = (f32[2,64,64]{2,1,0:T(8,128)S(1)}, f32[2,64,64]{2,1,0:T(8,128)S(1)}, u32[]{:S(2)}, u32[]{:S(2)}) collective-permute-start(f32[2,64,64]{2,1,0:T(8,128)S(1)} %fusion.33), channel_id=1, source_target_pairs={{0,8},{8,0},{16,24},{24,16},{32,40},{40,32},{48,56},{56,48},{64,72... | collective-permute-start | bytes 98312 | tf_op jit(solution)/shard_map/ppermute | solution.py:55
  56.4 1.4 %fusion.19 = f32[64,1,16,512]{3,0,2,1:T(8,128)S(1)} fusion(f32[64,1,16,512]{3,0,2,1:T(8,128)S(1)} %get-tuple-element.25, f32[64,1,16,512]{3,0,2,1:T(8,128)S(1)} %get-tuple-element.24, f32[64,1,16,512]{3,0,2,1:T(8,128)S(1)} %get-tuple-element.23, f32[64,1,16,512]{3,0,2,1:T(8,128)S(1)} %get-tuple-element.22, f32[64,1,16,512]{3,0,2,1:T(8,128)S(1)} %fusion.15, ...), kind=kLoop, calls=%fused_computation.35 | loop fusion | flops 2621440 | bytes 12615680 | tf_op jit(solution)/shard_map/add | solution.py:38
  57.8 0.0 collective-permute-done.7
  57.8 2.8 %collective-permute-start.8 = (f32[2,64,64]{2,1,0:T(8,128)S(1)}, f32[2,64,64]{2,1,0:T(8,128)S(1)}, u32[]{:S(2)}, u32[]{:S(2)}) collective-permute-start(f32[2,64,64]{2,1,0:T(8,128)S(1)} %add.122), channel_id=1, source_target_pairs={{0,16},{8,24},{16,0},{24,8},{32,48},{40,56},{48,32},{56,40},{64,80... | collective-permute-start | bytes 98312 | tf_op jit(solution)/shard_map/ppermute | solution.py:55
  60.7 2.7 %collective-permute-done.8 = f32[2,64,64]{2,1,0:T(8,128)S(1)} collective-permute-done((f32[2,64,64]{2,1,0:T(8,128)S(1)}, f32[2,64,64]{2,1,0:T(8,128)S(1)}, u32[]{:S(2)}, u32[]{:S(2)}) %collective-permute-start.8) | collective-permute-done | bytes 32800 | tf_op jit(solution)/shard_map/ppermute | solution.py:55
  63.3 3.9 %collective-permute-start.9 = (f32[2,64,64]{2,1,0:T(8,128)S(1)}, f32[2,64,64]{2,1,0:T(8,128)S(1)}, u32[]{:S(2)}, u32[]{:S(2)}) collective-permute-start(f32[2,64,64]{2,1,0:T(8,128)S(1)} %add.127), channel_id=1, source_target_pairs={{0,48},{8,56},{16,32},{24,40},{32,16},{40,24},{48,0},{56,8},{64,11... | collective-permute-start | bytes 98312 | tf_op jit(solution)/shard_map/ppermute | solution.py:55
  67.3 2.2 %collective-permute-done.9 = f32[2,64,64]{2,1,0:T(8,128)S(1)} collective-permute-done((f32[2,64,64]{2,1,0:T(8,128)S(1)}, f32[2,64,64]{2,1,0:T(8,128)S(1)}, u32[]{:S(2)}, u32[]{:S(2)}) %collective-permute-start.9) | collective-permute-done | bytes 32800 | tf_op jit(solution)/shard_map/ppermute | solution.py:55
  69.5 1.8 %collective-permute-start.10 = (f32[2,64,64]{2,1,0:T(8,128)S(1)}, f32[2,64,64]{2,1,0:T(8,128)S(1)}, u32[]{:S(2)}, u32[]{:S(2)}) collective-permute-start(f32[2,64,64]{2,1,0:T(8,128)S(1)} %add.128), channel_id=1, source_target_pairs={{0,64},{8,72},{16,80},{24,88},{32,96},{40,104},{48,112},{56,120},{... | collective-permute-start | bytes 98312 | tf_op jit(solution)/shard_map/ppermute | solution.py:55
  71.3 2.6 %collective-permute-done.10 = f32[2,64,64]{2,1,0:T(8,128)S(1)} collective-permute-done((f32[2,64,64]{2,1,0:T(8,128)S(1)}, f32[2,64,64]{2,1,0:T(8,128)S(1)}, u32[]{:S(2)}, u32[]{:S(2)}) %collective-permute-start.10) | collective-permute-done | bytes 32800 | tf_op jit(solution)/shard_map/ppermute | solution.py:55
  73.9 0.6 slice_bitcast_fusion
  74.5 0.0 collective-permute-start.11
  74.5 7.8 %shard_map.41 = f32[64,64]{1,0:T(8,128)} custom-call(f32[64,64]{1,0:T(8,128)} %get-tuple-element.45.g_ref), custom_call_target="tpu_custom_call" | custom-call | tf_op jit(solution)/shard_map/pallas_call | solution.py:100
  82.3 0.0 collective-permute-done.11
  82.4 1.8 %convolution_bitcast_fusion = f32[64,1,8,512]{3,0,2,1:T(8,128)S(1)} fusion(f32[64,1,16,512]{3,0,2,1:T(8,128)S(1)} %fusion.19, f32[64,64]{1,0:T(8,128)} %shard_map.41), kind=kOutput, calls=%fused_computation.41 | convolution fusion | flops 201326592 | bytes 2113536 | tf_op jit(solution)/shard_map/ab,blij->alij/dot_general | solution.py:150
  84.2 1.6 %copy.10 = f32[64,1,8,512]{3,2,1,0:T(8,128)} copy(f32[64,1,8,512]{3,0,2,1:T(8,128)S(1)} %convolution_bitcast_fusion) | data formatting | bytes 2097152 | tf_op jit(solution)/shard_map/ab,blij->alij/dot_general | solution.py:150
  85.7 4.2 %all-to-all-start.1 = ((f32[64,1,8,512]{3,2,1,0:T(8,128)}), f32[64,1,8,512]{3,2,1,0:T(8,128)S(1)}, u32[]{:S(2)}, u32[]{:S(2)}) async-start(f32[64,1,8,512]{3,2,1,0:T(8,128)} %copy.10), calls=%async_computation.1 | async-start | bytes 2097152 | tf_op jit(solution)/shard_map/all_to_all | solution.py:154
  89.9 3.2 %collective-permute-start.12 = (f32[64,64]{1,0:T(8,128)S(1)}, f32[64,64]{1,0:T(8,128)S(1)}, u32[]{:S(2)}, u32[]{:S(2)}) collective-permute-start(f32[64,64]{1,0:T(8,128)S(1)} %fusion.32), channel_id=1, source_target_pairs={{0,3},{1,2},{2,1},{3,0},{4,7},{5,6},{6,5},{7,4},{8,11},{9,10},{10,... | collective-permute-start | bytes 49160 | tf_op jit(solution)/shard_map/ppermute | solution.py:55
  93.1 9.8 %collective-permute-done.12 = f32[64,64]{1,0:T(8,128)S(1)} collective-permute-done((f32[64,64]{1,0:T(8,128)S(1)}, f32[64,64]{1,0:T(8,128)S(1)}, u32[]{:S(2)}, u32[]{:S(2)}) %collective-permute-start.12) | collective-permute-done | bytes 16416 | tf_op jit(solution)/shard_map/ppermute | solution.py:55
  102.9 0.6 add_multiply_fusion
  103.5 1.4 %all-to-all-done.1 = f32[64,1,8,512]{3,2,1,0:T(8,128)S(1)} async-done(((f32[64,1,8,512]{3,2,1,0:T(8,128)}), f32[64,1,8,512]{3,2,1,0:T(8,128)S(1)}, u32[]{:S(2)}, u32[]{:S(2)}) %all-to-all-start.1) | async-done | bytes 1048608 | tf_op jit(solution)/shard_map/all_to_all | solution.py:154
  105.0 1.1 %copy.18 = f32[8,8,1,8,512]{4,3,0,1,2:T(8,128)} copy(f32[8,8,1,8,512]{4,3,1,0,2:T(8,128)S(1)} %bitcast.62) | data formatting | bytes 2097152 | tf_op jit(solution)/shard_map/all_to_all | solution.py:154
  (14 shorter events, 0.1 us)
Async XLA Ops:
  0.6 9.4 %copy-start = (bf16[2,5,1,8,512]{4,3,2,1,0:T(8,128)(2,1)S(1)}, bf16[2,5,1,8,512]{4,3,2,1,0:T(8,128)(2,1)}, u32[]{:S(2)}) copy-start(bf16[2,5,1,8,512]{4,3,2,1,0:T(8,128)(2,1)} %param.3) | copy-start | bytes 245764
  3.0 24.2 %all-to-all-start = ((f32[8,8,8,512]{3,2,0,1:T(8,128)}), f32[8,8,8,512]{3,2,0,1:T(8,128)S(1)}, u32[]{:S(2)}, u32[]{:S(2)}) async-start(f32[8,8,8,512]{3,2,0,1:T(8,128)} %copy.7), calls=%async_computation | async-start | bytes 2097152 | tf_op jit(solution)/shard_map/all_to_all | solution.py:116
  10.0 20.8 %collective-permute-start.1 = (bf16[2,5,1,4,512]{4,3,2,1,0:T(4,128)(2,1)S(1)}, bf16[2,5,1,4,512]{4,3,2,1,0:T(4,128)(2,1)S(1)}, u32[]{:S(2)}, u32[]{:S(2)}) collective-permute-start(bf16[2,5,1,4,512]{4,3,2,1,0:T(4,128)(2,1)S(1)} %get-tuple-element.42), channel_id=1, source_target_pairs={{0,8},{8,16},{16,24},{24,32},{32,40},{40,48},{48,56},{56,64},{64,7... | collective-permute-start | bytes 122888 | tf_op jit(solution)/shard_map/ppermute | solution.py:16
  11.5 19.4 %collective-permute-start.2 = (bf16[2,5,1,4,512]{4,3,2,1,0:T(4,128)(2,1)S(1)}, bf16[2,5,1,4,512]{4,3,2,1,0:T(4,128)(2,1)S(1)}, u32[]{:S(2)}, u32[]{:S(2)}) collective-permute-start(bf16[2,5,1,4,512]{4,3,2,1,0:T(4,128)(2,1)S(1)} %get-tuple-element.43), channel_id=1, source_target_pairs={{8,0},{16,8},{24,16},{32,24},{40,32},{48,40},{56,48},{64,56},{72,6... | collective-permute-start | bytes 122888 | tf_op jit(solution)/shard_map/ppermute | solution.py:17
  27.9 9.2 %collective-permute-start.3 = (f32[64,1,4,512]{3,0,2,1:T(8,128)S(1)}, f32[64,1,4,512]{3,0,2,1:T(8,128)S(1)}, u32[]{:S(2)}, u32[]{:S(2)}) collective-permute-start(f32[64,1,4,512]{3,0,2,1:T(8,128)S(1)} %get-tuple-element.30), channel_id=1, source_target_pairs={{0,8},{8,16},{16,24},{24,32},{32,40},{40,48},{48,56},{56,64},{64,7... | collective-permute-start | bytes 1572872 | tf_op jit(solution)/shard_map/ppermute | solution.py:16
  29.6 7.5 %collective-permute-start.4 = (f32[64,1,4,512]{3,0,2,1:T(8,128)S(1)}, f32[64,1,4,512]{3,0,2,1:T(8,128)S(1)}, u32[]{:S(2)}, u32[]{:S(2)}) collective-permute-start(f32[64,1,4,512]{3,0,2,1:T(8,128)S(1)} %get-tuple-element.31), channel_id=1, source_target_pairs={{8,0},{16,8},{24,16},{32,24},{40,32},{48,40},{56,48},{64,56},{72,6... | collective-permute-start | bytes 1572872 | tf_op jit(solution)/shard_map/ppermute | solution.py:17
  33.1 4.0 %collective-permute-start = (f32[64,64]{1,0:T(8,128)S(1)}, f32[64,64]{1,0:T(8,128)S(1)}, u32[]{:S(2)}, u32[]{:S(2)}) collective-permute-start(f32[64,64]{1,0:T(8,128)S(1)} %convolution_bitcast_fusion.2), channel_id=1, source_target_pairs={{0,1},{1,0},{2,3},{3,2},{4,5},{5,4},{6,7},{7,6},{8,9},{9,8},{10,11... | collective-permute-start | bytes 49160 | tf_op jit(solution)/shard_map/ppermute | solution.py:55
  38.6 5.2 %collective-permute-start.5 = (f32[64,64]{1,0:T(8,128)S(1)}, f32[64,64]{1,0:T(8,128)S(1)}, u32[]{:S(2)}, u32[]{:S(2)}) collective-permute-start(f32[64,64]{1,0:T(8,128)S(1)} %add.107), channel_id=1, source_target_pairs={{0,3},{1,2},{2,1},{3,0},{4,7},{5,6},{6,5},{7,4},{8,11},{9,10},{10,... | collective-permute-start | bytes 49160 | tf_op jit(solution)/shard_map/ppermute | solution.py:55
  46.0 5.8 %collective-permute-start.6 = (f32[2,64,64]{2,1,0:T(8,128)S(1)}, f32[2,64,64]{2,1,0:T(8,128)S(1)}, u32[]{:S(2)}, u32[]{:S(2)}) collective-permute-start(f32[2,64,64]{2,1,0:T(8,128)S(1)} %pad_maximum_fusion.1), channel_id=1, source_target_pairs={{0,4},{1,5},{2,6},{3,7},{4,0},{5,1},{6,2},{7,3},{8,12},{9,13},{10,... | collective-permute-start | bytes 98312 | tf_op jit(solution)/shard_map/ppermute | solution.py:55
  53.2 4.7 %collective-permute-start.7 = (f32[2,64,64]{2,1,0:T(8,128)S(1)}, f32[2,64,64]{2,1,0:T(8,128)S(1)}, u32[]{:S(2)}, u32[]{:S(2)}) collective-permute-start(f32[2,64,64]{2,1,0:T(8,128)S(1)} %fusion.33), channel_id=1, source_target_pairs={{0,8},{8,0},{16,24},{24,16},{32,40},{40,32},{48,56},{56,48},{64,72... | collective-permute-start | bytes 98312 | tf_op jit(solution)/shard_map/ppermute | solution.py:55
  57.8 5.5 %collective-permute-start.8 = (f32[2,64,64]{2,1,0:T(8,128)S(1)}, f32[2,64,64]{2,1,0:T(8,128)S(1)}, u32[]{:S(2)}, u32[]{:S(2)}) collective-permute-start(f32[2,64,64]{2,1,0:T(8,128)S(1)} %add.122), channel_id=1, source_target_pairs={{0,16},{8,24},{16,0},{24,8},{32,48},{40,56},{48,32},{56,40},{64,80... | collective-permute-start | bytes 98312 | tf_op jit(solution)/shard_map/ppermute | solution.py:55
  63.3 6.2 %collective-permute-start.9 = (f32[2,64,64]{2,1,0:T(8,128)S(1)}, f32[2,64,64]{2,1,0:T(8,128)S(1)}, u32[]{:S(2)}, u32[]{:S(2)}) collective-permute-start(f32[2,64,64]{2,1,0:T(8,128)S(1)} %add.127), channel_id=1, source_target_pairs={{0,48},{8,56},{16,32},{24,40},{32,16},{40,24},{48,0},{56,8},{64,11... | collective-permute-start | bytes 98312 | tf_op jit(solution)/shard_map/ppermute | solution.py:55
  69.5 4.3 %collective-permute-start.10 = (f32[2,64,64]{2,1,0:T(8,128)S(1)}, f32[2,64,64]{2,1,0:T(8,128)S(1)}, u32[]{:S(2)}, u32[]{:S(2)}) collective-permute-start(f32[2,64,64]{2,1,0:T(8,128)S(1)} %add.128), channel_id=1, source_target_pairs={{0,64},{8,72},{16,80},{24,88},{32,96},{40,104},{48,112},{56,120},{... | collective-permute-start | bytes 98312 | tf_op jit(solution)/shard_map/ppermute | solution.py:55
  74.5 7.8 %collective-permute-start.11 = (f32[64,64]{1,0:T(8,128)S(1)}, f32[64,64]{1,0:T(8,128)S(1)}, u32[]{:S(2)}, u32[]{:S(2)}) collective-permute-start(f32[64,64]{1,0:T(8,128)S(1)} %get-tuple-element.44), channel_id=1, source_target_pairs={{0,1},{1,0},{2,3},{3,2},{4,5},{5,4},{6,7},{7,6},{8,9},{9,8},{10,11... | collective-permute-start | bytes 49160 | tf_op jit(solution)/shard_map/ppermute | solution.py:55
  85.7 19.2 %all-to-all-start.1 = ((f32[64,1,8,512]{3,2,1,0:T(8,128)}), f32[64,1,8,512]{3,2,1,0:T(8,128)S(1)}, u32[]{:S(2)}, u32[]{:S(2)}) async-start(f32[64,1,8,512]{3,2,1,0:T(8,128)} %copy.10), calls=%async_computation.1 | async-start | bytes 2097152 | tf_op jit(solution)/shard_map/all_to_all | solution.py:154
  89.9 13.0 %collective-permute-start.12 = (f32[64,64]{1,0:T(8,128)S(1)}, f32[64,64]{1,0:T(8,128)S(1)}, u32[]{:S(2)}, u32[]{:S(2)}) collective-permute-start(f32[64,64]{1,0:T(8,128)S(1)} %fusion.32), channel_id=1, source_target_pairs={{0,3},{1,2},{2,1},{3,0},{4,7},{5,6},{6,5},{7,4},{8,11},{9,10},{10,... | collective-permute-start | bytes 49160 | tf_op jit(solution)/shard_map/ppermute | solution.py:55
